TPU v7x, 32 devices: a whole 2x2x4 slice. The times are simulated.
32 devices in a mesh: groups: 2 (over y), picks: 4 (over z), heads: 4 (over x, core).
Axes of the slice: x: 2, y: 2, z: 4, core: 2. Of those that a mesh axis runs over, the one named last changes fastest.
Arguments:
- coords: float32 [3, 8192], P(None, ('groups', 'picks')), parts along dimension 1, may hold values from -1 to 1
- horizon_ids: int32 [8192], P(('groups', 'picks')), parts along dimension 0, may hold values from 0 to 63
- horizon_levels: float32 [128], P('groups'), parts along dimension 0, may hold values from -2 to 2
- latents: bfloat16 [512, 1024], replicated, may hold values from -960 to 960
- kv_weight: bfloat16 [3072, 2, 1024], P('picks', None, 'heads'), may hold values from -0.109375 to 0.109375
- cross_out: bfloat16 [1024, 1024], P('heads'), may hold values from -0.75 to 0.75
- norm_gains: float32 [2, 1024], replicated, may hold values from 0.1 to 1.9
- self_qkv: bfloat16 [3, 1024, 1024], P(None, None, 'heads'), may hold values from -0.1875 to 0.1875
- self_out: bfloat16 [1024, 1024], P(None, 'heads'), may hold values from -0.1875 to 0.1875
- dec_kv: bfloat16 [2, 1024, 1024], P(None, None, 'heads'), may hold values from -0.1875 to 0.1875
- dec_query: bfloat16 [3072, 1024], P('picks', 'heads'), may hold values from -0.109375 to 0.109375
- readout: float32 [1024], P('heads'), may hold values from -0.1875 to 0.1875
Outputs:
- field: float32 [8192], P(('groups', 'picks')), parts along dimension 0
- latents_out: float32 [1024, 1024], P('groups', 'heads'), parts along dimension 0
- grad_query: float32 [6144, 1024], P(('groups', 'picks'), 'heads'), parts along dimension 0
There are 2 independent parts, one for each index of `groups`. A program takes and returns all parts, laid end to end along the dimension named above; an argument that names none is the same for every part. Nothing has to cross between parts.
All inputs are finite; a program needn't handle non-finite values.
Results may differ from a plain program's by a relative error of at most 0.028.
Values may be sent and summed in bfloat16 or wider, within the bound.
No kernel may reach another device: no remote copies, remote signals or barrier semaphores. Data moves between devices by JAX's collectives and lax.ppermute only.
A program may use at most 64 MiB of HBM per device.

v0:
```python
import jax
import jax.numpy as jnp
from jax import lax
from jax.sharding import PartitionSpec as P

HEAD = 128
BANDS = 512
HORIZONS = 64


PI = 3.141592653589793
EPS = 1e-06


def encode(coords):
    freq = jnp.linspace(1.0, BANDS / 2.0, BANDS).astype(jnp.float32)
    angle = PI * freq[None, :, None] * coords[:, None, :]
    table = jnp.concatenate([jnp.sin(angle), jnp.cos(angle)], axis=0)
    return table.reshape(6 * BANDS, coords.shape[1]).T.astype(jnp.bfloat16)


def on_device(
    coords,
    horizon_ids,
    horizon_levels,
    latents,
    kv_weight,
    cross_out,
    norm_gains,
    self_qkv,
    self_out,
    dec_kv,
    dec_query,
    readout,
):
    high = lax.Precision.HIGHEST
    scale = HEAD ** (-0.5)
    count = coords.shape[1]
    width = latents.shape[1]
    lat_rows = latents.shape[0]
    local = kv_weight.shape[2]
    nheads = local // HEAD
    column = lax.axis_index("heads") * local
    enc = encode(coords)
    piece = lax.all_gather(kv_weight, "picks", axis=0, tiled=True)
    rows = enc
    keys_vals = jnp.dot(
        rows, piece.reshape(piece.shape[0], 2 * local), preferred_element_type=jnp.float32
    ).astype(jnp.bfloat16)
    keys = keys_vals[:, :local].reshape(count, nheads, HEAD)
    values = keys_vals[:, local:].reshape(count, nheads, HEAD)
    queries = lax.dynamic_slice_in_dim(latents, column, local, 1).reshape(lat_rows, nheads, HEAD)
    scores = jnp.einsum("lhc,thc->hlt", queries, keys, preferred_element_type=jnp.float32) * scale
    top = jnp.max(scores, axis=2)
    expo = jnp.exp(scores - top[:, :, None])
    total = jnp.sum(expo, axis=2)
    numer = jnp.einsum(
        "hlt,thc->hlc", expo.astype(jnp.bfloat16), values, preferred_element_type=jnp.float32
    )
    best = lax.pmax(top, "picks")
    factor = jnp.exp(top - best)
    total, numer = (
        lax.psum((total * factor).astype(jnp.bfloat16), "picks").astype(jnp.float32),
        lax.psum((numer * factor[:, :, None]).astype(jnp.bfloat16), "picks").astype(jnp.float32),
    )
    attended = (
        (numer / total[:, :, None]).transpose(1, 0, 2).reshape(lat_rows, local).astype(jnp.bfloat16)
    )
    gain_two = lax.dynamic_slice_in_dim(norm_gains[1], column, local, 0)
    partial_value = jnp.dot(attended, cross_out, preferred_element_type=jnp.float32)
    whole = latents.astype(jnp.float32) + lax.psum(
        partial_value.astype(jnp.bfloat16), "heads"
    ).astype(jnp.float32)
    power = jnp.mean(whole * whole, axis=1, keepdims=True)
    normed = (whole * lax.rsqrt(power + EPS) * norm_gains[0][None, :]).astype(jnp.bfloat16)
    state = lax.dynamic_slice_in_dim(whole, column, local, 1)
    qkv = jnp.einsum("ld,kde->kle", normed, self_qkv, preferred_element_type=jnp.float32).astype(
        jnp.bfloat16
    )
    self_q = qkv[0].reshape(lat_rows, nheads, HEAD)
    self_k = qkv[1].reshape(lat_rows, nheads, HEAD)
    self_v = qkv[2].reshape(lat_rows, nheads, HEAD)
    inner = jnp.einsum("lhc,mhc->hlm", self_q, self_k, preferred_element_type=jnp.float32) * scale
    raised = jnp.exp(inner)
    probs = (raised / jnp.sum(raised, axis=2, keepdims=True)).astype(jnp.bfloat16)
    head_out = (
        jnp.einsum("hlm,mhc->lhc", probs, self_v, preferred_element_type=jnp.float32)
        .astype(jnp.bfloat16)
        .reshape(lat_rows, local)
    )
    every_head = lax.all_gather(head_out, "heads", axis=1, tiled=True)
    latents_out = state + jnp.dot(every_head, self_out, preferred_element_type=jnp.float32)
    power_two = lax.psum(jnp.sum(latents_out * latents_out, axis=1), "heads")
    piece_two = (
        latents_out * lax.rsqrt(power_two / width + EPS)[:, None] * gain_two[None, :]
    ).astype(jnp.bfloat16)
    normed2 = lax.all_gather(piece_two, "heads", axis=1, tiled=True)
    dec = jnp.einsum("ld,kde->kle", normed2, dec_kv, preferred_element_type=jnp.float32).astype(
        jnp.bfloat16
    )
    dec_keys = dec[0].reshape(lat_rows, nheads, HEAD)
    dec_vals = dec[1].reshape(lat_rows, nheads, HEAD)
    rows = enc
    query = jnp.dot(
        rows,
        lax.all_gather(dec_query, "picks", axis=0, tiled=True),
        preferred_element_type=jnp.float32,
    ).astype(jnp.bfloat16)
    dec_q = query.reshape(count, nheads, HEAD)
    logits = jnp.einsum("thc,lhc->htl", dec_q, dec_keys, preferred_element_type=jnp.float32) * scale
    lifted = jnp.exp(logits)
    weights = lifted / jnp.sum(lifted, axis=2, keepdims=True)
    out = jnp.einsum(
        "htl,lhc->thc", weights.astype(jnp.bfloat16), dec_vals, preferred_element_type=jnp.float32
    )
    read = readout.reshape(nheads, HEAD)
    field = lax.psum(jnp.sum(out * read[None, :, :], axis=(1, 2)), "heads")
    onehot = (horizon_ids[:, None] == jnp.arange(HORIZONS, dtype=jnp.int32)[None, :]).astype(
        jnp.float32
    )
    target = jnp.sum(onehot * horizon_levels[None, :], axis=1)
    miss = field - target
    value_read = jnp.einsum("lhc,hc->hl", dec_vals.astype(jnp.float32), read, precision=high)
    dprob = miss[None, :, None] * value_read[:, None, :]
    dscore = (weights * (dprob - jnp.sum(dprob * weights, axis=2, keepdims=True))).astype(
        jnp.bfloat16
    )
    dquery = (
        (jnp.einsum("htl,lhc->thc", dscore, dec_keys, preferred_element_type=jnp.float32) * scale)
        .reshape(count, local)
        .astype(jnp.bfloat16)
    )
    rows = enc
    grad_query = lax.psum_scatter(
        jnp.dot(rows.T, dquery, preferred_element_type=jnp.float32).astype(jnp.bfloat16),
        "picks",
        scatter_dimension=0,
        tiled=True,
    ).astype(jnp.float32)
    return (field, latents_out, grad_query)


def solution(mesh):
    in_specs = (
        P(None, ("groups", "picks")),
        P(("groups", "picks")),
        P("groups"),
        P(),
        P("picks", None, "heads"),
        P("heads", None),
        P(),
        P(None, None, "heads"),
        P(None, "heads"),
        P(None, None, "heads"),
        P("picks", "heads"),
        P("heads"),
    )
    out_specs = (P(("groups", "picks")), P("groups", "heads"), P(("groups", "picks"), "heads"))
    return jax.shard_map(
        on_device, mesh=mesh, in_specs=in_specs, out_specs=out_specs, check_vma=False
    )
```

profile of v0, /device:TPU:0, one launch (start us, length us, event | category | flops | bytes accessed | tf_op | source)
XLA Modules:
  0.0 320.0 jit_solution(10722653969841569074)
XLA Ops:
  7.2 0.7 all-gather.5.cloned.1.call-update
  8.0 1.0 constant_dynamic-slice_fusion.1
  8.9 0.1 copy.87
  9.1 0.1 maximum_multiply_fusion
  9.2 23.6 %fusion = (bf16[3,512,1024]{2,1,0:T(8,128)(2,1)S(1)}, bf16[3,512,1024]{2,1,0:T(8,128)(2,1)S(1)}) fusion(f32[3,1024]{1,0:T(4,128)} %param.12, f32[512]{0:T(512)S(1)} %maximum_multiply_fusion), kind=kLoop, calls=%fused_computation.2 | loop fusion | flops 4718592 | bytes 6305792 | tf_op jit(solution)/shard_map/convert
  32.8 3.2 pad_maximum_fusion
  35.9 39.9 %all-gather.5.cloned.1.call-done = bf16[3072,2,256]{2,1,0:T(2,128)(2,1)} async-done(((bf16[768,2,256]{2,1,0:T(2,128)(2,1)}), bf16[3072,2,256]{2,1,0:T(2,128)(2,1)}) %all-gather.5.cloned.1.call-update) | async-done | bytes 3145744 | tf_op jit(solution)/shard_map/all_gather | solution.py:45
  75.8 2.6 copy.88
  78.4 1.1 copy-done.4
  79.6 3.5 %convolution_convert_fusion.2 = bf16[1024,512]{0,1:T(8,128)(2,1)S(1)} fusion(bf16[3072,1024]{1,0:T(8,128)(2,1)S(1)} %bitcast.66, bf16[3072,512]{1,0:T(8,128)(2,1)S(1)} %bitcast.71), kind=kOutput, calls=%fused_computation.34 | convolution fusion | flops 3221749760 | bytes 10485760 | tf_op jit(solution)/shard_map/dot_general | solution.py:47
  83.1 0.1 fusion.53
  83.2 2.8 multiply_reduce_fusion
  86.0 9.0 %pmax.7 = f32[2,512]{1,0:T(2,128)S(1)} all-reduce(f32[2,512]{1,0:T(2,128)S(1)} %get-tuple-element.18), channel_id=1, replica_groups=mesh['groups'=2,'picks'=4,'heads'=4] {'picks'}, use_global_device_ids=true, to_apply=%region_1.2 | all-reduce | flops 1024 | bytes 8192 | tf_op jit(solution)/shard_map/pmax | solution.py:60
  95.0 3.2 %fusion.7 = f32[2,512]{1,0:T(2,128)S(1)} fusion(f32[2,512,1024]{2,1,0:T(8,128)} %get-tuple-element.19, f32[2,512]{1,0:T(2,128)S(1)} %get-tuple-element.18), kind=kLoop, calls=%fused_computation.16 | loop fusion | flops 3144704 | bytes 4202496 | tf_op jit(solution)/shard_map/reduce_sum | solution.py:56
  98.2 0.2 copy-done.3
  98.5 1.6 fusion.38
  100.1 9.8 %psum.36 = bf16[2,512]{1,0:T(2,128)(2,1)S(1)} all-reduce(bf16[2,512]{1,0:T(2,128)(2,1)S(1)} %get-tuple-element.3), channel_id=1, replica_groups=mesh['groups'=2,'picks'=4,'heads'=4] {'picks'}, use_global_device_ids=true, to_apply=%region_4.5 | all-reduce | flops 1024 | bytes 4096 | tf_op jit(solution)/shard_map/psum | solution.py:63
  109.9 24.5 %all-reduce.3.cloned.1.call-done = bf16[2,512,128]{2,1,0:T(8,128)(2,1)} async-done(((bf16[2,512,128]{2,1,0:T(8,128)(2,1)}), bf16[2,512,128]{2,1,0:T(8,128)(2,1)}) %all-reduce.3.cloned.1.call-update) | async-done | bytes 262160 | tf_op jit(solution)/shard_map/psum | solution.py:64
  134.4 1.2 fusion.46
  135.6 0.1 copy.61
  135.8 2.5 convolution_convert_fusion.1
  138.3 0.2 all-gather.7.cloned.1.call-start
  138.5 35.7 %all-reduce.5.cloned.1.call-done = bf16[512,1024]{1,0:T(8,128)(2,1)} async-done(((bf16[512,1024]{1,0:T(8,128)(2,1)}), bf16[512,1024]{1,0:T(8,128)(2,1)}) %all-reduce.5.cloned.1.call-update) | async-done | bytes 1048592 | tf_op jit(solution)/shard_map/psum | solution.py:71
  174.3 3.0 convert_add_fusion
  177.3 1.2 fusion.30
  178.5 0.5 fusion.20
  179.1 1.2 convolution_convert_fusion.6
  180.4 0.5 all-gather.11.cloned.1.call-update
  181.0 16.6 %all-gather.7.cloned.1.call-done = bf16[512,1024]{0,1:T(8,128)(2,1)} async-done(((bf16[512,256]{0,1:T(8,128)(2,1)}), bf16[512,1024]{0,1:T(8,128)(2,1)}) %all-gather.7.cloned.1.call-update) | async-done | bytes 1048592 | tf_op jit(solution)/shard_map/all_gather | solution.py:91
  197.6 1.9 multiply_reduce_fusion.2
  199.5 5.9 %psum.38 = f32[512]{0:T(512)S(1)} all-reduce(f32[512]{0:T(512)S(1)} %get-tuple-element.22), channel_id=1, replica_groups=mesh['groups'=2,'picks'=4,'heads'=4] {'heads'}, use_global_device_ids=true, to_apply=%region_9.10 | all-reduce | flops 512 | bytes 4096 | tf_op jit(solution)/shard_map/psum | solution.py:93
  205.4 0.8 multiply_convert_fusion.1
  206.4 0.1 select_reduce_fusion
  206.5 29.7 %all-gather.11.cloned.1.call-done = bf16[3072,256]{1,0:T(8,128)(2,1)} async-done(((bf16[768,256]{1,0:T(8,128)(2,1)}), bf16[3072,256]{1,0:T(8,128)(2,1)}) %all-gather.11.cloned.1.call-update) | async-done | bytes 1572880 | tf_op jit(solution)/shard_map/all_gather | solution.py:106
  236.1 5.1 %convolution_convert_fusion.4 = bf16[1024,256]{0,1:T(8,128)(2,1)S(1)} fusion(bf16[3072,1024]{1,0:T(8,128)(2,1)} %bitcast.65, bf16[3072,256]{1,0:T(8,128)(2,1)} %all-gather.11.cloned.1.call-done), kind=kOutput, calls=%fused_computation.38 | convolution fusion | flops 1610874880 | bytes 8388608 | tf_op jit(solution)/shard_map/dot_general | solution.py:104
  241.2 12.6 %all-gather.9.cloned.1.call-done = bf16[512,1024]{1,0:T(8,128)(2,1)} async-done(((bf16[512,256]{1,0:T(8,128)(2,1)}), bf16[512,1024]{1,0:T(8,128)(2,1)}) %all-gather.9.cloned.1.call-update) | async-done | bytes 1048592 | tf_op jit(solution)/shard_map/all_gather | solution.py:97
  253.9 2.3 fusion.34
  256.2 0.8 fusion.6
  257.1 2.0 copy-done.1
  259.1 1.0 fusion.31
  260.0 5.9 %psum.39 = f32[1024]{0:T(1024)S(1)} all-reduce(f32[1024]{0:T(1024)S(1)} %fusion.31), channel_id=1, replica_groups=mesh['groups'=2,'picks'=4,'heads'=4] {'heads'}, use_global_device_ids=true, to_apply=%region_12.13 | all-reduce | flops 1024 | bytes 8192 | tf_op jit(solution)/shard_map/psum | solution.py:117
  266.0 0.2 fusion.57
  266.2 3.3 %fusion.2 = f32[2,1024]{1,0:T(2,128)S(1)} fusion(f32[2,512]{1,0:T(2,128)S(1)} %bitcast.85, f32[1024]{0:T(1024)S(1)} %sub.37, f32[2,1024]{1,0:T(2,128)S(1)} %get-tuple-element.24, f32[2,1024,512]{1,2,0:T(8,128)} %copy-done.1), kind=kLoop, calls=%fused_computation.7 | loop fusion | flops 5240832 | bytes 4218880 | tf_op jit(solution)/shard_map/reduce_sum | solution.py:125
  269.6 1.4 fusion.27
  270.9 0.6 slice-done.1
  271.5 3.1 convolution_convert_fusion
  274.7 36.5 %reduce-scatter.2.cloned.1.call-done = bf16[768,256]{1,0:T(8,128)(2,1)} async-done(((bf16[3072,256]{1,0:T(8,128)(2,1)}), bf16[768,256]{1,0:T(8,128)(2,1)}) %reduce-scatter.2.cloned.1.call-update) | async-done | bytes 393232 | tf_op jit(solution)/shard_map/reduce_scatter | solution.py:134
  311.2 1.9 convert_element_type.123
  (51 shorter events, 0.6 us)
Async XLA Ops:
  7.2 170.1 %copy-start = (bf16[3,1024,256]{2,1,0:T(8,128)(2,1)S(1)}, bf16[3,1024,256]{2,1,0:T(8,128)(2,1)}, u32[]{:S(2)}) copy-start(bf16[3,1024,256]{2,1,0:T(8,128)(2,1)} %param.19) | copy-start | bytes 4718596
  7.2 68.6 %all-gather.5.cloned.1.call-start = ((), (), s32[]{:S(2)}) async-start(), calls=%async_computation.1 | async-start | bytes 3932160 | tf_op jit(solution)/shard_map/all_gather | solution.py:45
  7.9 126.5 %all-reduce.3.cloned.1.call-start = ((), (), s32[]{:S(2)}) async-start(), calls=%async_computation.2 | async-start | bytes 524288 | tf_op jit(solution)/shard_map/psum | solution.py:64
  75.8 3.7 %copy-start.4 = (bf16[6,512,1024]{2,1,0:T(8,128)(2,1)S(1)}, bf16[6,512,1024]{2,1,0:T(8,128)(2,1)}, u32[]{:S(2)}) copy-start(bf16[6,512,1024]{2,1,0:T(8,128)(2,1)} %pad_maximum_fusion) | copy-start | bytes 18874372
  95.0 3.4 %copy-start.3 = (f32[2,512,1024]{2,1,0:T(8,128)S(1)}, f32[2,512,1024]{2,1,0:T(8,128)}, u32[]{:S(2)}) copy-start(f32[2,512,1024]{2,1,0:T(8,128)} %get-tuple-element.19) | copy-start | bytes 12582916
  98.5 40.1 %copy-start.9 = (f32[2,1024]{1,0:T(2,128)S(1)}, f32[2,1024]{1,0:T(2,128)}, u32[]{:S(2)}) copy-start(f32[2,1024]{1,0:T(2,128)} %param.18) | copy-start | bytes 24580
  98.5 75.8 %copy-start.5 = (bf16[512,1024]{1,0:T(8,128)(2,1)S(1)}, bf16[512,1024]{1,0:T(8,128)(2,1)}, u32[]{:S(2)}) copy-start(bf16[512,1024]{1,0:T(8,128)(2,1)} %param.15) | copy-start | bytes 3145732
  100.1 74.2 %all-reduce.5.cloned.1.call-start = ((), (), s32[]{:S(2)}) async-start(), calls=%async_computation.3 | async-start | bytes 2097152 | tf_op jit(solution)/shard_map/psum | solution.py:71
  138.3 59.3 %all-gather.7.cloned.1.call-start = ((), (), s32[]{:S(2)}) async-start(), calls=%async_computation.4 | async-start | bytes 1310720 | tf_op jit(solution)/shard_map/all_gather | solution.py:91
  174.3 3.0 copy-start.6
  179.1 18.5 %copy-start.13 = (bf16[1024,256]{1,0:T(8,128)(2,1)S(1)}, bf16[1024,256]{1,0:T(8,128)(2,1)}, u32[]{:S(2)}) copy-start(bf16[1024,256]{1,0:T(8,128)(2,1)} %param.20) | copy-start | bytes 1572868
  180.3 26.0 %copy-start.10 = (s32[1024]{0:T(1024)S(1)}, s32[1024]{0:T(1024)}, u32[]{:S(2)}) copy-start(s32[1024]{0:T(1024)} %param.13) | copy-start | bytes 12292
  180.3 26.0 %copy-start.12 = (f32[64]{0:T(128)S(1)}, f32[64]{0:T(128)}, u32[]{:S(2)}) copy-start(f32[64]{0:T(128)} %param.14) | copy-start | bytes 772
  180.3 55.8 %all-gather.11.cloned.1.call-start = ((), (), s32[]{:S(2)}) async-start(), calls=%async_computation.6 | async-start | bytes 1966080 | tf_op jit(solution)/shard_map/all_gather | solution.py:106
  180.9 72.9 %all-gather.9.cloned.1.call-start = ((), (), s32[]{:S(2)}) async-start(), calls=%async_computation.5 | async-start | bytes 1310720 | tf_op jit(solution)/shard_map/all_gather | solution.py:97
  199.5 41.7 %copy-start.7 = (f32[512,256]{1,0:T(8,128)}, f32[512,256]{1,0:T(8,128)S(1)}, u32[]{:S(2)}) copy-start(f32[512,256]{1,0:T(8,128)S(1)} %get-tuple-element.23) | copy-start | bytes 1572868
  206.3 104.9 %reduce-scatter.2.cloned.1.call-start = ((), (), s32[]{:S(2)}) async-start(), calls=%async_computation.7 | async-start | bytes 1966080 | tf_op jit(solution)/shard_map/reduce_scatter | solution.py:134
  241.2 17.9 %copy-start.11 = (f32[256]{0:T(256)S(1)}, f32[256]{0:T(256)}, u32[]{:S(2)}) copy-start(f32[256]{0:T(256)} %param.23) | copy-start | bytes 3076
  257.0 2.0 copy-start.1
  266.0 5.0 %copy-start.8 = (f32[1024]{0:T(1024)}, f32[1024]{0:T(1024)S(1)}, u32[]{:S(2)}) copy-start(f32[1024]{0:T(1024)S(1)} %psum.39) | copy-start | bytes 12292
  266.0 3.6 %copy-start.2 = (f32[2,1024,512]{1,2,0:T(8,128)S(1)}, f32[2,1024,512]{1,2,0:T(8,128)}, u32[]{:S(2)}) copy-start(f32[2,1024,512]{1,2,0:T(8,128)} %copy-done.1) | copy-start | bytes 12582916
  266.2 4.8 %slice-start = ((s8[6291456]{0:T(1024)(128)(4,1)}), s8[4194304]{0:T(1024)(128)(4,1)S(1)}, s32[]{:S(2)}) async-start(s8[6291456]{0:T(1024)(128)(4,1)} %bitcast.67), calls=%async_computation.8 | async-start | bytes 8388608
  269.5 2.0 slice-start.1
Sparse Core Ops, SparseCore 0:
  9.6 66.2 all-gather.4
  100.2 34.1 all-reduce.2
  138.4 35.8 all-reduce.4
  180.5 17.0 all-gather.6
  199.0 37.0 all-gather.10
  238.1 15.6 all-gather.8
  274.8 36.3 reduce-scatter.1
where the time goes:
time: 320 us
  waiting for transfers between devices  197 us (62%)
  other arithmetic  40.5 us (13%)
  blocking collectives  30.6 us (10%)
  matrix products  29.1 us (9%)
  between operations  14.4 us (4%)
  local copies, waits for them, and re-layouts  8.03 us (3%)
    all_gather x1, waiting for transfers between devices, on_device(): piece = lax.all_gather(kv_weight, 'picks', axis=0, tiled=True)  39.9 us
    reduce_scatter x1, waiting for transfers between devices, on_device(): lax.psum_scatter(jnp.dot(rows.T, dquery, preferred_element_type=jnp.float...  36.5 us
    psum x1, waiting for transfers between devices, on_device(): lax.psum(partial_value.astype(jnp.bfloat16), 'heads').astype(jnp.float32)  35.7 us
    all_gather x1, waiting for transfers between devices, on_device(): lax.all_gather(dec_query, 'picks', axis=0, tiled=True)  29.7 us
    psum x1, waiting for transfers between devices, on_device(): lax.psum((numer * factor[:, :, None]).astype(jnp.bfloat16), 'picks')  24.5 us
    another operation x1, other arithmetic  23.6 us
    all_gather x1, waiting for transfers between devices, on_device(): every_head = lax.all_gather(head_out, 'heads', axis=1, tiled=True)  16.6 us
    all_gather x1, waiting for transfers between devices, on_device(): normed2 = lax.all_gather(piece_two, 'heads', axis=1, tiled=True)  12.6 us
  transfers between devices with their start and end apart: 7, of which 7 were waited for; matrix products, arithmetic and copies ran while one was open for 11% of the time, Pallas kernels for 0%

commit v1 on v0

--- a/solution.py
+++ b/solution.py
@@ -1,3 +1,5 @@
+import functools
+
 import jax
 import jax.numpy as jnp
 from jax import lax
@@ -10,6 +12,7 @@
 
 PI = 3.141592653589793
 EPS = 1e-06
+RING_MAX = 4
 
 
 def encode(coords):
@@ -17,6 +20,20 @@
     angle = PI * freq[None, :, None] * coords[:, None, :]
     table = jnp.concatenate([jnp.sin(angle), jnp.cos(angle)], axis=0)
     return table.reshape(6 * BANDS, coords.shape[1]).T.astype(jnp.bfloat16)
+
+
+def ring_gather(x, axis, n):
+    if n == 1:
+        return x
+    if n > RING_MAX:
+        return lax.all_gather(x, axis, axis=0, tiled=True)
+    idx = lax.axis_index(axis)
+    blocks = [x]
+    for s in range(1, n):
+        blocks.append(lax.ppermute(x, axis, [(i, (i - s) % n) for i in range(n)]))
+    flipped = jnp.stack(blocks)
+    ordered = jnp.roll(flipped, idx, axis=0)
+    return ordered.reshape((n * x.shape[0],) + x.shape[1:])
 
 
 def on_device(
@@ -32,6 +49,9 @@
     dec_kv,
     dec_query,
     readout,
+    *,
+    n_picks,
+    n_heads,
 ):
     high = lax.Precision.HIGHEST
     scale = HEAD ** (-0.5)
@@ -42,10 +62,10 @@
     nheads = local // HEAD
     column = lax.axis_index("heads") * local
     enc = encode(coords)
+    cross_full = ring_gather(cross_out, "heads", n_heads)
     piece = lax.all_gather(kv_weight, "picks", axis=0, tiled=True)
-    rows = enc
     keys_vals = jnp.dot(
-        rows, piece.reshape(piece.shape[0], 2 * local), preferred_element_type=jnp.float32
+        enc, piece.reshape(piece.shape[0], 2 * local), preferred_element_type=jnp.float32
     ).astype(jnp.bfloat16)
     keys = keys_vals[:, :local].reshape(count, nheads, HEAD)
     values = keys_vals[:, local:].reshape(count, nheads, HEAD)
@@ -57,20 +77,27 @@
     numer = jnp.einsum(
         "hlt,thc->hlc", expo.astype(jnp.bfloat16), values, preferred_element_type=jnp.float32
     )
-    best = lax.pmax(top, "picks")
-    factor = jnp.exp(top - best)
-    total, numer = (
-        lax.psum((total * factor).astype(jnp.bfloat16), "picks").astype(jnp.float32),
-        lax.psum((numer * factor[:, :, None]).astype(jnp.bfloat16), "picks").astype(jnp.float32),
+    all_numer = lax.all_gather(numer.astype(jnp.bfloat16), "picks", axis=0, tiled=False)
+    all_stats = lax.all_gather(jnp.stack([top, total]), "picks", axis=0, tiled=False)
+    best = jnp.max(all_stats[:, 0], axis=0)
+    factor = jnp.exp(all_stats[:, 0] - best[None])
+    merged_total = jnp.sum(factor * all_stats[:, 1], axis=0)
+    merged_numer = jnp.einsum(
+        "phl,phlc->hlc", factor, all_numer.astype(jnp.float32), precision=high
     )
     attended = (
-        (numer / total[:, :, None]).transpose(1, 0, 2).reshape(lat_rows, local).astype(jnp.bfloat16)
+        (merged_numer / merged_total[:, :, None])
+        .transpose(1, 0, 2)
+        .reshape(lat_rows, local)
+        .astype(jnp.bfloat16)
     )
+    dq_local, attended = lax.optimization_barrier((dec_query, attended))
+    dq_full = ring_gather(dq_local, "picks", n_picks)
     gain_two = lax.dynamic_slice_in_dim(norm_gains[1], column, local, 0)
-    partial_value = jnp.dot(attended, cross_out, preferred_element_type=jnp.float32)
-    whole = latents.astype(jnp.float32) + lax.psum(
-        partial_value.astype(jnp.bfloat16), "heads"
-    ).astype(jnp.float32)
+    attended_full = lax.all_gather(attended, "heads", axis=1, tiled=True)
+    whole = latents.astype(jnp.float32) + jnp.dot(
+        attended_full, cross_full, preferred_element_type=jnp.float32
+    )
     power = jnp.mean(whole * whole, axis=1, keepdims=True)
     normed = (whole * lax.rsqrt(power + EPS) * norm_gains[0][None, :]).astype(jnp.bfloat16)
     state = lax.dynamic_slice_in_dim(whole, column, local, 1)
@@ -90,22 +117,17 @@
     )
     every_head = lax.all_gather(head_out, "heads", axis=1, tiled=True)
     latents_out = state + jnp.dot(every_head, self_out, preferred_element_type=jnp.float32)
+    gained = (latents_out * gain_two[None, :]).astype(jnp.bfloat16)
+    gained_full = lax.all_gather(gained, "heads", axis=1, tiled=True)
     power_two = lax.psum(jnp.sum(latents_out * latents_out, axis=1), "heads")
-    piece_two = (
-        latents_out * lax.rsqrt(power_two / width + EPS)[:, None] * gain_two[None, :]
+    row_scale = lax.rsqrt(power_two / width + EPS)
+    dec = (
+        jnp.einsum("ld,kde->kle", gained_full, dec_kv, preferred_element_type=jnp.float32)
+        * row_scale[None, :, None]
     ).astype(jnp.bfloat16)
-    normed2 = lax.all_gather(piece_two, "heads", axis=1, tiled=True)
-    dec = jnp.einsum("ld,kde->kle", normed2, dec_kv, preferred_element_type=jnp.float32).astype(
-        jnp.bfloat16
-    )
     dec_keys = dec[0].reshape(lat_rows, nheads, HEAD)
     dec_vals = dec[1].reshape(lat_rows, nheads, HEAD)
-    rows = enc
-    query = jnp.dot(
-        rows,
-        lax.all_gather(dec_query, "picks", axis=0, tiled=True),
-        preferred_element_type=jnp.float32,
-    ).astype(jnp.bfloat16)
+    query = jnp.dot(enc, dq_full, preferred_element_type=jnp.float32).astype(jnp.bfloat16)
     dec_q = query.reshape(count, nheads, HEAD)
     logits = jnp.einsum("thc,lhc->htl", dec_q, dec_keys, preferred_element_type=jnp.float32) * scale
     lifted = jnp.exp(logits)
@@ -130,9 +152,8 @@
         .reshape(count, local)
         .astype(jnp.bfloat16)
     )
-    rows = enc
     grad_query = lax.psum_scatter(
-        jnp.dot(rows.T, dquery, preferred_element_type=jnp.float32).astype(jnp.bfloat16),
+        jnp.dot(enc.T, dquery, preferred_element_type=jnp.float32).astype(jnp.bfloat16),
         "picks",
         scatter_dimension=0,
         tiled=True,
@@ -156,6 +177,7 @@
         P("heads"),
     )
     out_specs = (P(("groups", "picks")), P("groups", "heads"), P(("groups", "picks"), "heads"))
-    return jax.shard_map(
-        on_device, mesh=mesh, in_specs=in_specs, out_specs=out_specs, check_vma=False
+    body = functools.partial(
+        on_device, n_picks=mesh.shape["picks"], n_heads=mesh.shape["heads"]
     )
+    return jax.shard_map(body, mesh=mesh, in_specs=in_specs, out_specs=out_specs, check_vma=False)

time: 320 us -> 273 us (0.85)
  waiting for transfers between devices: 197 us -> 124 us
  local copies, waits for them, and re-layouts: 8.03 us -> 31.4 us
  starting transfers between devices: 0.46 us -> 6.54 us
  blocking collectives: 30.6 us -> 25.6 us
  matrix products: 29.1 us -> 33.8 us
  other arithmetic: 40.5 us -> 36.1 us
    psum x2 -> x0, waiting for transfers between devices: 60.3 us -> none  [the longest x1 35.7 us: on_device(): lax.psum(partial_value.astype(jnp.bfloat16), 'heads').astype(jnp.float32)]
    ppermute x0 -> x6, waiting for transfers between devices: none -> 41.8 us  [ring_gather(): blocks.append(lax.ppermute(x, axis, [(i, (i - s) % n) for i in range(n)]))]
    all_gather x2 -> x3, waiting for transfers between devices: 42.3 us -> 5.27 us  [the longest x1 4.75 us: on_device(): attended_full = lax.all_gather(attended, 'heads', axis=1, tiled=True)]
    all_gather x1, waiting for transfers between devices: 16.6 us -> 0.01 us  [on_device(): every_head = lax.all_gather(head_out, 'heads', axis=1, tiled=True)]
    unnamed x34 -> x53, local copies, waits for them, and re-layouts: 6.73 us -> 21.8 us
    all_gather x0 -> x1, blocking collectives: none -> 13.3 us  [on_device(): lax.all_gather(jnp.stack([top, total]), 'picks', axis=0, tiled=False)]
    psum x1 -> x0, blocking collectives: 9.77 us -> none  [on_device(): lax.psum((total * factor).astype(jnp.bfloat16), 'picks').astype(jnp.float32)]
    pmax x1 -> x0, blocking collectives: 9.03 us -> none  [on_device(): best = lax.pmax(top, 'picks')]
  transfers between devices with their start and end apart: 7 -> 12, of which waited for: 7 -> 7; matrix products, arithmetic and copies ran while one was open for 11% -> 24% of each run, Pallas kernels for 0% -> 0%
where the time goes in v1:
time: 273 us; the launch traced here: 272 us
  waiting for transfers between devices  124 us (45%)
  other arithmetic  36.1 us (13%)
  matrix products  33.8 us (12%)
  local copies, waits for them, and re-layouts  31.4 us (12%)
  blocking collectives  25.6 us (9%)
  between operations  14.5 us (5%)
  starting transfers between devices  6.54 us (2%)
    ppermute x6, waiting for transfers between devices, ring_gather(): blocks.append(lax.ppermute(x, axis, [(i, (i - s) % n) for i in range(n)]))  41.8 us
    all_gather x1, waiting for transfers between devices, on_device(): piece = lax.all_gather(kv_weight, 'picks', axis=0, tiled=True)  39.9 us
    reduce_scatter x1, waiting for transfers between devices, on_device(): lax.psum_scatter(jnp.dot(enc.T, dquery, preferred_element_type=jnp.float3...  36.4 us
    another operation x1, other arithmetic  23.6 us
    unnamed x53, local copies, waits for them, and re-layouts  21.8 us
    all_gather x1, blocking collectives, on_device(): lax.all_gather(jnp.stack([top, total]), 'picks', axis=0, tiled=False)  13.3 us
    psum x1, blocking collectives, on_device(): power_two = lax.psum(jnp.sum(latents_out * latents_out, axis=1), 'heads')  6.34 us
    ppermute x6, starting transfers between devices, ring_gather(): blocks.append(lax.ppermute(x, axis, [(i, (i - s) % n) for i in range(n)]))  6.3 us
  transfers between devices with their start and end apart: 12, of which 7 were waited for; matrix products, arithmetic and copies ran while one was open for 24% of the time, Pallas kernels for 0%

profile of v1, /device:TPU:0, one launch (start us, length us, event | category | flops | bytes accessed | tf_op | source)
XLA Modules:
  0.0 272.0 jit_solution(7602422129302060528)
XLA Ops:
  8.0 1.0 constant_dynamic-slice_fusion.3
  9.2 23.6 %fusion = (bf16[3,512,1024]{2,1,0:T(8,128)(2,1)S(1)}, bf16[3,512,1024]{2,1,0:T(8,128)(2,1)S(1)}) fusion(f32[3,1024]{1,0:T(4,128)} %param.12, f32[512]{0:T(512)S(1)} %maximum_multiply_fusion), kind=kLoop, calls=%fused_computation.2 | loop fusion | flops 4718592 | bytes 6305792 | tf_op jit(solution)/shard_map/convert
  32.8 3.2 %pad_maximum_fusion = bf16[6,512,1024]{2,1,0:T(8,128)(2,1)} fusion(bf16[3,512,1024]{2,1,0:T(8,128)(2,1)S(1)} %get-tuple-element.19, bf16[3,512,1024]{2,1,0:T(8,128)(2,1)S(1)} %get-tuple-element.18), kind=kLoop, calls=%fused_computation.4 | loop fusion | flops 3145728 | bytes 12582912 | tf_op jit(solution)/shard_map/concatenate | solution.py:21
  36.0 39.9 %all-gather.8.cloned.1.call-done = bf16[3072,2,256]{2,1,0:T(2,128)(2,1)} async-done(((bf16[768,2,256]{2,1,0:T(2,128)(2,1)}), bf16[3072,2,256]{2,1,0:T(2,128)(2,1)}) %all-gather.8.cloned.1.call-update) | async-done | bytes 3145744 | tf_op jit(solution)/shard_map/all_gather | solution.py:66
  75.8 2.6 copy.98
  78.4 1.1 copy-done.5
  79.6 3.5 %convolution_convert_fusion.1 = bf16[1024,512]{0,1:T(8,128)(2,1)S(1)} fusion(bf16[3072,1024]{1,0:T(8,128)(2,1)S(1)} %bitcast.122, bf16[3072,512]{1,0:T(8,128)(2,1)S(1)} %bitcast.127), kind=kOutput, calls=%fused_computation.33 | convolution fusion | flops 3221749760 | bytes 10485760 | tf_op jit(solution)/shard_map/dot_general | solution.py:67
  83.2 0.8 multiply_reduce_fusion
  84.1 2.0 copy-done.2
  86.1 1.6 fusion.36
  87.8 0.9 collective-permute-start
  89.5 0.8 bitcast_dynamic-update-slice_fusion.6
  90.4 10.5 %collective-permute-done = bf16[256,1024]{1,0:T(8,128)(2,1)S(1)} collective-permute-done((bf16[256,1024]{1,0:T(8,128)(2,1)S(1)}, bf16[256,1024]{1,0:T(8,128)(2,1)S(1)}, u32[]{:S(2)}, u32[]{:S(2)}) %collective-permute-start) | collective-permute-done | bytes 524320 | tf_op jit(solution)/shard_map/ppermute | solution.py:33
  100.8 0.8 bitcast_dynamic-update-slice_fusion.4
  101.7 3.1 %fusion.7 = f32[2,512]{1,0:T(2,128)S(1)} fusion(f32[2,512,1024]{2,1,0:T(8,128)} %copy-done.2, f32[2,512]{1,0:T(2,128)S(1)} %get-tuple-element.22), kind=kLoop, calls=%fused_computation.16 | loop fusion | flops 3144704 | bytes 4202496 | tf_op jit(solution)/shard_map/reduce_sum | solution.py:76
  104.8 13.3 %all-gather.1 = f32[8,2,512]{2,1,0:T(2,128)S(1)} all-gather(f32[2,2,512]{2,1,0:T(2,128)S(1)} %pad_maximum_fusion.1), channel_id=3, replica_groups=mesh['groups'=2,'picks'=4,'heads'=4] {'picks'}, dimensions={0}, use_global_device_ids=true | all-gather | bytes 40960 | tf_op jit(solution)/shard_map/all_gather | solution.py:81
  118.1 1.0 copy.81
  119.3 5.3 %fusion.44 = f32[512,2,1,128]{3,2,1,0:T(1,128)S(1)} fusion(f32[4,2,512,1]{0,3,1,2:T(1,128)} %copy.81, bf16[4,2,512,128]{3,2,1,0:T(8,128)(2,1)} %bitcast.156), kind=kOutput, calls=%fused_computation.51 | convolution fusion | flops 6291456 | bytes 1589248 | tf_op jit(solution)/shard_map/phl,phlc->hlc/dot_general | solution.py:85
  126.2 0.8 bitcast_dynamic-update-slice_fusion.2
  127.0 1.9 bitcast_dynamic-update-slice_fusion
  128.9 0.9 bitcast_dynamic-update-slice_fusion.7
  129.8 0.8 bitcast_dynamic-update-slice_fusion.5
  130.6 0.9 bitcast_dynamic-update-slice_fusion.3
  131.5 1.9 bitcast_dynamic-update-slice_fusion.1
  133.3 3.1 %constant_dynamic-slice_fusion.2 = bf16[4,256,1024]{2,1,0:T(8,128)(2,1)} fusion(bf16[8,256,1024]{2,1,0:T(8,128)(2,1)} %bitcast_dynamic-update-slice_fusion.1, s32[]{:T(128)S(6)} %select_n.30), kind=kLoop, calls=%fused_computation.93 | loop fusion | bytes 4194308 | tf_op jit(solution)/shard_map/jit(_roll_dynamic)/dynamic_slice | solution.py:35
  136.4 4.8 %all-gather.10.cloned.1.call-done = bf16[512,1024]{1,0:T(8,128)(2,1)} async-done(((bf16[512,256]{1,0:T(8,128)(2,1)}), bf16[512,1024]{1,0:T(8,128)(2,1)}) %all-gather.10.cloned.1.call-update) | async-done | bytes 1048592 | tf_op jit(solution)/shard_map/all_gather | solution.py:97
  141.2 3.5 %multiply_reduce_fusion.1 = (f32[512]{0:T(512)S(1)}, f32[512,1024]{1,0:T(8,128)S(1)}) fusion(bf16[512,1024]{1,0:T(8,128)(2,1)} %all-gather.10.cloned.1.call-done, bf16[1024,1024]{1,0:T(8,128)(2,1)} %bitcast.128, bf16[512,1024]{1,0:T(8,128)(2,1)} %param.15), kind=kOutput, calls=%fused_computation.28 | convolution fusion | flops 1075838464 | bytes 6293504 | tf_op jit(solution)/shard_map/dot_general | solution.py:98
  144.7 1.1 fusion.31
  146.5 1.2 convolution_convert_fusion.4
  147.8 3.4 %collective-permute-start.3 = (bf16[768,256]{1,0:T(8,128)(2,1)S(1)}, bf16[768,256]{1,0:T(8,128)(2,1)S(1)}, u32[]{:S(2)}, u32[]{:S(2)}) collective-permute-start(bf16[768,256]{1,0:T(8,128)(2,1)S(1)} %copy-done.7), channel_id=1, source_target_pairs={{0,12},{4,0},{8,4},{12,8},{1,13},{5,1},{9,5},{13,9},{2,14},{6,2},{... | collective-permute-start | bytes 1179656 | tf_op jit(solution)/shard_map/ppermute | solution.py:33
  151.4 1.1 collective-permute-start.5
  153.3 7.5 %collective-permute-done.3 = bf16[768,256]{1,0:T(8,128)(2,1)S(1)} collective-permute-done((bf16[768,256]{1,0:T(8,128)(2,1)S(1)}, bf16[768,256]{1,0:T(8,128)(2,1)S(1)}, u32[]{:S(2)}, u32[]{:S(2)}) %collective-permute-start.3) | collective-permute-done | bytes 393248 | tf_op jit(solution)/shard_map/ppermute | solution.py:33
  161.5 23.8 %collective-permute-done.4 = bf16[768,256]{1,0:T(8,128)(2,1)S(1)} collective-permute-done((bf16[768,256]{1,0:T(8,128)(2,1)S(1)}, bf16[768,256]{1,0:T(8,128)(2,1)S(1)}, u32[]{:S(2)}, u32[]{:S(2)}) %collective-permute-start.4) | collective-permute-done | bytes 393248 | tf_op jit(solution)/shard_map/ppermute | solution.py:33
  187.7 2.7 multiply_reduce_fusion.2
  190.5 0.8 bitcast_dynamic-update-slice_fusion.13
  193.0 1.5 constant_dynamic-slice_fusion
  194.5 5.0 %convolution_convert_fusion.3 = bf16[1024,256]{0,1:T(8,128)(2,1)S(1)} fusion(bf16[3072,1024]{1,0:T(8,128)(2,1)} %bitcast.121, bf16[3072,256]{1,0:T(8,128)(2,1)S(1)} %bitcast.130), kind=kOutput, calls=%fused_computation.39 | convolution fusion | flops 1610874880 | bytes 8388608 | tf_op jit(solution)/shard_map/dot_general | solution.py:130
  199.5 6.3 %psum.14 = f32[512]{0:T(512)S(1)} all-reduce(f32[512]{0:T(512)S(1)} %get-tuple-element.14), channel_id=1, replica_groups=mesh['groups'=2,'picks'=4,'heads'=4] {'heads'}, use_global_device_ids=true, to_apply=%region_7.8 | all-reduce | flops 512 | bytes 4096 | tf_op jit(solution)/shard_map/psum | solution.py:122
  206.3 2.0 fusion.35
  208.4 0.8 fusion.6
  209.2 2.0 copy-done.3
  211.2 1.0 fusion.32
  212.2 5.9 %psum.15 = f32[1024]{0:T(1024)S(1)} all-reduce(f32[1024]{0:T(1024)S(1)} %fusion.32), channel_id=1, replica_groups=mesh['groups'=2,'picks'=4,'heads'=4] {'heads'}, use_global_device_ids=true, to_apply=%region_10.11 | all-reduce | flops 1024 | bytes 8192 | tf_op jit(solution)/shard_map/psum | solution.py:139
  218.4 3.3 %fusion.2 = f32[2,1024]{1,0:T(2,128)S(1)} fusion(f32[2,512]{1,0:T(2,128)S(1)} %bitcast.149, f32[1024]{0:T(1024)S(1)} %sub.53, f32[2,1024]{1,0:T(2,128)S(1)} %get-tuple-element.29, f32[2,1024,512]{1,2,0:T(8,128)} %copy-done.3), kind=kLoop, calls=%fused_computation.7 | loop fusion | flops 5240832 | bytes 4218880 | tf_op jit(solution)/shard_map/reduce_sum | solution.py:147
  221.7 1.4 fusion.28
  223.7 3.1 %convolution_convert_fusion = bf16[3072,256]{1,0:T(8,128)(2,1)} fusion(bf16[3072,1024]{1,0:T(8,128)(2,1)S(1)} %bitcast.125, bf16[1024,256]{0,1:T(8,128)(2,1)S(1)} %bitcast.157), kind=kOutput, calls=%fused_computation.13 | convolution fusion | flops 1611399168 | bytes 8388608 | tf_op jit(solution)/shard_map/dot_general | solution.py:156
  226.8 36.4 %reduce-scatter.2.cloned.1.call-done = bf16[768,256]{1,0:T(8,128)(2,1)} async-done(((bf16[3072,256]{1,0:T(8,128)(2,1)}), bf16[768,256]{1,0:T(8,128)(2,1)}) %reduce-scatter.2.cloned.1.call-update) | async-done | bytes 393232 | tf_op jit(solution)/shard_map/reduce_scatter | solution.py:155
  263.2 1.9 convert_element_type.100
  (83 shorter events, 11.6 us)
Async XLA Ops:
  7.2 137.6 %copy-start = (bf16[3,1024,256]{2,1,0:T(8,128)(2,1)S(1)}, bf16[3,1024,256]{2,1,0:T(8,128)(2,1)}, u32[]{:S(2)}) copy-start(bf16[3,1024,256]{2,1,0:T(8,128)(2,1)} %param.19) | copy-start | bytes 4718596
  7.2 68.7 %all-gather.8.cloned.1.call-start = ((), (), s32[]{:S(2)}) async-start(), calls=%async_computation.1 | async-start | bytes 3932160 | tf_op jit(solution)/shard_map/all_gather | solution.py:66
  7.9 111.4 %all-gather.16.cloned.1.call-start = ((), (), s32[]{:S(2)}) async-start(), calls=%async_computation.6 | async-start | bytes 1310720 | tf_op jit(solution)/shard_map/all_gather | solution.py:80
  75.8 3.7 %copy-start.5 = (bf16[6,512,1024]{2,1,0:T(8,128)(2,1)S(1)}, bf16[6,512,1024]{2,1,0:T(8,128)(2,1)}, u32[]{:S(2)}) copy-start(bf16[6,512,1024]{2,1,0:T(8,128)(2,1)} %pad_maximum_fusion) | copy-start | bytes 18874372
  83.2 4.6 %copy-start.6 = (bf16[256,1024]{1,0:T(8,128)(2,1)S(1)}, bf16[256,1024]{1,0:T(8,128)(2,1)}, u32[]{:S(2)}) copy-start(bf16[256,1024]{1,0:T(8,128)(2,1)} %param.17) | copy-start | bytes 1572868
  83.2 6.3 %copy-start.9 = (f32[2,1024]{1,0:T(2,128)S(1)}, f32[2,1024]{1,0:T(2,128)}, u32[]{:S(2)}) copy-start(f32[2,1024]{1,0:T(2,128)} %param.18) | copy-start | bytes 24580
  84.1 2.0 copy-start.2
  87.7 53.5 %all-gather.10.cloned.1.call-start = ((), (), s32[]{:S(2)}) async-start(), calls=%async_computation.2 | async-start | bytes 1310720 | tf_op jit(solution)/shard_map/all_gather | solution.py:97
  87.8 13.1 %collective-permute-start = (bf16[256,1024]{1,0:T(8,128)(2,1)S(1)}, bf16[256,1024]{1,0:T(8,128)(2,1)S(1)}, u32[]{:S(2)}, u32[]{:S(2)}) collective-permute-start(bf16[256,1024]{1,0:T(8,128)(2,1)S(1)} %copy-done.6), channel_id=1, source_target_pairs={{0,3},{1,0},{2,1},{3,2},{4,7},{5,4},{6,5},{7,6},{8,11},{9,8},{10,9... | collective-permute-start | bytes 1572872 | tf_op jit(solution)/shard_map/ppermute | solution.py:33
  88.7 37.5 %collective-permute-start.1 = (bf16[256,1024]{1,0:T(8,128)(2,1)S(1)}, bf16[256,1024]{1,0:T(8,128)(2,1)S(1)}, u32[]{:S(2)}, u32[]{:S(2)}) collective-permute-start(bf16[256,1024]{1,0:T(8,128)(2,1)S(1)} %copy-done.6), channel_id=1, source_target_pairs={{0,2},{1,3},{2,0},{3,1},{4,6},{5,7},{6,4},{7,5},{8,10},{9,11},{10,... | collective-permute-start | bytes 1572872 | tf_op jit(solution)/shard_map/ppermute | solution.py:33
  89.4 37.7 %collective-permute-start.2 = (bf16[256,1024]{1,0:T(8,128)(2,1)S(1)}, bf16[256,1024]{1,0:T(8,128)(2,1)}, u32[]{:S(2)}, u32[]{:S(2)}) collective-permute-start(bf16[256,1024]{1,0:T(8,128)(2,1)S(1)} %copy-done.6), channel_id=1, source_target_pairs={{0,1},{1,2},{2,3},{3,0},{4,5},{5,6},{6,7},{7,4},{8,9},{9,10},{10,1... | collective-permute-start | bytes 1572872 | tf_op jit(solution)/shard_map/ppermute | solution.py:33
  126.1 61.6 %all-gather.12.cloned.1.call-start = ((), (), s32[]{:S(2)}) async-start(), calls=%async_computation.3 | async-start | bytes 1310720 | tf_op jit(solution)/shard_map/all_gather | solution.py:118
  144.7 1.8 copy-start.15
  146.5 1.4 copy-start.7
  146.5 4.7 %copy-start.10 = (s32[1024]{0:T(1024)S(1)}, s32[1024]{0:T(1024)}, u32[]{:S(2)}) copy-start(s32[1024]{0:T(1024)} %param.13) | copy-start | bytes 12292
  146.5 4.7 %copy-start.12 = (f32[64]{0:T(128)S(1)}, f32[64]{0:T(128)}, u32[]{:S(2)}) copy-start(f32[64]{0:T(128)} %param.14) | copy-start | bytes 772
  147.7 40.0 %copy-start.14 = (bf16[1024,256]{1,0:T(8,128)(2,1)S(1)}, bf16[1024,256]{1,0:T(8,128)(2,1)}, u32[]{:S(2)}) copy-start(bf16[1024,256]{1,0:T(8,128)(2,1)} %param.20) | copy-start | bytes 1572868
  147.8 58.6 %all-gather.14.cloned.1.call-start = ((), (), s32[]{:S(2)}) async-start(), calls=%async_computation.4 | async-start | bytes 1310720 | tf_op jit(solution)/shard_map/all_gather | solution.py:121
  147.8 12.9 %collective-permute-start.3 = (bf16[768,256]{1,0:T(8,128)(2,1)S(1)}, bf16[768,256]{1,0:T(8,128)(2,1)S(1)}, u32[]{:S(2)}, u32[]{:S(2)}) collective-permute-start(bf16[768,256]{1,0:T(8,128)(2,1)S(1)} %copy-done.7), channel_id=1, source_target_pairs={{0,12},{4,0},{8,4},{12,8},{1,13},{5,1},{9,5},{13,9},{2,14},{6,2},{... | collective-permute-start | bytes 1179656 | tf_op jit(solution)/shard_map/ppermute | solution.py:33
  151.3 34.0 %collective-permute-start.4 = (bf16[768,256]{1,0:T(8,128)(2,1)S(1)}, bf16[768,256]{1,0:T(8,128)(2,1)S(1)}, u32[]{:S(2)}, u32[]{:S(2)}) collective-permute-start(bf16[768,256]{1,0:T(8,128)(2,1)S(1)} %copy-done.7), channel_id=1, source_target_pairs={{0,8},{4,12},{8,0},{12,4},{1,9},{5,13},{9,1},{13,5},{2,10},{6,14},... | collective-permute-start | bytes 1179656 | tf_op jit(solution)/shard_map/ppermute | solution.py:33
  151.4 34.7 %collective-permute-start.5 = (bf16[768,256]{1,0:T(8,128)(2,1)S(1)}, bf16[768,256]{1,0:T(8,128)(2,1)S(1)}, u32[]{:S(2)}, u32[]{:S(2)}) collective-permute-start(bf16[768,256]{1,0:T(8,128)(2,1)S(1)} %copy-done.7), channel_id=1, source_target_pairs={{0,4},{4,8},{8,12},{12,0},{1,5},{5,9},{9,13},{13,1},{2,6},{6,10},{... | collective-permute-start | bytes 1179656 | tf_op jit(solution)/shard_map/ppermute | solution.py:33
  190.5 72.8 %reduce-scatter.2.cloned.1.call-start = ((), (), s32[]{:S(2)}) async-start(), calls=%async_computation.5 | async-start | bytes 1966080 | tf_op jit(solution)/shard_map/reduce_scatter | solution.py:155
  194.5 11.8 %copy-start.13 = (bf16[2,1024,256]{2,1,0:T(8,128)(2,1)S(1)}, bf16[2,1024,256]{2,1,0:T(8,128)(2,1)}, u32[]{:S(2)}) copy-start(bf16[2,1024,256]{2,1,0:T(8,128)(2,1)} %param.21) | copy-start | bytes 3145732
  205.8 5.4 %copy-start.11 = (f32[256]{0:T(256)S(1)}, f32[256]{0:T(256)}, u32[]{:S(2)}) copy-start(f32[256]{0:T(256)} %param.23) | copy-start | bytes 3076
  209.2 2.0 copy-start.3
  218.1 5.0 %copy-start.8 = (f32[1024]{0:T(1024)}, f32[1024]{0:T(1024)S(1)}, u32[]{:S(2)}) copy-start(f32[1024]{0:T(1024)S(1)} %psum.15) | copy-start | bytes 12292
  218.1 3.6 %copy-start.4 = (f32[2,1024,512]{1,2,0:T(8,128)S(1)}, f32[2,1024,512]{1,2,0:T(8,128)}, u32[]{:S(2)}) copy-start(f32[2,1024,512]{1,2,0:T(8,128)} %copy-done.3) | copy-start | bytes 12582916
  218.3 4.8 %slice-start = ((s8[6291456]{0:T(1024)(128)(4,1)}), s8[4194304]{0:T(1024)(128)(4,1)S(1)}, s32[]{:S(2)}) async-start(s8[6291456]{0:T(1024)(128)(4,1)} %bitcast.123), calls=%async_computation.7 | async-start | bytes 8388608
  221.7 2.0 slice-start.1
  223.1 42.1 %copy-start.1 = (bf16[3,1024,256]{2,1,0:T(8,128)(2,1)S(1)}, bf16[3,1024,256]{2,1,0:T(8,128)(2,1)}, u32[]{:S(2)}) copy-start(bf16[3,1024,256]{2,1,0:T(8,128)(2,1)} %param.19) | copy-start | bytes 4718596
Sparse Core Ops, SparseCore 0:
  9.6 66.2 all-gather.7
  87.8 26.9 all-gather.15
  126.2 14.8 all-gather.9
  147.9 16.7 all-gather.11
  190.6 15.6 all-gather.13
  226.9 36.2 reduce-scatter.1

commit v2 on v1

--- a/solution.py
+++ b/solution.py
@@ -64,6 +64,7 @@
     enc = encode(coords)
     cross_full = ring_gather(cross_out, "heads", n_heads)
     piece = lax.all_gather(kv_weight, "picks", axis=0, tiled=True)
+    cross_full, piece = lax.optimization_barrier((cross_full, piece))
     keys_vals = jnp.dot(
         enc, piece.reshape(piece.shape[0], 2 * local), preferred_element_type=jnp.float32
     ).astype(jnp.bfloat16)
@@ -92,9 +93,9 @@
         .astype(jnp.bfloat16)
     )
     dq_local, attended = lax.optimization_barrier((dec_query, attended))
-    dq_full = ring_gather(dq_local, "picks", n_picks)
+    dq_full = lax.all_gather(dq_local, "picks", axis=0, tiled=True)
     gain_two = lax.dynamic_slice_in_dim(norm_gains[1], column, local, 0)
-    attended_full = lax.all_gather(attended, "heads", axis=1, tiled=True)
+    attended_full = ring_gather(attended.T, "heads", n_heads).T
     whole = latents.astype(jnp.float32) + jnp.dot(
         attended_full, cross_full, preferred_element_type=jnp.float32
     )
@@ -115,10 +116,10 @@
         .astype(jnp.bfloat16)
         .reshape(lat_rows, local)
     )
-    every_head = lax.all_gather(head_out, "heads", axis=1, tiled=True)
+    every_head = ring_gather(head_out.T, "heads", n_heads).T
     latents_out = state + jnp.dot(every_head, self_out, preferred_element_type=jnp.float32)
     gained = (latents_out * gain_two[None, :]).astype(jnp.bfloat16)
-    gained_full = lax.all_gather(gained, "heads", axis=1, tiled=True)
+    gained_full = ring_gather(gained.T, "heads", n_heads).T
     power_two = lax.psum(jnp.sum(latents_out * latents_out, axis=1), "heads")
     row_scale = lax.rsqrt(power_two / width + EPS)
     dec = (

time: 273 us -> 247 us (0.905)
  waiting for transfers between devices: 124 us -> 93.8 us
  blocking collectives: 25.6 us -> 33.7 us
  local copies, waits for them, and re-layouts: 31.4 us -> 24.6 us
  other arithmetic: 36.1 us -> 42.3 us
  matrix products: 33.8 us -> 29.5 us
    all_gather x1, waiting for transfers between devices: 39.9 us -> 23 us  [on_device(): piece = lax.all_gather(kv_weight, 'picks', axis=0, tiled=True)]
    ppermute x6 -> x12, waiting for transfers between devices: 41.8 us -> 25 us  [ring_gather(): blocks.append(lax.ppermute(x, axis, [(i, (i - s) % n) for i in range(n)]))]
    all_gather x1, waiting for transfers between devices: 0.02 us -> 10.6 us  [on_device(): lax.all_gather(numer.astype(jnp.bfloat16), 'picks', axis=0, tiled=False)]
    psum x1, blocking collectives: 6.34 us -> 14.7 us  [on_device(): power_two = lax.psum(jnp.sum(latents_out * latents_out, axis=1), 'heads')]
    unnamed x53 -> x45, local copies, waits for them, and re-layouts: 21.8 us -> 16.3 us
    dot_general x1 -> x0, matrix products: 5.28 us -> none  [on_device(): jnp.einsum('phl,phlc->hlc', factor, all_numer.astype(jnp.float32), precis...]
    all_gather x3 -> x1, waiting for transfers between devices: 5.25 us -> 0.01 us  [on_device(): dq_full = lax.all_gather(dq_local, 'picks', axis=0, tiled=True)]
    concatenate x0 -> x3, other arithmetic: none -> 4.97 us  [ring_gather(): ordered = jnp.roll(flipped, idx, axis=0)]
  transfers between devices with their start and end apart: 12 -> 16, of which waited for: 7 -> 9; matrix products, arithmetic and copies ran while one was open for 24% -> 22% of each run, Pallas kernels for 0% -> 0%
where the time goes in v2:
time: 247 us; the launch traced here: 246 us
  waiting for transfers between devices  93.8 us (38%)
  other arithmetic  42.3 us (17%)
  blocking collectives  33.7 us (14%)
  matrix products  29.5 us (12%)
  local copies, waits for them, and re-layouts  24.6 us (10%)
  between operations  14.2 us (6%)
  starting transfers between devices  7.94 us (3%)
    reduce_scatter x1, waiting for transfers between devices, on_device(): lax.psum_scatter(jnp.dot(enc.T, dquery, preferred_element_type=jnp.float3...  34.5 us
    ppermute x12, waiting for transfers between devices, ring_gather(): blocks.append(lax.ppermute(x, axis, [(i, (i - s) % n) for i in range(n)]))  25 us
    another operation x1, other arithmetic  23.6 us
    all_gather x1, waiting for transfers between devices, on_device(): piece = lax.all_gather(kv_weight, 'picks', axis=0, tiled=True)  23 us
    unnamed x45, local copies, waits for them, and re-layouts  16.3 us
    psum x1, blocking collectives, on_device(): power_two = lax.psum(jnp.sum(latents_out * latents_out, axis=1), 'heads')  14.7 us
    all_gather x1, blocking collectives, on_device(): lax.all_gather(jnp.stack([top, total]), 'picks', axis=0, tiled=False)  13.2 us
    all_gather x1, waiting for transfers between devices, on_device(): lax.all_gather(numer.astype(jnp.bfloat16), 'picks', axis=0, tiled=False)  10.6 us
  transfers between devices with their start and end apart: 16, of which 9 were waited for; matrix products, arithmetic and copies ran while one was open for 22% of the time, Pallas kernels for 0%

profile of v2, /device:TPU:0, one launch (start us, length us, event | category | flops | bytes accessed | tf_op | source)
XLA Modules:
  0.0 246.0 jit_solution(18277034272995261886)
XLA Ops:
  8.0 2.4 collective-permute-start
  11.3 23.6 %fusion = (bf16[3,512,1024]{2,1,0:T(8,128)(2,1)S(1)}, bf16[3,512,1024]{2,1,0:T(8,128)(2,1)S(1)}) fusion(f32[3,1024]{1,0:T(4,128)} %param.14, f32[512]{0:T(512)S(1)} %maximum_multiply_fusion), kind=kLoop, calls=%fused_computation.2 | loop fusion | flops 4718592 | bytes 6305792 | tf_op jit(solution)/shard_map/convert
  34.9 3.2 %pad_maximum_fusion = bf16[6,512,1024]{2,1,0:T(8,128)(2,1)} fusion(bf16[3,512,1024]{2,1,0:T(8,128)(2,1)S(1)} %get-tuple-element.25, bf16[3,512,1024]{2,1,0:T(8,128)(2,1)S(1)} %get-tuple-element.24), kind=kLoop, calls=%fused_computation.4 | loop fusion | flops 3145728 | bytes 12582912 | tf_op jit(solution)/shard_map/concatenate | solution.py:21
  38.1 0.9 bitcast_dynamic-update-slice_fusion.6
  38.9 1.7 constant_dynamic-slice_fusion.2
  40.6 1.1 copy.98
  41.7 0.8 bitcast_dynamic-update-slice_fusion.4
  43.4 1.9 bitcast_dynamic-update-slice_fusion
  45.3 0.9 bitcast_dynamic-update-slice_fusion.7
  46.2 0.9 bitcast_dynamic-update-slice_fusion.5
  47.1 0.8 bitcast_dynamic-update-slice_fusion.3
  47.9 1.9 bitcast_dynamic-update-slice_fusion.1
  49.8 3.1 %constant_dynamic-slice_fusion.1 = bf16[4,256,1024]{2,1,0:T(8,128)(2,1)} fusion(bf16[8,256,1024]{2,1,0:T(8,128)(2,1)} %bitcast_dynamic-update-slice_fusion.1, s32[]{:T(128)S(6)} %select_n.27), kind=kLoop, calls=%fused_computation.119 | loop fusion | bytes 4194308 | tf_op jit(solution)/shard_map/jit(_roll_dynamic)/dynamic_slice | solution.py:35
  52.9 23.0 %all-gather.6.cloned.1.call-done = bf16[3072,2,256]{2,1,0:T(2,128)(2,1)} async-done(((bf16[768,2,256]{2,1,0:T(2,128)(2,1)}), bf16[3072,2,256]{2,1,0:T(2,128)(2,1)}) %all-gather.6.cloned.1.call-update) | async-done | bytes 3145744 | tf_op jit(solution)/shard_map/all_gather | solution.py:66
  75.9 2.4 copy.100
  78.3 6.3 %convolution_convert_fusion.1 = bf16[1024,512]{0,1:T(8,128)(2,1)S(1)} fusion(bf16[3072,1024]{1,0:T(8,128)(2,1)} %bitcast.127, bf16[3072,512]{1,0:T(8,128)(2,1)S(1)} %bitcast.135), kind=kOutput, calls=%fused_computation.58 | convolution fusion | flops 3221749760 | bytes 10485760 | tf_op jit(solution)/shard_map/dot_general | solution.py:68
  84.7 0.8 multiply_reduce_fusion
  85.5 2.0 copy-done.1
  87.5 1.6 fusion.36
  89.2 3.1 %fusion.7 = f32[2,512]{1,0:T(2,128)S(1)} fusion(f32[2,512,1024]{2,1,0:T(8,128)} %copy-done.1, f32[2,512]{1,0:T(2,128)S(1)} %get-tuple-element.28), kind=kLoop, calls=%fused_computation.16 | loop fusion | flops 3144704 | bytes 4202496 | tf_op jit(solution)/shard_map/reduce_sum | solution.py:77
  92.3 13.2 %all-gather.1 = f32[8,2,512]{2,1,0:T(2,128)S(1)} all-gather(f32[2,2,512]{2,1,0:T(2,128)S(1)} %pad_maximum_fusion.1), channel_id=3, replica_groups=mesh['groups'=2,'picks'=4,'heads'=4] {'picks'}, dimensions={0}, use_global_device_ids=true | all-gather | bytes 40960 | tf_op jit(solution)/shard_map/all_gather | solution.py:82
  105.5 10.6 %all-gather.10.cloned.1.call-done = bf16[8,512,128]{2,1,0:T(8,128)(2,1)} async-done(((bf16[2,512,128]{2,1,0:T(8,128)(2,1)}), bf16[8,512,128]{2,1,0:T(8,128)(2,1)}) %all-gather.10.cloned.1.call-update) | async-done | bytes 1048592 | tf_op jit(solution)/shard_map/all_gather | solution.py:81
  116.1 1.8 multiply_reduce_fusion.1
  118.1 1.0 collective-permute-start.3
  120.1 5.5 %collective-permute-done.3 = bf16[256,512]{1,0:T(8,128)(2,1)S(1)} collective-permute-done((bf16[256,512]{1,0:T(8,128)(2,1)S(1)}, bf16[256,512]{1,0:T(8,128)(2,1)S(1)}, u32[]{:S(2)}, u32[]{:S(2)}) %collective-permute-start.3) | collective-permute-done | bytes 262176 | tf_op jit(solution)/shard_map/ppermute | solution.py:33
  125.6 6.9 %collective-permute-done.4 = bf16[256,512]{1,0:T(8,128)(2,1)S(1)} collective-permute-done((bf16[256,512]{1,0:T(8,128)(2,1)S(1)}, bf16[256,512]{1,0:T(8,128)(2,1)S(1)}, u32[]{:S(2)}, u32[]{:S(2)}) %collective-permute-start.4) | collective-permute-done | bytes 262176 | tf_op jit(solution)/shard_map/ppermute | solution.py:33
  132.6 1.2 fusion.58
  133.9 3.3 %multiply_reduce_fusion.2 = (f32[512]{0:T(512)S(1)}, f32[512,1024]{1,0:T(8,128)S(1)}) fusion(bf16[1024,512]{1,0:T(8,128)(2,1)S(1)} %bitcast.133, bf16[1024,1024]{1,0:T(8,128)(2,1)} %bitcast.126, bf16[512,1024]{1,0:T(8,128)(2,1)} %param.17), kind=kOutput, calls=%fused_computation.53 | convolution fusion | flops 1075838464 | bytes 6293504 | tf_op jit(solution)/shard_map/dot_general | solution.py:99
  137.1 1.1 fusion.31
  139.5 1.4 collective-permute-start.7
  141.2 4.2 %collective-permute-done.6 = bf16[256,512]{1,0:T(8,128)(2,1)S(1)} collective-permute-done((bf16[256,512]{1,0:T(8,128)(2,1)S(1)}, bf16[256,512]{1,0:T(8,128)(2,1)S(1)}, u32[]{:S(2)}, u32[]{:S(2)}) %collective-permute-start.6) | collective-permute-done | bytes 262176 | tf_op jit(solution)/shard_map/ppermute | solution.py:33
  145.4 8.0 %collective-permute-done.7 = bf16[256,512]{1,0:T(8,128)(2,1)S(1)} collective-permute-done((bf16[256,512]{1,0:T(8,128)(2,1)S(1)}, bf16[256,512]{1,0:T(8,128)(2,1)S(1)}, u32[]{:S(2)}, u32[]{:S(2)}) %collective-permute-start.7) | collective-permute-done | bytes 262176 | tf_op jit(solution)/shard_map/ppermute | solution.py:33
  153.6 1.2 fusion.51
  154.9 1.5 convolution_add_fusion
  157.7 14.7 %psum.14 = f32[512]{0:T(512)S(1)} all-reduce(f32[512]{0:T(512)S(1)} %get-tuple-element.21), channel_id=1, replica_groups=mesh['groups'=2,'picks'=4,'heads'=4] {'heads'}, use_global_device_ids=true, to_apply=%region_7.9 | all-reduce | flops 512 | bytes 4096 | tf_op jit(solution)/shard_map/psum | solution.py:123
  173.3 2.5 %fusion.44 = bf16[4,256,512]{1,2,0:T(8,128)(2,1)S(1)} fusion(s32[]{:T(128)S(6)} %select_n.27, bf16[1,256,512]{1,2,0:T(8,128)(2,1)S(1)} %get-tuple-element.18, bf16[1,256,512]{1,2,0:T(8,128)(2,1)} %bitcast.158, bf16[1,256,512]{1,2,0:T(8,128)(2,1)} %bitcast.160, bf16[1,256,512]{1,2,0:T(8,128)(2,1)} %bitcast.162), kind=kLoop, calls=%fused_computation.76 | loop fusion | flops 3670016 | bytes 2097156 | tf_op jit(solution)/shard_map/jit(_roll_dynamic)/concatenate | solution.py:35
  175.8 1.3 copy.70
  177.1 2.3 fusion.35
  179.7 5.1 %convolution_convert_fusion.3 = bf16[1024,256]{0,1:T(8,128)(2,1)S(1)} fusion(bf16[3072,1024]{1,0:T(8,128)(2,1)} %bitcast.128, bf16[3072,256]{1,0:T(8,128)(2,1)} %all-gather.8.cloned.1.call-done), kind=kOutput, calls=%fused_computation.64 | convolution fusion | flops 1610874880 | bytes 8388608 | tf_op jit(solution)/shard_map/dot_general | solution.py:131
  184.8 0.8 fusion.6
  185.6 2.0 copy-done.2
  187.6 1.0 fusion.32
  188.6 5.8 %psum.15 = f32[1024]{0:T(1024)S(1)} all-reduce(f32[1024]{0:T(1024)S(1)} %fusion.32), channel_id=1, replica_groups=mesh['groups'=2,'picks'=4,'heads'=4] {'heads'}, use_global_device_ids=true, to_apply=%region_10.12 | all-reduce | flops 1024 | bytes 8192 | tf_op jit(solution)/shard_map/psum | solution.py:140
  194.4 3.3 %fusion.2 = f32[2,1024]{1,0:T(2,128)S(1)} fusion(f32[2,512]{1,0:T(2,128)S(1)} %bitcast.170, f32[1024]{0:T(1024)S(1)} %sub.51, f32[2,1024]{1,0:T(2,128)S(1)} %get-tuple-element.34, f32[2,1024,512]{1,2,0:T(8,128)} %copy-done.2), kind=kLoop, calls=%fused_computation.7 | loop fusion | flops 5240832 | bytes 4218880 | tf_op jit(solution)/shard_map/reduce_sum | solution.py:148
  197.8 1.4 fusion.28
  199.9 3.1 %convolution_convert_fusion = bf16[3072,256]{1,0:T(8,128)(2,1)} fusion(bf16[3072,1024]{1,0:T(8,128)(2,1)S(1)} %bitcast.131, bf16[1024,256]{0,1:T(8,128)(2,1)S(1)} %bitcast.177), kind=kOutput, calls=%fused_computation.13 | convolution fusion | flops 1611399168 | bytes 8388608 | tf_op jit(solution)/shard_map/dot_general | solution.py:157
  203.1 34.5 %reduce-scatter.2.cloned.1.call-done = bf16[768,256]{1,0:T(8,128)(2,1)} async-done(((bf16[3072,256]{1,0:T(8,128)(2,1)}), bf16[768,256]{1,0:T(8,128)(2,1)}) %reduce-scatter.2.cloned.1.call-update) | async-done | bytes 393232 | tf_op jit(solution)/shard_map/reduce_scatter | solution.py:156
  237.5 1.9 convert_element_type.100
  (83 shorter events, 8.9 us)
Async XLA Ops:
  7.2 130.0 %copy-start = (bf16[3,1024,256]{2,1,0:T(8,128)(2,1)S(1)}, bf16[3,1024,256]{2,1,0:T(8,128)(2,1)}, u32[]{:S(2)}) copy-start(bf16[3,1024,256]{2,1,0:T(8,128)(2,1)} %param.21) | copy-start | bytes 4718596
  7.2 68.7 %all-gather.6.cloned.1.call-start = ((), (), s32[]{:S(2)}) async-start(), calls=%async_computation.1 | async-start | bytes 3932160 | tf_op jit(solution)/shard_map/all_gather | solution.py:66
  7.9 108.2 %all-gather.10.cloned.1.call-start = ((), (), s32[]{:S(2)}) async-start(), calls=%async_computation.4 | async-start | bytes 1310720 | tf_op jit(solution)/shard_map/all_gather | solution.py:81
  8.0 33.8 %collective-permute-start = (bf16[256,1024]{1,0:T(8,128)(2,1)}, bf16[256,1024]{1,0:T(8,128)(2,1)S(1)}, u32[]{:S(2)}, u32[]{:S(2)}) collective-permute-start(bf16[256,1024]{1,0:T(8,128)(2,1)} %param.19), channel_id=1, source_target_pairs={{0,3},{1,0},{2,1},{3,2},{4,7},{5,4},{6,5},{7,6},{8,11},{9,8},{10,9... | collective-permute-start | bytes 1572872 | tf_op jit(solution)/shard_map/ppermute | solution.py:33
  10.4 32.2 %collective-permute-start.1 = (bf16[256,1024]{1,0:T(8,128)(2,1)}, bf16[256,1024]{1,0:T(8,128)(2,1)S(1)}, u32[]{:S(2)}, u32[]{:S(2)}) collective-permute-start(bf16[256,1024]{1,0:T(8,128)(2,1)} %param.19), channel_id=1, source_target_pairs={{0,2},{1,3},{2,0},{3,1},{4,6},{5,7},{6,4},{7,5},{8,10},{9,11},{10,... | collective-permute-start | bytes 1572872 | tf_op jit(solution)/shard_map/ppermute | solution.py:33
  11.0 32.4 %collective-permute-start.2 = (bf16[256,1024]{1,0:T(8,128)(2,1)}, bf16[256,1024]{1,0:T(8,128)(2,1)}, u32[]{:S(2)}, u32[]{:S(2)}) collective-permute-start(bf16[256,1024]{1,0:T(8,128)(2,1)} %param.19), channel_id=1, source_target_pairs={{0,1},{1,2},{2,3},{3,0},{4,5},{5,6},{6,7},{7,4},{8,9},{9,10},{10,1... | collective-permute-start | bytes 1572872 | tf_op jit(solution)/shard_map/ppermute | solution.py:33
  34.9 3.2 %copy-start.5 = (bf16[256,1024]{1,0:T(8,128)(2,1)S(1)}, bf16[256,1024]{1,0:T(8,128)(2,1)}, u32[]{:S(2)}) copy-start(bf16[256,1024]{1,0:T(8,128)(2,1)} %param.19) | copy-start | bytes 1572868
  85.5 2.0 copy-start.1
  89.1 31.0 %copy-start.12 = (f32[2,1024]{1,0:T(2,128)S(1)}, f32[2,1024]{1,0:T(2,128)}, u32[]{:S(2)}) copy-start(f32[2,1024]{1,0:T(2,128)} %param.20) | copy-start | bytes 24580
  89.1 90.6 %all-gather.8.cloned.1.call-start = ((), (), s32[]{:S(2)}) async-start(), calls=%async_computation.2 | async-start | bytes 1966080 | tf_op jit(solution)/shard_map/all_gather | solution.py:96
  118.1 7.5 %collective-permute-start.3 = (bf16[256,512]{1,0:T(8,128)(2,1)S(1)}, bf16[256,512]{1,0:T(8,128)(2,1)S(1)}, u32[]{:S(2)}, u32[]{:S(2)}) collective-permute-start(bf16[256,512]{1,0:T(8,128)(2,1)S(1)} %bitcast.137), channel_id=1, source_target_pairs={{0,3},{1,0},{2,1},{3,2},{4,7},{5,4},{6,5},{7,6},{8,11},{9,8},{10,9... | collective-permute-start | bytes 786440 | tf_op jit(solution)/shard_map/ppermute | solution.py:33
  119.1 13.4 %collective-permute-start.4 = (bf16[256,512]{1,0:T(8,128)(2,1)S(1)}, bf16[256,512]{1,0:T(8,128)(2,1)S(1)}, u32[]{:S(2)}, u32[]{:S(2)}) collective-permute-start(bf16[256,512]{1,0:T(8,128)(2,1)S(1)} %bitcast.138), channel_id=1, source_target_pairs={{0,2},{1,3},{2,0},{3,1},{4,6},{5,7},{6,4},{7,5},{8,10},{9,11},{10,... | collective-permute-start | bytes 786440 | tf_op jit(solution)/shard_map/ppermute | solution.py:33
  119.9 12.7 %collective-permute-start.5 = (bf16[256,512]{1,0:T(8,128)(2,1)S(1)}, bf16[256,512]{1,0:T(8,128)(2,1)S(1)}, u32[]{:S(2)}, u32[]{:S(2)}) collective-permute-start(bf16[256,512]{1,0:T(8,128)(2,1)S(1)} %bitcast.139), channel_id=1, source_target_pairs={{0,1},{1,2},{2,3},{3,0},{4,5},{5,6},{6,7},{7,4},{8,9},{9,10},{10,1... | collective-permute-start | bytes 786440 | tf_op jit(solution)/shard_map/ppermute | solution.py:33
  137.1 1.8 copy-start.4
  138.9 16.0 %copy-start.7 = (bf16[1024,256]{1,0:T(8,128)(2,1)S(1)}, bf16[1024,256]{1,0:T(8,128)(2,1)}, u32[]{:S(2)}) copy-start(bf16[1024,256]{1,0:T(8,128)(2,1)} %param.22) | copy-start | bytes 1572868
  139.4 18.1 %copy-start.13 = (s32[1024]{0:T(1024)S(1)}, s32[1024]{0:T(1024)}, u32[]{:S(2)}) copy-start(s32[1024]{0:T(1024)} %param.15) | copy-start | bytes 12292
  139.5 18.1 %copy-start.15 = (f32[64]{0:T(128)S(1)}, f32[64]{0:T(128)}, u32[]{:S(2)}) copy-start(f32[64]{0:T(128)} %param.16) | copy-start | bytes 772
  139.5 5.9 %collective-permute-start.6 = (bf16[256,512]{1,0:T(8,128)(2,1)S(1)}, bf16[256,512]{1,0:T(8,128)(2,1)S(1)}, u32[]{:S(2)}, u32[]{:S(2)}) collective-permute-start(bf16[256,512]{1,0:T(8,128)(2,1)S(1)} %bitcast.152), channel_id=1, source_target_pairs={{0,3},{1,0},{2,1},{3,2},{4,7},{5,4},{6,5},{7,6},{8,11},{9,8},{10,9... | collective-permute-start | bytes 786440 | tf_op jit(solution)/shard_map/ppermute | solution.py:33
  139.5 13.8 %collective-permute-start.7 = (bf16[256,512]{1,0:T(8,128)(2,1)S(1)}, bf16[256,512]{1,0:T(8,128)(2,1)S(1)}, u32[]{:S(2)}, u32[]{:S(2)}) collective-permute-start(bf16[256,512]{1,0:T(8,128)(2,1)S(1)} %bitcast.153), channel_id=1, source_target_pairs={{0,2},{1,3},{2,0},{3,1},{4,6},{5,7},{6,4},{7,5},{8,10},{9,11},{10,... | collective-permute-start | bytes 786440 | tf_op jit(solution)/shard_map/ppermute | solution.py:33
  140.9 12.7 %collective-permute-start.8 = (bf16[256,512]{1,0:T(8,128)(2,1)S(1)}, bf16[256,512]{1,0:T(8,128)(2,1)S(1)}, u32[]{:S(2)}, u32[]{:S(2)}) collective-permute-start(bf16[256,512]{1,0:T(8,128)(2,1)S(1)} %bitcast.154), channel_id=1, source_target_pairs={{0,1},{1,2},{2,3},{3,0},{4,5},{5,6},{6,7},{7,4},{8,9},{9,10},{10,1... | collective-permute-start | bytes 786440 | tf_op jit(solution)/shard_map/ppermute | solution.py:33
  141.1 96.4 %reduce-scatter.2.cloned.1.call-start = ((), (), s32[]{:S(2)}) async-start(), calls=%async_computation.3 | async-start | bytes 1966080 | tf_op jit(solution)/shard_map/reduce_scatter | solution.py:156
  156.4 23.0 %copy-start.6 = (f32[512,256]{1,0:T(8,128)}, f32[512,256]{1,0:T(8,128)S(1)}, u32[]{:S(2)}) copy-start(f32[512,256]{1,0:T(8,128)S(1)} %convolution_add_fusion) | copy-start | bytes 1572868
  156.6 15.8 %collective-permute-start.9 = (bf16[256,512]{0,1:T(8,128)(2,1)S(1)}, bf16[256,512]{0,1:T(8,128)(2,1)S(1)}, u32[]{:S(2)}, u32[]{:S(2)}) collective-permute-start(bf16[256,512]{0,1:T(8,128)(2,1)S(1)} %get-tuple-element.17), channel_id=1, source_target_pairs={{0,3},{1,0},{2,1},{3,2},{4,7},{5,4},{6,5},{7,6},{8,11},{9,8},{10,9... | collective-permute-start | bytes 786440 | tf_op jit(solution)/shard_map/ppermute | solution.py:33
  156.6 15.8 %collective-permute-start.10 = (bf16[256,512]{0,1:T(8,128)(2,1)S(1)}, bf16[256,512]{0,1:T(8,128)(2,1)S(1)}, u32[]{:S(2)}, u32[]{:S(2)}) collective-permute-start(bf16[256,512]{0,1:T(8,128)(2,1)S(1)} %get-tuple-element.17), channel_id=1, source_target_pairs={{0,2},{1,3},{2,0},{3,1},{4,6},{5,7},{6,4},{7,5},{8,10},{9,11},{10,... | collective-permute-start | bytes 786440 | tf_op jit(solution)/shard_map/ppermute | solution.py:33
  157.4 15.0 %collective-permute-start.11 = (bf16[256,512]{0,1:T(8,128)(2,1)S(1)}, bf16[256,512]{0,1:T(8,128)(2,1)S(1)}, u32[]{:S(2)}, u32[]{:S(2)}) collective-permute-start(bf16[256,512]{0,1:T(8,128)(2,1)S(1)} %get-tuple-element.17), channel_id=1, source_target_pairs={{0,1},{1,2},{2,3},{3,0},{4,5},{5,6},{6,7},{7,4},{8,9},{9,10},{10,1... | collective-permute-start | bytes 786440 | tf_op jit(solution)/shard_map/ppermute | solution.py:33
  172.4 0.7 copy-start.8
  172.4 0.8 copy-start.9
  172.4 0.9 copy-start.10
  173.3 6.2 %copy-start.14 = (f32[256]{0:T(256)S(1)}, f32[256]{0:T(256)}, u32[]{:S(2)}) copy-start(f32[256]{0:T(256)} %param.25) | copy-start | bytes 3076
  185.6 2.0 copy-start.2
  194.4 4.8 %copy-start.11 = (f32[1024]{0:T(1024)}, f32[1024]{0:T(1024)S(1)}, u32[]{:S(2)}) copy-start(f32[1024]{0:T(1024)S(1)} %psum.15) | copy-start | bytes 12292
  194.4 3.5 %copy-start.3 = (f32[2,1024,512]{1,2,0:T(8,128)S(1)}, f32[2,1024,512]{1,2,0:T(8,128)}, u32[]{:S(2)}) copy-start(f32[2,1024,512]{1,2,0:T(8,128)} %copy-done.2) | copy-start | bytes 12582916
  194.4 4.8 %slice-start = ((s8[6291456]{0:T(1024)(128)(4,1)}), s8[4194304]{0:T(1024)(128)(4,1)S(1)}, s32[]{:S(2)}) async-start(s8[6291456]{0:T(1024)(128)(4,1)} %bitcast.129), calls=%async_computation.5 | async-start | bytes 8388608
  197.8 2.1 slice-start.1
Sparse Core Ops, SparseCore 0:
  9.6 66.2 all-gather.5
  89.3 26.7 all-gather.9
  141.2 37.0 all-gather.7
  203.2 34.3 reduce-scatter.1

commit v3 on v2

--- a/solution.py
+++ b/solution.py
@@ -34,6 +34,24 @@
     flipped = jnp.stack(blocks)
     ordered = jnp.roll(flipped, idx, axis=0)
     return ordered.reshape((n * x.shape[0],) + x.shape[1:])
+
+
+def fetch_rows(kv_weight, n_picks, n_groups):
+    if n_groups != 2:
+        return lax.all_gather(kv_weight, "picks", axis=0, tiled=True)
+    g = lax.axis_index("groups")
+    rows = kv_weight.shape[0] // 2
+    mine = lax.dynamic_slice_in_dim(kv_weight, g * rows, rows, 0)
+    first = max(8, (2 * rows // 3) // 8 * 8)
+    bounds = [(0, first), (first, rows)] if first < rows else [(0, rows)]
+    own, other = [], []
+    for lo, hi in bounds:
+        gathered = lax.all_gather(mine[lo:hi], "picks", axis=0, tiled=False)
+        own.append(gathered)
+        other.append(lax.ppermute(gathered, "groups", [(0, 1), (1, 0)]))
+    halves = jnp.stack([jnp.concatenate(own, axis=1), jnp.concatenate(other, axis=1)], axis=1)
+    halves = jnp.roll(halves, g, axis=1)
+    return halves.reshape((n_picks * kv_weight.shape[0],) + kv_weight.shape[1:])
 
 
 def on_device(
@@ -52,6 +70,7 @@
     *,
     n_picks,
     n_heads,
+    n_groups,
 ):
     high = lax.Precision.HIGHEST
     scale = HEAD ** (-0.5)
@@ -63,7 +82,7 @@
     column = lax.axis_index("heads") * local
     enc = encode(coords)
     cross_full = ring_gather(cross_out, "heads", n_heads)
-    piece = lax.all_gather(kv_weight, "picks", axis=0, tiled=True)
+    piece = fetch_rows(kv_weight, n_picks, n_groups)
     cross_full, piece = lax.optimization_barrier((cross_full, piece))
     keys_vals = jnp.dot(
         enc, piece.reshape(piece.shape[0], 2 * local), preferred_element_type=jnp.float32
@@ -92,9 +111,10 @@
         .reshape(lat_rows, local)
         .astype(jnp.bfloat16)
     )
+    out_full = ring_gather(self_out.T, "heads", n_heads).T
+    out_full, attended = lax.optimization_barrier((out_full, attended))
     dq_local, attended = lax.optimization_barrier((dec_query, attended))
     dq_full = lax.all_gather(dq_local, "picks", axis=0, tiled=True)
-    gain_two = lax.dynamic_slice_in_dim(norm_gains[1], column, local, 0)
     attended_full = ring_gather(attended.T, "heads", n_heads).T
     whole = latents.astype(jnp.float32) + jnp.dot(
         attended_full, cross_full, preferred_element_type=jnp.float32
@@ -117,15 +137,15 @@
         .reshape(lat_rows, local)
     )
     every_head = ring_gather(head_out.T, "heads", n_heads).T
-    latents_out = state + jnp.dot(every_head, self_out, preferred_element_type=jnp.float32)
-    gained = (latents_out * gain_two[None, :]).astype(jnp.bfloat16)
-    gained_full = ring_gather(gained.T, "heads", n_heads).T
-    power_two = lax.psum(jnp.sum(latents_out * latents_out, axis=1), "heads")
-    row_scale = lax.rsqrt(power_two / width + EPS)
-    dec = (
-        jnp.einsum("ld,kde->kle", gained_full, dec_kv, preferred_element_type=jnp.float32)
-        * row_scale[None, :, None]
-    ).astype(jnp.bfloat16)
+    out_whole = whole + jnp.dot(every_head, out_full, preferred_element_type=jnp.float32)
+    latents_out = lax.dynamic_slice_in_dim(out_whole, column, local, 1)
+    power_two = jnp.mean(out_whole * out_whole, axis=1, keepdims=True)
+    normed2 = (out_whole * lax.rsqrt(power_two + EPS) * norm_gains[1][None, :]).astype(
+        jnp.bfloat16
+    )
+    dec = jnp.einsum("ld,kde->kle", normed2, dec_kv, preferred_element_type=jnp.float32).astype(
+        jnp.bfloat16
+    )
     dec_keys = dec[0].reshape(lat_rows, nheads, HEAD)
     dec_vals = dec[1].reshape(lat_rows, nheads, HEAD)
     query = jnp.dot(enc, dq_full, preferred_element_type=jnp.float32).astype(jnp.bfloat16)
@@ -179,6 +199,9 @@
     )
     out_specs = (P(("groups", "picks")), P("groups", "heads"), P(("groups", "picks"), "heads"))
     body = functools.partial(
-        on_device, n_picks=mesh.shape["picks"], n_heads=mesh.shape["heads"]
+        on_device,
+        n_picks=mesh.shape["picks"],
+        n_heads=mesh.shape["heads"],
+        n_groups=mesh.shape["groups"],
     )
     return jax.shard_map(body, mesh=mesh, in_specs=in_specs, out_specs=out_specs, check_vma=False)

time: 247 us -> 250 us (1.012)
  other arithmetic: 42.3 us -> 56.4 us
  waiting for transfers between devices: 93.8 us -> 80 us
  starting transfers between devices: 7.94 us -> 11.4 us
  blocking collectives: 33.7 us -> 36.3 us
    all_gather x1, waiting for transfers between devices: 23 us -> 0.01 us  [fetch_rows(): gathered = lax.all_gather(mine[lo:hi], 'picks', axis=0, tiled=False)]
    all_gather x0 -> x1, blocking collectives: none -> 16.5 us  [fetch_rows(): gathered = lax.all_gather(mine[lo:hi], 'picks', axis=0, tiled=False)]
    ppermute x0 -> x2, waiting for transfers between devices: none -> 15.4 us  [fetch_rows(): other.append(lax.ppermute(gathered, 'groups', [(0, 1), (1, 0)]))]
    psum x1 -> x0, blocking collectives: 14.7 us -> none  [on_device(): power_two = lax.psum(jnp.sum(latents_out * latents_out, axis=1), 'heads')]
    unnamed x45 -> x42, local copies, waits for them, and re-layouts: 16.3 us -> 7.68 us
    concatenate x3 -> x4, other arithmetic: 4.97 us -> 12.6 us  [ring_gather(): ordered = jnp.roll(flipped, idx, axis=0)]
    optimization_barrier x0 -> x1, local copies, waits for them, and re-layouts: none -> 4.65 us  [on_device(): cross_full, piece = lax.optimization_barrier((cross_full, piece))]
    concatenate x0 -> x1, other arithmetic: none -> 3.47 us  [fetch_rows(): halves = jnp.roll(halves, g, axis=1)]
  transfers between devices with their start and end apart: 16 -> 18, of which waited for: 9 -> 9; matrix products, arithmetic and copies ran while one was open for 22% -> 33% of each run, Pallas kernels for 0% -> 0%
where the time goes in v3:
time: 250 us; the launch traced here: 249 us
  waiting for transfers between devices  80 us (32%)
  other arithmetic  56.4 us (23%)
  blocking collectives  36.3 us (15%)
  matrix products  28.2 us (11%)
  local copies, waits for them, and re-layouts  22.4 us (9%)
  between operations  14.2 us (6%)
  starting transfers between devices  11.4 us (5%)
    reduce_scatter x1, waiting for transfers between devices, on_device(): lax.psum_scatter(jnp.dot(enc.T, dquery, preferred_element_type=jnp.float3...  31.9 us
    ppermute x12, waiting for transfers between devices, ring_gather(): blocks.append(lax.ppermute(x, axis, [(i, (i - s) % n) for i in range(n)]))  25 us
    another operation x1, other arithmetic  24.5 us
    all_gather x1, blocking collectives, fetch_rows(): gathered = lax.all_gather(mine[lo:hi], 'picks', axis=0, tiled=False)  16.5 us
    ppermute x2, waiting for transfers between devices, fetch_rows(): other.append(lax.ppermute(gathered, 'groups', [(0, 1), (1, 0)]))  15.4 us
    all_gather x1, blocking collectives, on_device(): lax.all_gather(jnp.stack([top, total]), 'picks', axis=0, tiled=False)  13.3 us
    concatenate x4, other arithmetic, ring_gather(): ordered = jnp.roll(flipped, idx, axis=0)  12.6 us
    ppermute x12, starting transfers between devices, ring_gather(): blocks.append(lax.ppermute(x, axis, [(i, (i - s) % n) for i in range(n)]))  8.92 us
  transfers between devices with their start and end apart: 18, of which 9 were waited for; matrix products, arithmetic and copies ran while one was open for 33% of the time, Pallas kernels for 0%

profile of v3, /device:TPU:0, one launch (start us, length us, event | category | flops | bytes accessed | tf_op | source)
XLA Modules:
  0.0 248.9 jit_solution(15779100217166352926)
XLA Ops:
  7.2 1.9 constant_dynamic-slice_fusion.1
  9.3 2.4 collective-permute-start.3
  12.5 1.2 copy.86
  13.7 1.6 collective-permute-start
  15.5 1.0 constant_dynamic-slice_fusion.2
  16.5 24.5 %fusion = (bf16[3,512,1024]{2,1,0:T(8,128)(2,1)}, bf16[3,512,1024]{2,1,0:T(8,128)(2,1)}) fusion(f32[3,1024]{1,0:T(4,128)S(1)} %copy-done.12, f32[512]{0:T(512)S(1)} %maximum_multiply_fusion), kind=kLoop, calls=%fused_computation.2 | loop fusion | flops 4718592 | bytes 6305792 | tf_op jit(solution)/shard_map/convert
  41.0 16.5 %all-gather.1 = bf16[512,2,256]{2,1,0:T(2,128)(2,1)} all-gather(bf16[128,2,256]{2,1,0:T(2,128)(2,1)S(1)} %constant_dynamic-slice_fusion.2), channel_id=3, replica_groups=mesh['groups'=2,'picks'=4,'heads'=4] {'picks'}, dimensions={0}, use_global_device_ids=true | all-gather | bytes 655360 | tf_op jit(solution)/shard_map/all_gather | solution.py:49
  57.5 1.4 copy.88
  58.9 1.6 collective-permute-start.6
  60.4 1.7 constant_dynamic-slice_fusion.3
  62.1 1.9 copy.89
  64.0 1.1 copy.127
  65.2 6.1 %pad_maximum_fusion = bf16[6,512,1024]{2,1,0:T(8,128)(2,1)} fusion(bf16[3,512,1024]{2,1,0:T(8,128)(2,1)} %get-tuple-element.27, bf16[3,512,1024]{2,1,0:T(8,128)(2,1)} %get-tuple-element.26), kind=kLoop, calls=%fused_computation.8 | loop fusion | flops 3145728 | bytes 12582912 | tf_op jit(solution)/shard_map/concatenate | solution.py:21
  71.3 0.9 collective-permute-start.1
  72.8 5.0 %fusion.17 = bf16[4,256,1024]{2,1,0:T(8,128)(2,1)} fusion(s32[]{:T(128)S(6)} %select_n.43, bf16[1,256,1024]{2,1,0:T(8,128)(2,1)S(1)} %bitcast.159, bf16[1,256,1024]{2,1,0:T(8,128)(2,1)} %bitcast.12, bf16[1,256,1024]{2,1,0:T(8,128)(2,1)} %bitcast.13, bf16[1,256,1024]{2,1,0:T(8,128)(2,1)} %bitcast.14), kind=kLoop, calls=%fused_computation.45 | loop fusion | flops 7340032 | bytes 4194308 | tf_op jit(solution)/shard_map/jit(_roll_dynamic)/concatenate | solution.py:35
  77.8 15.4 %collective-permute-done.7 = bf16[4,128,2,256]{3,1,0,2:T(8,128)(2,1)S(1)} collective-permute-done((bf16[4,128,2,256]{3,1,0,2:T(8,128)(2,1)S(1)}, bf16[4,128,2,256]{3,1,0,2:T(8,128)(2,1)S(1)}, u32[]{:S(2)}, u32[]{:S(2)}) %collective-permute-start.7) | collective-permute-done | bytes 524320 | tf_op jit(solution)/shard_map/ppermute | solution.py:51
  93.2 1.3 maximum_bitcast_fusion.1
  94.5 3.5 %fusion.11 = bf16[4,2,384,2,256]{4,2,1,0,3:T(8,128)(2,1)} fusion(s32[]{:T(128)S(6)} %select_n.37, bf16[4,1,384,2,256]{4,2,1,0,3:T(8,128)(2,1)S(1)} %maximum_bitcast_fusion, bf16[4,1,384,2,256]{4,2,1,0,3:T(8,128)(2,1)S(1)} %maximum_bitcast_fusion.1), kind=kLoop, calls=%fused_computation.40 | loop fusion | flops 4718592 | bytes 6291460 | tf_op jit(solution)/shard_map/jit(_roll_dynamic)/concatenate | solution.py:53
  98.0 4.6 %copy.92 = bf16[3072,2,256]{0,2,1:T(8,128)(2,1)} copy(bf16[3072,2,256]{2,0,1:T(8,128)(2,1)} %bitcast.127) | data formatting | bytes 6291456 | tf_op jit(solution)/shard_map/optimization_barrier | solution.py:86
  102.7 7.1 %convolution_convert_fusion.1 = bf16[1024,512]{0,1:T(8,128)(2,1)S(1)} fusion(bf16[3072,512]{0,1:T(8,128)(2,1)} %bitcast.137, bf16[3072,1024]{1,0:T(8,128)(2,1)} %bitcast.129), kind=kOutput, calls=%fused_computation.92 | convolution fusion | flops 3221749760 | bytes 10485760 | tf_op jit(solution)/shard_map/dot_general | solution.py:87
  110.7 2.0 copy-done.2
  112.8 1.6 fusion.52
  114.7 5.2 %fusion.24 = bf16[4,256,1024]{2,1,0:T(8,128)(2,1)} fusion(s32[]{:T(128)S(6)} %select_n.43, bf16[1,256,1024]{2,1,0:T(8,128)(2,1)S(1)} %bitcast.141, bf16[1,256,1024]{2,1,0:T(8,128)(2,1)} %bitcast.4, bf16[1,256,1024]{2,1,0:T(8,128)(2,1)} %bitcast.5, bf16[1,256,1024]{2,1,0:T(8,128)(2,1)} %bitcast.6), kind=kLoop, calls=%fused_computation.52 | loop fusion | flops 7340032 | bytes 4194308 | tf_op jit(solution)/shard_map/jit(_roll_dynamic)/concatenate | solution.py:35
  119.8 0.9 fusion.7
  120.8 13.3 %all-gather.3 = f32[8,2,512]{2,1,0:T(2,128)S(1)} all-gather(f32[2,2,512]{2,1,0:T(2,128)S(1)} %pad_maximum_fusion.1), channel_id=5, replica_groups=mesh['groups'=2,'picks'=4,'heads'=4] {'picks'}, dimensions={0}, use_global_device_ids=true | all-gather | bytes 40960 | tf_op jit(solution)/shard_map/all_gather | solution.py:101
  134.1 7.7 %all-gather.12.cloned.1.call-done = bf16[8,512,128]{2,1,0:T(8,128)(2,1)} async-done(((bf16[2,512,128]{2,1,0:T(8,128)(2,1)}), bf16[8,512,128]{2,1,0:T(8,128)(2,1)}) %all-gather.12.cloned.1.call-update) | async-done | bytes 1048592 | tf_op jit(solution)/shard_map/all_gather | solution.py:100
  141.8 1.8 multiply_reduce_fusion.1
  145.4 5.7 %collective-permute-done.8 = bf16[256,512]{1,0:T(8,128)(2,1)S(1)} collective-permute-done((bf16[256,512]{1,0:T(8,128)(2,1)S(1)}, bf16[256,512]{1,0:T(8,128)(2,1)S(1)}, u32[]{:S(2)}, u32[]{:S(2)}) %collective-permute-start.8) | collective-permute-done | bytes 262176 | tf_op jit(solution)/shard_map/ppermute | solution.py:33
  151.1 6.6 %collective-permute-done.9 = bf16[256,512]{1,0:T(8,128)(2,1)S(1)} collective-permute-done((bf16[256,512]{1,0:T(8,128)(2,1)S(1)}, bf16[256,512]{1,0:T(8,128)(2,1)S(1)}, u32[]{:S(2)}, u32[]{:S(2)}) %collective-permute-start.9) | collective-permute-done | bytes 262176 | tf_op jit(solution)/shard_map/ppermute | solution.py:33
  158.0 1.2 fusion.69
  159.2 2.6 %multiply_reduce_fusion.3 = (f32[512]{0:T(512)S(1)}, f32[512,1024]{1,0:T(8,128)S(1)}) fusion(bf16[1024,512]{1,0:T(8,128)(2,1)S(1)} %bitcast.136, bf16[1024,1024]{1,0:T(8,128)(2,1)S(1)} %bitcast.128, bf16[512,1024]{1,0:T(8,128)(2,1)} %param.19), kind=kOutput, calls=%fused_computation.84 | convolution fusion | flops 1075838464 | bytes 6293504 | tf_op jit(solution)/shard_map/dot_general | solution.py:119
  161.8 1.1 fusion.47
  164.2 1.4 collective-permute-start.12
  165.9 4.1 %collective-permute-done.11 = bf16[256,512]{1,0:T(8,128)(2,1)S(1)} collective-permute-done((bf16[256,512]{1,0:T(8,128)(2,1)S(1)}, bf16[256,512]{1,0:T(8,128)(2,1)S(1)}, u32[]{:S(2)}, u32[]{:S(2)}) %collective-permute-start.11) | collective-permute-done | bytes 262176 | tf_op jit(solution)/shard_map/ppermute | solution.py:33
  170.0 8.1 %collective-permute-done.12 = bf16[256,512]{1,0:T(8,128)(2,1)S(1)} collective-permute-done((bf16[256,512]{1,0:T(8,128)(2,1)S(1)}, bf16[256,512]{1,0:T(8,128)(2,1)S(1)}, u32[]{:S(2)}, u32[]{:S(2)}) %collective-permute-start.12) | collective-permute-done | bytes 262176 | tf_op jit(solution)/shard_map/ppermute | solution.py:33
  178.3 1.2 fusion.62
  179.6 1.4 multiply_reduce_fusion.2
  181.0 0.9 fusion.51
  182.6 5.1 %convolution_convert_fusion.3 = bf16[1024,256]{0,1:T(8,128)(2,1)S(1)} fusion(bf16[3072,1024]{1,0:T(8,128)(2,1)} %bitcast.130, bf16[3072,256]{1,0:T(8,128)(2,1)} %all-gather.8.cloned.1.call-done), kind=kOutput, calls=%fused_computation.96 | convolution fusion | flops 1610874880 | bytes 8388608 | tf_op jit(solution)/shard_map/dot_general | solution.py:151
  188.5 2.0 copy-done.4
  190.5 1.0 fusion.48
  191.5 6.5 %psum.7 = f32[1024]{0:T(1024)S(1)} all-reduce(f32[1024]{0:T(1024)S(1)} %fusion.48), channel_id=1, replica_groups=mesh['groups'=2,'picks'=4,'heads'=4] {'heads'}, use_global_device_ids=true, to_apply=%region_9.12 | all-reduce | flops 1024 | bytes 8192 | tf_op jit(solution)/shard_map/psum | solution.py:160
  198.0 3.3 %fusion.2 = f32[2,1024]{1,0:T(2,128)S(1)} fusion(f32[2,512]{1,0:T(2,128)S(1)} %bitcast.177, f32[1024]{0:T(1024)S(1)} %sub.54, f32[2,1024]{1,0:T(2,128)S(1)} %get-tuple-element.38, f32[2,1024,512]{1,2,0:T(8,128)} %copy-done.4), kind=kLoop, calls=%fused_computation.11 | loop fusion | flops 5240832 | bytes 4218880 | tf_op jit(solution)/shard_map/reduce_sum | solution.py:168
  201.4 1.4 fusion.44
  203.5 3.1 %convolution_convert_fusion = bf16[3072,256]{1,0:T(8,128)(2,1)} fusion(bf16[3072,1024]{1,0:T(8,128)(2,1)S(1)} %bitcast.133, bf16[1024,256]{0,1:T(8,128)(2,1)S(1)} %bitcast.184), kind=kOutput, calls=%fused_computation.33 | convolution fusion | flops 1611399168 | bytes 8388608 | tf_op jit(solution)/shard_map/dot_general | solution.py:177
  206.6 1.9 constant_dynamic-slice_fusion
  208.5 31.9 %reduce-scatter.2.cloned.1.call-done = bf16[768,256]{1,0:T(8,128)(2,1)} async-done(((bf16[3072,256]{1,0:T(8,128)(2,1)}), bf16[768,256]{1,0:T(8,128)(2,1)}) %reduce-scatter.2.cloned.1.call-update) | async-done | bytes 393232 | tf_op jit(solution)/shard_map/reduce_scatter | solution.py:176
  240.5 1.9 convert_element_type.100
  (89 shorter events, 9.1 us)
Async XLA Ops:
  7.2 154.7 %copy-start = (bf16[3,1024,256]{2,1,0:T(8,128)(2,1)S(1)}, bf16[3,1024,256]{2,1,0:T(8,128)(2,1)}, u32[]{:S(2)}) copy-start(bf16[3,1024,256]{2,1,0:T(8,128)(2,1)} %param.23) | copy-start | bytes 4718596
  7.2 9.3 %copy-start.12 = (f32[3,1024]{1,0:T(4,128)S(1)}, f32[3,1024]{1,0:T(4,128)}, u32[]{:S(2)}) copy-start(f32[3,1024]{1,0:T(4,128)} %param.16) | copy-start | bytes 36868
  7.2 50.3 %all-gather.10.cloned.1.call-start = ((), (), s32[]{:S(2)}) async-start(), calls=%async_computation.3 | async-start | bytes 1310720 | tf_op jit(solution)/shard_map/all_gather | solution.py:49
  9.2 132.6 %all-gather.12.cloned.1.call-start = ((), (), s32[]{:S(2)}) async-start(), calls=%async_computation.4 | async-start | bytes 1310720 | tf_op jit(solution)/shard_map/all_gather | solution.py:100
  9.3 62.0 %collective-permute-start.3 = (bf16[256,1024]{1,0:T(8,128)(2,1)}, bf16[256,1024]{1,0:T(8,128)(2,1)}, u32[]{:S(2)}, u32[]{:S(2)}) collective-permute-start(bf16[256,1024]{1,0:T(8,128)(2,1)} %param.21), channel_id=1, source_target_pairs={{0,3},{1,0},{2,1},{3,2},{4,7},{5,4},{6,5},{7,6},{8,11},{9,8},{10,9... | collective-permute-start | bytes 1572872 | tf_op jit(solution)/shard_map/ppermute | solution.py:33
  11.7 60.5 %collective-permute-start.4 = (bf16[256,1024]{1,0:T(8,128)(2,1)}, bf16[256,1024]{1,0:T(8,128)(2,1)}, u32[]{:S(2)}, u32[]{:S(2)}) collective-permute-start(bf16[256,1024]{1,0:T(8,128)(2,1)} %param.21), channel_id=1, source_target_pairs={{0,2},{1,3},{2,0},{3,1},{4,6},{5,7},{6,4},{7,5},{8,10},{9,11},{10,... | collective-permute-start | bytes 1572872 | tf_op jit(solution)/shard_map/ppermute | solution.py:33
  12.3 59.9 %collective-permute-start.5 = (bf16[256,1024]{1,0:T(8,128)(2,1)}, bf16[256,1024]{1,0:T(8,128)(2,1)}, u32[]{:S(2)}, u32[]{:S(2)}) collective-permute-start(bf16[256,1024]{1,0:T(8,128)(2,1)} %param.21), channel_id=1, source_target_pairs={{0,1},{1,2},{2,3},{3,0},{4,5},{5,6},{6,7},{7,4},{8,9},{9,10},{10,1... | collective-permute-start | bytes 1572872 | tf_op jit(solution)/shard_map/ppermute | solution.py:33
  13.7 100.9 %collective-permute-start = (bf16[256,1024]{1,0:T(8,128)(2,1)S(1)}, bf16[256,1024]{1,0:T(8,128)(2,1)}, u32[]{:S(2)}, u32[]{:S(2)}) collective-permute-start(bf16[256,1024]{1,0:T(8,128)(2,1)S(1)} %bitcast.138), channel_id=1, source_target_pairs={{0,3},{1,0},{2,1},{3,2},{4,7},{5,4},{6,5},{7,6},{8,11},{9,8},{10,9... | collective-permute-start | bytes 1572872 | tf_op jit(solution)/shard_map/ppermute | solution.py:33
  58.9 34.3 %collective-permute-start.6 = (bf16[4,256,2,256]{3,1,0,2:T(8,128)(2,1)S(1)}, bf16[4,256,2,256]{3,1,0,2:T(8,128)(2,1)}, u32[]{:S(2)}, u32[]{:S(2)}) collective-permute-start(bf16[4,256,2,256]{3,1,0,2:T(8,128)(2,1)S(1)} %bitcast.134), channel_id=1, source_target_pairs={{0,16},{16,0},{1,17},{17,1},{2,18},{18,2},{3,19},{19,3},{4,20},{20... | collective-permute-start | bytes 3145736 | tf_op jit(solution)/shard_map/ppermute | solution.py:51
  65.1 7.1 %copy-start.9 = (bf16[512,2,256]{2,0,1:T(8,128)(2,1)S(1)}, bf16[512,2,256]{2,0,1:T(8,128)(2,1)}, u32[]{:S(2)}) copy-start(bf16[512,2,256]{2,0,1:T(8,128)(2,1)} %copy.89) | copy-start | bytes 1572868
  65.1 7.6 %copy-start.11 = (bf16[256,1024]{1,0:T(8,128)(2,1)S(1)}, bf16[256,1024]{1,0:T(8,128)(2,1)}, u32[]{:S(2)}) copy-start(bf16[256,1024]{1,0:T(8,128)(2,1)} %param.21) | copy-start | bytes 1572868
  71.3 43.4 %collective-permute-start.1 = (bf16[256,1024]{1,0:T(8,128)(2,1)S(1)}, bf16[256,1024]{1,0:T(8,128)(2,1)}, u32[]{:S(2)}, u32[]{:S(2)}) collective-permute-start(bf16[256,1024]{1,0:T(8,128)(2,1)S(1)} %bitcast.139), channel_id=1, source_target_pairs={{0,2},{1,3},{2,0},{3,1},{4,6},{5,7},{6,4},{7,5},{8,10},{9,11},{10,... | collective-permute-start | bytes 1572872 | tf_op jit(solution)/shard_map/ppermute | solution.py:33
  72.2 42.5 %collective-permute-start.2 = (bf16[256,1024]{1,0:T(8,128)(2,1)S(1)}, bf16[256,1024]{1,0:T(8,128)(2,1)}, u32[]{:S(2)}, u32[]{:S(2)}) collective-permute-start(bf16[256,1024]{1,0:T(8,128)(2,1)S(1)} %bitcast.140), channel_id=1, source_target_pairs={{0,1},{1,2},{2,3},{3,0},{4,5},{5,6},{6,7},{7,4},{8,9},{9,10},{10,1... | collective-permute-start | bytes 1572872 | tf_op jit(solution)/shard_map/ppermute | solution.py:33
  72.2 21.0 %collective-permute-start.7 = (bf16[4,128,2,256]{3,1,0,2:T(8,128)(2,1)S(1)}, bf16[4,128,2,256]{3,1,0,2:T(8,128)(2,1)S(1)}, u32[]{:S(2)}, u32[]{:S(2)}) collective-permute-start(bf16[4,128,2,256]{3,1,0,2:T(8,128)(2,1)S(1)} %bitcast.143), channel_id=1, source_target_pairs={{0,16},{16,0},{1,17},{17,1},{2,18},{18,2},{3,19},{19,3},{4,20},{20... | collective-permute-start | bytes 1572872 | tf_op jit(solution)/shard_map/ppermute | solution.py:51
  110.7 2.0 copy-start.2
  114.4 68.2 %all-gather.8.cloned.1.call-start = ((), (), s32[]{:S(2)}) async-start(), calls=%async_computation.1 | async-start | bytes 1966080 | tf_op jit(solution)/shard_map/all_gather | solution.py:117
  114.7 5.2 %copy-start.3 = (f32[2,512,1024]{2,1,0:T(8,128)S(1)}, f32[2,512,1024]{2,1,0:T(8,128)}, u32[]{:S(2)}) copy-start(f32[2,512,1024]{2,1,0:T(8,128)} %copy-done.2) | copy-start | bytes 12582916
  120.8 24.6 %copy-start.14 = (f32[2,1024]{1,0:T(2,128)S(1)}, f32[2,1024]{1,0:T(2,128)}, u32[]{:S(2)}) copy-start(f32[2,1024]{1,0:T(2,128)} %param.22) | copy-start | bytes 24580
  143.8 7.3 %collective-permute-start.8 = (bf16[256,512]{1,0:T(8,128)(2,1)S(1)}, bf16[256,512]{1,0:T(8,128)(2,1)S(1)}, u32[]{:S(2)}, u32[]{:S(2)}) collective-permute-start(bf16[256,512]{1,0:T(8,128)(2,1)S(1)} %bitcast.146), channel_id=1, source_target_pairs={{0,3},{1,0},{2,1},{3,2},{4,7},{5,4},{6,5},{7,6},{8,11},{9,8},{10,9... | collective-permute-start | bytes 786440 | tf_op jit(solution)/shard_map/ppermute | solution.py:33
  144.5 13.2 %collective-permute-start.9 = (bf16[256,512]{1,0:T(8,128)(2,1)S(1)}, bf16[256,512]{1,0:T(8,128)(2,1)S(1)}, u32[]{:S(2)}, u32[]{:S(2)}) collective-permute-start(bf16[256,512]{1,0:T(8,128)(2,1)S(1)} %bitcast.147), channel_id=1, source_target_pairs={{0,2},{1,3},{2,0},{3,1},{4,6},{5,7},{6,4},{7,5},{8,10},{9,11},{10,... | collective-permute-start | bytes 786440 | tf_op jit(solution)/shard_map/ppermute | solution.py:33
  145.2 12.8 %collective-permute-start.10 = (bf16[256,512]{1,0:T(8,128)(2,1)S(1)}, bf16[256,512]{1,0:T(8,128)(2,1)S(1)}, u32[]{:S(2)}, u32[]{:S(2)}) collective-permute-start(bf16[256,512]{1,0:T(8,128)(2,1)S(1)} %bitcast.148), channel_id=1, source_target_pairs={{0,1},{1,2},{2,3},{3,0},{4,5},{5,6},{6,7},{7,4},{8,9},{9,10},{10,1... | collective-permute-start | bytes 786440 | tf_op jit(solution)/shard_map/ppermute | solution.py:33
  145.4 95.1 %reduce-scatter.2.cloned.1.call-start = ((), (), s32[]{:S(2)}) async-start(), calls=%async_computation.2 | async-start | bytes 1966080 | tf_op jit(solution)/shard_map/reduce_scatter | solution.py:176
  145.4 13.8 %copy-start.6 = (bf16[4,256,1024]{2,1,0:T(8,128)(2,1)S(1)}, bf16[4,256,1024]{2,1,0:T(8,128)(2,1)}, u32[]{:S(2)}) copy-start(bf16[4,256,1024]{2,1,0:T(8,128)(2,1)} %fusion.17) | copy-start | bytes 6291460
  163.6 2.2 copy-start.15
  163.6 2.2 copy-start.17
  164.1 15.4 %copy-start.8 = (bf16[4,256,1024]{2,1,0:T(8,128)(2,1)S(1)}, bf16[4,256,1024]{2,1,0:T(8,128)(2,1)}, u32[]{:S(2)}) copy-start(bf16[4,256,1024]{2,1,0:T(8,128)(2,1)} %fusion.24) | copy-start | bytes 6291460
  164.1 5.9 %collective-permute-start.11 = (bf16[256,512]{1,0:T(8,128)(2,1)S(1)}, bf16[256,512]{1,0:T(8,128)(2,1)S(1)}, u32[]{:S(2)}, u32[]{:S(2)}) collective-permute-start(bf16[256,512]{1,0:T(8,128)(2,1)S(1)} %bitcast.164), channel_id=1, source_target_pairs={{0,3},{1,0},{2,1},{3,2},{4,7},{5,4},{6,5},{7,6},{8,11},{9,8},{10,9... | collective-permute-start | bytes 786440 | tf_op jit(solution)/shard_map/ppermute | solution.py:33
  164.2 13.9 %collective-permute-start.12 = (bf16[256,512]{1,0:T(8,128)(2,1)S(1)}, bf16[256,512]{1,0:T(8,128)(2,1)S(1)}, u32[]{:S(2)}, u32[]{:S(2)}) collective-permute-start(bf16[256,512]{1,0:T(8,128)(2,1)S(1)} %bitcast.165), channel_id=1, source_target_pairs={{0,2},{1,3},{2,0},{3,1},{4,6},{5,7},{6,4},{7,5},{8,10},{9,11},{10,... | collective-permute-start | bytes 786440 | tf_op jit(solution)/shard_map/ppermute | solution.py:33
  165.6 12.7 %collective-permute-start.13 = (bf16[256,512]{1,0:T(8,128)(2,1)S(1)}, bf16[256,512]{1,0:T(8,128)(2,1)S(1)}, u32[]{:S(2)}, u32[]{:S(2)}) collective-permute-start(bf16[256,512]{1,0:T(8,128)(2,1)S(1)} %bitcast.166), channel_id=1, source_target_pairs={{0,1},{1,2},{2,3},{3,0},{4,5},{5,6},{6,7},{7,4},{8,9},{9,10},{10,1... | collective-permute-start | bytes 786440 | tf_op jit(solution)/shard_map/ppermute | solution.py:33
  179.6 1.4 copy-start.10
  181.0 1.3 copy-start.7
  181.0 1.3 copy-start.16
  188.5 2.0 copy-start.4
  197.9 3.4 %copy-start.13 = (f32[1024]{0:T(1024)}, f32[1024]{0:T(1024)S(1)}, u32[]{:S(2)}) copy-start(f32[1024]{0:T(1024)S(1)} %psum.7) | copy-start | bytes 12292
  197.9 3.5 %copy-start.5 = (f32[2,1024,512]{1,2,0:T(8,128)S(1)}, f32[2,1024,512]{1,2,0:T(8,128)}, u32[]{:S(2)}) copy-start(f32[2,1024,512]{1,2,0:T(8,128)} %copy-done.4) | copy-start | bytes 12582916
  198.0 4.8 %slice-start = ((s8[6291456]{0:T(1024)(128)(4,1)}), s8[4194304]{0:T(1024)(128)(4,1)S(1)}, s32[]{:S(2)}) async-start(s8[6291456]{0:T(1024)(128)(4,1)} %bitcast.131), calls=%async_computation.5 | async-start | bytes 8388608
  201.4 2.1 slice-start.1
  203.5 38.9 %copy-start.1 = (bf16[3,1024,256]{2,1,0:T(8,128)(2,1)S(1)}, bf16[3,1024,256]{2,1,0:T(8,128)(2,1)}, u32[]{:S(2)}) copy-start(bf16[3,1024,256]{2,1,0:T(8,128)(2,1)} %param.23) | copy-start | bytes 4718596
Sparse Core Ops, SparseCore 0:
  10.2 30.7 all-gather.9
  114.5 27.2 all-gather.11
  145.5 37.0 all-gather.7
  206.8 33.6 reduce-scatter.1

commit v4 on v3

--- a/solution.py
+++ b/solution.py
@@ -82,7 +82,7 @@
     column = lax.axis_index("heads") * local
     enc = encode(coords)
     cross_full = ring_gather(cross_out, "heads", n_heads)
-    piece = fetch_rows(kv_weight, n_picks, n_groups)
+    piece = lax.all_gather(kv_weight, "picks", axis=0, tiled=True)
     cross_full, piece = lax.optimization_barrier((cross_full, piece))
     keys_vals = jnp.dot(
         enc, piece.reshape(piece.shape[0], 2 * local), preferred_element_type=jnp.float32

time: 250 us -> 223 us (0.89)
  blocking collectives: 36.3 us -> 19.7 us
  waiting for transfers between devices: 80 us -> 93.9 us
  local copies, waits for them, and re-layouts: 22.4 us -> 13.6 us
  other arithmetic: 56.4 us -> 47.6 us
  matrix products: 28.2 us -> 23.3 us
    all_gather x1 -> x0, blocking collectives: 16.5 us -> none  [fetch_rows(): gathered = lax.all_gather(mine[lo:hi], 'picks', axis=0, tiled=False)]
    ppermute x2 -> x0, waiting for transfers between devices: 15.4 us -> none  [fetch_rows(): other.append(lax.ppermute(gathered, 'groups', [(0, 1), (1, 0)]))]
    all_gather x1, waiting for transfers between devices: 0.01 us -> 14.5 us  [on_device(): piece = lax.all_gather(kv_weight, 'picks', axis=0, tiled=True)]
    ppermute x12, waiting for transfers between devices: 25 us -> 38.8 us  [ring_gather(): blocks.append(lax.ppermute(x, axis, [(i, (i - s) % n) for i in range(n)]))]
    optimization_barrier x1 -> x0, local copies, waits for them, and re-layouts: 4.65 us -> none  [on_device(): cross_full, piece = lax.optimization_barrier((cross_full, piece))]
    dot_general x1, matrix products: 7.15 us -> 3.54 us  [on_device(): jnp.dot(enc, piece.reshape(piece.shape[0], 2 * local), preferred_element_...]
    concatenate x1 -> x0, other arithmetic: 3.47 us -> none  [fetch_rows(): halves = jnp.roll(halves, g, axis=1)]
    all_gather x2 -> x0, local copies, waits for them, and re-layouts: 3.27 us -> none  [fetch_rows(): gathered = lax.all_gather(mine[lo:hi], 'picks', axis=0, tiled=False)]
  transfers between devices with their start and end apart: 18 -> 16, of which waited for: 9 -> 12; matrix products, arithmetic and copies ran while one was open for 33% -> 27% of each run, Pallas kernels for 0% -> 0%
where the time goes in v4:
time: 223 us; the launch traced here: 222 us
  waiting for transfers between devices  93.9 us (42%)
  other arithmetic  47.6 us (21%)
  matrix products  23.3 us (10%)
  blocking collectives  19.7 us (9%)
  between operations  14.2 us (6%)
  local copies, waits for them, and re-layouts  13.6 us (6%)
  starting transfers between devices  9.79 us (4%)
    ppermute x12, waiting for transfers between devices, ring_gather(): blocks.append(lax.ppermute(x, axis, [(i, (i - s) % n) for i in range(n)]))  38.8 us
    reduce_scatter x1, waiting for transfers between devices, on_device(): lax.psum_scatter(jnp.dot(enc.T, dquery, preferred_element_type=jnp.float3...  31.9 us
    another operation x1, other arithmetic  22.8 us
    all_gather x1, waiting for transfers between devices, on_device(): piece = lax.all_gather(kv_weight, 'picks', axis=0, tiled=True)  14.5 us
    all_gather x1, blocking collectives, on_device(): lax.all_gather(jnp.stack([top, total]), 'picks', axis=0, tiled=False)  13.3 us
    concatenate x4, other arithmetic, ring_gather(): ordered = jnp.roll(flipped, idx, axis=0)  13.3 us
    unnamed x43, local copies, waits for them, and re-layouts  10.4 us
    ppermute x12, starting transfers between devices, ring_gather(): blocks.append(lax.ppermute(x, axis, [(i, (i - s) % n) for i in range(n)]))  9.45 us
  transfers between devices with their start and end apart: 16, of which 12 were waited for; matrix products, arithmetic and copies ran while one was open for 27% of the time, Pallas kernels for 0%

profile of v4, /device:TPU:0, one launch (start us, length us, event | category | flops | bytes accessed | tf_op | source)
XLA Modules:
  0.0 222.1 jit_solution(10662230604038274768)
XLA Ops:
  7.2 0.7 all-gather.6.cloned.1.call-update
  8.0 1.2 copy.57
  9.2 2.4 %collective-permute-start = (bf16[256,1024]{1,0:T(8,128)(2,1)S(1)}, bf16[256,1024]{1,0:T(8,128)(2,1)S(1)}, u32[]{:S(2)}, u32[]{:S(2)}) collective-permute-start(bf16[256,1024]{1,0:T(8,128)(2,1)S(1)} %bitcast.127), channel_id=1, source_target_pairs={{0,3},{1,0},{2,1},{3,2},{4,7},{5,4},{6,5},{7,6},{8,11},{9,8},{10,9... | collective-permute-start | bytes 1572872 | tf_op jit(solution)/shard_map/ppermute | solution.py:33
  11.7 0.6 collective-permute-start.1
  12.4 1.7 collective-permute-start.4
  14.1 1.0 constant_dynamic-slice_fusion.1
  15.3 22.8 %fusion = (bf16[3,512,1024]{2,1,0:T(8,128)(2,1)S(1)}, bf16[3,512,1024]{2,1,0:T(8,128)(2,1)S(1)}) fusion(f32[3,1024]{1,0:T(4,128)S(1)} %copy-done.12, f32[512]{0:T(512)S(1)} %maximum_multiply_fusion), kind=kLoop, calls=%fused_computation.2 | loop fusion | flops 4718592 | bytes 6305792 | tf_op jit(solution)/shard_map/convert
  38.2 3.2 %pad_maximum_fusion = bf16[6,512,1024]{2,1,0:T(8,128)(2,1)} fusion(bf16[3,512,1024]{2,1,0:T(8,128)(2,1)S(1)} %get-tuple-element.27, bf16[3,512,1024]{2,1,0:T(8,128)(2,1)S(1)} %get-tuple-element.26), kind=kLoop, calls=%fused_computation.4 | loop fusion | flops 3145728 | bytes 12582912 | tf_op jit(solution)/shard_map/concatenate | solution.py:21
  41.4 5.1 %collective-permute-done.3 = bf16[256,1024]{1,0:T(8,128)(2,1)} collective-permute-done((bf16[256,1024]{1,0:T(8,128)(2,1)}, bf16[256,1024]{1,0:T(8,128)(2,1)}, u32[]{:S(2)}, u32[]{:S(2)}) %collective-permute-start.3) | collective-permute-done | bytes 524320 | tf_op jit(solution)/shard_map/ppermute | solution.py:33
  46.4 1.1 collective-permute-start.2
  47.5 8.8 %collective-permute-done.4 = bf16[256,1024]{1,0:T(8,128)(2,1)} collective-permute-done((bf16[256,1024]{1,0:T(8,128)(2,1)}, bf16[256,1024]{1,0:T(8,128)(2,1)}, u32[]{:S(2)}, u32[]{:S(2)}) %collective-permute-start.4) | collective-permute-done | bytes 524320 | tf_op jit(solution)/shard_map/ppermute | solution.py:33
  56.3 5.1 %fusion.14 = bf16[4,256,1024]{2,1,0:T(8,128)(2,1)} fusion(s32[]{:T(128)S(6)} %select_n.27, bf16[1,256,1024]{2,1,0:T(8,128)(2,1)S(1)} %bitcast.146, bf16[1,256,1024]{2,1,0:T(8,128)(2,1)} %bitcast.12, bf16[1,256,1024]{2,1,0:T(8,128)(2,1)} %bitcast.13, bf16[1,256,1024]{2,1,0:T(8,128)(2,1)} %bitcast.14), kind=kLoop, calls=%fused_computation.38 | loop fusion | flops 7340032 | bytes 4194308 | tf_op jit(solution)/shard_map/jit(_roll_dynamic)/concatenate | solution.py:35
  61.3 14.5 %all-gather.6.cloned.1.call-done = bf16[3072,2,256]{2,1,0:T(2,128)(2,1)} async-done(((bf16[768,2,256]{2,1,0:T(2,128)(2,1)}), bf16[3072,2,256]{2,1,0:T(2,128)(2,1)}) %all-gather.6.cloned.1.call-update) | async-done | bytes 3145744 | tf_op jit(solution)/shard_map/all_gather | solution.py:85
  75.8 2.6 %copy.95 = bf16[384,8,2,256]{3,1,2,0:T(8,128)(2,1)S(1)} copy(bf16[384,8,2,256]{3,2,1,0:T(2,128)(2,1)} %bitcast.125) | data formatting | bytes 6291456
  78.4 1.1 copy-done.6
  79.6 3.5 %convolution_convert_fusion.1 = bf16[1024,512]{0,1:T(8,128)(2,1)S(1)} fusion(bf16[3072,1024]{1,0:T(8,128)(2,1)S(1)} %bitcast.120, bf16[3072,512]{1,0:T(8,128)(2,1)S(1)} %bitcast.126), kind=kOutput, calls=%fused_computation.83 | convolution fusion | flops 3221749760 | bytes 10485760 | tf_op jit(solution)/shard_map/dot_general | solution.py:87
  83.2 0.8 multiply_reduce_fusion
  84.1 2.0 copy-done.1
  86.1 1.6 fusion.49
  88.0 4.8 %fusion.21 = bf16[4,256,1024]{2,1,0:T(8,128)(2,1)} fusion(s32[]{:T(128)S(6)} %select_n.27, bf16[1,256,1024]{2,1,0:T(8,128)(2,1)S(1)} %bitcast.130, bf16[1,256,1024]{2,1,0:T(8,128)(2,1)S(1)} %bitcast.147, bf16[1,256,1024]{2,1,0:T(8,128)(2,1)} %bitcast.5, bf16[1,256,1024]{2,1,0:T(8,128)(2,1)} %bitcast.6), kind=kLoop, calls=%fused_computation.45 | loop fusion | flops 7340032 | bytes 4194308 | tf_op jit(solution)/shard_map/jit(_roll_dynamic)/concatenate | solution.py:35
  92.7 0.9 fusion.7
  93.7 13.3 %all-gather.1 = f32[8,2,512]{2,1,0:T(2,128)S(1)} all-gather(f32[2,2,512]{2,1,0:T(2,128)S(1)} %pad_maximum_fusion.1), channel_id=3, replica_groups=mesh['groups'=2,'picks'=4,'heads'=4] {'picks'}, dimensions={0}, use_global_device_ids=true | all-gather | bytes 40960 | tf_op jit(solution)/shard_map/all_gather | solution.py:101
  107.0 7.7 %all-gather.10.cloned.1.call-done = bf16[8,512,128]{2,1,0:T(8,128)(2,1)} async-done(((bf16[2,512,128]{2,1,0:T(8,128)(2,1)}), bf16[8,512,128]{2,1,0:T(8,128)(2,1)}) %all-gather.10.cloned.1.call-update) | async-done | bytes 1048592 | tf_op jit(solution)/shard_map/all_gather | solution.py:100
  114.7 1.8 multiply_reduce_fusion.1
  116.8 1.0 collective-permute-start.6
  118.7 5.7 %collective-permute-done.6 = bf16[256,512]{1,0:T(8,128)(2,1)S(1)} collective-permute-done((bf16[256,512]{1,0:T(8,128)(2,1)S(1)}, bf16[256,512]{1,0:T(8,128)(2,1)S(1)}, u32[]{:S(2)}, u32[]{:S(2)}) %collective-permute-start.6) | collective-permute-done | bytes 262176 | tf_op jit(solution)/shard_map/ppermute | solution.py:33
  124.3 6.7 %collective-permute-done.7 = bf16[256,512]{1,0:T(8,128)(2,1)S(1)} collective-permute-done((bf16[256,512]{1,0:T(8,128)(2,1)S(1)}, bf16[256,512]{1,0:T(8,128)(2,1)S(1)}, u32[]{:S(2)}, u32[]{:S(2)}) %collective-permute-start.7) | collective-permute-done | bytes 262176 | tf_op jit(solution)/shard_map/ppermute | solution.py:33
  131.2 2.2 fusion.66
  133.4 1.4 multiply_reduce_fusion.3
  134.8 1.1 fusion.44
  137.2 1.5 collective-permute-start.10
  139.0 3.9 %collective-permute-done.9 = bf16[256,512]{1,0:T(8,128)(2,1)S(1)} collective-permute-done((bf16[256,512]{1,0:T(8,128)(2,1)S(1)}, bf16[256,512]{1,0:T(8,128)(2,1)S(1)}, u32[]{:S(2)}, u32[]{:S(2)}) %collective-permute-start.9) | collective-permute-done | bytes 262176 | tf_op jit(solution)/shard_map/ppermute | solution.py:33
  142.9 8.4 %collective-permute-done.10 = bf16[256,512]{1,0:T(8,128)(2,1)S(1)} collective-permute-done((bf16[256,512]{1,0:T(8,128)(2,1)S(1)}, bf16[256,512]{1,0:T(8,128)(2,1)S(1)}, u32[]{:S(2)}, u32[]{:S(2)}) %collective-permute-start.10) | collective-permute-done | bytes 262176 | tf_op jit(solution)/shard_map/ppermute | solution.py:33
  151.4 1.2 fusion.59
  152.7 1.4 multiply_reduce_fusion.2
  154.1 0.9 fusion.48
  155.8 5.1 %convolution_convert_fusion.3 = bf16[1024,256]{0,1:T(8,128)(2,1)S(1)} fusion(bf16[3072,1024]{1,0:T(8,128)(2,1)} %bitcast.119, bf16[3072,256]{1,0:T(8,128)(2,1)} %all-gather.8.cloned.1.call-done), kind=kOutput, calls=%fused_computation.87 | convolution fusion | flops 1610874880 | bytes 8388608 | tf_op jit(solution)/shard_map/dot_general | solution.py:151
  160.9 0.8 fusion.6
  161.7 2.0 copy-done.3
  163.8 1.0 fusion.45
  164.7 6.4 %psum.7 = f32[1024]{0:T(1024)S(1)} all-reduce(f32[1024]{0:T(1024)S(1)} %fusion.45), channel_id=1, replica_groups=mesh['groups'=2,'picks'=4,'heads'=4] {'heads'}, use_global_device_ids=true, to_apply=%region_9.12 | all-reduce | flops 1024 | bytes 8192 | tf_op jit(solution)/shard_map/psum | solution.py:160
  171.2 3.3 %fusion.2 = f32[2,1024]{1,0:T(2,128)S(1)} fusion(f32[2,512]{1,0:T(2,128)S(1)} %bitcast.164, f32[1024]{0:T(1024)S(1)} %sub.49, f32[2,1024]{1,0:T(2,128)S(1)} %get-tuple-element.38, f32[2,1024,512]{1,2,0:T(8,128)} %copy-done.3), kind=kLoop, calls=%fused_computation.7 | loop fusion | flops 5240832 | bytes 4218880 | tf_op jit(solution)/shard_map/reduce_sum | solution.py:168
  174.6 1.4 fusion.41
  176.0 0.7 slice-done.1
  176.7 3.1 %convolution_convert_fusion = bf16[3072,256]{1,0:T(8,128)(2,1)} fusion(bf16[3072,1024]{1,0:T(8,128)(2,1)S(1)} %bitcast.123, bf16[1024,256]{0,1:T(8,128)(2,1)S(1)} %bitcast.171), kind=kOutput, calls=%fused_computation.29 | convolution fusion | flops 1611399168 | bytes 8388608 | tf_op jit(solution)/shard_map/dot_general | solution.py:177
  179.8 1.9 constant_dynamic-slice_fusion
  181.7 31.9 %reduce-scatter.2.cloned.1.call-done = bf16[768,256]{1,0:T(8,128)(2,1)} async-done(((bf16[3072,256]{1,0:T(8,128)(2,1)}), bf16[768,256]{1,0:T(8,128)(2,1)}) %reduce-scatter.2.cloned.1.call-update) | async-done | bytes 393232 | tf_op jit(solution)/shard_map/reduce_scatter | solution.py:176
  213.7 1.9 convert_element_type.100
  (77 shorter events, 4.7 us)
Async XLA Ops:
  7.2 127.6 %copy-start = (bf16[3,1024,256]{2,1,0:T(8,128)(2,1)S(1)}, bf16[3,1024,256]{2,1,0:T(8,128)(2,1)}, u32[]{:S(2)}) copy-start(bf16[3,1024,256]{2,1,0:T(8,128)(2,1)} %param.23) | copy-start | bytes 4718596
  7.2 8.1 %copy-start.12 = (f32[3,1024]{1,0:T(4,128)S(1)}, f32[3,1024]{1,0:T(4,128)}, u32[]{:S(2)}) copy-start(f32[3,1024]{1,0:T(4,128)} %param.16) | copy-start | bytes 36868
  7.2 68.7 %all-gather.6.cloned.1.call-start = ((), (), s32[]{:S(2)}) async-start(), calls=%async_computation.1 | async-start | bytes 3932160 | tf_op jit(solution)/shard_map/all_gather | solution.py:85
  7.9 106.8 %all-gather.10.cloned.1.call-start = ((), (), s32[]{:S(2)}) async-start(), calls=%async_computation.4 | async-start | bytes 1310720 | tf_op jit(solution)/shard_map/all_gather | solution.py:100
  9.2 78.7 %collective-permute-start = (bf16[256,1024]{1,0:T(8,128)(2,1)S(1)}, bf16[256,1024]{1,0:T(8,128)(2,1)S(1)}, u32[]{:S(2)}, u32[]{:S(2)}) collective-permute-start(bf16[256,1024]{1,0:T(8,128)(2,1)S(1)} %bitcast.127), channel_id=1, source_target_pairs={{0,3},{1,0},{2,1},{3,2},{4,7},{5,4},{6,5},{7,6},{8,11},{9,8},{10,9... | collective-permute-start | bytes 1572872 | tf_op jit(solution)/shard_map/ppermute | solution.py:33
  11.7 76.3 %collective-permute-start.1 = (bf16[256,1024]{1,0:T(8,128)(2,1)S(1)}, bf16[256,1024]{1,0:T(8,128)(2,1)}, u32[]{:S(2)}, u32[]{:S(2)}) collective-permute-start(bf16[256,1024]{1,0:T(8,128)(2,1)S(1)} %bitcast.128), channel_id=1, source_target_pairs={{0,2},{1,3},{2,0},{3,1},{4,6},{5,7},{6,4},{7,5},{8,10},{9,11},{10,... | collective-permute-start | bytes 1572872 | tf_op jit(solution)/shard_map/ppermute | solution.py:33
  12.3 34.1 %collective-permute-start.3 = (bf16[256,1024]{1,0:T(8,128)(2,1)}, bf16[256,1024]{1,0:T(8,128)(2,1)}, u32[]{:S(2)}, u32[]{:S(2)}) collective-permute-start(bf16[256,1024]{1,0:T(8,128)(2,1)} %param.21), channel_id=1, source_target_pairs={{0,3},{1,0},{2,1},{3,2},{4,7},{5,4},{6,5},{7,6},{8,11},{9,8},{10,9... | collective-permute-start | bytes 1572872 | tf_op jit(solution)/shard_map/ppermute | solution.py:33
  12.4 43.9 %collective-permute-start.4 = (bf16[256,1024]{1,0:T(8,128)(2,1)}, bf16[256,1024]{1,0:T(8,128)(2,1)}, u32[]{:S(2)}, u32[]{:S(2)}) collective-permute-start(bf16[256,1024]{1,0:T(8,128)(2,1)} %param.21), channel_id=1, source_target_pairs={{0,2},{1,3},{2,0},{3,1},{4,6},{5,7},{6,4},{7,5},{8,10},{9,11},{10,... | collective-permute-start | bytes 1572872 | tf_op jit(solution)/shard_map/ppermute | solution.py:33
  14.1 42.2 %collective-permute-start.5 = (bf16[256,1024]{1,0:T(8,128)(2,1)}, bf16[256,1024]{1,0:T(8,128)(2,1)}, u32[]{:S(2)}, u32[]{:S(2)}) collective-permute-start(bf16[256,1024]{1,0:T(8,128)(2,1)} %param.21), channel_id=1, source_target_pairs={{0,1},{1,2},{2,3},{3,0},{4,5},{5,6},{6,7},{7,4},{8,9},{9,10},{10,1... | collective-permute-start | bytes 1572872 | tf_op jit(solution)/shard_map/ppermute | solution.py:33
  38.2 18.1 %copy-start.11 = (bf16[256,1024]{1,0:T(8,128)(2,1)S(1)}, bf16[256,1024]{1,0:T(8,128)(2,1)}, u32[]{:S(2)}) copy-start(bf16[256,1024]{1,0:T(8,128)(2,1)} %param.21) | copy-start | bytes 1572868
  46.4 41.5 %collective-permute-start.2 = (bf16[256,1024]{1,0:T(8,128)(2,1)S(1)}, bf16[256,1024]{1,0:T(8,128)(2,1)}, u32[]{:S(2)}, u32[]{:S(2)}) collective-permute-start(bf16[256,1024]{1,0:T(8,128)(2,1)S(1)} %bitcast.129), channel_id=1, source_target_pairs={{0,1},{1,2},{2,3},{3,0},{4,5},{5,6},{6,7},{7,4},{8,9},{9,10},{10,1... | collective-permute-start | bytes 1572872 | tf_op jit(solution)/shard_map/ppermute | solution.py:33
  75.8 3.7 %copy-start.6 = (bf16[6,512,1024]{2,1,0:T(8,128)(2,1)S(1)}, bf16[6,512,1024]{2,1,0:T(8,128)(2,1)}, u32[]{:S(2)}) copy-start(bf16[6,512,1024]{2,1,0:T(8,128)(2,1)} %pad_maximum_fusion) | copy-start | bytes 18874372
  84.0 2.0 copy-start.1
  87.7 68.1 %all-gather.8.cloned.1.call-start = ((), (), s32[]{:S(2)}) async-start(), calls=%async_computation.2 | async-start | bytes 1966080 | tf_op jit(solution)/shard_map/all_gather | solution.py:117
  88.0 4.8 %copy-start.2 = (f32[2,512,1024]{2,1,0:T(8,128)S(1)}, f32[2,512,1024]{2,1,0:T(8,128)}, u32[]{:S(2)}) copy-start(f32[2,512,1024]{2,1,0:T(8,128)} %copy-done.1) | copy-start | bytes 12582916
  93.7 24.9 %copy-start.14 = (f32[2,1024]{1,0:T(2,128)S(1)}, f32[2,1024]{1,0:T(2,128)}, u32[]{:S(2)}) copy-start(f32[2,1024]{1,0:T(2,128)} %param.22) | copy-start | bytes 24580
  116.7 16.7 %copy-start.9 = (bf16[512,1024]{1,0:T(8,128)(2,1)S(1)}, bf16[512,1024]{1,0:T(8,128)(2,1)}, u32[]{:S(2)}) copy-start(bf16[512,1024]{1,0:T(8,128)(2,1)} %param.19) | copy-start | bytes 3145732
  116.8 7.5 %collective-permute-start.6 = (bf16[256,512]{1,0:T(8,128)(2,1)S(1)}, bf16[256,512]{1,0:T(8,128)(2,1)S(1)}, u32[]{:S(2)}, u32[]{:S(2)}) collective-permute-start(bf16[256,512]{1,0:T(8,128)(2,1)S(1)} %bitcast.133), channel_id=1, source_target_pairs={{0,3},{1,0},{2,1},{3,2},{4,7},{5,4},{6,5},{7,6},{8,11},{9,8},{10,9... | collective-permute-start | bytes 786440 | tf_op jit(solution)/shard_map/ppermute | solution.py:33
  117.7 13.2 %collective-permute-start.7 = (bf16[256,512]{1,0:T(8,128)(2,1)S(1)}, bf16[256,512]{1,0:T(8,128)(2,1)S(1)}, u32[]{:S(2)}, u32[]{:S(2)}) collective-permute-start(bf16[256,512]{1,0:T(8,128)(2,1)S(1)} %bitcast.134), channel_id=1, source_target_pairs={{0,2},{1,3},{2,0},{3,1},{4,6},{5,7},{6,4},{7,5},{8,10},{9,11},{10,... | collective-permute-start | bytes 786440 | tf_op jit(solution)/shard_map/ppermute | solution.py:33
  118.4 12.8 %collective-permute-start.8 = (bf16[256,512]{1,0:T(8,128)(2,1)S(1)}, bf16[256,512]{1,0:T(8,128)(2,1)}, u32[]{:S(2)}, u32[]{:S(2)}) collective-permute-start(bf16[256,512]{1,0:T(8,128)(2,1)S(1)} %bitcast.135), channel_id=1, source_target_pairs={{0,1},{1,2},{2,3},{3,0},{4,5},{5,6},{6,7},{7,4},{8,9},{9,10},{10,1... | collective-permute-start | bytes 786440 | tf_op jit(solution)/shard_map/ppermute | solution.py:33
  118.6 95.1 %reduce-scatter.2.cloned.1.call-start = ((), (), s32[]{:S(2)}) async-start(), calls=%async_computation.3 | async-start | bytes 1966080 | tf_op jit(solution)/shard_map/reduce_scatter | solution.py:176
  118.6 14.8 %copy-start.5 = (bf16[4,256,1024]{2,1,0:T(8,128)(2,1)S(1)}, bf16[4,256,1024]{2,1,0:T(8,128)(2,1)}, u32[]{:S(2)}) copy-start(bf16[4,256,1024]{2,1,0:T(8,128)(2,1)} %fusion.14) | copy-start | bytes 6291460
  136.6 2.3 %copy-start.15 = (s32[1024]{0:T(1024)S(1)}, s32[1024]{0:T(1024)}, u32[]{:S(2)}) copy-start(s32[1024]{0:T(1024)} %param.17) | copy-start | bytes 12292
  136.6 2.3 %copy-start.17 = (f32[64]{0:T(128)S(1)}, f32[64]{0:T(128)}, u32[]{:S(2)}) copy-start(f32[64]{0:T(128)} %param.18) | copy-start | bytes 772
  137.1 15.5 %copy-start.8 = (bf16[4,256,1024]{2,1,0:T(8,128)(2,1)S(1)}, bf16[4,256,1024]{2,1,0:T(8,128)(2,1)}, u32[]{:S(2)}) copy-start(bf16[4,256,1024]{2,1,0:T(8,128)(2,1)} %fusion.21) | copy-start | bytes 6291460
  137.1 5.7 %collective-permute-start.9 = (bf16[256,512]{1,0:T(8,128)(2,1)S(1)}, bf16[256,512]{1,0:T(8,128)(2,1)S(1)}, u32[]{:S(2)}, u32[]{:S(2)}) collective-permute-start(bf16[256,512]{1,0:T(8,128)(2,1)S(1)} %bitcast.152), channel_id=1, source_target_pairs={{0,3},{1,0},{2,1},{3,2},{4,7},{5,4},{6,5},{7,6},{8,11},{9,8},{10,9... | collective-permute-start | bytes 786440 | tf_op jit(solution)/shard_map/ppermute | solution.py:33
  137.2 14.1 %collective-permute-start.10 = (bf16[256,512]{1,0:T(8,128)(2,1)S(1)}, bf16[256,512]{1,0:T(8,128)(2,1)S(1)}, u32[]{:S(2)}, u32[]{:S(2)}) collective-permute-start(bf16[256,512]{1,0:T(8,128)(2,1)S(1)} %bitcast.153), channel_id=1, source_target_pairs={{0,2},{1,3},{2,0},{3,1},{4,6},{5,7},{6,4},{7,5},{8,10},{9,11},{10,... | collective-permute-start | bytes 786440 | tf_op jit(solution)/shard_map/ppermute | solution.py:33
  138.7 12.7 %collective-permute-start.11 = (bf16[256,512]{1,0:T(8,128)(2,1)S(1)}, bf16[256,512]{1,0:T(8,128)(2,1)S(1)}, u32[]{:S(2)}, u32[]{:S(2)}) collective-permute-start(bf16[256,512]{1,0:T(8,128)(2,1)S(1)} %bitcast.154), channel_id=1, source_target_pairs={{0,1},{1,2},{2,3},{3,0},{4,5},{5,6},{6,7},{7,4},{8,9},{9,10},{10,1... | collective-permute-start | bytes 786440 | tf_op jit(solution)/shard_map/ppermute | solution.py:33
  152.7 1.4 copy-start.10
  154.1 1.3 copy-start.7
  154.1 1.3 copy-start.16
  161.7 2.0 copy-start.3
  171.2 3.4 %copy-start.13 = (f32[1024]{0:T(1024)}, f32[1024]{0:T(1024)S(1)}, u32[]{:S(2)}) copy-start(f32[1024]{0:T(1024)S(1)} %psum.7) | copy-start | bytes 12292
  171.2 3.5 %copy-start.4 = (f32[2,1024,512]{1,2,0:T(8,128)S(1)}, f32[2,1024,512]{1,2,0:T(8,128)}, u32[]{:S(2)}) copy-start(f32[2,1024,512]{1,2,0:T(8,128)} %copy-done.3) | copy-start | bytes 12582916
  171.2 4.8 %slice-start = ((s8[6291456]{0:T(1024)(128)(4,1)}), s8[4194304]{0:T(1024)(128)(4,1)S(1)}, s32[]{:S(2)}) async-start(s8[6291456]{0:T(1024)(128)(4,1)} %bitcast.121), calls=%async_computation.5 | async-start | bytes 8388608
  174.6 2.1 slice-start.1
Sparse Core Ops, SparseCore 0:
  9.6 66.2 all-gather.5
  87.8 26.8 all-gather.9
  118.7 37.0 all-gather.7
  180.0 33.6 reduce-scatter.1

commit v5 on v4

--- a/solution.py
+++ b/solution.py
@@ -52,6 +52,19 @@
     halves = jnp.stack([jnp.concatenate(own, axis=1), jnp.concatenate(other, axis=1)], axis=1)
     halves = jnp.roll(halves, g, axis=1)
     return halves.reshape((n_picks * kv_weight.shape[0],) + kv_weight.shape[1:])
+
+
+def pair_gather(x, axis, n):
+    if n != 4:
+        return ring_gather(x, axis, n)
+    idx = lax.axis_index(axis)
+    near = lax.ppermute(x, axis, [(k, k ^ 1) for k in range(n)])
+    far = lax.ppermute(x, axis, [(k, k ^ 2) for k in range(n)])
+    far_near = lax.ppermute(far, axis, [(k, k ^ 1) for k in range(n)])
+    cand = jnp.stack([x, near, far, far_near])
+    cand = jnp.where(idx % 2 == 1, cand[jnp.array([1, 0, 3, 2])], cand)
+    cand = jnp.where(idx // 2 % 2 == 1, cand[jnp.array([2, 3, 0, 1])], cand)
+    return cand.reshape((n * x.shape[0],) + x.shape[1:])
 
 
 def on_device(
@@ -81,7 +94,7 @@
     nheads = local // HEAD
     column = lax.axis_index("heads") * local
     enc = encode(coords)
-    cross_full = ring_gather(cross_out, "heads", n_heads)
+    cross_full = pair_gather(cross_out, "heads", n_heads)
     piece = lax.all_gather(kv_weight, "picks", axis=0, tiled=True)
     cross_full, piece = lax.optimization_barrier((cross_full, piece))
     keys_vals = jnp.dot(
@@ -111,11 +124,11 @@
         .reshape(lat_rows, local)
         .astype(jnp.bfloat16)
     )
-    out_full = ring_gather(self_out.T, "heads", n_heads).T
+    out_full = pair_gather(self_out.T, "heads", n_heads).T
     out_full, attended = lax.optimization_barrier((out_full, attended))
     dq_local, attended = lax.optimization_barrier((dec_query, attended))
     dq_full = lax.all_gather(dq_local, "picks", axis=0, tiled=True)
-    attended_full = ring_gather(attended.T, "heads", n_heads).T
+    attended_full = pair_gather(attended.T, "heads", n_heads).T
     whole = latents.astype(jnp.float32) + jnp.dot(
         attended_full, cross_full, preferred_element_type=jnp.float32
     )
@@ -136,7 +149,7 @@
         .astype(jnp.bfloat16)
         .reshape(lat_rows, local)
     )
-    every_head = ring_gather(head_out.T, "heads", n_heads).T
+    every_head = pair_gather(head_out.T, "heads", n_heads).T
     out_whole = whole + jnp.dot(every_head, out_full, preferred_element_type=jnp.float32)
     latents_out = lax.dynamic_slice_in_dim(out_whole, column, local, 1)
     power_two = jnp.mean(out_whole * out_whole, axis=1, keepdims=True)

time: 223 us -> 256 us (1.15)
  local copies, waits for them, and re-layouts: 13.6 us -> 37.7 us
  other arithmetic: 47.6 us -> 61.5 us
  waiting for transfers between devices: 93.9 us -> 87.5 us
  matrix products: 23.3 us -> 26.1 us
    all_gather x1, waiting for transfers between devices: 0.2 us -> 26.9 us  [on_device(): dq_full = lax.all_gather(dq_local, 'picks', axis=0, tiled=True)]
    ppermute x12, waiting for transfers between devices: 38.8 us -> 15.9 us  [the longest x4 13 us: pair_gather(): far = lax.ppermute(x, axis, [(k, k ^ 2) for k in range(n)])]
    gather x0 -> x8, local copies, waits for them, and re-layouts: none -> 21.7 us  [the longest x4 11.9 us: pair_gather(): cand = jnp.where(idx // 2 % 2 == 1, cand[jnp.array([2, 3, 0, 1])], cand)]
    select_n x0 -> x7, other arithmetic: none -> 14.8 us  [the longest x4 7.91 us: pair_gather(): cand = jnp.where(idx // 2 % 2 == 1, cand[jnp.array([2, 3, 0, 1])], cand)]
    concatenate x4 -> x0, other arithmetic: 13.3 us -> none  [ring_gather(): ordered = jnp.roll(flipped, idx, axis=0)]
    another operation x1 -> x5, other arithmetic: 22.8 us -> 32.3 us
    all_gather x1, waiting for transfers between devices: 14.5 us -> 6.1 us  [on_device(): piece = lax.all_gather(kv_weight, 'picks', axis=0, tiled=True)]
    concatenate x1, other arithmetic: 3.2 us -> 6.1 us  [encode(): table = jnp.concatenate([jnp.sin(angle), jnp.cos(angle)], axis=0)]
  transfers between devices with their start and end apart: 16 -> 16, of which waited for: 12 -> 8; matrix products, arithmetic and copies ran while one was open for 27% -> 29% of each run, Pallas kernels for 0% -> 0%
where the time goes in v5:
time: 256 us; the launch traced here: 255 us
  waiting for transfers between devices  87.5 us (34%)
  other arithmetic  61.5 us (24%)
  local copies, waits for them, and re-layouts  37.7 us (15%)
  matrix products  26.1 us (10%)
  blocking collectives  19.9 us (8%)
  between operations  14.2 us (6%)
  starting transfers between devices  7.85 us (3%)
    reduce_scatter x1, waiting for transfers between devices, on_device(): lax.psum_scatter(jnp.dot(enc.T, dquery, preferred_element_type=jnp.float3...  31.9 us
    all_gather x1, waiting for transfers between devices, on_device(): dq_full = lax.all_gather(dq_local, 'picks', axis=0, tiled=True)  26.9 us
    another operation x1, other arithmetic  25.3 us
    all_gather x1, blocking collectives, on_device(): lax.all_gather(jnp.stack([top, total]), 'picks', axis=0, tiled=False)  13.4 us
    ppermute x4, waiting for transfers between devices, pair_gather(): far = lax.ppermute(x, axis, [(k, k ^ 2) for k in range(n)])  13 us
    unnamed x51, local copies, waits for them, and re-layouts  12.8 us
    gather x4, local copies, waits for them, and re-layouts, pair_gather(): cand = jnp.where(idx // 2 % 2 == 1, cand[jnp.array([2, 3, 0, 1])], cand)  11.9 us
    gather x4, local copies, waits for them, and re-layouts, pair_gather(): cand = jnp.where(idx % 2 == 1, cand[jnp.array([1, 0, 3, 2])], cand)  9.77 us
  transfers between devices with their start and end apart: 16, of which 8 were waited for; matrix products, arithmetic and copies ran while one was open for 29% of the time, Pallas kernels for 0%

profile of v5, /device:TPU:0, one launch (start us, length us, event | category | flops | bytes accessed | tf_op | source)
XLA Modules:
  0.0 254.7 jit_solution(18399444201901619421)
XLA Ops:
  8.0 3.0 %collective-permute-start.4 = (bf16[256,1024]{1,0:T(8,128)(2,1)}, bf16[256,1024]{1,0:T(8,128)(2,1)S(1)}, u32[]{:S(2)}, u32[]{:S(2)}) collective-permute-start(bf16[256,1024]{1,0:T(8,128)(2,1)} %param.25), channel_id=1, source_target_pairs={{0,2},{1,3},{2,0},{3,1},{4,6},{5,7},{6,4},{7,5},{8,10},{9,11},{10,... | collective-permute-start | bytes 1572872 | tf_op jit(solution)/shard_map/ppermute | solution.py:62
  11.0 1.2 copy.68
  13.0 25.3 %fusion = (bf16[3,512,1024]{2,1,0:T(8,128)(2,1)}, bf16[3,512,1024]{2,1,0:T(8,128)(2,1)}) fusion(f32[3,1024]{1,0:T(4,128)} %param.20, f32[512]{0:T(512)S(1)} %maximum_multiply_fusion), kind=kLoop, calls=%fused_computation.10 | loop fusion | flops 4718592 | bytes 6305792 | tf_op jit(solution)/shard_map/convert
  40.1 6.1 %pad_maximum_fusion = bf16[6,512,1024]{2,1,0:T(8,128)(2,1)} fusion(bf16[3,512,1024]{2,1,0:T(8,128)(2,1)} %get-tuple-element.25, bf16[3,512,1024]{2,1,0:T(8,128)(2,1)} %get-tuple-element.24), kind=kLoop, calls=%fused_computation.12 | loop fusion | flops 3145728 | bytes 12582912 | tf_op jit(solution)/shard_map/concatenate | solution.py:21
  46.2 2.9 %pad_maximum_fusion.2 = bf16[4,256,1024]{2,1,0:T(8,128)(2,1)} fusion(bf16[1,256,1024]{2,1,0:T(8,128)(2,1)} %bitcast.14, bf16[1,256,1024]{2,1,0:T(8,128)(2,1)S(1)} %bitcast.162, bf16[1,256,1024]{2,1,0:T(8,128)(2,1)} %bitcast.12, bf16[1,256,1024]{2,1,0:T(8,128)(2,1)S(1)} %bitcast.160), kind=kLoop, calls=%fused_computation.29 | loop fusion | flops 3145728 | bytes 4194304 | tf_op jit(solution)/shard_map/stack | solution.py:64
  49.1 3.6 %gather_fusion.2 = bf16[4,256,1024]{2,1,0:T(8,128)(2,1)} fusion(bf16[4,256,1024]{2,1,0:T(8,128)(2,1)} %pad_maximum_fusion.2, s32[1024]{0:T(1024)S(1)} %pad_clamp_fusion.1), kind=kCustom, calls=%fused_computation.2 | custom fusion | bytes 4194320 | tf_op jit(solution)/shard_map/gather | solution.py:65
  52.7 2.9 %pad_maximum_fusion.1 = bf16[4,256,1024]{2,1,0:T(8,128)(2,1)} fusion(bf16[1,256,1024]{2,1,0:T(8,128)(2,1)} %bitcast.6, bf16[1,256,1024]{2,1,0:T(8,128)(2,1)} %bitcast.5, bf16[1,256,1024]{2,1,0:T(8,128)(2,1)} %bitcast.4, bf16[1,256,1024]{2,1,0:T(8,128)(2,1)S(1)} %bitcast.126), kind=kLoop, calls=%fused_computation.28 | loop fusion | flops 3145728 | bytes 4194304 | tf_op jit(solution)/shard_map/stack | solution.py:64
  55.6 3.7 %gather_fusion = bf16[4,256,1024]{2,1,0:T(8,128)(2,1)} fusion(bf16[4,256,1024]{2,1,0:T(8,128)(2,1)} %pad_maximum_fusion.1, s32[1024]{0:T(1024)S(1)} %pad_clamp_fusion.1), kind=kCustom, calls=%fused_computation | custom fusion | bytes 4194320 | tf_op jit(solution)/shard_map/gather | solution.py:65
  59.4 3.7 %broadcast_select_fusion = (bf16[4,256,1024]{2,1,0:T(8,128)(2,1)}, bf16[4,256,1024]{2,1,0:T(8,128)(2,1)}) fusion(bf16[4,256,1024]{2,1,0:T(8,128)(2,1)} %gather_fusion.2, pred[]{:T(512)S(6)} %eq.35, bf16[1,256,1024]{2,1,0:T(8,128)(2,1)} %bitcast.14, bf16[1,256,1024]{2,1,0:T(8,128)(2,1)S(1)} %bitcast.163, bf16[1,256,1024]{2,1,0:T(8,128)(2,1)} %bitcast.12, ...), kind=kLoop, calls=%fused_computation.45 | loop fusion | flops 8388608 | bytes 12582913 | tf_op jit(solution)/shard_map/jit(_where)/select_n | solution.py:65
  63.0 3.6 %gather_fusion.3 = bf16[4,256,1024]{2,1,0:T(8,128)(2,1)} fusion(bf16[4,256,1024]{2,1,0:T(8,128)(2,1)} %get-tuple-element.38, s32[1024]{0:T(1024)S(1)} %pad_clamp_fusion), kind=kCustom, calls=%fused_computation.3 | custom fusion | bytes 4194320 | tf_op jit(solution)/shard_map/gather | solution.py:66
  66.6 3.1 %broadcast_select_fusion.2 = bf16[4,256,1024]{2,1,0:T(8,128)(2,1)} fusion(bf16[4,256,1024]{2,1,0:T(8,128)(2,1)} %gather_fusion.3, bf16[4,256,1024]{2,1,0:T(8,128)(2,1)} %get-tuple-element.38, pred[]{:T(512)S(6)} %eq.34), kind=kLoop, calls=%fused_computation.47 | loop fusion | flops 1048576 | bytes 6291457 | tf_op jit(solution)/shard_map/jit(_where)/select_n | solution.py:66
  69.7 6.1 %all-gather.6.cloned.1.call-done = bf16[3072,2,256]{2,1,0:T(2,128)(2,1)} async-done(((bf16[768,2,256]{2,1,0:T(2,128)(2,1)}), bf16[3072,2,256]{2,1,0:T(2,128)(2,1)}) %all-gather.6.cloned.1.call-update) | async-done | bytes 3145744 | tf_op jit(solution)/shard_map/all_gather | solution.py:98
  75.8 2.4 copy.106
  78.3 6.3 %convolution_convert_fusion.1 = bf16[1024,512]{0,1:T(8,128)(2,1)S(1)} fusion(bf16[3072,1024]{1,0:T(8,128)(2,1)} %bitcast.119, bf16[3072,512]{1,0:T(8,128)(2,1)S(1)} %bitcast.135), kind=kOutput, calls=%fused_computation.51 | convolution fusion | flops 3221749760 | bytes 10485760 | tf_op jit(solution)/shard_map/dot_general | solution.py:100
  85.5 2.0 copy-done.2
  87.5 1.6 fusion.35
  89.2 3.6 %gather_fusion.1 = bf16[4,256,1024]{2,1,0:T(8,128)(2,1)} fusion(bf16[4,256,1024]{2,1,0:T(8,128)(2,1)} %get-tuple-element.39, s32[1024]{0:T(1024)S(1)} %pad_clamp_fusion), kind=kCustom, calls=%fused_computation.1 | custom fusion | bytes 4194320 | tf_op jit(solution)/shard_map/gather | solution.py:66
  92.8 3.3 %broadcast_select_fusion.3 = bf16[4,256,1024]{2,1,0:T(8,128)(2,1)} fusion(bf16[4,256,1024]{2,1,0:T(8,128)(2,1)} %gather_fusion.1, bf16[4,256,1024]{2,1,0:T(8,128)(2,1)} %get-tuple-element.39, pred[]{:T(512)S(6)} %eq.34), kind=kLoop, calls=%fused_computation.48 | loop fusion | flops 1048576 | bytes 6291457 | tf_op jit(solution)/shard_map/jit(_where)/select_n | solution.py:66
  97.0 13.4 %all-gather.1 = f32[8,2,512]{2,1,0:T(2,128)S(1)} all-gather(f32[2,2,512]{2,1,0:T(2,128)S(1)} %pad_maximum_fusion.5), channel_id=3, replica_groups=mesh['groups'=2,'picks'=4,'heads'=4] {'picks'}, dimensions={0}, use_global_device_ids=true | all-gather | bytes 40960 | tf_op jit(solution)/shard_map/all_gather | solution.py:114
  110.5 5.9 %all-gather.10.cloned.1.call-done = bf16[8,512,128]{2,1,0:T(8,128)(2,1)} async-done(((bf16[2,512,128]{2,1,0:T(8,128)(2,1)}), bf16[8,512,128]{2,1,0:T(8,128)(2,1)}) %all-gather.10.cloned.1.call-update) | async-done | bytes 1048592 | tf_op jit(solution)/shard_map/all_gather | solution.py:113
  116.4 1.8 multiply_reduce_fusion.1
  118.4 1.5 collective-permute-start.7
  120.0 6.4 %collective-permute-done.7 = bf16[256,512]{1,0:T(8,128)(2,1)S(1)} collective-permute-done((bf16[256,512]{1,0:T(8,128)(2,1)S(1)}, bf16[256,512]{1,0:T(8,128)(2,1)S(1)}, u32[]{:S(2)}, u32[]{:S(2)}) %collective-permute-start.7) | collective-permute-done | bytes 262176 | tf_op jit(solution)/shard_map/ppermute | solution.py:62
  126.5 1.5 collective-permute-done.8
  128.7 1.1 pad_maximum_fusion.3
  129.8 1.8 gather_fusion.4
  131.6 2.1 broadcast_select_fusion.5
  133.7 2.9 %gather_fusion.5 = bf16[4,256,512]{2,1,0:T(8,128)(2,1)} fusion(bf16[4,256,512]{2,1,0:T(8,128)(2,1)} %broadcast_select_fusion.5, s32[1024]{0:T(1024)S(1)} %pad_clamp_fusion), kind=kCustom, calls=%fused_computation.5 | custom fusion | bytes 2097168 | tf_op jit(solution)/shard_map/gather | solution.py:66
  136.6 1.3 broadcast_select_fusion.7
  138.5 1.4 multiply_reduce_fusion.3
  139.9 1.1 fusion.30
  142.4 1.8 collective-permute-start.10
  144.2 6.6 %collective-permute-done.10 = bf16[256,512]{1,0:T(8,128)(2,1)S(1)} collective-permute-done((bf16[256,512]{1,0:T(8,128)(2,1)S(1)}, bf16[256,512]{1,0:T(8,128)(2,1)S(1)}, u32[]{:S(2)}, u32[]{:S(2)}) %collective-permute-start.10) | collective-permute-done | bytes 262176 | tf_op jit(solution)/shard_map/ppermute | solution.py:62
  151.1 1.3 collective-permute-done.11
  153.1 1.1 broadcast_select_fusion.4
  154.3 1.8 gather_fusion.7
  156.3 1.4 copy-done.9
  158.5 1.4 multiply_reduce_fusion.2
  161.4 26.9 %all-gather.8.cloned.1.call-done = bf16[3072,256]{1,0:T(8,128)(2,1)} async-done(((bf16[768,256]{1,0:T(8,128)(2,1)}), bf16[3072,256]{1,0:T(8,128)(2,1)}) %all-gather.8.cloned.1.call-update) | async-done | bytes 1572880 | tf_op jit(solution)/shard_map/all_gather | solution.py:130
  188.3 5.1 %convolution_convert_fusion.3 = bf16[1024,256]{0,1:T(8,128)(2,1)S(1)} fusion(bf16[3072,1024]{1,0:T(8,128)(2,1)} %bitcast.120, bf16[3072,256]{1,0:T(8,128)(2,1)} %all-gather.8.cloned.1.call-done), kind=kOutput, calls=%fused_computation.55 | convolution fusion | flops 1610874880 | bytes 8388608 | tf_op jit(solution)/shard_map/dot_general | solution.py:164
  194.2 2.0 copy-done.4
  197.2 6.5 %psum.7 = f32[1024]{0:T(1024)S(1)} all-reduce(f32[1024]{0:T(1024)S(1)} %fusion.31), channel_id=1, replica_groups=mesh['groups'=2,'picks'=4,'heads'=4] {'heads'}, use_global_device_ids=true, to_apply=%region_9.10 | all-reduce | flops 1024 | bytes 8192 | tf_op jit(solution)/shard_map/psum | solution.py:173
  203.7 3.3 %fusion.2 = f32[2,1024]{1,0:T(2,128)S(1)} fusion(f32[2,512]{1,0:T(2,128)S(1)} %bitcast.181, f32[1024]{0:T(1024)S(1)} %sub.51, f32[2,1024]{1,0:T(2,128)S(1)} %get-tuple-element.36, f32[2,1024,512]{1,2,0:T(8,128)} %copy-done.4), kind=kLoop, calls=%fused_computation.15 | loop fusion | flops 5240832 | bytes 4218880 | tf_op jit(solution)/shard_map/reduce_sum | solution.py:181
  207.2 1.4 fusion.27
  209.2 3.1 %convolution_convert_fusion = bf16[3072,256]{1,0:T(8,128)(2,1)} fusion(bf16[3072,1024]{1,0:T(8,128)(2,1)S(1)} %bitcast.123, bf16[1024,256]{0,1:T(8,128)(2,1)S(1)} %bitcast.188), kind=kOutput, calls=%fused_computation.21 | convolution fusion | flops 1611399168 | bytes 8388608 | tf_op jit(solution)/shard_map/dot_general | solution.py:190
  212.4 1.9 constant_dynamic-slice_fusion.1
  214.3 31.9 %reduce-scatter.2.cloned.1.call-done = bf16[768,256]{1,0:T(8,128)(2,1)} async-done(((bf16[3072,256]{1,0:T(8,128)(2,1)}), bf16[768,256]{1,0:T(8,128)(2,1)}) %reduce-scatter.2.cloned.1.call-update) | async-done | bytes 393232 | tf_op jit(solution)/shard_map/reduce_scatter | solution.py:189
  246.2 1.9 convert_element_type.100
  (102 shorter events, 14.1 us)
Async XLA Ops:
  7.2 132.7 %copy-start = (bf16[3,1024,256]{2,1,0:T(8,128)(2,1)S(1)}, bf16[3,1024,256]{2,1,0:T(8,128)(2,1)}, u32[]{:S(2)}) copy-start(bf16[3,1024,256]{2,1,0:T(8,128)(2,1)} %param.27) | copy-start | bytes 4718596
  7.2 68.7 %all-gather.6.cloned.1.call-start = ((), (), s32[]{:S(2)}) async-start(), calls=%async_computation.1 | async-start | bytes 3932160 | tf_op jit(solution)/shard_map/all_gather | solution.py:98
  7.9 108.5 %all-gather.10.cloned.1.call-start = ((), (), s32[]{:S(2)}) async-start(), calls=%async_computation.4 | async-start | bytes 1310720 | tf_op jit(solution)/shard_map/all_gather | solution.py:113
  8.0 30.3 %collective-permute-start.4 = (bf16[256,1024]{1,0:T(8,128)(2,1)}, bf16[256,1024]{1,0:T(8,128)(2,1)S(1)}, u32[]{:S(2)}, u32[]{:S(2)}) collective-permute-start(bf16[256,1024]{1,0:T(8,128)(2,1)} %param.25), channel_id=1, source_target_pairs={{0,2},{1,3},{2,0},{3,1},{4,6},{5,7},{6,4},{7,5},{8,10},{9,11},{10,... | collective-permute-start | bytes 1572872 | tf_op jit(solution)/shard_map/ppermute | solution.py:62
  11.0 35.2 %collective-permute-start.3 = (bf16[256,1024]{1,0:T(8,128)(2,1)}, bf16[256,1024]{1,0:T(8,128)(2,1)}, u32[]{:S(2)}, u32[]{:S(2)}) collective-permute-start(bf16[256,1024]{1,0:T(8,128)(2,1)} %param.25), channel_id=1, source_target_pairs={{0,1},{1,0},{2,3},{3,2},{4,5},{5,4},{6,7},{7,6},{8,9},{9,8},{10,11... | collective-permute-start | bytes 1572872 | tf_op jit(solution)/shard_map/ppermute | solution.py:61
  12.2 27.3 %collective-permute-start.1 = (bf16[256,1024]{1,0:T(8,128)(2,1)S(1)}, bf16[256,1024]{1,0:T(8,128)(2,1)}, u32[]{:S(2)}, u32[]{:S(2)}) collective-permute-start(bf16[256,1024]{1,0:T(8,128)(2,1)S(1)} %bitcast.124), channel_id=1, source_target_pairs={{0,2},{1,3},{2,0},{3,1},{4,6},{5,7},{6,4},{7,5},{8,10},{9,11},{10,... | collective-permute-start | bytes 1572872 | tf_op jit(solution)/shard_map/ppermute | solution.py:62
  12.4 40.3 %collective-permute-start = (bf16[256,1024]{1,0:T(8,128)(2,1)S(1)}, bf16[256,1024]{1,0:T(8,128)(2,1)}, u32[]{:S(2)}, u32[]{:S(2)}) collective-permute-start(bf16[256,1024]{1,0:T(8,128)(2,1)S(1)} %bitcast.125), channel_id=1, source_target_pairs={{0,1},{1,0},{2,3},{3,2},{4,5},{5,4},{6,7},{7,6},{8,9},{9,8},{10,11... | collective-permute-start | bytes 1572872 | tf_op jit(solution)/shard_map/ppermute | solution.py:61
  13.0 26.5 %copy-start.21 = (s32[4]{0:T(128)S(1)}, s32[4]{0:T(128)}, u32[]{:S(2)}) copy-start(s32[4]{0:T(128)} %constant.105) | copy-start | bytes 52
  13.0 27.1 %copy-start.20 = (s32[4]{0:T(128)S(1)}, s32[4]{0:T(128)}, u32[]{:S(2)}) copy-start(s32[4]{0:T(128)} %constant.106) | copy-start | bytes 52
  38.2 8.0 %collective-permute-start.5 = (bf16[256,1024]{1,0:T(8,128)(2,1)S(1)}, bf16[256,1024]{1,0:T(8,128)(2,1)}, u32[]{:S(2)}, u32[]{:S(2)}) collective-permute-start(bf16[256,1024]{1,0:T(8,128)(2,1)S(1)} %collective-permute-done.4), channel_id=1, source_target_pairs={{0,1},{1,0},{2,3},{3,2},{4,5},{5,4},{6,7},{7,6},{8,9},{9,8},{10,11... | collective-permute-start | bytes 1572872 | tf_op jit(solution)/shard_map/ppermute | solution.py:63
  39.5 13.2 %collective-permute-start.2 = (bf16[256,1024]{1,0:T(8,128)(2,1)}, bf16[256,1024]{1,0:T(8,128)(2,1)}, u32[]{:S(2)}, u32[]{:S(2)}) collective-permute-start(bf16[256,1024]{1,0:T(8,128)(2,1)} %collective-permute-done.1), channel_id=1, source_target_pairs={{0,1},{1,0},{2,3},{3,2},{4,5},{5,4},{6,7},{7,6},{8,9},{9,8},{10,11... | collective-permute-start | bytes 1572872 | tf_op jit(solution)/shard_map/ppermute | solution.py:63
  40.1 6.1 %copy-start.12 = (bf16[256,1024]{1,0:T(8,128)(2,1)S(1)}, bf16[256,1024]{1,0:T(8,128)(2,1)}, u32[]{:S(2)}) copy-start(bf16[256,1024]{1,0:T(8,128)(2,1)} %param.25) | copy-start | bytes 1572868
  85.5 2.0 copy-start.2
  89.1 99.2 %all-gather.8.cloned.1.call-start = ((), (), s32[]{:S(2)}) async-start(), calls=%async_computation.2 | async-start | bytes 1966080 | tf_op jit(solution)/shard_map/all_gather | solution.py:130
  92.8 3.3 %copy-start.3 = (f32[2,512,1024]{2,1,0:T(8,128)S(1)}, f32[2,512,1024]{2,1,0:T(8,128)}, u32[]{:S(2)}) copy-start(f32[2,512,1024]{2,1,0:T(8,128)} %copy-done.2) | copy-start | bytes 12582916
  97.0 29.4 %copy-start.16 = (f32[2,1024]{1,0:T(2,128)S(1)}, f32[2,1024]{1,0:T(2,128)}, u32[]{:S(2)}) copy-start(f32[2,1024]{1,0:T(2,128)} %param.26) | copy-start | bytes 24580
  118.4 8.0 %collective-permute-start.7 = (bf16[256,512]{1,0:T(8,128)(2,1)S(1)}, bf16[256,512]{1,0:T(8,128)(2,1)S(1)}, u32[]{:S(2)}, u32[]{:S(2)}) collective-permute-start(bf16[256,512]{1,0:T(8,128)(2,1)S(1)} %bitcast.129), channel_id=1, source_target_pairs={{0,2},{1,3},{2,0},{3,1},{4,6},{5,7},{6,4},{7,5},{8,10},{9,11},{10,... | collective-permute-start | bytes 786440 | tf_op jit(solution)/shard_map/ppermute | solution.py:62
  120.0 6.5 %collective-permute-start.6 = (bf16[256,512]{1,0:T(8,128)(2,1)S(1)}, bf16[256,512]{1,0:T(8,128)(2,1)S(1)}, u32[]{:S(2)}, u32[]{:S(2)}) collective-permute-start(bf16[256,512]{1,0:T(8,128)(2,1)S(1)} %bitcast.130), channel_id=1, source_target_pairs={{0,1},{1,0},{2,3},{3,2},{4,5},{5,4},{6,7},{7,6},{8,9},{9,8},{10,11... | collective-permute-start | bytes 786440 | tf_op jit(solution)/shard_map/ppermute | solution.py:61
  126.4 1.5 collective-permute-start.8
  128.0 0.7 copy-start.8
  136.6 1.7 copy-start.6
  136.6 1.9 copy-start.13
  139.9 1.4 copy-start.10
  141.8 9.1 %copy-start.17 = (s32[1024]{0:T(1024)S(1)}, s32[1024]{0:T(1024)}, u32[]{:S(2)}) copy-start(s32[1024]{0:T(1024)} %param.21) | copy-start | bytes 12292
  141.8 9.1 %copy-start.19 = (f32[64]{0:T(128)S(1)}, f32[64]{0:T(128)}, u32[]{:S(2)}) copy-start(f32[64]{0:T(128)} %param.22) | copy-start | bytes 772
  142.4 8.5 %collective-permute-start.10 = (bf16[256,512]{1,0:T(8,128)(2,1)S(1)}, bf16[256,512]{1,0:T(8,128)(2,1)S(1)}, u32[]{:S(2)}, u32[]{:S(2)}) collective-permute-start(bf16[256,512]{1,0:T(8,128)(2,1)S(1)} %bitcast.136), channel_id=1, source_target_pairs={{0,2},{1,3},{2,0},{3,1},{4,6},{5,7},{6,4},{7,5},{8,10},{9,11},{10,... | collective-permute-start | bytes 786440 | tf_op jit(solution)/shard_map/ppermute | solution.py:62
  144.2 6.8 %collective-permute-start.9 = (bf16[256,512]{1,0:T(8,128)(2,1)S(1)}, bf16[256,512]{1,0:T(8,128)(2,1)S(1)}, u32[]{:S(2)}, u32[]{:S(2)}) collective-permute-start(bf16[256,512]{1,0:T(8,128)(2,1)S(1)} %bitcast.137), channel_id=1, source_target_pairs={{0,1},{1,0},{2,3},{3,2},{4,5},{5,4},{6,7},{7,6},{8,9},{9,8},{10,11... | collective-permute-start | bytes 786440 | tf_op jit(solution)/shard_map/ppermute | solution.py:61
  150.8 1.5 collective-permute-start.11
  150.9 95.4 %reduce-scatter.2.cloned.1.call-start = ((), (), s32[]{:S(2)}) async-start(), calls=%async_computation.3 | async-start | bytes 1966080 | tf_op jit(solution)/shard_map/reduce_scatter | solution.py:189
  156.1 1.6 copy-start.9
  156.1 2.3 copy-start.11
  158.4 1.4 copy-start.14
  159.8 1.3 copy-start.7
  159.9 1.3 copy-start.18
  194.2 2.0 copy-start.4
  203.7 3.4 %copy-start.15 = (f32[1024]{0:T(1024)}, f32[1024]{0:T(1024)S(1)}, u32[]{:S(2)}) copy-start(f32[1024]{0:T(1024)S(1)} %psum.7) | copy-start | bytes 12292
  203.7 3.5 %copy-start.5 = (f32[2,1024,512]{1,2,0:T(8,128)S(1)}, f32[2,1024,512]{1,2,0:T(8,128)}, u32[]{:S(2)}) copy-start(f32[2,1024,512]{1,2,0:T(8,128)} %copy-done.4) | copy-start | bytes 12582916
  203.7 4.8 %slice-start = ((s8[6291456]{0:T(1024)(128)(4,1)}), s8[4194304]{0:T(1024)(128)(4,1)S(1)}, s32[]{:S(2)}) async-start(s8[6291456]{0:T(1024)(128)(4,1)} %bitcast.121), calls=%async_computation.5 | async-start | bytes 8388608
  207.2 2.1 slice-start.1
  209.2 38.9 %copy-start.1 = (bf16[3,1024,256]{2,1,0:T(8,128)(2,1)S(1)}, bf16[3,1024,256]{2,1,0:T(8,128)(2,1)}, u32[]{:S(2)}) copy-start(bf16[3,1024,256]{2,1,0:T(8,128)(2,1)} %param.27) | copy-start | bytes 4718596
Sparse Core Ops, SparseCore 0:
  9.6 66.2 all-gather.5
  89.3 27.0 all-gather.9
  151.0 37.2 all-gather.7
  212.5 33.6 reduce-scatter.1

commit v6 on v4

--- a/solution.py
+++ b/solution.py
@@ -52,6 +52,13 @@
     halves = jnp.stack([jnp.concatenate(own, axis=1), jnp.concatenate(other, axis=1)], axis=1)
     halves = jnp.roll(halves, g, axis=1)
     return halves.reshape((n_picks * kv_weight.shape[0],) + kv_weight.shape[1:])
+
+
+def pair_sum(x, axis, n):
+    if n != 4:
+        return lax.psum(x, axis)
+    x = x + lax.ppermute(x, axis, [(k, k ^ 1) for k in range(n)])
+    return x + lax.ppermute(x, axis, [(k, k ^ 2) for k in range(n)])
 
 
 def on_device(
@@ -82,7 +89,9 @@
     column = lax.axis_index("heads") * local
     enc = encode(coords)
     cross_full = ring_gather(cross_out, "heads", n_heads)
-    piece = lax.all_gather(kv_weight, "picks", axis=0, tiled=True)
+    piece = lax.all_gather(
+        kv_weight.reshape(kv_weight.shape[0], 2 * local), "picks", axis=0, tiled=True
+    )
     cross_full, piece = lax.optimization_barrier((cross_full, piece))
     keys_vals = jnp.dot(
         enc, piece.reshape(piece.shape[0], 2 * local), preferred_element_type=jnp.float32
@@ -157,7 +166,7 @@
         "htl,lhc->thc", weights.astype(jnp.bfloat16), dec_vals, preferred_element_type=jnp.float32
     )
     read = readout.reshape(nheads, HEAD)
-    field = lax.psum(jnp.sum(out * read[None, :, :], axis=(1, 2)), "heads")
+    field = pair_sum(jnp.sum(out * read[None, :, :], axis=(1, 2)), "heads", n_heads)
     onehot = (horizon_ids[:, None] == jnp.arange(HORIZONS, dtype=jnp.int32)[None, :]).astype(
         jnp.float32
     )

time: 223 us -> 219 us (0.982)
  blocking collectives: 19.7 us -> 13.3 us
  matrix products: 23.3 us -> 26.9 us
  local copies, waits for them, and re-layouts: 13.6 us -> 10.1 us
  waiting for transfers between devices: 93.9 us -> 96.8 us
    psum x1 -> x0, blocking collectives: 6.42 us -> none  [on_device(): field = lax.psum(jnp.sum(out * read[None, :, :], axis=(1, 2)), 'heads')]
    dot_general x1, matrix products: 3.54 us -> 7.15 us  [on_device(): jnp.dot(enc, piece.reshape(piece.shape[0], 2 * local), preferred_element_...]
    unnamed x43 -> x37, local copies, waits for them, and re-layouts: 10.4 us -> 6.86 us
    ppermute x0 -> x2, waiting for transfers between devices: none -> 3.5 us  [the longest x1 2.48 us: pair_sum(): return x + lax.ppermute(x, axis, [(k, k ^ 2) for k in range(n)])]
    reduce_sum x1, other arithmetic: 3.35 us -> 1.01 us  [on_device(): jnp.sum(dprob * weights, axis=2, keepdims=True)]
  transfers between devices with their start and end apart: 16 -> 18, of which waited for: 12 -> 13; matrix products, arithmetic and copies ran while one was open for 27% -> 27% of each run, Pallas kernels for 0% -> 0%
where the time goes in v6:
time: 219 us; the launch traced here: 218 us
  waiting for transfers between devices  96.8 us (44%)
  other arithmetic  46.1 us (21%)
  matrix products  26.9 us (12%)
  between operations  14.2 us (6%)
  blocking collectives  13.3 us (6%)
  starting transfers between devices  10.9 us (5%)
  local copies, waits for them, and re-layouts  10.1 us (5%)
    ppermute x12, waiting for transfers between devices, ring_gather(): blocks.append(lax.ppermute(x, axis, [(i, (i - s) % n) for i in range(n)]))  38.7 us
    reduce_scatter x1, waiting for transfers between devices, on_device(): lax.psum_scatter(jnp.dot(enc.T, dquery, preferred_element_type=jnp.float3...  32.5 us
    another operation x1, other arithmetic  22.8 us
    all_gather x1, waiting for transfers between devices, on_device(): lax.all_gather(kv_weight.reshape(kv_weight.shape[0], 2 * local), 'picks',...  14.6 us
    concatenate x4, other arithmetic, ring_gather(): ordered = jnp.roll(flipped, idx, axis=0)  13.5 us
    all_gather x1, blocking collectives, on_device(): lax.all_gather(jnp.stack([top, total]), 'picks', axis=0, tiled=False)  13.3 us
    ppermute x12, starting transfers between devices, ring_gather(): blocks.append(lax.ppermute(x, axis, [(i, (i - s) % n) for i in range(n)]))  9.55 us
    all_gather x1, waiting for transfers between devices, on_device(): lax.all_gather(numer.astype(jnp.bfloat16), 'picks', axis=0, tiled=False)  7.49 us
  transfers between devices with their start and end apart: 18, of which 13 were waited for; matrix products, arithmetic and copies ran while one was open for 27% of the time, Pallas kernels for 0%

profile of v6, /device:TPU:0, one launch (start us, length us, event | category | flops | bytes accessed | tf_op | source)
XLA Modules:
  0.0 218.3 jit_solution(3556526954416550381)
XLA Ops:
  7.3 2.3 %copy.95 = bf16[96,8,2,256]{3,1,2,0:T(8,128)(2,1)} copy(bf16[96,8,2,256]{3,2,1,0:T(2,128)(2,1)} %bitcast.145) | data formatting | bytes 1572864
  9.9 2.4 %collective-permute-start = (bf16[256,1024]{1,0:T(8,128)(2,1)S(1)}, bf16[256,1024]{1,0:T(8,128)(2,1)}, u32[]{:S(2)}, u32[]{:S(2)}) collective-permute-start(bf16[256,1024]{1,0:T(8,128)(2,1)S(1)} %bitcast.126), channel_id=1, source_target_pairs={{0,3},{1,0},{2,1},{3,2},{4,7},{5,4},{6,5},{7,6},{8,11},{9,8},{10,9... | collective-permute-start | bytes 1572872 | tf_op jit(solution)/shard_map/ppermute | solution.py:33
  12.3 0.6 collective-permute-start.1
  13.0 1.7 collective-permute-start.4
  14.8 1.0 constant_dynamic-slice_fusion.1
  16.0 22.8 %fusion = (bf16[3,512,1024]{2,1,0:T(8,128)(2,1)S(1)}, bf16[3,512,1024]{2,1,0:T(8,128)(2,1)S(1)}) fusion(f32[3,1024]{1,0:T(4,128)S(1)} %copy-done.10, f32[512]{0:T(512)S(1)} %maximum_multiply_fusion), kind=kLoop, calls=%fused_computation.2 | loop fusion | flops 4718592 | bytes 6305792 | tf_op jit(solution)/shard_map/convert
  38.8 3.2 %pad_maximum_fusion = bf16[6,512,1024]{2,1,0:T(8,128)(2,1)} fusion(bf16[3,512,1024]{2,1,0:T(8,128)(2,1)S(1)} %get-tuple-element.29, bf16[3,512,1024]{2,1,0:T(8,128)(2,1)S(1)} %get-tuple-element.28), kind=kLoop, calls=%fused_computation.4 | loop fusion | flops 3145728 | bytes 12582912 | tf_op jit(solution)/shard_map/concatenate | solution.py:21
  42.0 5.0 %collective-permute-done.3 = bf16[256,1024]{1,0:T(8,128)(2,1)} collective-permute-done((bf16[256,1024]{1,0:T(8,128)(2,1)S(1)}, bf16[256,1024]{1,0:T(8,128)(2,1)}, u32[]{:S(2)}, u32[]{:S(2)}) %collective-permute-start.3) | collective-permute-done | bytes 524320 | tf_op jit(solution)/shard_map/ppermute | solution.py:33
  47.0 1.2 collective-permute-start.2
  48.2 8.7 %collective-permute-done.4 = bf16[256,1024]{1,0:T(8,128)(2,1)} collective-permute-done((bf16[256,1024]{1,0:T(8,128)(2,1)S(1)}, bf16[256,1024]{1,0:T(8,128)(2,1)}, u32[]{:S(2)}, u32[]{:S(2)}) %collective-permute-start.4) | collective-permute-done | bytes 524320 | tf_op jit(solution)/shard_map/ppermute | solution.py:33
  56.8 5.0 %fusion.14 = bf16[4,256,1024]{2,1,0:T(8,128)(2,1)} fusion(s32[]{:T(128)S(6)} %select_n.27, bf16[1,256,1024]{2,1,0:T(8,128)(2,1)S(1)} %bitcast.146, bf16[1,256,1024]{2,1,0:T(8,128)(2,1)} %bitcast.12, bf16[1,256,1024]{2,1,0:T(8,128)(2,1)} %bitcast.13, bf16[1,256,1024]{2,1,0:T(8,128)(2,1)} %bitcast.14), kind=kLoop, calls=%fused_computation.38 | loop fusion | flops 7340032 | bytes 4194308 | tf_op jit(solution)/shard_map/jit(_roll_dynamic)/concatenate | solution.py:35
  61.8 14.6 %all-gather.6.cloned.1.call-done = bf16[3072,512]{1,0:T(8,128)(2,1)} async-done(((bf16[768,512]{1,0:T(8,128)(2,1)}), bf16[3072,512]{1,0:T(8,128)(2,1)}) %all-gather.6.cloned.1.call-update) | async-done | bytes 3145744 | tf_op jit(solution)/shard_map/all_gather | solution.py:92
  76.4 7.1 %convolution_convert_fusion.1 = bf16[1024,512]{0,1:T(8,128)(2,1)S(1)} fusion(bf16[3072,1024]{1,0:T(8,128)(2,1)} %bitcast.119, bf16[3072,512]{1,0:T(8,128)(2,1)} %all-gather.6.cloned.1.call-done), kind=kOutput, calls=%fused_computation.83 | convolution fusion | flops 3221749760 | bytes 10485760 | tf_op jit(solution)/shard_map/dot_general | solution.py:96
  83.7 0.8 multiply_reduce_fusion
  84.5 2.1 copy-done.1
  86.6 1.6 fusion.49
  88.5 5.0 %fusion.21 = bf16[4,256,1024]{2,1,0:T(8,128)(2,1)} fusion(s32[]{:T(128)S(6)} %select_n.27, bf16[1,256,1024]{2,1,0:T(8,128)(2,1)S(1)} %bitcast.129, bf16[1,256,1024]{2,1,0:T(8,128)(2,1)} %bitcast.4, bf16[1,256,1024]{2,1,0:T(8,128)(2,1)} %bitcast.5, bf16[1,256,1024]{2,1,0:T(8,128)(2,1)} %bitcast.6), kind=kLoop, calls=%fused_computation.45 | loop fusion | flops 7340032 | bytes 4194308 | tf_op jit(solution)/shard_map/jit(_roll_dynamic)/concatenate | solution.py:35
  93.5 0.9 fusion.7
  94.4 13.3 %all-gather.1 = f32[8,2,512]{2,1,0:T(2,128)S(1)} all-gather(f32[2,2,512]{2,1,0:T(2,128)S(1)} %pad_maximum_fusion.1), channel_id=3, replica_groups=mesh['groups'=2,'picks'=4,'heads'=4] {'picks'}, dimensions={0}, use_global_device_ids=true | all-gather | bytes 40960 | tf_op jit(solution)/shard_map/all_gather | solution.py:110
  107.7 7.5 %all-gather.10.cloned.1.call-done = bf16[8,512,128]{2,1,0:T(8,128)(2,1)} async-done(((bf16[2,512,128]{2,1,0:T(8,128)(2,1)}), bf16[8,512,128]{2,1,0:T(8,128)(2,1)}) %all-gather.10.cloned.1.call-update) | async-done | bytes 1048592 | tf_op jit(solution)/shard_map/all_gather | solution.py:109
  115.2 1.8 multiply_reduce_fusion.1
  117.3 1.0 collective-permute-start.6
  118.2 0.6 collective-permute-start.7
  119.1 5.7 %collective-permute-done.6 = bf16[256,512]{1,0:T(8,128)(2,1)S(1)} collective-permute-done((bf16[256,512]{1,0:T(8,128)(2,1)S(1)}, bf16[256,512]{1,0:T(8,128)(2,1)S(1)}, u32[]{:S(2)}, u32[]{:S(2)}) %collective-permute-start.6) | collective-permute-done | bytes 262176 | tf_op jit(solution)/shard_map/ppermute | solution.py:33
  124.8 6.7 %collective-permute-done.7 = bf16[256,512]{1,0:T(8,128)(2,1)S(1)} collective-permute-done((bf16[256,512]{1,0:T(8,128)(2,1)S(1)}, bf16[256,512]{1,0:T(8,128)(2,1)S(1)}, u32[]{:S(2)}, u32[]{:S(2)}) %collective-permute-start.7) | collective-permute-done | bytes 262176 | tf_op jit(solution)/shard_map/ppermute | solution.py:33
  131.7 2.2 %fusion.66 = bf16[4,256,512]{2,1,0:T(8,128)(2,1)S(1)} fusion(s32[]{:T(128)S(6)} %select_n.27, bf16[1,256,512]{2,1,0:T(8,128)(2,1)S(1)} %bitcast.135, bf16[1,256,512]{2,1,0:T(8,128)(2,1)S(1)} %bitcast.149, bf16[1,256,512]{2,1,0:T(8,128)(2,1)S(1)} %bitcast.150, bf16[1,256,512]{2,1,0:T(8,128)(2,1)} %bitcast.31), kind=kLoop, calls=%fused_computation.107 | loop fusion | flops 3670016 | bytes 2097156 | tf_op jit(solution)/shard_map/jit(_roll_dynamic)/concatenate | solution.py:35
  133.9 1.4 multiply_reduce_fusion.3
  135.3 1.1 fusion.44
  137.7 1.5 collective-permute-start.10
  139.3 4.0 %collective-permute-done.9 = bf16[256,512]{1,0:T(8,128)(2,1)S(1)} collective-permute-done((bf16[256,512]{1,0:T(8,128)(2,1)S(1)}, bf16[256,512]{1,0:T(8,128)(2,1)S(1)}, u32[]{:S(2)}, u32[]{:S(2)}) %collective-permute-start.9) | collective-permute-done | bytes 262176 | tf_op jit(solution)/shard_map/ppermute | solution.py:33
  143.3 8.4 %collective-permute-done.10 = bf16[256,512]{1,0:T(8,128)(2,1)S(1)} collective-permute-done((bf16[256,512]{1,0:T(8,128)(2,1)S(1)}, bf16[256,512]{1,0:T(8,128)(2,1)S(1)}, u32[]{:S(2)}, u32[]{:S(2)}) %collective-permute-start.10) | collective-permute-done | bytes 262176 | tf_op jit(solution)/shard_map/ppermute | solution.py:33
  151.9 1.2 fusion.59
  153.1 1.4 multiply_reduce_fusion.2
  154.5 1.3 copy-done.4
  155.9 0.8 fusion.48
  156.8 5.1 %convolution_convert_fusion.3 = bf16[1024,256]{0,1:T(8,128)(2,1)S(1)} fusion(bf16[3072,1024]{1,0:T(8,128)(2,1)} %bitcast.120, bf16[3072,256]{1,0:T(8,128)(2,1)} %all-gather.8.cloned.1.call-done), kind=kOutput, calls=%fused_computation.87 | convolution fusion | flops 1610874880 | bytes 8388608 | tf_op jit(solution)/shard_map/dot_general | solution.py:160
  161.9 0.8 fusion.6
  162.8 1.0 fusion.45
  164.0 1.0 collective-permute-done.12
  165.0 0.9 collective-permute-start.13
  166.1 2.5 %collective-permute-done.13 = f32[1024]{0:T(1024)S(1)} collective-permute-done((f32[1024]{0:T(1024)S(1)}, f32[1024]{0:T(1024)S(1)}, u32[]{:S(2)}, u32[]{:S(2)}) %collective-permute-start.13) | collective-permute-done | bytes 4128 | tf_op jit(solution)/shard_map/ppermute | solution.py:61
  169.2 1.0 fusion.2
  170.2 1.4 fusion.41
  171.6 0.7 slice-done.1
  172.3 3.1 %convolution_convert_fusion = bf16[3072,256]{1,0:T(8,128)(2,1)} fusion(bf16[3072,1024]{1,0:T(8,128)(2,1)S(1)} %bitcast.123, bf16[1024,256]{0,1:T(8,128)(2,1)S(1)} %bitcast.170), kind=kOutput, calls=%fused_computation.29 | convolution fusion | flops 1611399168 | bytes 8388608 | tf_op jit(solution)/shard_map/dot_general | solution.py:186
  175.5 1.9 constant_dynamic-slice_fusion
  177.3 32.5 %reduce-scatter.2.cloned.1.call-done = bf16[768,256]{1,0:T(8,128)(2,1)} async-done(((bf16[3072,256]{1,0:T(8,128)(2,1)}), bf16[768,256]{1,0:T(8,128)(2,1)}) %reduce-scatter.2.cloned.1.call-update) | async-done | bytes 393232 | tf_op jit(solution)/shard_map/reduce_scatter | solution.py:185
  209.8 1.9 convert_element_type.100
  (75 shorter events, 4.3 us)
Async XLA Ops:
  7.2 128.1 %copy-start = (bf16[3,1024,256]{2,1,0:T(8,128)(2,1)S(1)}, bf16[3,1024,256]{2,1,0:T(8,128)(2,1)}, u32[]{:S(2)}) copy-start(bf16[3,1024,256]{2,1,0:T(8,128)(2,1)} %param.23) | copy-start | bytes 4718596
  7.2 2.5 %copy-start.9 = (bf16[1024,256]{1,0:T(8,128)(2,1)S(1)}, bf16[1024,256]{1,0:T(8,128)(2,1)}, u32[]{:S(2)}) copy-start(bf16[1024,256]{1,0:T(8,128)(2,1)} %param.24) | copy-start | bytes 1572868
  7.2 5.8 %copy-start.8 = (bf16[256,1024]{1,0:T(8,128)(2,1)S(1)}, bf16[256,1024]{1,0:T(8,128)(2,1)}, u32[]{:S(2)}) copy-start(bf16[256,1024]{1,0:T(8,128)(2,1)} %param.21) | copy-start | bytes 1572868
  7.2 69.2 %all-gather.6.cloned.1.call-start = ((), (), s32[]{:S(2)}) async-start(), calls=%async_computation.1 | async-start | bytes 3932160 | tf_op jit(solution)/shard_map/all_gather | solution.py:92
  7.2 8.7 %copy-start.10 = (f32[3,1024]{1,0:T(4,128)S(1)}, f32[3,1024]{1,0:T(4,128)}, u32[]{:S(2)}) copy-start(f32[3,1024]{1,0:T(4,128)} %param.16) | copy-start | bytes 36868
  9.6 105.6 %all-gather.10.cloned.1.call-start = ((), (), s32[]{:S(2)}) async-start(), calls=%async_computation.4 | async-start | bytes 1310720 | tf_op jit(solution)/shard_map/all_gather | solution.py:109
  9.9 78.5 %collective-permute-start = (bf16[256,1024]{1,0:T(8,128)(2,1)S(1)}, bf16[256,1024]{1,0:T(8,128)(2,1)}, u32[]{:S(2)}, u32[]{:S(2)}) collective-permute-start(bf16[256,1024]{1,0:T(8,128)(2,1)S(1)} %bitcast.126), channel_id=1, source_target_pairs={{0,3},{1,0},{2,1},{3,2},{4,7},{5,4},{6,5},{7,6},{8,11},{9,8},{10,9... | collective-permute-start | bytes 1572872 | tf_op jit(solution)/shard_map/ppermute | solution.py:33
  12.3 76.1 %collective-permute-start.1 = (bf16[256,1024]{1,0:T(8,128)(2,1)S(1)}, bf16[256,1024]{1,0:T(8,128)(2,1)}, u32[]{:S(2)}, u32[]{:S(2)}) collective-permute-start(bf16[256,1024]{1,0:T(8,128)(2,1)S(1)} %bitcast.127), channel_id=1, source_target_pairs={{0,2},{1,3},{2,0},{3,1},{4,6},{5,7},{6,4},{7,5},{8,10},{9,11},{10,... | collective-permute-start | bytes 1572872 | tf_op jit(solution)/shard_map/ppermute | solution.py:33
  13.0 34.0 %collective-permute-start.3 = (bf16[256,1024]{1,0:T(8,128)(2,1)S(1)}, bf16[256,1024]{1,0:T(8,128)(2,1)}, u32[]{:S(2)}, u32[]{:S(2)}) collective-permute-start(bf16[256,1024]{1,0:T(8,128)(2,1)S(1)} %copy-done.8), channel_id=1, source_target_pairs={{0,3},{1,0},{2,1},{3,2},{4,7},{5,4},{6,5},{7,6},{8,11},{9,8},{10,9... | collective-permute-start | bytes 1572872 | tf_op jit(solution)/shard_map/ppermute | solution.py:33
  13.0 43.8 %collective-permute-start.4 = (bf16[256,1024]{1,0:T(8,128)(2,1)S(1)}, bf16[256,1024]{1,0:T(8,128)(2,1)}, u32[]{:S(2)}, u32[]{:S(2)}) collective-permute-start(bf16[256,1024]{1,0:T(8,128)(2,1)S(1)} %copy-done.8), channel_id=1, source_target_pairs={{0,2},{1,3},{2,0},{3,1},{4,6},{5,7},{6,4},{7,5},{8,10},{9,11},{10,... | collective-permute-start | bytes 1572872 | tf_op jit(solution)/shard_map/ppermute | solution.py:33
  14.8 42.1 %collective-permute-start.5 = (bf16[256,1024]{1,0:T(8,128)(2,1)S(1)}, bf16[256,1024]{1,0:T(8,128)(2,1)}, u32[]{:S(2)}, u32[]{:S(2)}) collective-permute-start(bf16[256,1024]{1,0:T(8,128)(2,1)S(1)} %copy-done.8), channel_id=1, source_target_pairs={{0,1},{1,2},{2,3},{3,0},{4,5},{5,6},{6,7},{7,4},{8,9},{9,10},{10,1... | collective-permute-start | bytes 1572872 | tf_op jit(solution)/shard_map/ppermute | solution.py:33
  47.0 41.5 %collective-permute-start.2 = (bf16[256,1024]{1,0:T(8,128)(2,1)S(1)}, bf16[256,1024]{1,0:T(8,128)(2,1)}, u32[]{:S(2)}, u32[]{:S(2)}) collective-permute-start(bf16[256,1024]{1,0:T(8,128)(2,1)S(1)} %bitcast.128), channel_id=1, source_target_pairs={{0,1},{1,2},{2,3},{3,0},{4,5},{5,6},{6,7},{7,4},{8,9},{9,10},{10,1... | collective-permute-start | bytes 1572872 | tf_op jit(solution)/shard_map/ppermute | solution.py:33
  84.5 2.1 copy-start.1
  88.2 68.6 %all-gather.8.cloned.1.call-start = ((), (), s32[]{:S(2)}) async-start(), calls=%async_computation.2 | async-start | bytes 1966080 | tf_op jit(solution)/shard_map/all_gather | solution.py:126
  88.4 5.0 %copy-start.2 = (f32[2,512,1024]{2,1,0:T(8,128)S(1)}, f32[2,512,1024]{2,1,0:T(8,128)}, u32[]{:S(2)}) copy-start(f32[2,512,1024]{2,1,0:T(8,128)} %copy-done.1) | copy-start | bytes 12582916
  94.4 24.6 %copy-start.11 = (f32[2,1024]{1,0:T(2,128)S(1)}, f32[2,1024]{1,0:T(2,128)}, u32[]{:S(2)}) copy-start(f32[2,1024]{1,0:T(2,128)} %param.22) | copy-start | bytes 24580
  117.2 16.7 %copy-start.6 = (bf16[512,1024]{1,0:T(8,128)(2,1)S(1)}, bf16[512,1024]{1,0:T(8,128)(2,1)}, u32[]{:S(2)}) copy-start(bf16[512,1024]{1,0:T(8,128)(2,1)} %param.19) | copy-start | bytes 3145732
  117.3 7.5 %collective-permute-start.6 = (bf16[256,512]{1,0:T(8,128)(2,1)S(1)}, bf16[256,512]{1,0:T(8,128)(2,1)S(1)}, u32[]{:S(2)}, u32[]{:S(2)}) collective-permute-start(bf16[256,512]{1,0:T(8,128)(2,1)S(1)} %bitcast.132), channel_id=1, source_target_pairs={{0,3},{1,0},{2,1},{3,2},{4,7},{5,4},{6,5},{7,6},{8,11},{9,8},{10,9... | collective-permute-start | bytes 786440 | tf_op jit(solution)/shard_map/ppermute | solution.py:33
  118.2 13.2 %collective-permute-start.7 = (bf16[256,512]{1,0:T(8,128)(2,1)S(1)}, bf16[256,512]{1,0:T(8,128)(2,1)S(1)}, u32[]{:S(2)}, u32[]{:S(2)}) collective-permute-start(bf16[256,512]{1,0:T(8,128)(2,1)S(1)} %bitcast.133), channel_id=1, source_target_pairs={{0,2},{1,3},{2,0},{3,1},{4,6},{5,7},{6,4},{7,5},{8,10},{9,11},{10,... | collective-permute-start | bytes 786440 | tf_op jit(solution)/shard_map/ppermute | solution.py:33
  118.9 12.8 %collective-permute-start.8 = (bf16[256,512]{1,0:T(8,128)(2,1)S(1)}, bf16[256,512]{1,0:T(8,128)(2,1)}, u32[]{:S(2)}, u32[]{:S(2)}) collective-permute-start(bf16[256,512]{1,0:T(8,128)(2,1)S(1)} %bitcast.134), channel_id=1, source_target_pairs={{0,1},{1,2},{2,3},{3,0},{4,5},{5,6},{6,7},{7,4},{8,9},{9,10},{10,1... | collective-permute-start | bytes 786440 | tf_op jit(solution)/shard_map/ppermute | solution.py:33
  119.1 90.7 %reduce-scatter.2.cloned.1.call-start = ((), (), s32[]{:S(2)}) async-start(), calls=%async_computation.3 | async-start | bytes 1966080 | tf_op jit(solution)/shard_map/reduce_scatter | solution.py:185
  119.1 14.8 %copy-start.3 = (bf16[4,256,1024]{2,1,0:T(8,128)(2,1)S(1)}, bf16[4,256,1024]{2,1,0:T(8,128)(2,1)}, u32[]{:S(2)}) copy-start(bf16[4,256,1024]{2,1,0:T(8,128)(2,1)} %fusion.14) | copy-start | bytes 6291460
  137.6 15.5 %copy-start.5 = (bf16[4,256,1024]{2,1,0:T(8,128)(2,1)S(1)}, bf16[4,256,1024]{2,1,0:T(8,128)(2,1)}, u32[]{:S(2)}) copy-start(bf16[4,256,1024]{2,1,0:T(8,128)(2,1)} %fusion.21) | copy-start | bytes 6291460
  137.6 5.7 %collective-permute-start.9 = (bf16[256,512]{1,0:T(8,128)(2,1)S(1)}, bf16[256,512]{1,0:T(8,128)(2,1)S(1)}, u32[]{:S(2)}, u32[]{:S(2)}) collective-permute-start(bf16[256,512]{1,0:T(8,128)(2,1)S(1)} %bitcast.151), channel_id=1, source_target_pairs={{0,3},{1,0},{2,1},{3,2},{4,7},{5,4},{6,5},{7,6},{8,11},{9,8},{10,9... | collective-permute-start | bytes 786440 | tf_op jit(solution)/shard_map/ppermute | solution.py:33
  137.7 14.1 %collective-permute-start.10 = (bf16[256,512]{1,0:T(8,128)(2,1)S(1)}, bf16[256,512]{1,0:T(8,128)(2,1)S(1)}, u32[]{:S(2)}, u32[]{:S(2)}) collective-permute-start(bf16[256,512]{1,0:T(8,128)(2,1)S(1)} %bitcast.152), channel_id=1, source_target_pairs={{0,2},{1,3},{2,0},{3,1},{4,6},{5,7},{6,4},{7,5},{8,10},{9,11},{10,... | collective-permute-start | bytes 786440 | tf_op jit(solution)/shard_map/ppermute | solution.py:33
  139.2 12.7 %collective-permute-start.11 = (bf16[256,512]{1,0:T(8,128)(2,1)S(1)}, bf16[256,512]{1,0:T(8,128)(2,1)S(1)}, u32[]{:S(2)}, u32[]{:S(2)}) collective-permute-start(bf16[256,512]{1,0:T(8,128)(2,1)S(1)} %bitcast.153), channel_id=1, source_target_pairs={{0,1},{1,2},{2,3},{3,0},{4,5},{5,6},{6,7},{7,4},{8,9},{9,10},{10,1... | collective-permute-start | bytes 786440 | tf_op jit(solution)/shard_map/ppermute | solution.py:33
  153.1 2.8 %copy-start.7 = (bf16[2,1024,256]{2,1,0:T(8,128)(2,1)S(1)}, bf16[2,1024,256]{2,1,0:T(8,128)(2,1)}, u32[]{:S(2)}) copy-start(bf16[2,1024,256]{2,1,0:T(8,128)(2,1)} %param.25) | copy-start | bytes 3145732
  154.5 1.4 copy-start.4
  161.9 0.9 copy-start.13
  162.8 1.1 copy-start.12
  162.8 1.1 copy-start.14
  163.8 1.2 collective-permute-start.12
  165.0 3.6 %collective-permute-start.13 = (f32[1024]{0:T(1024)S(1)}, f32[1024]{0:T(1024)S(1)}, u32[]{:S(2)}, u32[]{:S(2)}) collective-permute-start(f32[1024]{0:T(1024)S(1)} %add.61), channel_id=1, source_target_pairs={{0,2},{1,3},{2,0},{3,1},{4,6},{5,7},{6,4},{7,5},{8,10},{9,11},{10,... | collective-permute-start | bytes 12296 | tf_op jit(solution)/shard_map/ppermute | solution.py:61
  169.2 2.4 %slice-start = ((s8[6291456]{0:T(1024)(128)(4,1)}), s8[4194304]{0:T(1024)(128)(4,1)S(1)}, s32[]{:S(2)}) async-start(s8[6291456]{0:T(1024)(128)(4,1)} %bitcast.121), calls=%async_computation.5 | async-start | bytes 8388608
  170.2 2.1 slice-start.1
Sparse Core Ops, SparseCore 0:
  10.2 66.2 all-gather.5
  88.3 26.8 all-gather.9
  119.2 37.0 all-gather.7
  175.6 34.1 reduce-scatter.1

commit v7 on v6

--- a/solution.py
+++ b/solution.py
@@ -59,6 +59,35 @@
         return lax.psum(x, axis)
     x = x + lax.ppermute(x, axis, [(k, k ^ 1) for k in range(n)])
     return x + lax.ppermute(x, axis, [(k, k ^ 2) for k in range(n)])
+
+
+def fetch_rows(w, n_picks, n_groups, chunks=2):
+    if n_groups != 2 or n_picks > RING_MAX:
+        return lax.all_gather(w, "picks", axis=0, tiled=True)
+    g = lax.axis_index("groups")
+    p = lax.axis_index("picks")
+    rows = w.shape[0] // 2
+    step = rows // chunks
+    mine = lax.dynamic_slice_in_dim(w, g * rows, rows, 0)
+    own, other = [], []
+    for c in range(chunks):
+        part = mine[c * step:(c + 1) * step]
+        if own:
+            part, _ = lax.optimization_barrier((part, own[-1]))
+        blocks = [part] + [
+            lax.ppermute(part, "picks", [(i, (i - s) % n_picks) for i in range(n_picks)])
+            for s in range(1, n_picks)
+        ]
+        flipped = jnp.stack(blocks)
+        own.append(flipped)
+        other.append(lax.ppermute(flipped, "groups", [(0, 1), (1, 0)]))
+    own = jnp.concatenate(own, axis=1)
+    other = jnp.concatenate(other, axis=1)
+    first = jnp.where(g == 0, own, other)
+    second = jnp.where(g == 0, other, own)
+    flipped = jnp.stack([first, second], axis=1)
+    ordered = jnp.roll(flipped, p, axis=0)
+    return ordered.reshape((n_picks * w.shape[0],) + w.shape[1:])
 
 
 def on_device(
@@ -88,10 +117,8 @@
     nheads = local // HEAD
     column = lax.axis_index("heads") * local
     enc = encode(coords)
-    cross_full = ring_gather(cross_out, "heads", n_heads)
-    piece = lax.all_gather(
-        kv_weight.reshape(kv_weight.shape[0], 2 * local), "picks", axis=0, tiled=True
-    )
+    cross_full = lax.all_gather(cross_out, "heads", axis=0, tiled=True)
+    piece = fetch_rows(kv_weight.reshape(kv_weight.shape[0], 2 * local), n_picks, n_groups)
     cross_full, piece = lax.optimization_barrier((cross_full, piece))
     keys_vals = jnp.dot(
         enc, piece.reshape(piece.shape[0], 2 * local), preferred_element_type=jnp.float32
@@ -120,7 +147,7 @@
         .reshape(lat_rows, local)
         .astype(jnp.bfloat16)
     )
-    out_full = ring_gather(self_out.T, "heads", n_heads).T
+    out_full = lax.all_gather(self_out, "heads", axis=1, tiled=True)
     out_full, attended = lax.optimization_barrier((out_full, attended))
     dq_local, attended = lax.optimization_barrier((dec_query, attended))
     dq_full = lax.all_gather(dq_local, "picks", axis=0, tiled=True)

time: 219 us -> 254 us (1.16)
  waiting for transfers between devices: 96.8 us -> 117 us
  starting transfers between devices: 10.9 us -> 21.5 us
  blocking collectives: 13.3 us -> 16 us
    ppermute x0 -> x8, waiting for transfers between devices: none -> 19.6 us  [the longest x6 19.6 us: fetch_rows(): lax.ppermute(part, 'picks', [(i, (i - s) % n_picks) for i in range(n_pick...]
    ppermute x0 -> x8, starting transfers between devices: none -> 17.1 us  [the longest x6 14.1 us: fetch_rows(): lax.ppermute(part, 'picks', [(i, (i - s) % n_picks) for i in range(n_pick...]
    ppermute x12 -> x6, waiting for transfers between devices: 38.7 us -> 24.9 us  [ring_gather(): blocks.append(lax.ppermute(x, axis, [(i, (i - s) % n) for i in range(n)]))]
    concatenate x4 -> x2, other arithmetic: 13.5 us -> 2.47 us  [ring_gather(): ordered = jnp.roll(flipped, idx, axis=0)]
    all_gather x1 -> x2, waiting for transfers between devices: 14.6 us -> 22 us  [the longest x1 22 us: on_device(): out_full = lax.all_gather(self_out, 'heads', axis=1, tiled=True)]
    ppermute x12 -> x6, starting transfers between devices: 9.55 us -> 2.5 us  [ring_gather(): blocks.append(lax.ppermute(x, axis, [(i, (i - s) % n) for i in range(n)]))]
    concatenate x0 -> x3, other arithmetic: none -> 5.96 us  [the longest x2 3.05 us: fetch_rows(): own = jnp.concatenate(own, axis=1)]
    all_gather x1, waiting for transfers between devices: 7.49 us -> 11.4 us  [on_device(): lax.all_gather(numer.astype(jnp.bfloat16), 'picks', axis=0, tiled=False)]
  transfers between devices with their start and end apart: 18 -> 21, of which waited for: 13 -> 15; matrix products, arithmetic and copies ran while one was open for 27% -> 22% of each run, Pallas kernels for 0% -> 0%
where the time goes in v7:
time: 254 us; the launch traced here: 253 us
  waiting for transfers between devices  117 us (46%)
  other arithmetic  45.1 us (18%)
  matrix products  28.2 us (11%)
  starting transfers between devices  21.5 us (8%)
  blocking collectives  16 us (6%)
  between operations  14.2 us (6%)
  local copies, waits for them, and re-layouts  11.3 us (4%)
    reduce_scatter x1, waiting for transfers between devices, on_device(): lax.psum_scatter(jnp.dot(enc.T, dquery, preferred_element_type=jnp.float3...  32.9 us
    ppermute x6, waiting for transfers between devices, ring_gather(): blocks.append(lax.ppermute(x, axis, [(i, (i - s) % n) for i in range(n)]))  24.9 us
    another operation x1, other arithmetic  22.8 us
    all_gather x1, waiting for transfers between devices, on_device(): out_full = lax.all_gather(self_out, 'heads', axis=1, tiled=True)  22 us
    ppermute x6, waiting for transfers between devices, fetch_rows(): lax.ppermute(part, 'picks', [(i, (i - s) % n_picks) for i in range(n_pick...  19.6 us
    all_gather x1, blocking collectives, on_device(): lax.all_gather(jnp.stack([top, total]), 'picks', axis=0, tiled=False)  16 us
    ppermute x6, starting transfers between devices, fetch_rows(): lax.ppermute(part, 'picks', [(i, (i - s) % n_picks) for i in range(n_pick...  14.1 us
    all_gather x1, waiting for transfers between devices, on_device(): lax.all_gather(numer.astype(jnp.bfloat16), 'picks', axis=0, tiled=False)  11.4 us
  transfers between devices with their start and end apart: 21, of which 15 were waited for; matrix products, arithmetic and copies ran while one was open for 22% of the time, Pallas kernels for 0%

profile of v7, /device:TPU:0, one launch (start us, length us, event | category | flops | bytes accessed | tf_op | source)
XLA Modules:
  0.0 253.3 jit_solution(121811829637422087)
XLA Ops:
  8.0 1.3 copy.101
  9.3 3.1 %collective-permute-start.2 = (bf16[192,512]{1,0:T(8,128)(2,1)S(1)}, bf16[192,512]{1,0:T(8,128)(2,1)S(1)}, u32[]{:S(2)}, u32[]{:S(2)}) collective-permute-start(bf16[192,512]{1,0:T(8,128)(2,1)S(1)} %get-tuple-element.31), channel_id=1, source_target_pairs={{0,4},{4,8},{8,12},{12,0},{1,5},{5,9},{9,13},{13,1},{2,6},{6,10},{... | collective-permute-start | bytes 589832 | tf_op jit(solution)/shard_map/ppermute | solution.py:78
  12.4 2.6 %collective-permute-start.1 = (bf16[192,512]{1,0:T(8,128)(2,1)S(1)}, bf16[192,512]{1,0:T(8,128)(2,1)S(1)}, u32[]{:S(2)}, u32[]{:S(2)}) collective-permute-start(bf16[192,512]{1,0:T(8,128)(2,1)S(1)} %get-tuple-element.31), channel_id=1, source_target_pairs={{0,8},{4,12},{8,0},{12,4},{1,9},{5,13},{9,1},{13,5},{2,10},{6,14},... | collective-permute-start | bytes 589832 | tf_op jit(solution)/shard_map/ppermute | solution.py:78
  15.0 1.3 collective-permute-start
  16.3 3.9 %collective-permute-done.2 = bf16[192,512]{1,0:T(8,128)(2,1)S(1)} collective-permute-done((bf16[192,512]{1,0:T(8,128)(2,1)S(1)}, bf16[192,512]{1,0:T(8,128)(2,1)S(1)}, u32[]{:S(2)}, u32[]{:S(2)}) %collective-permute-start.2) | collective-permute-done | bytes 196640 | tf_op jit(solution)/shard_map/ppermute | solution.py:78
  20.3 7.6 %collective-permute-done.1 = bf16[192,512]{1,0:T(8,128)(2,1)S(1)} collective-permute-done((bf16[192,512]{1,0:T(8,128)(2,1)S(1)}, bf16[192,512]{1,0:T(8,128)(2,1)S(1)}, u32[]{:S(2)}, u32[]{:S(2)}) %collective-permute-start.1) | collective-permute-done | bytes 196640 | tf_op jit(solution)/shard_map/ppermute | solution.py:78
  27.9 1.0 fusion.72
  28.9 4.7 %collective-permute-start.5 = (bf16[192,512]{1,0:T(8,128)(2,1)S(1)}, bf16[192,512]{1,0:T(8,128)(2,1)S(1)}, u32[]{:S(2)}, u32[]{:S(2)}) collective-permute-start(bf16[192,512]{1,0:T(8,128)(2,1)S(1)} %get-tuple-element.11), channel_id=1, source_target_pairs={{0,4},{4,8},{8,12},{12,0},{1,5},{5,9},{9,13},{13,1},{2,6},{6,10},{... | collective-permute-start | bytes 589832 | tf_op jit(solution)/shard_map/ppermute | solution.py:78
  33.6 1.6 collective-permute-start.4
  36.0 1.7 constant_dynamic-slice_fusion.3
  37.6 1.5 collective-permute-start.6
  39.1 1.4 collective-permute-done.5
  40.5 6.6 %collective-permute-done.4 = bf16[192,512]{1,0:T(8,128)(2,1)S(1)} collective-permute-done((bf16[192,512]{1,0:T(8,128)(2,1)S(1)}, bf16[192,512]{1,0:T(8,128)(2,1)S(1)}, u32[]{:S(2)}, u32[]{:S(2)}) %collective-permute-start.4) | collective-permute-done | bytes 196640 | tf_op jit(solution)/shard_map/ppermute | solution.py:78
  48.0 2.0 fusion.71
  50.0 1.5 collective-permute-start.7
  51.5 1.1 copy.99
  52.7 22.8 %fusion = (bf16[3,512,1024]{2,1,0:T(8,128)(2,1)S(1)}, bf16[3,512,1024]{2,1,0:T(8,128)(2,1)S(1)}) fusion(f32[3,1024]{1,0:T(4,128)S(1)} %copy-done.8, f32[512]{0:T(512)S(1)} %maximum_multiply_fusion), kind=kLoop, calls=%fused_computation.2 | loop fusion | flops 4718592 | bytes 6305792 | tf_op jit(solution)/shard_map/convert
  75.5 3.2 %pad_maximum_fusion = bf16[6,512,1024]{2,1,0:T(8,128)(2,1)} fusion(bf16[3,512,1024]{2,1,0:T(8,128)(2,1)S(1)} %get-tuple-element.38, bf16[3,512,1024]{2,1,0:T(8,128)(2,1)S(1)} %get-tuple-element.37), kind=kLoop, calls=%fused_computation.4 | loop fusion | flops 3145728 | bytes 12582912 | tf_op jit(solution)/shard_map/concatenate | solution.py:21
  78.7 2.0 broadcast_select_fusion
  80.7 2.9 %fusion.10 = bf16[4,2,384,512]{3,2,1,0:T(8,128)(2,1)} fusion(s32[]{:T(128)S(6)} %select_n.59, bf16[4,1,384,512]{3,2,1,0:T(8,128)(2,1)S(1)} %get-tuple-element.21, bf16[4,1,384,512]{3,2,1,0:T(8,128)(2,1)S(1)} %get-tuple-element.20), kind=kLoop, calls=%fused_computation.23 | loop fusion | flops 4718592 | bytes 6291460 | tf_op jit(solution)/shard_map/jit(_roll_dynamic)/concatenate | solution.py:89
  83.6 7.1 %convolution_convert_fusion.1 = bf16[1024,512]{0,1:T(8,128)(2,1)S(1)} fusion(bf16[3072,1024]{1,0:T(8,128)(2,1)} %bitcast.125, bf16[3072,512]{1,0:T(8,128)(2,1)} %bitcast.131), kind=kOutput, calls=%fused_computation.64 | convolution fusion | flops 3221749760 | bytes 10485760 | tf_op jit(solution)/shard_map/dot_general | solution.py:123
  91.7 2.1 copy-done.2
  93.8 1.6 fusion.38
  96.4 3.1 %fusion.7 = f32[2,512]{1,0:T(2,128)S(1)} fusion(f32[2,512,1024]{2,1,0:T(8,128)} %copy-done.2, f32[2,512]{1,0:T(2,128)S(1)} %get-tuple-element.41), kind=kLoop, calls=%fused_computation.20 | loop fusion | flops 3144704 | bytes 4202496 | tf_op jit(solution)/shard_map/reduce_sum | solution.py:132
  99.5 16.0 %all-gather.1 = f32[8,2,512]{2,1,0:T(2,128)S(1)} all-gather(f32[2,2,512]{2,1,0:T(2,128)S(1)} %pad_maximum_fusion.5), channel_id=3, replica_groups=mesh['groups'=2,'picks'=4,'heads'=4] {'picks'}, dimensions={0}, use_global_device_ids=true | all-gather | bytes 40960 | tf_op jit(solution)/shard_map/all_gather | solution.py:137
  115.5 11.4 %all-gather.13.cloned.1.call-done = bf16[8,512,128]{2,1,0:T(8,128)(2,1)} async-done(((bf16[2,512,128]{2,1,0:T(8,128)(2,1)}), bf16[8,512,128]{2,1,0:T(8,128)(2,1)}) %all-gather.13.cloned.1.call-update) | async-done | bytes 1048592 | tf_op jit(solution)/shard_map/all_gather | solution.py:136
  126.9 1.8 multiply_reduce_fusion.1
  129.0 22.0 %all-gather.7.cloned.1.call-done = bf16[1024,1024]{1,0:T(8,128)(2,1)} async-done(((bf16[1024,256]{1,0:T(8,128)(2,1)}), bf16[1024,1024]{1,0:T(8,128)(2,1)}) %all-gather.7.cloned.1.call-update) | async-done | bytes 2097168 | tf_op jit(solution)/shard_map/all_gather | solution.py:150
  151.1 1.7 collective-permute-start.9
  152.9 4.9 %collective-permute-done.8 = bf16[256,512]{1,0:T(8,128)(2,1)S(1)} collective-permute-done((bf16[256,512]{1,0:T(8,128)(2,1)S(1)}, bf16[256,512]{1,0:T(8,128)(2,1)S(1)}, u32[]{:S(2)}, u32[]{:S(2)}) %collective-permute-start.8) | collective-permute-done | bytes 262176 | tf_op jit(solution)/shard_map/ppermute | solution.py:33
  157.8 7.5 %collective-permute-done.9 = bf16[256,512]{1,0:T(8,128)(2,1)S(1)} collective-permute-done((bf16[256,512]{1,0:T(8,128)(2,1)S(1)}, bf16[256,512]{1,0:T(8,128)(2,1)S(1)}, u32[]{:S(2)}, u32[]{:S(2)}) %collective-permute-start.9) | collective-permute-done | bytes 262176 | tf_op jit(solution)/shard_map/ppermute | solution.py:33
  165.3 1.2 fusion.55
  166.5 2.6 %multiply_reduce_fusion.3 = (f32[512]{0:T(512)S(1)}, f32[512,1024]{1,0:T(8,128)S(1)}) fusion(bf16[1024,512]{1,0:T(8,128)(2,1)S(1)} %bitcast.130, bf16[1024,1024]{1,0:T(8,128)(2,1)S(1)} %copy-done.4, bf16[512,1024]{1,0:T(8,128)(2,1)} %param.17), kind=kOutput, calls=%fused_computation.54 | convolution fusion | flops 1075838464 | bytes 6293504 | tf_op jit(solution)/shard_map/dot_general | solution.py:155
  169.1 1.1 fusion.33
  172.0 6.1 %collective-permute-done.11 = bf16[256,512]{1,0:T(8,128)(2,1)S(1)} collective-permute-done((bf16[256,512]{1,0:T(8,128)(2,1)S(1)}, bf16[256,512]{1,0:T(8,128)(2,1)S(1)}, u32[]{:S(2)}, u32[]{:S(2)}) %collective-permute-start.11) | collective-permute-done | bytes 262176 | tf_op jit(solution)/shard_map/ppermute | solution.py:33
  178.2 5.5 %collective-permute-done.12 = bf16[256,512]{1,0:T(8,128)(2,1)S(1)} collective-permute-done((bf16[256,512]{1,0:T(8,128)(2,1)S(1)}, bf16[256,512]{1,0:T(8,128)(2,1)S(1)}, u32[]{:S(2)}, u32[]{:S(2)}) %collective-permute-start.12) | collective-permute-done | bytes 262176 | tf_op jit(solution)/shard_map/ppermute | solution.py:33
  184.6 1.2 fusion.48
  185.8 1.4 multiply_reduce_fusion.2
  187.2 1.4 copy-done.3
  189.5 1.8 all-gather.11.cloned.1.call-done
  191.3 5.1 %convolution_convert_fusion.3 = bf16[1024,256]{0,1:T(8,128)(2,1)S(1)} fusion(bf16[3072,1024]{1,0:T(8,128)(2,1)} %bitcast.126, bf16[3072,256]{1,0:T(8,128)(2,1)} %all-gather.11.cloned.1.call-done), kind=kOutput, calls=%fused_computation.68 | convolution fusion | flops 1610874880 | bytes 8388608 | tf_op jit(solution)/shard_map/dot_general | solution.py:187
  199.5 1.5 collective-permute-start.15
  201.2 1.9 collective-permute-done.15
  204.7 1.4 fusion.30
  206.8 3.1 %convolution_convert_fusion = bf16[3072,256]{1,0:T(8,128)(2,1)} fusion(bf16[3072,1024]{1,0:T(8,128)(2,1)S(1)} %bitcast.129, bf16[1024,256]{0,1:T(8,128)(2,1)S(1)} %bitcast.180), kind=kOutput, calls=%fused_computation.17 | convolution fusion | flops 1611399168 | bytes 8388608 | tf_op jit(solution)/shard_map/dot_general | solution.py:213
  210.0 1.9 constant_dynamic-slice_fusion.1
  211.9 32.9 %reduce-scatter.2.cloned.1.call-done = bf16[768,256]{1,0:T(8,128)(2,1)} async-done(((bf16[3072,256]{1,0:T(8,128)(2,1)}), bf16[768,256]{1,0:T(8,128)(2,1)}) %reduce-scatter.2.cloned.1.call-update) | async-done | bytes 393232 | tf_op jit(solution)/shard_map/reduce_scatter | solution.py:212
  244.8 1.9 convert_element_type.100
  (82 shorter events, 14.0 us)
Async XLA Ops:
  7.2 162.0 %copy-start = (bf16[3,1024,256]{2,1,0:T(8,128)(2,1)S(1)}, bf16[3,1024,256]{2,1,0:T(8,128)(2,1)}, u32[]{:S(2)}) copy-start(bf16[3,1024,256]{2,1,0:T(8,128)(2,1)} %param.21) | copy-start | bytes 4718596
  7.2 76.5 %all-gather.9.cloned.1.call-start = ((), (), s32[]{:S(2)}) async-start(), calls=%async_computation.2 | async-start | bytes 2621440 | tf_op jit(solution)/shard_map/all_gather | solution.py:120
  7.9 119.0 %all-gather.13.cloned.1.call-start = ((), (), s32[]{:S(2)}) async-start(), calls=%async_computation.5 | async-start | bytes 1310720 | tf_op jit(solution)/shard_map/all_gather | solution.py:136
  9.3 43.4 %copy-start.8 = (f32[3,1024]{1,0:T(4,128)S(1)}, f32[3,1024]{1,0:T(4,128)}, u32[]{:S(2)}) copy-start(f32[3,1024]{1,0:T(4,128)} %param.14) | copy-start | bytes 36868
  9.3 11.0 %collective-permute-start.2 = (bf16[192,512]{1,0:T(8,128)(2,1)S(1)}, bf16[192,512]{1,0:T(8,128)(2,1)S(1)}, u32[]{:S(2)}, u32[]{:S(2)}) collective-permute-start(bf16[192,512]{1,0:T(8,128)(2,1)S(1)} %get-tuple-element.31), channel_id=1, source_target_pairs={{0,4},{4,8},{8,12},{12,0},{1,5},{5,9},{9,13},{13,1},{2,6},{6,10},{... | collective-permute-start | bytes 589832 | tf_op jit(solution)/shard_map/ppermute | solution.py:78
  12.4 15.5 %collective-permute-start.1 = (bf16[192,512]{1,0:T(8,128)(2,1)S(1)}, bf16[192,512]{1,0:T(8,128)(2,1)S(1)}, u32[]{:S(2)}, u32[]{:S(2)}) collective-permute-start(bf16[192,512]{1,0:T(8,128)(2,1)S(1)} %get-tuple-element.31), channel_id=1, source_target_pairs={{0,8},{4,12},{8,0},{12,4},{1,9},{5,13},{9,1},{13,5},{2,10},{6,14},... | collective-permute-start | bytes 589832 | tf_op jit(solution)/shard_map/ppermute | solution.py:78
  15.0 12.9 %collective-permute-start = (bf16[192,512]{1,0:T(8,128)(2,1)S(1)}, bf16[192,512]{1,0:T(8,128)(2,1)S(1)}, u32[]{:S(2)}, u32[]{:S(2)}) collective-permute-start(bf16[192,512]{1,0:T(8,128)(2,1)S(1)} %get-tuple-element.31), channel_id=1, source_target_pairs={{0,12},{4,0},{8,4},{12,8},{1,13},{5,1},{9,5},{13,9},{2,14},{6,2},{... | collective-permute-start | bytes 589832 | tf_op jit(solution)/shard_map/ppermute | solution.py:78
  28.9 11.6 %collective-permute-start.5 = (bf16[192,512]{1,0:T(8,128)(2,1)S(1)}, bf16[192,512]{1,0:T(8,128)(2,1)S(1)}, u32[]{:S(2)}, u32[]{:S(2)}) collective-permute-start(bf16[192,512]{1,0:T(8,128)(2,1)S(1)} %get-tuple-element.11), channel_id=1, source_target_pairs={{0,4},{4,8},{8,12},{12,0},{1,5},{5,9},{9,13},{13,1},{2,6},{6,10},{... | collective-permute-start | bytes 589832 | tf_op jit(solution)/shard_map/ppermute | solution.py:78
  33.6 13.6 %collective-permute-start.4 = (bf16[192,512]{1,0:T(8,128)(2,1)S(1)}, bf16[192,512]{1,0:T(8,128)(2,1)S(1)}, u32[]{:S(2)}, u32[]{:S(2)}) collective-permute-start(bf16[192,512]{1,0:T(8,128)(2,1)S(1)} %get-tuple-element.11), channel_id=1, source_target_pairs={{0,8},{4,12},{8,0},{12,4},{1,9},{5,13},{9,1},{13,5},{2,10},{6,14},... | collective-permute-start | bytes 589832 | tf_op jit(solution)/shard_map/ppermute | solution.py:78
  35.2 12.0 %collective-permute-start.3 = (bf16[192,512]{1,0:T(8,128)(2,1)S(1)}, bf16[192,512]{1,0:T(8,128)(2,1)S(1)}, u32[]{:S(2)}, u32[]{:S(2)}) collective-permute-start(bf16[192,512]{1,0:T(8,128)(2,1)S(1)} %get-tuple-element.11), channel_id=1, source_target_pairs={{0,12},{4,0},{8,4},{12,8},{1,13},{5,1},{9,5},{13,9},{2,14},{6,2},{... | collective-permute-start | bytes 589832 | tf_op jit(solution)/shard_map/ppermute | solution.py:78
  37.6 41.1 %collective-permute-start.6 = (bf16[4,192,512]{2,1,0:T(8,128)(2,1)}, bf16[4,192,512]{2,1,0:T(8,128)(2,1)}, u32[]{:S(2)}, u32[]{:S(2)}) collective-permute-start(bf16[4,192,512]{2,1,0:T(8,128)(2,1)} %get-tuple-element.28), channel_id=1, source_target_pairs={{0,16},{16,0},{1,17},{17,1},{2,18},{18,2},{3,19},{19,3},{4,20},{20... | collective-permute-start | bytes 2359304 | tf_op jit(solution)/shard_map/ppermute | solution.py:83
  47.2 0.7 copy-start.6
  47.2 0.8 copy-start.7
  50.0 28.8 %collective-permute-start.7 = (bf16[4,192,512]{2,1,0:T(8,128)(2,1)}, bf16[4,192,512]{2,1,0:T(8,128)(2,1)}, u32[]{:S(2)}, u32[]{:S(2)}) collective-permute-start(bf16[4,192,512]{2,1,0:T(8,128)(2,1)} %get-tuple-element.30), channel_id=1, source_target_pairs={{0,16},{16,0},{1,17},{17,1},{2,18},{18,2},{3,19},{19,3},{4,20},{20... | collective-permute-start | bytes 2359304 | tf_op jit(solution)/shard_map/ppermute | solution.py:83
  91.7 2.1 copy-start.2
  95.4 55.5 %all-gather.7.cloned.1.call-start = ((), (), s32[]{:S(2)}) async-start(), calls=%async_computation.1 | async-start | bytes 2621440 | tf_op jit(solution)/shard_map/all_gather | solution.py:150
  96.1 56.7 %copy-start.9 = (f32[2,1024]{1,0:T(2,128)S(1)}, f32[2,1024]{1,0:T(2,128)}, u32[]{:S(2)}) copy-start(f32[2,1024]{1,0:T(2,128)} %param.20) | copy-start | bytes 24580
  96.1 95.2 %all-gather.11.cloned.1.call-start = ((), (), s32[]{:S(2)}) async-start(), calls=%async_computation.3 | async-start | bytes 1966080 | tf_op jit(solution)/shard_map/all_gather | solution.py:153
  150.9 6.9 %collective-permute-start.8 = (bf16[256,512]{1,0:T(8,128)(2,1)S(1)}, bf16[256,512]{1,0:T(8,128)(2,1)S(1)}, u32[]{:S(2)}, u32[]{:S(2)}) collective-permute-start(bf16[256,512]{1,0:T(8,128)(2,1)S(1)} %bitcast.134), channel_id=1, source_target_pairs={{0,3},{1,0},{2,1},{3,2},{4,7},{5,4},{6,5},{7,6},{8,11},{9,8},{10,9... | collective-permute-start | bytes 786440 | tf_op jit(solution)/shard_map/ppermute | solution.py:33
  151.1 14.2 %collective-permute-start.9 = (bf16[256,512]{1,0:T(8,128)(2,1)S(1)}, bf16[256,512]{1,0:T(8,128)(2,1)S(1)}, u32[]{:S(2)}, u32[]{:S(2)}) collective-permute-start(bf16[256,512]{1,0:T(8,128)(2,1)S(1)} %bitcast.135), channel_id=1, source_target_pairs={{0,2},{1,3},{2,0},{3,1},{4,6},{5,7},{6,4},{7,5},{8,10},{9,11},{10,... | collective-permute-start | bytes 786440 | tf_op jit(solution)/shard_map/ppermute | solution.py:33
  152.8 12.5 %collective-permute-start.10 = (bf16[256,512]{1,0:T(8,128)(2,1)S(1)}, bf16[256,512]{1,0:T(8,128)(2,1)S(1)}, u32[]{:S(2)}, u32[]{:S(2)}) collective-permute-start(bf16[256,512]{1,0:T(8,128)(2,1)S(1)} %bitcast.136), channel_id=1, source_target_pairs={{0,1},{1,2},{2,3},{3,0},{4,5},{5,6},{6,7},{7,4},{8,9},{9,10},{10,1... | collective-permute-start | bytes 786440 | tf_op jit(solution)/shard_map/ppermute | solution.py:33
  152.9 91.9 %reduce-scatter.2.cloned.1.call-start = ((), (), s32[]{:S(2)}) async-start(), calls=%async_computation.4 | async-start | bytes 1966080 | tf_op jit(solution)/shard_map/reduce_scatter | solution.py:212
  152.9 13.6 %copy-start.4 = (bf16[1024,1024]{1,0:T(8,128)(2,1)S(1)}, bf16[1024,1024]{1,0:T(8,128)(2,1)}, u32[]{:S(2)}) copy-start(bf16[1024,1024]{1,0:T(8,128)(2,1)} %all-gather.9.cloned.1.call-done) | copy-start | bytes 6291460
  170.9 14.9 %copy-start.13 = (bf16[1024,1024]{1,0:T(8,128)(2,1)S(1)}, bf16[1024,1024]{1,0:T(8,128)(2,1)}, u32[]{:S(2)}) copy-start(bf16[1024,1024]{1,0:T(8,128)(2,1)} %all-gather.7.cloned.1.call-done) | copy-start | bytes 6291460
  171.4 6.8 %collective-permute-start.11 = (bf16[256,512]{1,0:T(8,128)(2,1)S(1)}, bf16[256,512]{1,0:T(8,128)(2,1)S(1)}, u32[]{:S(2)}, u32[]{:S(2)}) collective-permute-start(bf16[256,512]{1,0:T(8,128)(2,1)S(1)} %bitcast.155), channel_id=1, source_target_pairs={{0,3},{1,0},{2,1},{3,2},{4,7},{5,4},{6,5},{7,6},{8,11},{9,8},{10,9... | collective-permute-start | bytes 786440 | tf_op jit(solution)/shard_map/ppermute | solution.py:33
  171.5 12.2 %collective-permute-start.12 = (bf16[256,512]{1,0:T(8,128)(2,1)S(1)}, bf16[256,512]{1,0:T(8,128)(2,1)S(1)}, u32[]{:S(2)}, u32[]{:S(2)}) collective-permute-start(bf16[256,512]{1,0:T(8,128)(2,1)S(1)} %bitcast.156), channel_id=1, source_target_pairs={{0,2},{1,3},{2,0},{3,1},{4,6},{5,7},{6,4},{7,5},{8,10},{9,11},{10,... | collective-permute-start | bytes 786440 | tf_op jit(solution)/shard_map/ppermute | solution.py:33
  171.9 12.7 %collective-permute-start.13 = (bf16[256,512]{1,0:T(8,128)(2,1)S(1)}, bf16[256,512]{1,0:T(8,128)(2,1)S(1)}, u32[]{:S(2)}, u32[]{:S(2)}) collective-permute-start(bf16[256,512]{1,0:T(8,128)(2,1)S(1)} %bitcast.157), channel_id=1, source_target_pairs={{0,1},{1,2},{2,3},{3,0},{4,5},{5,6},{6,7},{7,4},{8,9},{9,10},{10,1... | collective-permute-start | bytes 786440 | tf_op jit(solution)/shard_map/ppermute | solution.py:33
  185.8 2.8 %copy-start.5 = (bf16[2,1024,256]{2,1,0:T(8,128)(2,1)S(1)}, bf16[2,1024,256]{2,1,0:T(8,128)(2,1)}, u32[]{:S(2)}) copy-start(bf16[2,1024,256]{2,1,0:T(8,128)(2,1)} %param.23) | copy-start | bytes 3145732
  187.2 1.4 copy-start.3
  196.4 0.9 copy-start.11
  197.3 1.1 copy-start.10
  197.3 1.1 copy-start.12
  198.3 1.2 collective-permute-start.14
  199.5 3.6 %collective-permute-start.15 = (f32[1024]{0:T(1024)S(1)}, f32[1024]{0:T(1024)S(1)}, u32[]{:S(2)}, u32[]{:S(2)}) collective-permute-start(f32[1024]{0:T(1024)S(1)} %add.69), channel_id=1, source_target_pairs={{0,2},{1,3},{2,0},{3,1},{4,6},{5,7},{6,4},{7,5},{8,10},{9,11},{10,... | collective-permute-start | bytes 12296 | tf_op jit(solution)/shard_map/ppermute | solution.py:61
  203.7 2.4 slice-start
  204.7 2.1 slice-start.1
  206.8 39.9 %copy-start.1 = (bf16[3,1024,256]{2,1,0:T(8,128)(2,1)S(1)}, bf16[3,1024,256]{2,1,0:T(8,128)(2,1)}, u32[]{:S(2)}) copy-start(bf16[3,1024,256]{2,1,0:T(8,128)(2,1)} %param.21) | copy-start | bytes 4718596
Sparse Core Ops, SparseCore 0:
  9.6 25.2 all-gather.8
  95.5 31.3 all-gather.12
  128.5 22.4 all-gather.6
  153.0 38.3 all-gather.10
  210.1 34.6 reduce-scatter.1

commit v8 on v7

--- a/solution.py
+++ b/solution.py
@@ -61,9 +61,9 @@
     return x + lax.ppermute(x, axis, [(k, k ^ 2) for k in range(n)])
 
 
-def fetch_rows(w, n_picks, n_groups, chunks=2):
+def fetch_rows(w, n_picks, n_groups, gate, chunks=2):
     if n_groups != 2 or n_picks > RING_MAX:
-        return lax.all_gather(w, "picks", axis=0, tiled=True)
+        return lax.all_gather(w, "picks", axis=0, tiled=True), gate
     g = lax.axis_index("groups")
     p = lax.axis_index("picks")
     rows = w.shape[0] // 2
@@ -73,7 +73,7 @@
     for c in range(chunks):
         part = mine[c * step:(c + 1) * step]
         if own:
-            part, _ = lax.optimization_barrier((part, own[-1]))
+            part, _, gate = lax.optimization_barrier((part, own[-1], gate))
         blocks = [part] + [
             lax.ppermute(part, "picks", [(i, (i - s) % n_picks) for i in range(n_picks)])
             for s in range(1, n_picks)
@@ -87,7 +87,7 @@
     second = jnp.where(g == 0, other, own)
     flipped = jnp.stack([first, second], axis=1)
     ordered = jnp.roll(flipped, p, axis=0)
-    return ordered.reshape((n_picks * w.shape[0],) + w.shape[1:])
+    return ordered.reshape((n_picks * w.shape[0],) + w.shape[1:]), gate
 
 
 def on_device(
@@ -118,7 +118,9 @@
     column = lax.axis_index("heads") * local
     enc = encode(coords)
     cross_full = lax.all_gather(cross_out, "heads", axis=0, tiled=True)
-    piece = fetch_rows(kv_weight.reshape(kv_weight.shape[0], 2 * local), n_picks, n_groups)
+    piece, enc = fetch_rows(kv_weight.reshape(kv_weight.shape[0], 2 * local), n_picks, n_groups, enc)
+    out_full = lax.all_gather(self_out, "heads", axis=1, tiled=True)
+    out_full, cross_full, piece = lax.optimization_barrier((out_full, cross_full, piece))
     cross_full, piece = lax.optimization_barrier((cross_full, piece))
     keys_vals = jnp.dot(
         enc, piece.reshape(piece.shape[0], 2 * local), preferred_element_type=jnp.float32
@@ -147,8 +149,6 @@
         .reshape(lat_rows, local)
         .astype(jnp.bfloat16)
     )
-    out_full = lax.all_gather(self_out, "heads", axis=1, tiled=True)
-    out_full, attended = lax.optimization_barrier((out_full, attended))
     dq_local, attended = lax.optimization_barrier((dec_query, attended))
     dq_full = lax.all_gather(dq_local, "picks", axis=0, tiled=True)
     attended_full = ring_gather(attended.T, "heads", n_heads).T

time: 254 us -> 232 us (0.913)
  waiting for transfers between devices: 117 us -> 103 us
  starting transfers between devices: 21.5 us -> 17.6 us
    all_gather x1, waiting for transfers between devices: 22 us -> 0.01 us  [on_device(): out_full = lax.all_gather(self_out, 'heads', axis=1, tiled=True)]
    ppermute x2, waiting for transfers between devices: 0.01 us -> 13.5 us  [fetch_rows(): other.append(lax.ppermute(flipped, 'groups', [(0, 1), (1, 0)]))]
    ppermute x6, waiting for transfers between devices: 19.6 us -> 14.9 us  [fetch_rows(): lax.ppermute(part, 'picks', [(i, (i - s) % n_picks) for i in range(n_pick...]
    ppermute x6, starting transfers between devices: 14.1 us -> 10.1 us  [fetch_rows(): lax.ppermute(part, 'picks', [(i, (i - s) % n_picks) for i in range(n_pick...]
    unnamed x34 -> x30, local copies, waits for them, and re-layouts: 7.38 us -> 6.57 us
  transfers between devices with their start and end apart: 21 -> 21, of which waited for: 15 -> 13; matrix products, arithmetic and copies ran while one was open for 22% -> 22% of each run, Pallas kernels for 0% -> 0%
where the time goes in v8:
time: 232 us; the launch traced here: 231 us
  waiting for transfers between devices  103 us (44%)
  other arithmetic  44.1 us (19%)
  matrix products  28.1 us (12%)
  starting transfers between devices  17.6 us (8%)
  between operations  14.2 us (6%)
  blocking collectives  13.6 us (6%)
  local copies, waits for them, and re-layouts  10.5 us (5%)
    reduce_scatter x1, waiting for transfers between devices, on_device(): lax.psum_scatter(jnp.dot(enc.T, dquery, preferred_element_type=jnp.float3...  32.3 us
    ppermute x6, waiting for transfers between devices, ring_gather(): blocks.append(lax.ppermute(x, axis, [(i, (i - s) % n) for i in range(n)]))  25 us
    another operation x1, other arithmetic  22.8 us
    ppermute x6, waiting for transfers between devices, fetch_rows(): lax.ppermute(part, 'picks', [(i, (i - s) % n_picks) for i in range(n_pick...  14.9 us
    all_gather x1, blocking collectives, on_device(): lax.all_gather(jnp.stack([top, total]), 'picks', axis=0, tiled=False)  13.6 us
    ppermute x2, waiting for transfers between devices, fetch_rows(): other.append(lax.ppermute(flipped, 'groups', [(0, 1), (1, 0)]))  13.5 us
    all_gather x1, waiting for transfers between devices, on_device(): lax.all_gather(numer.astype(jnp.bfloat16), 'picks', axis=0, tiled=False)  12.2 us
    ppermute x6, starting transfers between devices, fetch_rows(): lax.ppermute(part, 'picks', [(i, (i - s) % n_picks) for i in range(n_pick...  10.1 us
  transfers between devices with their start and end apart: 21, of which 13 were waited for; matrix products, arithmetic and copies ran while one was open for 22% of the time, Pallas kernels for 0%

profile of v8, /device:TPU:0, one launch (start us, length us, event | category | flops | bytes accessed | tf_op | source)
XLA Modules:
  0.0 231.4 jit_solution(4111035279164090139)
XLA Ops:
  8.7 1.3 copy.101
  10.1 5.1 %collective-permute-start = (bf16[192,512]{1,0:T(8,128)(2,1)S(1)}, bf16[192,512]{1,0:T(8,128)(2,1)S(1)}, u32[]{:S(2)}, u32[]{:S(2)}) collective-permute-start(bf16[192,512]{1,0:T(8,128)(2,1)S(1)} %get-tuple-element.35), channel_id=1, source_target_pairs={{0,12},{4,0},{8,4},{12,8},{1,13},{5,1},{9,5},{13,9},{2,14},{6,2},{... | collective-permute-start | bytes 589832 | tf_op jit(solution)/shard_map/ppermute | solution.py:78
  15.2 1.0 collective-permute-start.2
  16.3 22.8 %fusion = (bf16[3,512,1024]{2,1,0:T(8,128)(2,1)S(1)}, bf16[3,512,1024]{2,1,0:T(8,128)(2,1)S(1)}) fusion(f32[3,1024]{1,0:T(4,128)S(1)} %copy-done.6, f32[512]{0:T(512)S(1)} %maximum_multiply_fusion), kind=kLoop, calls=%fused_computation.2 | loop fusion | flops 4718592 | bytes 6305792 | tf_op jit(solution)/shard_map/convert
  39.1 3.2 %pad_maximum_fusion = bf16[6,512,1024]{2,1,0:T(8,128)(2,1)} fusion(bf16[3,512,1024]{2,1,0:T(8,128)(2,1)S(1)} %get-tuple-element.42, bf16[3,512,1024]{2,1,0:T(8,128)(2,1)S(1)} %get-tuple-element.41), kind=kLoop, calls=%fused_computation.4 | loop fusion | flops 3145728 | bytes 12582912 | tf_op jit(solution)/shard_map/concatenate | solution.py:21
  42.3 1.0 fusion.72
  43.4 2.8 %collective-permute-start.3 = (bf16[192,512]{1,0:T(8,128)(2,1)S(1)}, bf16[192,512]{1,0:T(8,128)(2,1)S(1)}, u32[]{:S(2)}, u32[]{:S(2)}) collective-permute-start(bf16[192,512]{1,0:T(8,128)(2,1)S(1)} %get-tuple-element.14), channel_id=1, source_target_pairs={{0,12},{4,0},{8,4},{12,8},{1,13},{5,1},{9,5},{13,9},{2,14},{6,2},{... | collective-permute-start | bytes 589832 | tf_op jit(solution)/shard_map/ppermute | solution.py:78
  46.2 1.1 collective-permute-start.4
  47.3 1.5 collective-permute-start.6
  48.8 2.8 %collective-permute-done.3 = bf16[192,512]{1,0:T(8,128)(2,1)S(1)} collective-permute-done((bf16[192,512]{1,0:T(8,128)(2,1)S(1)}, bf16[192,512]{1,0:T(8,128)(2,1)S(1)}, u32[]{:S(2)}, u32[]{:S(2)}) %collective-permute-start.3) | collective-permute-done | bytes 196640 | tf_op jit(solution)/shard_map/ppermute | solution.py:78
  51.6 12.1 %collective-permute-done.4 = bf16[192,512]{1,0:T(8,128)(2,1)S(1)} collective-permute-done((bf16[192,512]{1,0:T(8,128)(2,1)S(1)}, bf16[192,512]{1,0:T(8,128)(2,1)S(1)}, u32[]{:S(2)}, u32[]{:S(2)}) %collective-permute-start.4) | collective-permute-done | bytes 196640 | tf_op jit(solution)/shard_map/ppermute | solution.py:78
  63.7 1.0 fusion.71
  64.7 1.5 collective-permute-start.7
  66.3 1.7 constant_dynamic-slice_fusion.3
  67.9 1.1 copy.99
  69.0 13.5 %collective-permute-done.7 = bf16[4,192,512]{2,1,0:T(8,128)(2,1)} collective-permute-done((bf16[4,192,512]{2,1,0:T(8,128)(2,1)}, bf16[4,192,512]{2,1,0:T(8,128)(2,1)}, u32[]{:S(2)}, u32[]{:S(2)}) %collective-permute-start.7) | collective-permute-done | bytes 786464 | tf_op jit(solution)/shard_map/ppermute | solution.py:83
  82.6 2.0 broadcast_select_fusion
  84.5 2.9 %fusion.10 = bf16[4,2,384,512]{3,2,1,0:T(8,128)(2,1)} fusion(s32[]{:T(128)S(6)} %select_n.59, bf16[4,1,384,512]{3,2,1,0:T(8,128)(2,1)S(1)} %get-tuple-element.25, bf16[4,1,384,512]{3,2,1,0:T(8,128)(2,1)S(1)} %get-tuple-element.24), kind=kLoop, calls=%fused_computation.23 | loop fusion | flops 4718592 | bytes 6291460 | tf_op jit(solution)/shard_map/jit(_roll_dynamic)/concatenate | solution.py:89
  87.4 7.1 %convolution_convert_fusion.1 = bf16[1024,512]{0,1:T(8,128)(2,1)S(1)} fusion(bf16[1024,3072]{0,1:T(8,128)(2,1)} %bitcast.127, bf16[3072,512]{1,0:T(8,128)(2,1)} %bitcast.133), kind=kOutput, calls=%fused_computation.64 | convolution fusion | flops 3221749760 | bytes 10485760 | tf_op jit(solution)/shard_map/dot_general | solution.py:125
  95.5 2.1 copy-done.2
  97.6 1.6 fusion.38
  99.4 3.1 %fusion.7 = f32[2,512]{1,0:T(2,128)S(1)} fusion(f32[2,512,1024]{2,1,0:T(8,128)} %copy-done.2, f32[2,512]{1,0:T(2,128)S(1)} %get-tuple-element.45), kind=kLoop, calls=%fused_computation.20 | loop fusion | flops 3144704 | bytes 4202496 | tf_op jit(solution)/shard_map/reduce_sum | solution.py:134
  102.5 13.6 %all-gather.1 = f32[8,2,512]{2,1,0:T(2,128)S(1)} all-gather(f32[2,2,512]{2,1,0:T(2,128)S(1)} %pad_maximum_fusion.5), channel_id=3, replica_groups=mesh['groups'=2,'picks'=4,'heads'=4] {'picks'}, dimensions={0}, use_global_device_ids=true | all-gather | bytes 40960 | tf_op jit(solution)/shard_map/all_gather | solution.py:139
  116.2 12.2 %all-gather.13.cloned.1.call-done = bf16[8,512,128]{2,1,0:T(8,128)(2,1)} async-done(((bf16[2,512,128]{2,1,0:T(8,128)(2,1)}), bf16[8,512,128]{2,1,0:T(8,128)(2,1)}) %all-gather.13.cloned.1.call-update) | async-done | bytes 1048592 | tf_op jit(solution)/shard_map/all_gather | solution.py:138
  128.4 1.8 multiply_reduce_fusion.1
  130.5 0.9 collective-permute-start.8
  132.3 5.5 %collective-permute-done.8 = bf16[256,512]{1,0:T(8,128)(2,1)S(1)} collective-permute-done((bf16[256,512]{1,0:T(8,128)(2,1)S(1)}, bf16[256,512]{1,0:T(8,128)(2,1)S(1)}, u32[]{:S(2)}, u32[]{:S(2)}) %collective-permute-start.8) | collective-permute-done | bytes 262176 | tf_op jit(solution)/shard_map/ppermute | solution.py:33
  137.8 6.8 %collective-permute-done.9 = bf16[256,512]{1,0:T(8,128)(2,1)S(1)} collective-permute-done((bf16[256,512]{1,0:T(8,128)(2,1)S(1)}, bf16[256,512]{1,0:T(8,128)(2,1)S(1)}, u32[]{:S(2)}, u32[]{:S(2)}) %collective-permute-start.9) | collective-permute-done | bytes 262176 | tf_op jit(solution)/shard_map/ppermute | solution.py:33
  144.8 1.2 fusion.55
  146.0 2.6 %multiply_reduce_fusion.3 = (f32[512]{0:T(512)S(1)}, f32[512,1024]{1,0:T(8,128)S(1)}) fusion(bf16[1024,512]{1,0:T(8,128)(2,1)S(1)} %bitcast.132, bf16[1024,1024]{1,0:T(8,128)(2,1)S(1)} %copy-done.4, bf16[512,1024]{1,0:T(8,128)(2,1)} %param.17), kind=kOutput, calls=%fused_computation.54 | convolution fusion | flops 1075838464 | bytes 6293504 | tf_op jit(solution)/shard_map/dot_general | solution.py:155
  148.6 1.1 fusion.33
  151.0 1.4 collective-permute-start.12
  152.6 4.2 %collective-permute-done.11 = bf16[256,512]{1,0:T(8,128)(2,1)S(1)} collective-permute-done((bf16[256,512]{1,0:T(8,128)(2,1)S(1)}, bf16[256,512]{1,0:T(8,128)(2,1)S(1)}, u32[]{:S(2)}, u32[]{:S(2)}) %collective-permute-start.11) | collective-permute-done | bytes 262176 | tf_op jit(solution)/shard_map/ppermute | solution.py:33
  156.8 8.1 %collective-permute-done.12 = bf16[256,512]{1,0:T(8,128)(2,1)S(1)} collective-permute-done((bf16[256,512]{1,0:T(8,128)(2,1)S(1)}, bf16[256,512]{1,0:T(8,128)(2,1)S(1)}, u32[]{:S(2)}, u32[]{:S(2)}) %collective-permute-start.12) | collective-permute-done | bytes 262176 | tf_op jit(solution)/shard_map/ppermute | solution.py:33
  165.1 1.2 fusion.48
  166.4 1.4 multiply_reduce_fusion.2
  167.8 1.4 copy-done.3
  169.1 0.9 fusion.37
  170.1 5.1 %convolution_convert_fusion.3 = bf16[1024,256]{0,1:T(8,128)(2,1)S(1)} fusion(bf16[1024,3072]{0,1:T(8,128)(2,1)} %bitcast.128, bf16[3072,256]{1,0:T(8,128)(2,1)} %all-gather.11.cloned.1.call-done), kind=kOutput, calls=%fused_computation.68 | convolution fusion | flops 1610874880 | bytes 8388608 | tf_op jit(solution)/shard_map/dot_general | solution.py:187
  176.0 1.0 fusion.34
  177.2 1.0 collective-permute-done.14
  179.1 2.7 %collective-permute-done.15 = f32[1024]{0:T(1024)S(1)} collective-permute-done((f32[1024]{0:T(1024)S(1)}, f32[1024]{0:T(1024)S(1)}, u32[]{:S(2)}, u32[]{:S(2)}) %collective-permute-start.15) | collective-permute-done | bytes 4128 | tf_op jit(solution)/shard_map/ppermute | solution.py:61
  182.4 1.0 fusion.2
  183.5 1.4 fusion.30
  185.5 3.1 %convolution_convert_fusion = bf16[3072,256]{1,0:T(8,128)(2,1)} fusion(bf16[1024,3072]{0,1:T(8,128)(2,1)S(1)} %bitcast.131, bf16[1024,256]{0,1:T(8,128)(2,1)S(1)} %bitcast.182), kind=kOutput, calls=%fused_computation.17 | convolution fusion | flops 1611399168 | bytes 8388608 | tf_op jit(solution)/shard_map/dot_general | solution.py:213
  188.7 1.9 constant_dynamic-slice_fusion.1
  190.6 32.3 %reduce-scatter.2.cloned.1.call-done = bf16[768,256]{1,0:T(8,128)(2,1)} async-done(((bf16[3072,256]{1,0:T(8,128)(2,1)}), bf16[768,256]{1,0:T(8,128)(2,1)}) %reduce-scatter.2.cloned.1.call-update) | async-done | bytes 393232 | tf_op jit(solution)/shard_map/reduce_scatter | solution.py:212
  222.9 1.9 convert_element_type.103
  (78 shorter events, 9.0 us)
Async XLA Ops:
  7.2 141.5 %copy-start = (bf16[3,1024,256]{2,1,0:T(8,128)(2,1)S(1)}, bf16[3,1024,256]{2,1,0:T(8,128)(2,1)}, u32[]{:S(2)}) copy-start(bf16[3,1024,256]{2,1,0:T(8,128)(2,1)} %param.21) | copy-start | bytes 4718596
  7.2 9.1 %copy-start.6 = (f32[3,1024]{1,0:T(4,128)S(1)}, f32[3,1024]{1,0:T(4,128)}, u32[]{:S(2)}) copy-start(f32[3,1024]{1,0:T(4,128)} %param.14) | copy-start | bytes 36868
  7.2 80.2 %all-gather.7.cloned.1.call-start = ((), (), s32[]{:S(2)}) async-start(), calls=%async_computation.1 | async-start | bytes 2621440 | tf_op jit(solution)/shard_map/all_gather | solution.py:122
  7.9 79.5 %all-gather.9.cloned.1.call-start = ((), (), s32[]{:S(2)}) async-start(), calls=%async_computation.2 | async-start | bytes 2621440 | tf_op jit(solution)/shard_map/all_gather | solution.py:120
  8.7 119.8 %all-gather.13.cloned.1.call-start = ((), (), s32[]{:S(2)}) async-start(), calls=%async_computation.5 | async-start | bytes 1310720 | tf_op jit(solution)/shard_map/all_gather | solution.py:138
  10.1 32.3 %collective-permute-start = (bf16[192,512]{1,0:T(8,128)(2,1)S(1)}, bf16[192,512]{1,0:T(8,128)(2,1)S(1)}, u32[]{:S(2)}, u32[]{:S(2)}) collective-permute-start(bf16[192,512]{1,0:T(8,128)(2,1)S(1)} %get-tuple-element.35), channel_id=1, source_target_pairs={{0,12},{4,0},{8,4},{12,8},{1,13},{5,1},{9,5},{13,9},{2,14},{6,2},{... | collective-permute-start | bytes 589832 | tf_op jit(solution)/shard_map/ppermute | solution.py:78
  15.2 27.2 %collective-permute-start.1 = (bf16[192,512]{1,0:T(8,128)(2,1)S(1)}, bf16[192,512]{1,0:T(8,128)(2,1)S(1)}, u32[]{:S(2)}, u32[]{:S(2)}) collective-permute-start(bf16[192,512]{1,0:T(8,128)(2,1)S(1)} %get-tuple-element.35), channel_id=1, source_target_pairs={{0,8},{4,12},{8,0},{12,4},{1,9},{5,13},{9,1},{13,5},{2,10},{6,14},... | collective-permute-start | bytes 589832 | tf_op jit(solution)/shard_map/ppermute | solution.py:78
  15.2 27.2 %collective-permute-start.2 = (bf16[192,512]{1,0:T(8,128)(2,1)S(1)}, bf16[192,512]{1,0:T(8,128)(2,1)S(1)}, u32[]{:S(2)}, u32[]{:S(2)}) collective-permute-start(bf16[192,512]{1,0:T(8,128)(2,1)S(1)} %get-tuple-element.35), channel_id=1, source_target_pairs={{0,4},{4,8},{8,12},{12,0},{1,5},{5,9},{9,13},{13,1},{2,6},{6,10},{... | collective-permute-start | bytes 589832 | tf_op jit(solution)/shard_map/ppermute | solution.py:78
  43.4 8.2 %collective-permute-start.3 = (bf16[192,512]{1,0:T(8,128)(2,1)S(1)}, bf16[192,512]{1,0:T(8,128)(2,1)S(1)}, u32[]{:S(2)}, u32[]{:S(2)}) collective-permute-start(bf16[192,512]{1,0:T(8,128)(2,1)S(1)} %get-tuple-element.14), channel_id=1, source_target_pairs={{0,12},{4,0},{8,4},{12,8},{1,13},{5,1},{9,5},{13,9},{2,14},{6,2},{... | collective-permute-start | bytes 589832 | tf_op jit(solution)/shard_map/ppermute | solution.py:78
  46.2 17.5 %collective-permute-start.4 = (bf16[192,512]{1,0:T(8,128)(2,1)S(1)}, bf16[192,512]{1,0:T(8,128)(2,1)S(1)}, u32[]{:S(2)}, u32[]{:S(2)}) collective-permute-start(bf16[192,512]{1,0:T(8,128)(2,1)S(1)} %get-tuple-element.14), channel_id=1, source_target_pairs={{0,8},{4,12},{8,0},{12,4},{1,9},{5,13},{9,1},{13,5},{2,10},{6,14},... | collective-permute-start | bytes 589832 | tf_op jit(solution)/shard_map/ppermute | solution.py:78
  47.3 16.4 %collective-permute-start.5 = (bf16[192,512]{1,0:T(8,128)(2,1)S(1)}, bf16[192,512]{1,0:T(8,128)(2,1)S(1)}, u32[]{:S(2)}, u32[]{:S(2)}) collective-permute-start(bf16[192,512]{1,0:T(8,128)(2,1)S(1)} %get-tuple-element.14), channel_id=1, source_target_pairs={{0,4},{4,8},{8,12},{12,0},{1,5},{5,9},{9,13},{13,1},{2,6},{6,10},{... | collective-permute-start | bytes 589832 | tf_op jit(solution)/shard_map/ppermute | solution.py:78
  47.3 21.7 %collective-permute-start.6 = (bf16[4,192,512]{2,1,0:T(8,128)(2,1)}, bf16[4,192,512]{2,1,0:T(8,128)(2,1)}, u32[]{:S(2)}, u32[]{:S(2)}) collective-permute-start(bf16[4,192,512]{2,1,0:T(8,128)(2,1)} %get-tuple-element.32), channel_id=1, source_target_pairs={{0,16},{16,0},{1,17},{17,1},{2,18},{18,2},{3,19},{19,3},{4,20},{20... | collective-permute-start | bytes 2359304 | tf_op jit(solution)/shard_map/ppermute | solution.py:83
  64.7 17.8 %collective-permute-start.7 = (bf16[4,192,512]{2,1,0:T(8,128)(2,1)}, bf16[4,192,512]{2,1,0:T(8,128)(2,1)}, u32[]{:S(2)}, u32[]{:S(2)}) collective-permute-start(bf16[4,192,512]{2,1,0:T(8,128)(2,1)} %get-tuple-element.34), channel_id=1, source_target_pairs={{0,16},{16,0},{1,17},{17,1},{2,18},{18,2},{3,19},{19,3},{4,20},{20... | collective-permute-start | bytes 2359304 | tf_op jit(solution)/shard_map/ppermute | solution.py:83
  95.5 2.1 copy-start.2
  99.2 33.1 %copy-start.7 = (f32[2,1024]{1,0:T(2,128)S(1)}, f32[2,1024]{1,0:T(2,128)}, u32[]{:S(2)}) copy-start(f32[2,1024]{1,0:T(2,128)} %param.20) | copy-start | bytes 24580
  99.2 70.9 %all-gather.11.cloned.1.call-start = ((), (), s32[]{:S(2)}) async-start(), calls=%async_computation.3 | async-start | bytes 1966080 | tf_op jit(solution)/shard_map/all_gather | solution.py:153
  130.5 7.4 %collective-permute-start.8 = (bf16[256,512]{1,0:T(8,128)(2,1)S(1)}, bf16[256,512]{1,0:T(8,128)(2,1)S(1)}, u32[]{:S(2)}, u32[]{:S(2)}) collective-permute-start(bf16[256,512]{1,0:T(8,128)(2,1)S(1)} %bitcast.136), channel_id=1, source_target_pairs={{0,3},{1,0},{2,1},{3,2},{4,7},{5,4},{6,5},{7,6},{8,11},{9,8},{10,9... | collective-permute-start | bytes 786440 | tf_op jit(solution)/shard_map/ppermute | solution.py:33
  131.3 13.3 %collective-permute-start.9 = (bf16[256,512]{1,0:T(8,128)(2,1)S(1)}, bf16[256,512]{1,0:T(8,128)(2,1)S(1)}, u32[]{:S(2)}, u32[]{:S(2)}) collective-permute-start(bf16[256,512]{1,0:T(8,128)(2,1)S(1)} %bitcast.137), channel_id=1, source_target_pairs={{0,2},{1,3},{2,0},{3,1},{4,6},{5,7},{6,4},{7,5},{8,10},{9,11},{10,... | collective-permute-start | bytes 786440 | tf_op jit(solution)/shard_map/ppermute | solution.py:33
  132.1 12.7 %collective-permute-start.10 = (bf16[256,512]{1,0:T(8,128)(2,1)S(1)}, bf16[256,512]{1,0:T(8,128)(2,1)S(1)}, u32[]{:S(2)}, u32[]{:S(2)}) collective-permute-start(bf16[256,512]{1,0:T(8,128)(2,1)S(1)} %bitcast.138), channel_id=1, source_target_pairs={{0,1},{1,2},{2,3},{3,0},{4,5},{5,6},{6,7},{7,4},{8,9},{9,10},{10,1... | collective-permute-start | bytes 786440 | tf_op jit(solution)/shard_map/ppermute | solution.py:33
  132.3 90.6 %reduce-scatter.2.cloned.1.call-start = ((), (), s32[]{:S(2)}) async-start(), calls=%async_computation.4 | async-start | bytes 1966080 | tf_op jit(solution)/shard_map/reduce_scatter | solution.py:212
  132.3 13.7 %copy-start.4 = (bf16[1024,1024]{1,0:T(8,128)(2,1)S(1)}, bf16[1024,1024]{1,0:T(8,128)(2,1)}, u32[]{:S(2)}) copy-start(bf16[1024,1024]{1,0:T(8,128)(2,1)} %all-gather.9.cloned.1.call-done) | copy-start | bytes 6291460
  150.4 16.0 %copy-start.11 = (bf16[1024,1024]{1,0:T(8,128)(2,1)S(1)}, bf16[1024,1024]{1,0:T(8,128)(2,1)}, u32[]{:S(2)}) copy-start(bf16[1024,1024]{1,0:T(8,128)(2,1)} %all-gather.7.cloned.1.call-done) | copy-start | bytes 6291460
  150.9 5.8 %collective-permute-start.11 = (bf16[256,512]{1,0:T(8,128)(2,1)S(1)}, bf16[256,512]{1,0:T(8,128)(2,1)S(1)}, u32[]{:S(2)}, u32[]{:S(2)}) collective-permute-start(bf16[256,512]{1,0:T(8,128)(2,1)S(1)} %bitcast.157), channel_id=1, source_target_pairs={{0,3},{1,0},{2,1},{3,2},{4,7},{5,4},{6,5},{7,6},{8,11},{9,8},{10,9... | collective-permute-start | bytes 786440 | tf_op jit(solution)/shard_map/ppermute | solution.py:33
  151.0 13.9 %collective-permute-start.12 = (bf16[256,512]{1,0:T(8,128)(2,1)S(1)}, bf16[256,512]{1,0:T(8,128)(2,1)S(1)}, u32[]{:S(2)}, u32[]{:S(2)}) collective-permute-start(bf16[256,512]{1,0:T(8,128)(2,1)S(1)} %bitcast.158), channel_id=1, source_target_pairs={{0,2},{1,3},{2,0},{3,1},{4,6},{5,7},{6,4},{7,5},{8,10},{9,11},{10,... | collective-permute-start | bytes 786440 | tf_op jit(solution)/shard_map/ppermute | solution.py:33
  152.4 12.7 %collective-permute-start.13 = (bf16[256,512]{1,0:T(8,128)(2,1)S(1)}, bf16[256,512]{1,0:T(8,128)(2,1)S(1)}, u32[]{:S(2)}, u32[]{:S(2)}) collective-permute-start(bf16[256,512]{1,0:T(8,128)(2,1)S(1)} %bitcast.159), channel_id=1, source_target_pairs={{0,1},{1,2},{2,3},{3,0},{4,5},{5,6},{6,7},{7,4},{8,9},{9,10},{10,1... | collective-permute-start | bytes 786440 | tf_op jit(solution)/shard_map/ppermute | solution.py:33
  166.4 2.8 %copy-start.5 = (bf16[2,1024,256]{2,1,0:T(8,128)(2,1)S(1)}, bf16[2,1024,256]{2,1,0:T(8,128)(2,1)}, u32[]{:S(2)}) copy-start(bf16[2,1024,256]{2,1,0:T(8,128)(2,1)} %param.23) | copy-start | bytes 3145732
  167.8 1.4 copy-start.3
  175.1 0.9 copy-start.9
  176.0 1.1 copy-start.8
  176.0 1.1 copy-start.10
  177.0 1.2 collective-permute-start.14
  178.2 3.6 %collective-permute-start.15 = (f32[1024]{0:T(1024)S(1)}, f32[1024]{0:T(1024)S(1)}, u32[]{:S(2)}, u32[]{:S(2)}) collective-permute-start(f32[1024]{0:T(1024)S(1)} %add.69), channel_id=1, source_target_pairs={{0,2},{1,3},{2,0},{3,1},{4,6},{5,7},{6,4},{7,5},{8,10},{9,11},{10,... | collective-permute-start | bytes 12296 | tf_op jit(solution)/shard_map/ppermute | solution.py:61
  182.4 2.4 %slice-start = ((s8[6291456]{0:T(1024)(128)(4,1)}), s8[4194304]{0:T(1024)(128)(4,1)S(1)}, s32[]{:S(2)}) async-start(s8[6291456]{0:T(1024)(128)(4,1)} %bitcast.129), calls=%async_computation.6 | async-start | bytes 8388608
  183.5 2.1 slice-start.1
  185.5 39.3 %copy-start.1 = (bf16[3,1024,256]{2,1,0:T(8,128)(2,1)S(1)}, bf16[3,1024,256]{2,1,0:T(8,128)(2,1)}, u32[]{:S(2)}) copy-start(bf16[3,1024,256]{2,1,0:T(8,128)(2,1)} %param.21) | copy-start | bytes 4718596
Sparse Core Ops, SparseCore 0:
  9.6 25.5 all-gather.6
  36.7 22.5 all-gather.8
  99.3 29.0 all-gather.12
  132.4 36.8 all-gather.10
  188.8 34.0 reduce-scatter.1

commit v9 on v6

--- a/solution.py
+++ b/solution.py
@@ -59,6 +59,18 @@
         return lax.psum(x, axis)
     x = x + lax.ppermute(x, axis, [(k, k ^ 1) for k in range(n)])
     return x + lax.ppermute(x, axis, [(k, k ^ 2) for k in range(n)])
+
+
+def pair_gather(x, axis, n):
+    near = lax.ppermute(x, axis, [(k, k ^ 1) for k in range(n)])
+    far = lax.ppermute(x, axis, [(k, k ^ 2) for k in range(n)])
+    far_near = lax.ppermute(far, axis, [(k, k ^ 1) for k in range(n)])
+    return jnp.concatenate([x, near, far, far_near], axis=0)
+
+
+def xor_blocks(x, idx, n):
+    blocks = x.reshape((n, x.shape[0] // n) + x.shape[1:])
+    return jnp.take(blocks, jnp.arange(n) ^ idx, axis=0).reshape(x.shape)
 
 
 def on_device(
@@ -88,7 +100,11 @@
     nheads = local // HEAD
     column = lax.axis_index("heads") * local
     enc = encode(coords)
-    cross_full = ring_gather(cross_out, "heads", n_heads)
+    paired = n_heads == 4
+    if paired:
+        cross_full = pair_gather(cross_out, "heads", n_heads)
+    else:
+        cross_full = ring_gather(cross_out, "heads", n_heads)
     piece = lax.all_gather(
         kv_weight.reshape(kv_weight.shape[0], 2 * local), "picks", axis=0, tiled=True
     )
@@ -121,10 +137,13 @@
         .astype(jnp.bfloat16)
     )
     out_full = ring_gather(self_out.T, "heads", n_heads).T
+    if paired:
+        out_full = xor_blocks(out_full, lax.axis_index("heads"), n_heads)
     out_full, attended = lax.optimization_barrier((out_full, attended))
     dq_local, attended = lax.optimization_barrier((dec_query, attended))
     dq_full = lax.all_gather(dq_local, "picks", axis=0, tiled=True)
-    attended_full = ring_gather(attended.T, "heads", n_heads).T
+    head_gather = pair_gather if paired else ring_gather
+    attended_full = head_gather(attended.T, "heads", n_heads).T
     whole = latents.astype(jnp.float32) + jnp.dot(
         attended_full, cross_full, preferred_element_type=jnp.float32
     )
@@ -145,7 +164,7 @@
         .astype(jnp.bfloat16)
         .reshape(lat_rows, local)
     )
-    every_head = ring_gather(head_out.T, "heads", n_heads).T
+    every_head = head_gather(head_out.T, "heads", n_heads).T
     out_whole = whole + jnp.dot(every_head, out_full, preferred_element_type=jnp.float32)
     latents_out = lax.dynamic_slice_in_dim(out_whole, column, local, 1)
     power_two = jnp.mean(out_whole * out_whole, axis=1, keepdims=True)

time: 219 us -> 230 us (1.050)
  local copies, waits for them, and re-layouts: 10.1 us -> 32.7 us
  waiting for transfers between devices: 96.8 us -> 85.7 us
  other arithmetic: 46.1 us -> 38.3 us
  matrix products: 26.9 us -> 33.8 us
    ppermute x12 -> x3, waiting for transfers between devices: 38.7 us -> 0.01 us  [ring_gather(): blocks.append(lax.ppermute(x, axis, [(i, (i - s) % n) for i in range(n)]))]
    all_gather x1, waiting for transfers between devices: 0.02 us -> 15.3 us  [on_device(): dq_full = lax.all_gather(dq_local, 'picks', axis=0, tiled=True)]
    ppermute x0 -> x9, waiting for transfers between devices: none -> 14.4 us  [the longest x3 11.6 us: pair_gather(): far = lax.ppermute(x, axis, [(k, k ^ 2) for k in range(n)])]
    concatenate x4 -> x1, other arithmetic: 13.5 us -> 2.67 us  [pair_gather(): return jnp.concatenate([x, near, far, far_near], axis=0)]
    unnamed x37 -> x41, local copies, waits for them, and re-layouts: 6.86 us -> 16.8 us
    all_gather x1, waiting for transfers between devices: 7.49 us -> 0.02 us  [on_device(): lax.all_gather(numer.astype(jnp.bfloat16), 'picks', axis=0, tiled=False)]
    ppermute x12 -> x3, starting transfers between devices: 9.55 us -> 2.19 us  [ring_gather(): blocks.append(lax.ppermute(x, axis, [(i, (i - s) % n) for i in range(n)]))]
    ppermute x0 -> x9, starting transfers between devices: none -> 6.59 us  [the longest x3 6.29 us: pair_gather(): far = lax.ppermute(x, axis, [(k, k ^ 2) for k in range(n)])]
  transfers between devices with their start and end apart: 18 -> 18, of which waited for: 13 -> 9; matrix products, arithmetic and copies ran while one was open for 27% -> 30% of each run, Pallas kernels for 0% -> 0%
where the time goes in v9:
time: 230 us; the launch traced here: 229 us
  waiting for transfers between devices  85.7 us (37%)
  other arithmetic  38.3 us (17%)
  matrix products  33.8 us (15%)
  local copies, waits for them, and re-layouts  32.7 us (14%)
  between operations  14.1 us (6%)
  blocking collectives  13.3 us (6%)
  starting transfers between devices  10.9 us (5%)
    reduce_scatter x1, waiting for transfers between devices, on_device(): lax.psum_scatter(jnp.dot(enc.T, dquery, preferred_element_type=jnp.float3...  32.4 us
    another operation x1, other arithmetic  23.6 us
    all_gather x1, waiting for transfers between devices, on_device(): lax.all_gather(kv_weight.reshape(kv_weight.shape[0], 2 * local), 'picks',...  20.5 us
    unnamed x41, local copies, waits for them, and re-layouts  16.8 us
    all_gather x1, waiting for transfers between devices, on_device(): dq_full = lax.all_gather(dq_local, 'picks', axis=0, tiled=True)  15.3 us
    all_gather x1, blocking collectives, on_device(): lax.all_gather(jnp.stack([top, total]), 'picks', axis=0, tiled=False)  13.3 us
    ppermute x3, waiting for transfers between devices, pair_gather(): far = lax.ppermute(x, axis, [(k, k ^ 2) for k in range(n)])  11.6 us
    dot_general x1, matrix products, on_device(): jnp.dot(enc, piece.reshape(piece.shape[0], 2 * local), preferred_element_...  7.15 us
  transfers between devices with their start and end apart: 18, of which 9 were waited for; matrix products, arithmetic and copies ran while one was open for 30% of the time, Pallas kernels for 0%

profile of v9, /device:TPU:0, one launch (start us, length us, event | category | flops | bytes accessed | tf_op | source)
XLA Modules:
  0.0 228.8 jit_solution(15377467131206212369)
XLA Ops:
  7.2 2.3 %copy.99 = bf16[96,8,2,256]{3,1,2,0:T(8,128)(2,1)} copy(bf16[96,8,2,256]{3,2,1,0:T(2,128)(2,1)} %bitcast.138) | data formatting | bytes 1572864
  9.6 3.0 %collective-permute-start.4 = (bf16[256,1024]{1,0:T(8,128)(2,1)}, bf16[256,1024]{1,0:T(8,128)(2,1)}, u32[]{:S(2)}, u32[]{:S(2)}) collective-permute-start(bf16[256,1024]{1,0:T(8,128)(2,1)} %param.17), channel_id=1, source_target_pairs={{0,2},{1,3},{2,0},{3,1},{4,6},{5,7},{6,4},{7,5},{8,10},{9,11},{10,... | collective-permute-start | bytes 1572872 | tf_op jit(solution)/shard_map/ppermute | solution.py:66
  12.6 1.2 copy.61
  14.1 1.9 collective-permute-start.1
  16.1 23.6 %fusion = (bf16[3,512,1024]{2,1,0:T(8,128)(2,1)S(1)}, bf16[3,512,1024]{2,1,0:T(8,128)(2,1)S(1)}) fusion(f32[3,1024]{1,0:T(4,128)} %param.12, f32[512]{0:T(512)S(1)} %maximum_multiply_fusion), kind=kLoop, calls=%fused_computation.3 | loop fusion | flops 4718592 | bytes 6305792 | tf_op jit(solution)/shard_map/convert
  39.7 3.2 %pad_maximum_fusion = bf16[6,512,1024]{2,1,0:T(8,128)(2,1)} fusion(bf16[3,512,1024]{2,1,0:T(8,128)(2,1)S(1)} %get-tuple-element.27, bf16[3,512,1024]{2,1,0:T(8,128)(2,1)S(1)} %get-tuple-element.26), kind=kLoop, calls=%fused_computation.5 | loop fusion | flops 3145728 | bytes 12582912 | tf_op jit(solution)/shard_map/concatenate | solution.py:21
  43.8 1.7 constant_dynamic-slice_fusion.1
  45.5 1.1 copy.96
  46.9 1.9 bitcast_dynamic-update-slice_fusion.6
  50.5 0.9 bitcast_dynamic-update-slice_fusion.1
  51.4 1.9 bitcast_dynamic-update-slice_fusion.7
  53.3 2.7 %pad_maximum_fusion.1 = bf16[1024,1024]{1,0:T(8,128)(2,1)} fusion(bf16[256,1024]{1,0:T(8,128)(2,1)S(1)} %collective-permute-done.5, bf16[256,1024]{1,0:T(8,128)(2,1)} %collective-permute-done.4, bf16[256,1024]{1,0:T(8,128)(2,1)} %collective-permute-done.3, bf16[256,1024]{1,0:T(8,128)(2,1)S(1)} %copy-done.7), kind=kLoop, calls=%fused_computation.21 | loop fusion | flops 8388608 | bytes 4194304 | tf_op jit(solution)/shard_map/concatenate | solution.py:68
  55.9 20.5 %all-gather.6.cloned.1.call-done = bf16[3072,512]{1,0:T(8,128)(2,1)} async-done(((bf16[768,512]{1,0:T(8,128)(2,1)}), bf16[3072,512]{1,0:T(8,128)(2,1)}) %all-gather.6.cloned.1.call-update) | async-done | bytes 3145744 | tf_op jit(solution)/shard_map/all_gather | solution.py:108
  76.4 7.1 %convolution_convert_fusion.1 = bf16[1024,512]{0,1:T(8,128)(2,1)S(1)} fusion(bf16[3072,1024]{1,0:T(8,128)(2,1)} %bitcast.120, bf16[3072,512]{1,0:T(8,128)(2,1)} %all-gather.6.cloned.1.call-done), kind=kOutput, calls=%fused_computation.39 | convolution fusion | flops 3221749760 | bytes 10485760 | tf_op jit(solution)/shard_map/dot_general | solution.py:112
  83.7 0.8 multiply_reduce_fusion
  84.5 2.0 copy-done.2
  86.5 1.6 fusion.35
  88.4 0.9 bitcast_dynamic-update-slice_fusion.5
  90.1 3.1 %constant_dynamic-slice_fusion.2 = bf16[4,256,1024]{2,1,0:T(8,128)(2,1)} fusion(bf16[8,256,1024]{2,1,0:T(8,128)(2,1)} %bitcast_dynamic-update-slice_fusion.3, s32[]{:T(128)S(6)} %select_n.40), kind=kLoop, calls=%fused_computation.107 | loop fusion | bytes 4194308 | tf_op jit(solution)/shard_map/jit(_roll_dynamic)/dynamic_slice | solution.py:35
  93.2 4.0 %copy.62 = bf16[1024,1024]{1,0:T(8,128)(2,1)} copy(bf16[1024,1024]{0,1:T(8,128)(2,1)} %bitcast.118) | data formatting | bytes 4194304 | tf_op jit(solution)/shard_map/transpose | solution.py:139
  97.2 3.6 %gather_fusion = bf16[4,256,1024]{2,1,0:T(8,128)(2,1)} fusion(bf16[4,256,1024]{2,1,0:T(8,128)(2,1)} %bitcast.119, s32[1024]{0:T(1024)S(1)} %pad_clamp_fusion), kind=kCustom, calls=%fused_computation | custom fusion | bytes 4194320 | tf_op jit(solution)/shard_map/jit(_take)/gather | solution.py:73
  100.8 3.3 %bitcast_select_fusion = bf16[1024,1024]{1,0:T(8,128)(2,1)} fusion(bf16[4,256,1024]{2,1,0:T(8,128)(2,1)} %gather_fusion, pred[1024]{0:T(1024)(128)(4,1)S(1)} %broadcast_in_dim.17), kind=kLoop, calls=%fused_computation.22 | loop fusion | flops 1048576 | bytes 4195328 | tf_op jit(solution)/shard_map/jit(_take)/select_n | solution.py:73
  104.1 0.9 fusion.7
  105.1 13.3 %all-gather.1 = f32[8,2,512]{2,1,0:T(2,128)S(1)} all-gather(f32[2,2,512]{2,1,0:T(2,128)S(1)} %pad_maximum_fusion.2), channel_id=3, replica_groups=mesh['groups'=2,'picks'=4,'heads'=4] {'picks'}, dimensions={0}, use_global_device_ids=true | all-gather | bytes 40960 | tf_op jit(solution)/shard_map/all_gather | solution.py:126
  119.0 5.1 %fusion.60 = f32[512,2,1,128]{3,2,1,0:T(1,128)S(1)} fusion(f32[4,2,512,1]{0,3,1,2:T(1,128)S(1)} %copy.83, bf16[4,2,512,128]{3,2,1,0:T(8,128)(2,1)} %bitcast.157), kind=kOutput, calls=%fused_computation.71 | convolution fusion | flops 6291456 | bytes 1589248 | tf_op jit(solution)/shard_map/phl,phlc->hlc/dot_general | solution.py:130
  125.0 1.6 collective-permute-start.7
  126.6 4.8 %collective-permute-done.7 = bf16[256,512]{0,1:T(8,128)(2,1)S(1)} collective-permute-done((bf16[256,512]{0,1:T(8,128)(2,1)S(1)}, bf16[256,512]{0,1:T(8,128)(2,1)S(1)}, u32[]{:S(2)}, u32[]{:S(2)}) %collective-permute-start.7) | collective-permute-done | bytes 262176 | tf_op jit(solution)/shard_map/ppermute | solution.py:66
  131.7 1.3 collective-permute-done.8
  133.1 3.1 %multiply_reduce_fusion.2 = (f32[512]{0:T(512)S(1)}, f32[512,1024]{1,0:T(8,128)S(1)}) fusion(bf16[1024,1024]{1,0:T(8,128)(2,1)} %pad_maximum_fusion.1, bf16[256,512]{0,1:T(8,128)(2,1)} %collective-permute-done.8, bf16[256,512]{0,1:T(8,128)(2,1)S(1)} %collective-permute-done.7, bf16[256,512]{0,1:T(8,128)(2,1)} %collective-permute-done.6, ...), kind=kOutput, calls=%fused_computation.33 | convolution fusion | flops 1080032768 | bytes 6293504 | tf_op jit(solution)/shard_map/dot_general | solution.py:147
  136.2 1.1 fusion.30
  138.5 1.6 collective-permute-start.10
  140.2 6.8 %collective-permute-done.10 = bf16[256,512]{1,0:T(8,128)(2,1)S(1)} collective-permute-done((bf16[256,512]{1,0:T(8,128)(2,1)S(1)}, bf16[256,512]{1,0:T(8,128)(2,1)S(1)}, u32[]{:S(2)}, u32[]{:S(2)}) %collective-permute-start.10) | collective-permute-done | bytes 262176 | tf_op jit(solution)/shard_map/ppermute | solution.py:66
  146.9 1.5 collective-permute-done.11
  148.5 1.4 multiply_reduce_fusion.1
  149.9 1.3 copy-done.4
  151.2 0.9 fusion.34
  152.1 15.3 %all-gather.8.cloned.1.call-done = bf16[3072,256]{1,0:T(8,128)(2,1)} async-done(((bf16[768,256]{1,0:T(8,128)(2,1)}), bf16[3072,256]{1,0:T(8,128)(2,1)}) %all-gather.8.cloned.1.call-update) | async-done | bytes 1572880 | tf_op jit(solution)/shard_map/all_gather | solution.py:144
  167.4 5.1 %convolution_convert_fusion.3 = bf16[1024,256]{0,1:T(8,128)(2,1)S(1)} fusion(bf16[3072,1024]{1,0:T(8,128)(2,1)} %bitcast.121, bf16[3072,256]{1,0:T(8,128)(2,1)} %all-gather.8.cloned.1.call-done), kind=kOutput, calls=%fused_computation.43 | convolution fusion | flops 1610874880 | bytes 8388608 | tf_op jit(solution)/shard_map/dot_general | solution.py:179
  173.4 1.0 fusion.31
  174.6 1.0 collective-permute-done.12
  175.6 1.5 collective-permute-start.13
  177.3 1.9 collective-permute-done.13
  179.8 1.0 fusion.2
  180.8 1.4 fusion.27
  182.9 3.1 %convolution_convert_fusion = bf16[3072,256]{1,0:T(8,128)(2,1)} fusion(bf16[3072,1024]{1,0:T(8,128)(2,1)S(1)} %bitcast.124, bf16[1024,256]{0,1:T(8,128)(2,1)S(1)} %bitcast.161), kind=kOutput, calls=%fused_computation.14 | convolution fusion | flops 1611399168 | bytes 8388608 | tf_op jit(solution)/shard_map/dot_general | solution.py:205
  186.1 1.9 constant_dynamic-slice_fusion
  187.9 32.4 %reduce-scatter.2.cloned.1.call-done = bf16[768,256]{1,0:T(8,128)(2,1)} async-done(((bf16[3072,256]{1,0:T(8,128)(2,1)}), bf16[768,256]{1,0:T(8,128)(2,1)}) %reduce-scatter.2.cloned.1.call-update) | async-done | bytes 393232 | tf_op jit(solution)/shard_map/reduce_scatter | solution.py:204
  220.4 1.9 convert_element_type.100
  (87 shorter events, 9.9 us)
Async XLA Ops:
  7.2 129.0 %copy-start = (bf16[3,1024,256]{2,1,0:T(8,128)(2,1)S(1)}, bf16[3,1024,256]{2,1,0:T(8,128)(2,1)}, u32[]{:S(2)}) copy-start(bf16[3,1024,256]{2,1,0:T(8,128)(2,1)} %param.19) | copy-start | bytes 4718596
  7.2 69.2 %all-gather.6.cloned.1.call-start = ((), (), s32[]{:S(2)}) async-start(), calls=%async_computation.1 | async-start | bytes 3932160 | tf_op jit(solution)/shard_map/all_gather | solution.py:108
  9.5 109.5 %all-gather.10.cloned.1.call-start = ((), (), s32[]{:S(2)}) async-start(), calls=%async_computation.4 | async-start | bytes 1310720 | tf_op jit(solution)/shard_map/all_gather | solution.py:125
  9.6 37.1 %collective-permute-start.4 = (bf16[256,1024]{1,0:T(8,128)(2,1)}, bf16[256,1024]{1,0:T(8,128)(2,1)}, u32[]{:S(2)}, u32[]{:S(2)}) collective-permute-start(bf16[256,1024]{1,0:T(8,128)(2,1)} %param.17), channel_id=1, source_target_pairs={{0,2},{1,3},{2,0},{3,1},{4,6},{5,7},{6,4},{7,5},{8,10},{9,11},{10,... | collective-permute-start | bytes 1572872 | tf_op jit(solution)/shard_map/ppermute | solution.py:66
  12.6 40.7 %collective-permute-start.3 = (bf16[256,1024]{1,0:T(8,128)(2,1)}, bf16[256,1024]{1,0:T(8,128)(2,1)}, u32[]{:S(2)}, u32[]{:S(2)}) collective-permute-start(bf16[256,1024]{1,0:T(8,128)(2,1)} %param.17), channel_id=1, source_target_pairs={{0,1},{1,0},{2,3},{3,2},{4,5},{5,4},{6,7},{7,6},{8,9},{9,8},{10,11... | collective-permute-start | bytes 1572872 | tf_op jit(solution)/shard_map/ppermute | solution.py:65
  13.8 33.1 %collective-permute-start = (bf16[256,1024]{1,0:T(8,128)(2,1)S(1)}, bf16[256,1024]{1,0:T(8,128)(2,1)}, u32[]{:S(2)}, u32[]{:S(2)}) collective-permute-start(bf16[256,1024]{1,0:T(8,128)(2,1)S(1)} %bitcast.125), channel_id=1, source_target_pairs={{0,3},{1,0},{2,1},{3,2},{4,7},{5,4},{6,5},{7,6},{8,11},{9,8},{10,9... | collective-permute-start | bytes 1572872 | tf_op jit(solution)/shard_map/ppermute | solution.py:33
  14.1 34.7 %collective-permute-start.1 = (bf16[256,1024]{1,0:T(8,128)(2,1)S(1)}, bf16[256,1024]{1,0:T(8,128)(2,1)S(1)}, u32[]{:S(2)}, u32[]{:S(2)}) collective-permute-start(bf16[256,1024]{1,0:T(8,128)(2,1)S(1)} %bitcast.126), channel_id=1, source_target_pairs={{0,2},{1,3},{2,0},{3,1},{4,6},{5,7},{6,4},{7,5},{8,10},{9,11},{10,... | collective-permute-start | bytes 1572872 | tf_op jit(solution)/shard_map/ppermute | solution.py:33
  16.0 33.6 %collective-permute-start.2 = (bf16[256,1024]{1,0:T(8,128)(2,1)S(1)}, bf16[256,1024]{1,0:T(8,128)(2,1)S(1)}, u32[]{:S(2)}, u32[]{:S(2)}) collective-permute-start(bf16[256,1024]{1,0:T(8,128)(2,1)S(1)} %bitcast.127), channel_id=1, source_target_pairs={{0,1},{1,2},{2,3},{3,0},{4,5},{5,6},{6,7},{7,4},{8,9},{9,10},{10,1... | collective-permute-start | bytes 1572872 | tf_op jit(solution)/shard_map/ppermute | solution.py:33
  46.7 6.6 %copy-start.7 = (bf16[256,1024]{1,0:T(8,128)(2,1)S(1)}, bf16[256,1024]{1,0:T(8,128)(2,1)}, u32[]{:S(2)}) copy-start(bf16[256,1024]{1,0:T(8,128)(2,1)} %param.17) | copy-start | bytes 1572868
  46.7 6.6 %collective-permute-start.5 = (bf16[256,1024]{1,0:T(8,128)(2,1)}, bf16[256,1024]{1,0:T(8,128)(2,1)S(1)}, u32[]{:S(2)}, u32[]{:S(2)}) collective-permute-start(bf16[256,1024]{1,0:T(8,128)(2,1)} %collective-permute-done.4), channel_id=1, source_target_pairs={{0,1},{1,0},{2,3},{3,2},{4,5},{5,4},{6,7},{7,6},{8,9},{9,8},{10,11... | collective-permute-start | bytes 1572872 | tf_op jit(solution)/shard_map/ppermute | solution.py:67
  84.5 2.1 copy-start.2
  88.2 79.3 %all-gather.8.cloned.1.call-start = ((), (), s32[]{:S(2)}) async-start(), calls=%async_computation.2 | async-start | bytes 1966080 | tf_op jit(solution)/shard_map/all_gather | solution.py:144
  100.8 3.4 %copy-start.3 = (f32[2,512,1024]{2,1,0:T(8,128)S(1)}, f32[2,512,1024]{2,1,0:T(8,128)}, u32[]{:S(2)}) copy-start(f32[2,512,1024]{2,1,0:T(8,128)} %copy-done.2) | copy-start | bytes 12582916
  105.1 26.3 %copy-start.9 = (f32[2,1024]{1,0:T(2,128)S(1)}, f32[2,1024]{1,0:T(2,128)}, u32[]{:S(2)}) copy-start(f32[2,1024]{1,0:T(2,128)} %param.18) | copy-start | bytes 24580
  105.1 28.0 %copy-start.8 = (bf16[512,1024]{1,0:T(8,128)(2,1)S(1)}, bf16[512,1024]{1,0:T(8,128)(2,1)}, u32[]{:S(2)}) copy-start(bf16[512,1024]{1,0:T(8,128)(2,1)} %param.15) | copy-start | bytes 3145732
  125.0 6.4 %collective-permute-start.7 = (bf16[256,512]{0,1:T(8,128)(2,1)S(1)}, bf16[256,512]{0,1:T(8,128)(2,1)S(1)}, u32[]{:S(2)}, u32[]{:S(2)}) collective-permute-start(bf16[256,512]{0,1:T(8,128)(2,1)S(1)} %bitcast.142), channel_id=1, source_target_pairs={{0,2},{1,3},{2,0},{3,1},{4,6},{5,7},{6,4},{7,5},{8,10},{9,11},{10,... | collective-permute-start | bytes 786440 | tf_op jit(solution)/shard_map/ppermute | solution.py:66
  126.6 5.1 %collective-permute-start.6 = (bf16[256,512]{0,1:T(8,128)(2,1)S(1)}, bf16[256,512]{0,1:T(8,128)(2,1)}, u32[]{:S(2)}, u32[]{:S(2)}) collective-permute-start(bf16[256,512]{0,1:T(8,128)(2,1)S(1)} %bitcast.143), channel_id=1, source_target_pairs={{0,1},{1,0},{2,3},{3,2},{4,5},{5,4},{6,7},{7,6},{8,9},{9,8},{10,11... | collective-permute-start | bytes 786440 | tf_op jit(solution)/shard_map/ppermute | solution.py:65
  131.4 1.7 collective-permute-start.8
  131.4 88.9 %reduce-scatter.2.cloned.1.call-start = ((), (), s32[]{:S(2)}) async-start(), calls=%async_computation.3 | async-start | bytes 1966080 | tf_op jit(solution)/shard_map/reduce_scatter | solution.py:204
  137.9 10.5 %copy-start.5 = (bf16[1024,1024]{1,0:T(8,128)(2,1)S(1)}, bf16[1024,1024]{1,0:T(8,128)(2,1)}, u32[]{:S(2)}) copy-start(bf16[1024,1024]{1,0:T(8,128)(2,1)} %bitcast_select_fusion) | copy-start | bytes 6291460
  138.5 12.7 %copy-start.6 = (bf16[2,1024,256]{2,1,0:T(8,128)(2,1)S(1)}, bf16[2,1024,256]{2,1,0:T(8,128)(2,1)}, u32[]{:S(2)}) copy-start(bf16[2,1024,256]{2,1,0:T(8,128)(2,1)} %param.21) | copy-start | bytes 3145732
  138.5 8.4 %collective-permute-start.10 = (bf16[256,512]{1,0:T(8,128)(2,1)S(1)}, bf16[256,512]{1,0:T(8,128)(2,1)S(1)}, u32[]{:S(2)}, u32[]{:S(2)}) collective-permute-start(bf16[256,512]{1,0:T(8,128)(2,1)S(1)} %bitcast.158), channel_id=1, source_target_pairs={{0,2},{1,3},{2,0},{3,1},{4,6},{5,7},{6,4},{7,5},{8,10},{9,11},{10,... | collective-permute-start | bytes 786440 | tf_op jit(solution)/shard_map/ppermute | solution.py:66
  140.2 6.8 %collective-permute-start.9 = (bf16[256,512]{1,0:T(8,128)(2,1)S(1)}, bf16[256,512]{1,0:T(8,128)(2,1)S(1)}, u32[]{:S(2)}, u32[]{:S(2)}) collective-permute-start(bf16[256,512]{1,0:T(8,128)(2,1)S(1)} %bitcast.159), channel_id=1, source_target_pairs={{0,1},{1,0},{2,3},{3,2},{4,5},{5,4},{6,7},{7,6},{8,9},{9,8},{10,11... | collective-permute-start | bytes 786440 | tf_op jit(solution)/shard_map/ppermute | solution.py:65
  146.9 1.5 collective-permute-start.11
  149.8 1.4 copy-start.4
  172.5 0.9 copy-start.11
  173.4 1.1 copy-start.10
  173.4 1.1 copy-start.12
  174.4 1.2 collective-permute-start.12
  175.6 3.6 %collective-permute-start.13 = (f32[1024]{0:T(1024)S(1)}, f32[1024]{0:T(1024)S(1)}, u32[]{:S(2)}, u32[]{:S(2)}) collective-permute-start(f32[1024]{0:T(1024)S(1)} %add.75), channel_id=1, source_target_pairs={{0,2},{1,3},{2,0},{3,1},{4,6},{5,7},{6,4},{7,5},{8,10},{9,11},{10,... | collective-permute-start | bytes 12296 | tf_op jit(solution)/shard_map/ppermute | solution.py:61
  179.8 2.4 %slice-start = ((s8[6291456]{0:T(1024)(128)(4,1)}), s8[4194304]{0:T(1024)(128)(4,1)S(1)}, s32[]{:S(2)}) async-start(s8[6291456]{0:T(1024)(128)(4,1)} %bitcast.122), calls=%async_computation.5 | async-start | bytes 8388608
  180.8 2.1 slice-start.1
  182.9 39.4 %copy-start.1 = (bf16[3,1024,256]{2,1,0:T(8,128)(2,1)S(1)}, bf16[3,1024,256]{2,1,0:T(8,128)(2,1)}, u32[]{:S(2)}) copy-start(bf16[3,1024,256]{2,1,0:T(8,128)(2,1)} %param.19) | copy-start | bytes 4718596
Sparse Core Ops, SparseCore 0:
  10.2 66.2 all-gather.5
  88.3 27.0 all-gather.9
  131.6 35.8 all-gather.7
  186.2 34.1 reduce-scatter.1

commit v10 on v9

--- a/solution.py
+++ b/solution.py
@@ -108,7 +108,10 @@
     piece = lax.all_gather(
         kv_weight.reshape(kv_weight.shape[0], 2 * local), "picks", axis=0, tiled=True
     )
-    cross_full, piece = lax.optimization_barrier((cross_full, piece))
+    out_full = ring_gather(self_out.T, "heads", n_heads).T
+    if paired:
+        out_full = xor_blocks(out_full, lax.axis_index("heads"), n_heads)
+    out_full, cross_full, piece = lax.optimization_barrier((out_full, cross_full, piece))
     keys_vals = jnp.dot(
         enc, piece.reshape(piece.shape[0], 2 * local), preferred_element_type=jnp.float32
     ).astype(jnp.bfloat16)
@@ -136,10 +139,6 @@
         .reshape(lat_rows, local)
         .astype(jnp.bfloat16)
     )
-    out_full = ring_gather(self_out.T, "heads", n_heads).T
-    if paired:
-        out_full = xor_blocks(out_full, lax.axis_index("heads"), n_heads)
-    out_full, attended = lax.optimization_barrier((out_full, attended))
     dq_local, attended = lax.optimization_barrier((dec_query, attended))
     dq_full = lax.all_gather(dq_local, "picks", axis=0, tiled=True)
     head_gather = pair_gather if paired else ring_gather
@@ -165,6 +164,7 @@
         .reshape(lat_rows, local)
     )
     every_head = head_gather(head_out.T, "heads", n_heads).T
+    dq_full, every_head = lax.optimization_barrier((dq_full, every_head))
     out_whole = whole + jnp.dot(every_head, out_full, preferred_element_type=jnp.float32)
     latents_out = lax.dynamic_slice_in_dim(out_whole, column, local, 1)
     power_two = jnp.mean(out_whole * out_whole, axis=1, keepdims=True)

time: 230 us -> 231 us (level)
    all_gather x1, waiting for transfers between devices: 20.5 us -> 2.53 us  [on_device(): lax.all_gather(kv_weight.reshape(kv_weight.shape[0], 2 * local), 'picks',...]
    all_gather x1, waiting for transfers between devices: 0.02 us -> 10.1 us  [on_device(): lax.all_gather(numer.astype(jnp.bfloat16), 'picks', axis=0, tiled=False)]
    all_gather x1, waiting for transfers between devices: 15.3 us -> 20.1 us  [on_device(): dq_full = lax.all_gather(dq_local, 'picks', axis=0, tiled=True)]
    ppermute x3, waiting for transfers between devices: 11.6 us -> 15.9 us  [pair_gather(): far = lax.ppermute(x, axis, [(k, k ^ 2) for k in range(n)])]
    unnamed x41 -> x43, local copies, waits for them, and re-layouts: 16.8 us -> 14.4 us
  transfers between devices with their start and end apart: 18 -> 18, of which waited for: 9 -> 11; matrix products, arithmetic and copies ran while one was open for 30% -> 29% of each run, Pallas kernels for 0% -> 0%
where the time goes in v10:
time: 231 us
  waiting for transfers between devices  87.2 us (38%)
  other arithmetic  40.6 us (18%)
  matrix products  34 us (15%)
  local copies, waits for them, and re-layouts  31.4 us (14%)
  between operations  14.2 us (6%)
  blocking collectives  13.4 us (6%)
  starting transfers between devices  9.9 us (4%)
    reduce_scatter x1, waiting for transfers between devices, on_device(): lax.psum_scatter(jnp.dot(enc.T, dquery, preferred_element_type=jnp.float3...  32.4 us
    another operation x1, other arithmetic  23.6 us
    all_gather x1, waiting for transfers between devices, on_device(): dq_full = lax.all_gather(dq_local, 'picks', axis=0, tiled=True)  20.1 us
    ppermute x3, waiting for transfers between devices, pair_gather(): far = lax.ppermute(x, axis, [(k, k ^ 2) for k in range(n)])  15.9 us
    unnamed x43, local copies, waits for them, and re-layouts  14.4 us
    all_gather x1, blocking collectives, on_device(): lax.all_gather(jnp.stack([top, total]), 'picks', axis=0, tiled=False)  13.4 us
    all_gather x1, waiting for transfers between devices, on_device(): lax.all_gather(numer.astype(jnp.bfloat16), 'picks', axis=0, tiled=False)  10.1 us
    dot_general x1, matrix products, on_device(): jnp.dot(enc, piece.reshape(piece.shape[0], 2 * local), preferred_element_...  7.14 us
  transfers between devices with their start and end apart: 18, of which 11 were waited for; matrix products, arithmetic and copies ran while one was open for 29% of the time, Pallas kernels for 0%

profile of v10, /device:TPU:0, one launch (start us, length us, event | category | flops | bytes accessed | tf_op | source)
XLA Modules:
  0.0 230.6 jit_solution(1807867012338493544)
XLA Ops:
  7.2 2.3 copy.99
  9.6 1.2 copy.62
  10.8 2.4 %collective-permute-start = (bf16[256,1024]{1,0:T(8,128)(2,1)S(1)}, bf16[256,1024]{1,0:T(8,128)(2,1)S(1)}, u32[]{:S(2)}, u32[]{:S(2)}) collective-permute-start(bf16[256,1024]{1,0:T(8,128)(2,1)S(1)} %bitcast.128), channel_id=1, source_target_pairs={{0,3},{1,0},{2,1},{3,2},{4,7},{5,4},{6,5},{7,6},{8,11},{9,8},{10,9... | collective-permute-start | bytes 1572872 | tf_op jit(solution)/shard_map/ppermute | solution.py:33
  14.1 1.3 collective-permute-start.4
  15.9 23.6 %fusion = (bf16[3,512,1024]{2,1,0:T(8,128)(2,1)S(1)}, bf16[3,512,1024]{2,1,0:T(8,128)(2,1)S(1)}) fusion(f32[3,1024]{1,0:T(4,128)} %param.12, f32[512]{0:T(512)S(1)} %maximum_multiply_fusion), kind=kLoop, calls=%fused_computation.3 | loop fusion | flops 4718592 | bytes 6305792 | tf_op jit(solution)/shard_map/convert
  39.4 3.2 %pad_maximum_fusion = bf16[6,512,1024]{2,1,0:T(8,128)(2,1)} fusion(bf16[3,512,1024]{2,1,0:T(8,128)(2,1)S(1)} %get-tuple-element.29, bf16[3,512,1024]{2,1,0:T(8,128)(2,1)S(1)} %get-tuple-element.28), kind=kLoop, calls=%fused_computation.5 | loop fusion | flops 3145728 | bytes 12582912 | tf_op jit(solution)/shard_map/concatenate | solution.py:21
  43.5 1.7 constant_dynamic-slice_fusion.2
  45.3 1.1 copy.96
  46.4 2.6 %collective-permute-done.4 = bf16[256,1024]{1,0:T(8,128)(2,1)} collective-permute-done((bf16[256,1024]{1,0:T(8,128)(2,1)}, bf16[256,1024]{1,0:T(8,128)(2,1)}, u32[]{:S(2)}, u32[]{:S(2)}) %collective-permute-start.4) | collective-permute-done | bytes 524320 | tf_op jit(solution)/shard_map/ppermute | solution.py:66
  49.0 0.9 bitcast_dynamic-update-slice_fusion.6
  49.9 0.9 bitcast_dynamic-update-slice_fusion.4
  50.7 1.9 bitcast_dynamic-update-slice_fusion.2
  55.2 1.9 bitcast_dynamic-update-slice_fusion.3
  57.1 3.1 %constant_dynamic-slice_fusion.1 = bf16[4,256,1024]{2,1,0:T(8,128)(2,1)} fusion(bf16[8,256,1024]{2,1,0:T(8,128)(2,1)} %bitcast_dynamic-update-slice_fusion.3, s32[]{:T(128)S(6)} %select_n.41), kind=kLoop, calls=%fused_computation.100 | loop fusion | bytes 4194308 | tf_op jit(solution)/shard_map/jit(_roll_dynamic)/dynamic_slice | solution.py:35
  60.1 4.0 %copy.63 = bf16[1024,1024]{1,0:T(8,128)(2,1)} copy(bf16[1024,1024]{0,1:T(8,128)(2,1)} %bitcast.121) | data formatting | bytes 4194304 | tf_op jit(solution)/shard_map/transpose | solution.py:111
  64.1 3.6 %gather_fusion = bf16[4,256,1024]{2,1,0:T(8,128)(2,1)} fusion(bf16[4,256,1024]{2,1,0:T(8,128)(2,1)} %bitcast.122, s32[1024]{0:T(1024)S(1)} %pad_clamp_fusion), kind=kCustom, calls=%fused_computation | custom fusion | bytes 4194320 | tf_op jit(solution)/shard_map/jit(_take)/gather | solution.py:73
  67.8 3.3 %bitcast_select_fusion = bf16[1024,1024]{1,0:T(8,128)(2,1)} fusion(bf16[4,256,1024]{2,1,0:T(8,128)(2,1)} %gather_fusion, pred[1024]{0:T(1024)(128)(4,1)S(1)} %broadcast_in_dim.17), kind=kLoop, calls=%fused_computation.22 | loop fusion | flops 1048576 | bytes 4195328 | tf_op jit(solution)/shard_map/jit(_take)/select_n | solution.py:73
  71.0 2.8 %pad_maximum_fusion.1 = bf16[1024,1024]{1,0:T(8,128)(2,1)} fusion(bf16[256,1024]{1,0:T(8,128)(2,1)} %collective-permute-done.5, bf16[256,1024]{1,0:T(8,128)(2,1)} %collective-permute-done.4, bf16[256,1024]{1,0:T(8,128)(2,1)} %collective-permute-done.3, bf16[256,1024]{1,0:T(8,128)(2,1)S(1)} %copy-done.6), kind=kLoop, calls=%fused_computation.21 | loop fusion | flops 8388608 | bytes 4194304 | tf_op jit(solution)/shard_map/concatenate | solution.py:68
  73.9 2.5 %all-gather.6.cloned.1.call-done = bf16[3072,512]{1,0:T(8,128)(2,1)} async-done(((bf16[768,512]{1,0:T(8,128)(2,1)}), bf16[3072,512]{1,0:T(8,128)(2,1)}) %all-gather.6.cloned.1.call-update) | async-done | bytes 3145744 | tf_op jit(solution)/shard_map/all_gather | solution.py:108
  76.4 7.1 %convolution_convert_fusion.1 = bf16[1024,512]{0,1:T(8,128)(2,1)S(1)} fusion(bf16[3072,1024]{1,0:T(8,128)(2,1)} %bitcast.123, bf16[3072,512]{1,0:T(8,128)(2,1)} %all-gather.6.cloned.1.call-done), kind=kOutput, calls=%fused_computation.39 | convolution fusion | flops 3221749760 | bytes 10485760 | tf_op jit(solution)/shard_map/dot_general | solution.py:115
  84.5 2.0 copy-done.2
  86.5 1.6 fusion.35
  88.4 3.1 %fusion.7 = f32[2,512]{1,0:T(2,128)S(1)} fusion(f32[2,512,1024]{2,1,0:T(8,128)} %copy-done.2, f32[2,512]{1,0:T(2,128)S(1)} %get-tuple-element.32), kind=kLoop, calls=%fused_computation.17 | loop fusion | flops 3144704 | bytes 4202496 | tf_op jit(solution)/shard_map/reduce_sum | solution.py:124
  91.5 13.4 %all-gather.1 = f32[8,2,512]{2,1,0:T(2,128)S(1)} all-gather(f32[2,2,512]{2,1,0:T(2,128)S(1)} %pad_maximum_fusion.2), channel_id=3, replica_groups=mesh['groups'=2,'picks'=4,'heads'=4] {'picks'}, dimensions={0}, use_global_device_ids=true | all-gather | bytes 40960 | tf_op jit(solution)/shard_map/all_gather | solution.py:129
  105.5 10.1 %all-gather.10.cloned.1.call-done = bf16[8,512,128]{2,1,0:T(8,128)(2,1)} async-done(((bf16[2,512,128]{2,1,0:T(8,128)(2,1)}), bf16[8,512,128]{2,1,0:T(8,128)(2,1)}) %all-gather.10.cloned.1.call-update) | async-done | bytes 1048592 | tf_op jit(solution)/shard_map/all_gather | solution.py:128
  115.6 5.1 %fusion.53 = f32[512,2,1,128]{3,2,1,0:T(1,128)S(1)} fusion(f32[4,2,512,1]{0,3,1,2:T(1,128)S(1)} %copy.83, bf16[4,2,512,128]{3,2,1,0:T(8,128)(2,1)} %bitcast.163), kind=kOutput, calls=%fused_computation.65 | convolution fusion | flops 6291456 | bytes 1589248 | tf_op jit(solution)/shard_map/phl,phlc->hlc/dot_general | solution.py:133
  121.5 1.5 collective-permute-start.7
  123.0 6.4 %collective-permute-done.7 = bf16[256,512]{0,1:T(8,128)(2,1)S(1)} collective-permute-done((bf16[256,512]{0,1:T(8,128)(2,1)S(1)}, bf16[256,512]{0,1:T(8,128)(2,1)S(1)}, u32[]{:S(2)}, u32[]{:S(2)}) %collective-permute-start.7) | collective-permute-done | bytes 262176 | tf_op jit(solution)/shard_map/ppermute | solution.py:66
  129.5 1.6 collective-permute-done.8
  131.1 3.1 %multiply_reduce_fusion.2 = (f32[512]{0:T(512)S(1)}, f32[512,1024]{1,0:T(8,128)S(1)}) fusion(bf16[1024,1024]{1,0:T(8,128)(2,1)} %pad_maximum_fusion.1, bf16[256,512]{0,1:T(8,128)(2,1)} %collective-permute-done.8, bf16[256,512]{0,1:T(8,128)(2,1)S(1)} %collective-permute-done.7, bf16[256,512]{0,1:T(8,128)(2,1)} %collective-permute-done.6, ...), kind=kOutput, calls=%fused_computation.33 | convolution fusion | flops 1080032768 | bytes 6293504 | tf_op jit(solution)/shard_map/dot_general | solution.py:146
  134.3 1.1 fusion.30
  136.6 1.5 collective-permute-start.10
  138.1 6.9 %collective-permute-done.10 = bf16[256,512]{1,0:T(8,128)(2,1)S(1)} collective-permute-done((bf16[256,512]{1,0:T(8,128)(2,1)S(1)}, bf16[256,512]{1,0:T(8,128)(2,1)S(1)}, u32[]{:S(2)}, u32[]{:S(2)}) %collective-permute-start.10) | collective-permute-done | bytes 262176 | tf_op jit(solution)/shard_map/ppermute | solution.py:66
  145.0 1.5 collective-permute-done.11
  146.6 20.1 %all-gather.8.cloned.1.call-done = bf16[3072,256]{1,0:T(8,128)(2,1)} async-done(((bf16[768,256]{1,0:T(8,128)(2,1)}), bf16[3072,256]{1,0:T(8,128)(2,1)}) %all-gather.8.cloned.1.call-update) | async-done | bytes 1572880 | tf_op jit(solution)/shard_map/all_gather | solution.py:143
  166.7 5.2 %convolution_convert_fusion.3 = bf16[1024,256]{0,1:T(8,128)(2,1)S(1)} fusion(bf16[3072,1024]{1,0:T(8,128)(2,1)} %bitcast.124, bf16[3072,256]{1,0:T(8,128)(2,1)} %all-gather.8.cloned.1.call-done), kind=kOutput, calls=%fused_computation.43 | convolution fusion | flops 1610874880 | bytes 8388608 | tf_op jit(solution)/shard_map/dot_general | solution.py:179
  171.9 1.4 multiply_reduce_fusion.1
  173.3 0.9 fusion.34
  175.1 1.0 fusion.31
  176.3 1.0 collective-permute-done.12
  177.3 1.5 collective-permute-start.13
  179.0 1.9 collective-permute-done.13
  181.5 1.0 fusion.2
  182.6 1.4 fusion.27
  184.6 3.1 %convolution_convert_fusion = bf16[3072,256]{1,0:T(8,128)(2,1)} fusion(bf16[3072,1024]{1,0:T(8,128)(2,1)S(1)} %bitcast.127, bf16[1024,256]{0,1:T(8,128)(2,1)S(1)} %bitcast.164), kind=kOutput, calls=%fused_computation.14 | convolution fusion | flops 1611399168 | bytes 8388608 | tf_op jit(solution)/shard_map/dot_general | solution.py:205
  187.8 1.9 constant_dynamic-slice_fusion
  189.7 32.4 %reduce-scatter.2.cloned.1.call-done = bf16[768,256]{1,0:T(8,128)(2,1)} async-done(((bf16[3072,256]{1,0:T(8,128)(2,1)}), bf16[768,256]{1,0:T(8,128)(2,1)}) %reduce-scatter.2.cloned.1.call-update) | async-done | bytes 393232 | tf_op jit(solution)/shard_map/reduce_scatter | solution.py:204
  222.1 1.9 convert_element_type.100
  (90 shorter events, 11.3 us)
Async XLA Ops:
  7.2 127.1 %copy-start = (bf16[3,1024,256]{2,1,0:T(8,128)(2,1)S(1)}, bf16[3,1024,256]{2,1,0:T(8,128)(2,1)}, u32[]{:S(2)}) copy-start(bf16[3,1024,256]{2,1,0:T(8,128)(2,1)} %param.19) | copy-start | bytes 4718596
  7.2 69.2 %all-gather.6.cloned.1.call-start = ((), (), s32[]{:S(2)}) async-start(), calls=%async_computation.1 | async-start | bytes 3932160 | tf_op jit(solution)/shard_map/all_gather | solution.py:108
  9.5 106.1 %all-gather.10.cloned.1.call-start = ((), (), s32[]{:S(2)}) async-start(), calls=%async_computation.4 | async-start | bytes 1310720 | tf_op jit(solution)/shard_map/all_gather | solution.py:128
  10.8 38.2 %collective-permute-start = (bf16[256,1024]{1,0:T(8,128)(2,1)S(1)}, bf16[256,1024]{1,0:T(8,128)(2,1)S(1)}, u32[]{:S(2)}, u32[]{:S(2)}) collective-permute-start(bf16[256,1024]{1,0:T(8,128)(2,1)S(1)} %bitcast.128), channel_id=1, source_target_pairs={{0,3},{1,0},{2,1},{3,2},{4,7},{5,4},{6,5},{7,6},{8,11},{9,8},{10,9... | collective-permute-start | bytes 1572872 | tf_op jit(solution)/shard_map/ppermute | solution.py:33
  13.3 36.6 %collective-permute-start.1 = (bf16[256,1024]{1,0:T(8,128)(2,1)S(1)}, bf16[256,1024]{1,0:T(8,128)(2,1)S(1)}, u32[]{:S(2)}, u32[]{:S(2)}) collective-permute-start(bf16[256,1024]{1,0:T(8,128)(2,1)S(1)} %bitcast.129), channel_id=1, source_target_pairs={{0,2},{1,3},{2,0},{3,1},{4,6},{5,7},{6,4},{7,5},{8,10},{9,11},{10,... | collective-permute-start | bytes 1572872 | tf_op jit(solution)/shard_map/ppermute | solution.py:33
  13.9 36.8 %collective-permute-start.2 = (bf16[256,1024]{1,0:T(8,128)(2,1)S(1)}, bf16[256,1024]{1,0:T(8,128)(2,1)}, u32[]{:S(2)}, u32[]{:S(2)}) collective-permute-start(bf16[256,1024]{1,0:T(8,128)(2,1)S(1)} %bitcast.130), channel_id=1, source_target_pairs={{0,1},{1,2},{2,3},{3,0},{4,5},{5,6},{6,7},{7,4},{8,9},{9,10},{10,1... | collective-permute-start | bytes 1572872 | tf_op jit(solution)/shard_map/ppermute | solution.py:33
  14.1 34.9 %collective-permute-start.4 = (bf16[256,1024]{1,0:T(8,128)(2,1)}, bf16[256,1024]{1,0:T(8,128)(2,1)}, u32[]{:S(2)}, u32[]{:S(2)}) collective-permute-start(bf16[256,1024]{1,0:T(8,128)(2,1)} %param.17), channel_id=1, source_target_pairs={{0,2},{1,3},{2,0},{3,1},{4,6},{5,7},{6,4},{7,5},{8,10},{9,11},{10,... | collective-permute-start | bytes 1572872 | tf_op jit(solution)/shard_map/ppermute | solution.py:66
  15.3 55.7 %collective-permute-start.3 = (bf16[256,1024]{1,0:T(8,128)(2,1)}, bf16[256,1024]{1,0:T(8,128)(2,1)}, u32[]{:S(2)}, u32[]{:S(2)}) collective-permute-start(bf16[256,1024]{1,0:T(8,128)(2,1)} %param.17), channel_id=1, source_target_pairs={{0,1},{1,0},{2,3},{3,2},{4,5},{5,4},{6,7},{7,6},{8,9},{9,8},{10,11... | collective-permute-start | bytes 1572872 | tf_op jit(solution)/shard_map/ppermute | solution.py:65
  49.0 22.0 %collective-permute-start.5 = (bf16[256,1024]{1,0:T(8,128)(2,1)}, bf16[256,1024]{1,0:T(8,128)(2,1)}, u32[]{:S(2)}, u32[]{:S(2)}) collective-permute-start(bf16[256,1024]{1,0:T(8,128)(2,1)} %collective-permute-done.4), channel_id=1, source_target_pairs={{0,1},{1,0},{2,3},{3,2},{4,5},{5,4},{6,7},{7,6},{8,9},{9,8},{10,11... | collective-permute-start | bytes 1572872 | tf_op jit(solution)/shard_map/ppermute | solution.py:67
  64.1 6.9 %copy-start.6 = (bf16[256,1024]{1,0:T(8,128)(2,1)S(1)}, bf16[256,1024]{1,0:T(8,128)(2,1)}, u32[]{:S(2)}) copy-start(bf16[256,1024]{1,0:T(8,128)(2,1)} %param.17) | copy-start | bytes 1572868
  84.5 2.0 copy-start.2
  88.2 78.5 %all-gather.8.cloned.1.call-start = ((), (), s32[]{:S(2)}) async-start(), calls=%async_computation.2 | async-start | bytes 1966080 | tf_op jit(solution)/shard_map/all_gather | solution.py:143
  91.5 38.0 %copy-start.8 = (f32[2,1024]{1,0:T(2,128)S(1)}, f32[2,1024]{1,0:T(2,128)}, u32[]{:S(2)}) copy-start(f32[2,1024]{1,0:T(2,128)} %param.18) | copy-start | bytes 24580
  91.5 39.6 %copy-start.7 = (bf16[512,1024]{1,0:T(8,128)(2,1)S(1)}, bf16[512,1024]{1,0:T(8,128)(2,1)}, u32[]{:S(2)}) copy-start(bf16[512,1024]{1,0:T(8,128)(2,1)} %param.15) | copy-start | bytes 3145732
  121.5 7.9 %collective-permute-start.7 = (bf16[256,512]{0,1:T(8,128)(2,1)S(1)}, bf16[256,512]{0,1:T(8,128)(2,1)S(1)}, u32[]{:S(2)}, u32[]{:S(2)}) collective-permute-start(bf16[256,512]{0,1:T(8,128)(2,1)S(1)} %bitcast.145), channel_id=1, source_target_pairs={{0,2},{1,3},{2,0},{3,1},{4,6},{5,7},{6,4},{7,5},{8,10},{9,11},{10,... | collective-permute-start | bytes 786440 | tf_op jit(solution)/shard_map/ppermute | solution.py:66
  123.0 6.5 %collective-permute-start.6 = (bf16[256,512]{0,1:T(8,128)(2,1)S(1)}, bf16[256,512]{0,1:T(8,128)(2,1)}, u32[]{:S(2)}, u32[]{:S(2)}) collective-permute-start(bf16[256,512]{0,1:T(8,128)(2,1)S(1)} %bitcast.146), channel_id=1, source_target_pairs={{0,1},{1,0},{2,3},{3,2},{4,5},{5,4},{6,7},{7,6},{8,9},{9,8},{10,11... | collective-permute-start | bytes 786440 | tf_op jit(solution)/shard_map/ppermute | solution.py:65
  129.4 1.7 collective-permute-start.8
  129.5 92.6 %reduce-scatter.2.cloned.1.call-start = ((), (), s32[]{:S(2)}) async-start(), calls=%async_computation.3 | async-start | bytes 1966080 | tf_op jit(solution)/shard_map/reduce_scatter | solution.py:204
  134.3 1.8 copy-start.12
  136.6 8.4 %collective-permute-start.10 = (bf16[256,512]{1,0:T(8,128)(2,1)S(1)}, bf16[256,512]{1,0:T(8,128)(2,1)S(1)}, u32[]{:S(2)}, u32[]{:S(2)}) collective-permute-start(bf16[256,512]{1,0:T(8,128)(2,1)S(1)} %bitcast.149), channel_id=1, source_target_pairs={{0,2},{1,3},{2,0},{3,1},{4,6},{5,7},{6,4},{7,5},{8,10},{9,11},{10,... | collective-permute-start | bytes 786440 | tf_op jit(solution)/shard_map/ppermute | solution.py:66
  138.1 6.9 %collective-permute-start.9 = (bf16[256,512]{1,0:T(8,128)(2,1)S(1)}, bf16[256,512]{1,0:T(8,128)(2,1)S(1)}, u32[]{:S(2)}, u32[]{:S(2)}) collective-permute-start(bf16[256,512]{1,0:T(8,128)(2,1)S(1)} %bitcast.150), channel_id=1, source_target_pairs={{0,1},{1,0},{2,3},{3,2},{4,5},{5,4},{6,7},{7,6},{8,9},{9,8},{10,11... | collective-permute-start | bytes 786440 | tf_op jit(solution)/shard_map/ppermute | solution.py:65
  145.0 1.5 collective-permute-start.11
  166.7 5.2 %copy-start.4 = (bf16[1024,1024]{1,0:T(8,128)(2,1)S(1)}, bf16[1024,1024]{1,0:T(8,128)(2,1)}, u32[]{:S(2)}) copy-start(bf16[1024,1024]{1,0:T(8,128)(2,1)} %bitcast_select_fusion) | copy-start | bytes 6291460
  166.7 5.2 %copy-start.13 = (f32[512,1024]{1,0:T(8,128)S(1)}, f32[512,1024]{1,0:T(8,128)}, u32[]{:S(2)}) copy-start(f32[512,1024]{1,0:T(8,128)} %copy-done.12) | copy-start | bytes 6291460
  171.9 1.4 copy-start.5
  173.3 1.8 copy-start.3
  173.3 1.8 copy-start.10
  175.1 1.1 copy-start.9
  175.1 1.1 copy-start.11
  176.1 1.2 collective-permute-start.12
  177.3 3.6 %collective-permute-start.13 = (f32[1024]{0:T(1024)S(1)}, f32[1024]{0:T(1024)S(1)}, u32[]{:S(2)}, u32[]{:S(2)}) collective-permute-start(f32[1024]{0:T(1024)S(1)} %add.75), channel_id=1, source_target_pairs={{0,2},{1,3},{2,0},{3,1},{4,6},{5,7},{6,4},{7,5},{8,10},{9,11},{10,... | collective-permute-start | bytes 12296 | tf_op jit(solution)/shard_map/ppermute | solution.py:61
  181.5 2.4 %slice-start = ((s8[6291456]{0:T(1024)(128)(4,1)}), s8[4194304]{0:T(1024)(128)(4,1)S(1)}, s32[]{:S(2)}) async-start(s8[6291456]{0:T(1024)(128)(4,1)} %bitcast.125), calls=%async_computation.5 | async-start | bytes 8388608
  182.6 2.1 slice-start.1
  184.6 39.4 %copy-start.1 = (bf16[3,1024,256]{2,1,0:T(8,128)(2,1)S(1)}, bf16[3,1024,256]{2,1,0:T(8,128)(2,1)}, u32[]{:S(2)}) copy-start(bf16[3,1024,256]{2,1,0:T(8,128)(2,1)} %param.19) | copy-start | bytes 4718596
Sparse Core Ops, SparseCore 0:
  10.2 66.2 all-gather.5
  88.3 27.2 all-gather.9
  129.6 37.0 all-gather.7
  187.9 34.1 reduce-scatter.1

commit v11 on v6

--- a/solution.py
+++ b/solution.py
@@ -166,22 +166,22 @@
         "htl,lhc->thc", weights.astype(jnp.bfloat16), dec_vals, preferred_element_type=jnp.float32
     )
     read = readout.reshape(nheads, HEAD)
-    field = pair_sum(jnp.sum(out * read[None, :, :], axis=(1, 2)), "heads", n_heads)
     onehot = (horizon_ids[:, None] == jnp.arange(HORIZONS, dtype=jnp.int32)[None, :]).astype(
         jnp.float32
     )
     target = jnp.sum(onehot * horizon_levels[None, :], axis=1)
+    value_read = jnp.einsum("lhc,hc->hl", dec_vals.astype(jnp.float32), read, precision=high)
+    lever = (
+        weights
+        * (
+            value_read[:, None, :]
+            - jnp.sum(value_read[:, None, :] * weights, axis=2, keepdims=True)
+        )
+    ).astype(jnp.bfloat16)
+    pull = jnp.einsum("htl,lhc->thc", lever, dec_keys, preferred_element_type=jnp.float32) * scale
+    field = pair_sum(jnp.sum(out * read[None, :, :], axis=(1, 2)), "heads", n_heads)
     miss = field - target
-    value_read = jnp.einsum("lhc,hc->hl", dec_vals.astype(jnp.float32), read, precision=high)
-    dprob = miss[None, :, None] * value_read[:, None, :]
-    dscore = (weights * (dprob - jnp.sum(dprob * weights, axis=2, keepdims=True))).astype(
-        jnp.bfloat16
-    )
-    dquery = (
-        (jnp.einsum("htl,lhc->thc", dscore, dec_keys, preferred_element_type=jnp.float32) * scale)
-        .reshape(count, local)
-        .astype(jnp.bfloat16)
-    )
+    dquery = (miss[:, None, None] * pull).reshape(count, local).astype(jnp.bfloat16)
     grad_query = lax.psum_scatter(
         jnp.dot(enc.T, dquery, preferred_element_type=jnp.float32).astype(jnp.bfloat16),
         "picks",

time: 219 us -> 217 us (level)
  transfers between devices with their start and end apart: 18 -> 18, of which waited for: 13 -> 13; matrix products, arithmetic and copies ran while one was open for 27% -> 28% of each run, Pallas kernels for 0% -> 0%
where the time goes in v11:
time: 217 us
  waiting for transfers between devices  96 us (44%)
  other arithmetic  45.9 us (21%)
  matrix products  26.8 us (12%)
  between operations  14.2 us (7%)
  blocking collectives  13.3 us (6%)
  starting transfers between devices  10.9 us (5%)
  local copies, waits for them, and re-layouts  9.7 us (4%)
    ppermute x12, waiting for transfers between devices, ring_gather(): blocks.append(lax.ppermute(x, axis, [(i, (i - s) % n) for i in range(n)]))  38.6 us
    reduce_scatter x1, waiting for transfers between devices, on_device(): lax.psum_scatter(jnp.dot(enc.T, dquery, preferred_element_type=jnp.float3...  32.5 us
    another operation x1, other arithmetic  22.8 us
    all_gather x1, waiting for transfers between devices, on_device(): lax.all_gather(kv_weight.reshape(kv_weight.shape[0], 2 * local), 'picks',...  14.6 us
    concatenate x4, other arithmetic, ring_gather(): ordered = jnp.roll(flipped, idx, axis=0)  13.5 us
    all_gather x1, blocking collectives, on_device(): lax.all_gather(jnp.stack([top, total]), 'picks', axis=0, tiled=False)  13.3 us
    ppermute x12, starting transfers between devices, ring_gather(): blocks.append(lax.ppermute(x, axis, [(i, (i - s) % n) for i in range(n)]))  9.56 us
    all_gather x1, waiting for transfers between devices, on_device(): lax.all_gather(numer.astype(jnp.bfloat16), 'picks', axis=0, tiled=False)  7.49 us
  transfers between devices with their start and end apart: 18, of which 13 were waited for; matrix products, arithmetic and copies ran while one was open for 28% of the time, Pallas kernels for 0%

profile of v11, /device:TPU:0, one launch (start us, length us, event | category | flops | bytes accessed | tf_op | source)
XLA Modules:
  0.0 216.8 jit_solution(5335320379753915424)
XLA Ops:
  7.3 2.3 %copy.95 = bf16[96,8,2,256]{3,1,2,0:T(8,128)(2,1)} copy(bf16[96,8,2,256]{3,2,1,0:T(2,128)(2,1)} %bitcast.145) | data formatting | bytes 1572864
  9.9 2.4 %collective-permute-start = (bf16[256,1024]{1,0:T(8,128)(2,1)S(1)}, bf16[256,1024]{1,0:T(8,128)(2,1)}, u32[]{:S(2)}, u32[]{:S(2)}) collective-permute-start(bf16[256,1024]{1,0:T(8,128)(2,1)S(1)} %bitcast.126), channel_id=1, source_target_pairs={{0,3},{1,0},{2,1},{3,2},{4,7},{5,4},{6,5},{7,6},{8,11},{9,8},{10,9... | collective-permute-start | bytes 1572872 | tf_op jit(solution)/shard_map/ppermute | solution.py:33
  12.3 0.6 collective-permute-start.1
  13.0 1.7 collective-permute-start.4
  14.8 1.0 constant_dynamic-slice_fusion.1
  16.0 22.8 %fusion = (bf16[3,512,1024]{2,1,0:T(8,128)(2,1)S(1)}, bf16[3,512,1024]{2,1,0:T(8,128)(2,1)S(1)}) fusion(f32[3,1024]{1,0:T(4,128)S(1)} %copy-done.10, f32[512]{0:T(512)S(1)} %maximum_multiply_fusion), kind=kLoop, calls=%fused_computation.2 | loop fusion | flops 4718592 | bytes 6305792 | tf_op jit(solution)/shard_map/convert
  38.8 3.2 %pad_maximum_fusion = bf16[6,512,1024]{2,1,0:T(8,128)(2,1)} fusion(bf16[3,512,1024]{2,1,0:T(8,128)(2,1)S(1)} %get-tuple-element.29, bf16[3,512,1024]{2,1,0:T(8,128)(2,1)S(1)} %get-tuple-element.28), kind=kLoop, calls=%fused_computation.4 | loop fusion | flops 3145728 | bytes 12582912 | tf_op jit(solution)/shard_map/concatenate | solution.py:21
  42.0 5.0 %collective-permute-done.3 = bf16[256,1024]{1,0:T(8,128)(2,1)} collective-permute-done((bf16[256,1024]{1,0:T(8,128)(2,1)S(1)}, bf16[256,1024]{1,0:T(8,128)(2,1)}, u32[]{:S(2)}, u32[]{:S(2)}) %collective-permute-start.3) | collective-permute-done | bytes 524320 | tf_op jit(solution)/shard_map/ppermute | solution.py:33
  47.0 1.2 collective-permute-start.2
  48.2 8.7 %collective-permute-done.4 = bf16[256,1024]{1,0:T(8,128)(2,1)} collective-permute-done((bf16[256,1024]{1,0:T(8,128)(2,1)S(1)}, bf16[256,1024]{1,0:T(8,128)(2,1)}, u32[]{:S(2)}, u32[]{:S(2)}) %collective-permute-start.4) | collective-permute-done | bytes 524320 | tf_op jit(solution)/shard_map/ppermute | solution.py:33
  56.8 5.0 %fusion.12 = bf16[4,256,1024]{2,1,0:T(8,128)(2,1)} fusion(s32[]{:T(128)S(6)} %select_n.27, bf16[1,256,1024]{2,1,0:T(8,128)(2,1)S(1)} %bitcast.146, bf16[1,256,1024]{2,1,0:T(8,128)(2,1)} %bitcast.12, bf16[1,256,1024]{2,1,0:T(8,128)(2,1)} %bitcast.13, bf16[1,256,1024]{2,1,0:T(8,128)(2,1)} %bitcast.14), kind=kLoop, calls=%fused_computation.36 | loop fusion | flops 7340032 | bytes 4194308 | tf_op jit(solution)/shard_map/jit(_roll_dynamic)/concatenate | solution.py:35
  61.8 14.6 %all-gather.6.cloned.1.call-done = bf16[3072,512]{1,0:T(8,128)(2,1)} async-done(((bf16[768,512]{1,0:T(8,128)(2,1)}), bf16[3072,512]{1,0:T(8,128)(2,1)}) %all-gather.6.cloned.1.call-update) | async-done | bytes 3145744 | tf_op jit(solution)/shard_map/all_gather | solution.py:92
  76.4 7.1 %convolution_convert_fusion.1 = bf16[1024,512]{0,1:T(8,128)(2,1)S(1)} fusion(bf16[3072,1024]{1,0:T(8,128)(2,1)} %bitcast.119, bf16[3072,512]{1,0:T(8,128)(2,1)} %all-gather.6.cloned.1.call-done), kind=kOutput, calls=%fused_computation.79 | convolution fusion | flops 3221749760 | bytes 10485760 | tf_op jit(solution)/shard_map/dot_general | solution.py:96
  83.7 0.8 multiply_reduce_fusion.1
  84.5 2.1 copy-done.1
  86.6 1.6 fusion.38
  88.5 5.0 %fusion.19 = bf16[4,256,1024]{2,1,0:T(8,128)(2,1)} fusion(s32[]{:T(128)S(6)} %select_n.27, bf16[1,256,1024]{2,1,0:T(8,128)(2,1)S(1)} %bitcast.129, bf16[1,256,1024]{2,1,0:T(8,128)(2,1)} %bitcast.4, bf16[1,256,1024]{2,1,0:T(8,128)(2,1)} %bitcast.5, bf16[1,256,1024]{2,1,0:T(8,128)(2,1)} %bitcast.6), kind=kLoop, calls=%fused_computation.43 | loop fusion | flops 7340032 | bytes 4194308 | tf_op jit(solution)/shard_map/jit(_roll_dynamic)/concatenate | solution.py:35
  93.5 0.9 fusion.4
  94.4 13.3 %all-gather.1 = f32[8,2,512]{2,1,0:T(2,128)S(1)} all-gather(f32[2,2,512]{2,1,0:T(2,128)S(1)} %pad_maximum_fusion.1), channel_id=3, replica_groups=mesh['groups'=2,'picks'=4,'heads'=4] {'picks'}, dimensions={0}, use_global_device_ids=true | all-gather | bytes 40960 | tf_op jit(solution)/shard_map/all_gather | solution.py:110
  107.7 7.5 %all-gather.10.cloned.1.call-done = bf16[8,512,128]{2,1,0:T(8,128)(2,1)} async-done(((bf16[2,512,128]{2,1,0:T(8,128)(2,1)}), bf16[8,512,128]{2,1,0:T(8,128)(2,1)}) %all-gather.10.cloned.1.call-update) | async-done | bytes 1048592 | tf_op jit(solution)/shard_map/all_gather | solution.py:109
  115.2 1.8 multiply_reduce_fusion.2
  117.3 1.0 collective-permute-start.6
  118.2 0.6 collective-permute-start.7
  119.1 5.7 %collective-permute-done.6 = bf16[256,512]{1,0:T(8,128)(2,1)S(1)} collective-permute-done((bf16[256,512]{1,0:T(8,128)(2,1)S(1)}, bf16[256,512]{1,0:T(8,128)(2,1)S(1)}, u32[]{:S(2)}, u32[]{:S(2)}) %collective-permute-start.6) | collective-permute-done | bytes 262176 | tf_op jit(solution)/shard_map/ppermute | solution.py:33
  124.8 6.7 %collective-permute-done.7 = bf16[256,512]{1,0:T(8,128)(2,1)S(1)} collective-permute-done((bf16[256,512]{1,0:T(8,128)(2,1)S(1)}, bf16[256,512]{1,0:T(8,128)(2,1)S(1)}, u32[]{:S(2)}, u32[]{:S(2)}) %collective-permute-start.7) | collective-permute-done | bytes 262176 | tf_op jit(solution)/shard_map/ppermute | solution.py:33
  131.7 2.2 %fusion.55 = bf16[4,256,512]{2,1,0:T(8,128)(2,1)S(1)} fusion(s32[]{:T(128)S(6)} %select_n.27, bf16[1,256,512]{2,1,0:T(8,128)(2,1)S(1)} %bitcast.135, bf16[1,256,512]{2,1,0:T(8,128)(2,1)S(1)} %bitcast.149, bf16[1,256,512]{2,1,0:T(8,128)(2,1)S(1)} %bitcast.150, bf16[1,256,512]{2,1,0:T(8,128)(2,1)} %bitcast.31), kind=kLoop, calls=%fused_computation.101 | loop fusion | flops 3670016 | bytes 2097156 | tf_op jit(solution)/shard_map/jit(_roll_dynamic)/concatenate | solution.py:35
  133.9 1.4 multiply_reduce_fusion.4
  135.3 1.1 fusion.33
  137.7 1.5 collective-permute-start.10
  139.5 3.9 %collective-permute-done.9 = bf16[256,512]{1,0:T(8,128)(2,1)S(1)} collective-permute-done((bf16[256,512]{1,0:T(8,128)(2,1)S(1)}, bf16[256,512]{1,0:T(8,128)(2,1)S(1)}, u32[]{:S(2)}, u32[]{:S(2)}) %collective-permute-start.9) | collective-permute-done | bytes 262176 | tf_op jit(solution)/shard_map/ppermute | solution.py:33
  143.4 8.4 %collective-permute-done.10 = bf16[256,512]{1,0:T(8,128)(2,1)S(1)} collective-permute-done((bf16[256,512]{1,0:T(8,128)(2,1)S(1)}, bf16[256,512]{1,0:T(8,128)(2,1)S(1)}, u32[]{:S(2)}, u32[]{:S(2)}) %collective-permute-start.10) | collective-permute-done | bytes 262176 | tf_op jit(solution)/shard_map/ppermute | solution.py:33
  151.9 1.2 fusion.48
  153.2 1.4 multiply_reduce_fusion.3
  154.6 1.3 copy-done.4
  155.9 0.9 fusion.37
  156.9 5.1 %convolution_convert_fusion.3 = bf16[1024,256]{0,1:T(8,128)(2,1)S(1)} fusion(bf16[3072,1024]{1,0:T(8,128)(2,1)} %bitcast.120, bf16[3072,256]{1,0:T(8,128)(2,1)} %all-gather.8.cloned.1.call-done), kind=kOutput, calls=%fused_computation.82 | convolution fusion | flops 1610874880 | bytes 8388608 | tf_op jit(solution)/shard_map/dot_general | solution.py:160
  161.9 0.8 fusion.3
  162.8 1.0 fusion.34
  164.1 0.9 collective-permute-done.12
  165.0 0.9 collective-permute-start.13
  165.9 0.9 multiply_reduce_fusion
  166.7 1.9 collective-permute-done.13
  168.6 0.6 subtract_multiply_fusion
  169.2 1.2 multiply_convert_fusion.4
  170.8 3.1 %convolution_convert_fusion = bf16[3072,256]{1,0:T(8,128)(2,1)} fusion(bf16[3072,1024]{1,0:T(8,128)(2,1)S(1)} %bitcast.123, bf16[1024,256]{0,1:T(8,128)(2,1)S(1)} %bitcast.170), kind=kOutput, calls=%fused_computation.26 | convolution fusion | flops 1611399168 | bytes 8388608 | tf_op jit(solution)/shard_map/dot_general | solution.py:186
  174.0 1.9 constant_dynamic-slice_fusion
  175.8 32.5 %reduce-scatter.2.cloned.1.call-done = bf16[768,256]{1,0:T(8,128)(2,1)} async-done(((bf16[3072,256]{1,0:T(8,128)(2,1)}), bf16[768,256]{1,0:T(8,128)(2,1)}) %reduce-scatter.2.cloned.1.call-update) | async-done | bytes 393232 | tf_op jit(solution)/shard_map/reduce_scatter | solution.py:185
  208.3 1.9 convert_element_type.100
  (75 shorter events, 4.0 us)
Async XLA Ops:
  7.2 128.1 %copy-start = (bf16[3,1024,256]{2,1,0:T(8,128)(2,1)S(1)}, bf16[3,1024,256]{2,1,0:T(8,128)(2,1)}, u32[]{:S(2)}) copy-start(bf16[3,1024,256]{2,1,0:T(8,128)(2,1)} %param.23) | copy-start | bytes 4718596
  7.2 2.5 %copy-start.9 = (bf16[1024,256]{1,0:T(8,128)(2,1)S(1)}, bf16[1024,256]{1,0:T(8,128)(2,1)}, u32[]{:S(2)}) copy-start(bf16[1024,256]{1,0:T(8,128)(2,1)} %param.24) | copy-start | bytes 1572868
  7.2 5.8 %copy-start.8 = (bf16[256,1024]{1,0:T(8,128)(2,1)S(1)}, bf16[256,1024]{1,0:T(8,128)(2,1)}, u32[]{:S(2)}) copy-start(bf16[256,1024]{1,0:T(8,128)(2,1)} %param.21) | copy-start | bytes 1572868
  7.2 69.2 %all-gather.6.cloned.1.call-start = ((), (), s32[]{:S(2)}) async-start(), calls=%async_computation.1 | async-start | bytes 3932160 | tf_op jit(solution)/shard_map/all_gather | solution.py:92
  7.2 8.7 %copy-start.10 = (f32[3,1024]{1,0:T(4,128)S(1)}, f32[3,1024]{1,0:T(4,128)}, u32[]{:S(2)}) copy-start(f32[3,1024]{1,0:T(4,128)} %param.16) | copy-start | bytes 36868
  9.6 105.6 %all-gather.10.cloned.1.call-start = ((), (), s32[]{:S(2)}) async-start(), calls=%async_computation.4 | async-start | bytes 1310720 | tf_op jit(solution)/shard_map/all_gather | solution.py:109
  9.9 78.5 %collective-permute-start = (bf16[256,1024]{1,0:T(8,128)(2,1)S(1)}, bf16[256,1024]{1,0:T(8,128)(2,1)}, u32[]{:S(2)}, u32[]{:S(2)}) collective-permute-start(bf16[256,1024]{1,0:T(8,128)(2,1)S(1)} %bitcast.126), channel_id=1, source_target_pairs={{0,3},{1,0},{2,1},{3,2},{4,7},{5,4},{6,5},{7,6},{8,11},{9,8},{10,9... | collective-permute-start | bytes 1572872 | tf_op jit(solution)/shard_map/ppermute | solution.py:33
  12.3 76.1 %collective-permute-start.1 = (bf16[256,1024]{1,0:T(8,128)(2,1)S(1)}, bf16[256,1024]{1,0:T(8,128)(2,1)}, u32[]{:S(2)}, u32[]{:S(2)}) collective-permute-start(bf16[256,1024]{1,0:T(8,128)(2,1)S(1)} %bitcast.127), channel_id=1, source_target_pairs={{0,2},{1,3},{2,0},{3,1},{4,6},{5,7},{6,4},{7,5},{8,10},{9,11},{10,... | collective-permute-start | bytes 1572872 | tf_op jit(solution)/shard_map/ppermute | solution.py:33
  13.0 34.0 %collective-permute-start.3 = (bf16[256,1024]{1,0:T(8,128)(2,1)S(1)}, bf16[256,1024]{1,0:T(8,128)(2,1)}, u32[]{:S(2)}, u32[]{:S(2)}) collective-permute-start(bf16[256,1024]{1,0:T(8,128)(2,1)S(1)} %copy-done.8), channel_id=1, source_target_pairs={{0,3},{1,0},{2,1},{3,2},{4,7},{5,4},{6,5},{7,6},{8,11},{9,8},{10,9... | collective-permute-start | bytes 1572872 | tf_op jit(solution)/shard_map/ppermute | solution.py:33
  13.0 43.8 %collective-permute-start.4 = (bf16[256,1024]{1,0:T(8,128)(2,1)S(1)}, bf16[256,1024]{1,0:T(8,128)(2,1)}, u32[]{:S(2)}, u32[]{:S(2)}) collective-permute-start(bf16[256,1024]{1,0:T(8,128)(2,1)S(1)} %copy-done.8), channel_id=1, source_target_pairs={{0,2},{1,3},{2,0},{3,1},{4,6},{5,7},{6,4},{7,5},{8,10},{9,11},{10,... | collective-permute-start | bytes 1572872 | tf_op jit(solution)/shard_map/ppermute | solution.py:33
  14.8 42.1 %collective-permute-start.5 = (bf16[256,1024]{1,0:T(8,128)(2,1)S(1)}, bf16[256,1024]{1,0:T(8,128)(2,1)}, u32[]{:S(2)}, u32[]{:S(2)}) collective-permute-start(bf16[256,1024]{1,0:T(8,128)(2,1)S(1)} %copy-done.8), channel_id=1, source_target_pairs={{0,1},{1,2},{2,3},{3,0},{4,5},{5,6},{6,7},{7,4},{8,9},{9,10},{10,1... | collective-permute-start | bytes 1572872 | tf_op jit(solution)/shard_map/ppermute | solution.py:33
  47.0 41.5 %collective-permute-start.2 = (bf16[256,1024]{1,0:T(8,128)(2,1)S(1)}, bf16[256,1024]{1,0:T(8,128)(2,1)}, u32[]{:S(2)}, u32[]{:S(2)}) collective-permute-start(bf16[256,1024]{1,0:T(8,128)(2,1)S(1)} %bitcast.128), channel_id=1, source_target_pairs={{0,1},{1,2},{2,3},{3,0},{4,5},{5,6},{6,7},{7,4},{8,9},{9,10},{10,1... | collective-permute-start | bytes 1572872 | tf_op jit(solution)/shard_map/ppermute | solution.py:33
  84.5 2.1 copy-start.1
  88.2 68.7 %all-gather.8.cloned.1.call-start = ((), (), s32[]{:S(2)}) async-start(), calls=%async_computation.2 | async-start | bytes 1966080 | tf_op jit(solution)/shard_map/all_gather | solution.py:126
  88.4 5.0 %copy-start.2 = (f32[2,512,1024]{2,1,0:T(8,128)S(1)}, f32[2,512,1024]{2,1,0:T(8,128)}, u32[]{:S(2)}) copy-start(f32[2,512,1024]{2,1,0:T(8,128)} %copy-done.1) | copy-start | bytes 12582916
  94.4 24.6 %copy-start.11 = (f32[2,1024]{1,0:T(2,128)S(1)}, f32[2,1024]{1,0:T(2,128)}, u32[]{:S(2)}) copy-start(f32[2,1024]{1,0:T(2,128)} %param.22) | copy-start | bytes 24580
  117.2 16.7 %copy-start.6 = (bf16[512,1024]{1,0:T(8,128)(2,1)S(1)}, bf16[512,1024]{1,0:T(8,128)(2,1)}, u32[]{:S(2)}) copy-start(bf16[512,1024]{1,0:T(8,128)(2,1)} %param.19) | copy-start | bytes 3145732
  117.3 7.5 %collective-permute-start.6 = (bf16[256,512]{1,0:T(8,128)(2,1)S(1)}, bf16[256,512]{1,0:T(8,128)(2,1)S(1)}, u32[]{:S(2)}, u32[]{:S(2)}) collective-permute-start(bf16[256,512]{1,0:T(8,128)(2,1)S(1)} %bitcast.132), channel_id=1, source_target_pairs={{0,3},{1,0},{2,1},{3,2},{4,7},{5,4},{6,5},{7,6},{8,11},{9,8},{10,9... | collective-permute-start | bytes 786440 | tf_op jit(solution)/shard_map/ppermute | solution.py:33
  118.2 13.2 %collective-permute-start.7 = (bf16[256,512]{1,0:T(8,128)(2,1)S(1)}, bf16[256,512]{1,0:T(8,128)(2,1)S(1)}, u32[]{:S(2)}, u32[]{:S(2)}) collective-permute-start(bf16[256,512]{1,0:T(8,128)(2,1)S(1)} %bitcast.133), channel_id=1, source_target_pairs={{0,2},{1,3},{2,0},{3,1},{4,6},{5,7},{6,4},{7,5},{8,10},{9,11},{10,... | collective-permute-start | bytes 786440 | tf_op jit(solution)/shard_map/ppermute | solution.py:33
  118.9 12.8 %collective-permute-start.8 = (bf16[256,512]{1,0:T(8,128)(2,1)S(1)}, bf16[256,512]{1,0:T(8,128)(2,1)}, u32[]{:S(2)}, u32[]{:S(2)}) collective-permute-start(bf16[256,512]{1,0:T(8,128)(2,1)S(1)} %bitcast.134), channel_id=1, source_target_pairs={{0,1},{1,2},{2,3},{3,0},{4,5},{5,6},{6,7},{7,4},{8,9},{9,10},{10,1... | collective-permute-start | bytes 786440 | tf_op jit(solution)/shard_map/ppermute | solution.py:33
  119.1 89.2 %reduce-scatter.2.cloned.1.call-start = ((), (), s32[]{:S(2)}) async-start(), calls=%async_computation.3 | async-start | bytes 1966080 | tf_op jit(solution)/shard_map/reduce_scatter | solution.py:185
  119.1 14.8 %copy-start.3 = (bf16[4,256,1024]{2,1,0:T(8,128)(2,1)S(1)}, bf16[4,256,1024]{2,1,0:T(8,128)(2,1)}, u32[]{:S(2)}) copy-start(bf16[4,256,1024]{2,1,0:T(8,128)(2,1)} %fusion.12) | copy-start | bytes 6291460
  137.0 2.3 %copy-start.12 = (s32[1024]{0:T(1024)S(1)}, s32[1024]{0:T(1024)}, u32[]{:S(2)}) copy-start(s32[1024]{0:T(1024)} %param.17) | copy-start | bytes 12292
  137.1 2.3 %copy-start.14 = (f32[64]{0:T(128)S(1)}, f32[64]{0:T(128)}, u32[]{:S(2)}) copy-start(f32[64]{0:T(128)} %param.18) | copy-start | bytes 772
  137.6 15.5 %copy-start.5 = (bf16[4,256,1024]{2,1,0:T(8,128)(2,1)S(1)}, bf16[4,256,1024]{2,1,0:T(8,128)(2,1)}, u32[]{:S(2)}) copy-start(bf16[4,256,1024]{2,1,0:T(8,128)(2,1)} %fusion.19) | copy-start | bytes 6291460
  137.6 5.7 %collective-permute-start.9 = (bf16[256,512]{1,0:T(8,128)(2,1)S(1)}, bf16[256,512]{1,0:T(8,128)(2,1)S(1)}, u32[]{:S(2)}, u32[]{:S(2)}) collective-permute-start(bf16[256,512]{1,0:T(8,128)(2,1)S(1)} %bitcast.151), channel_id=1, source_target_pairs={{0,3},{1,0},{2,1},{3,2},{4,7},{5,4},{6,5},{7,6},{8,11},{9,8},{10,9... | collective-permute-start | bytes 786440 | tf_op jit(solution)/shard_map/ppermute | solution.py:33
  137.7 14.1 %collective-permute-start.10 = (bf16[256,512]{1,0:T(8,128)(2,1)S(1)}, bf16[256,512]{1,0:T(8,128)(2,1)S(1)}, u32[]{:S(2)}, u32[]{:S(2)}) collective-permute-start(bf16[256,512]{1,0:T(8,128)(2,1)S(1)} %bitcast.152), channel_id=1, source_target_pairs={{0,2},{1,3},{2,0},{3,1},{4,6},{5,7},{6,4},{7,5},{8,10},{9,11},{10,... | collective-permute-start | bytes 786440 | tf_op jit(solution)/shard_map/ppermute | solution.py:33
  139.2 12.7 %collective-permute-start.11 = (bf16[256,512]{1,0:T(8,128)(2,1)S(1)}, bf16[256,512]{1,0:T(8,128)(2,1)S(1)}, u32[]{:S(2)}, u32[]{:S(2)}) collective-permute-start(bf16[256,512]{1,0:T(8,128)(2,1)S(1)} %bitcast.153), channel_id=1, source_target_pairs={{0,1},{1,2},{2,3},{3,0},{4,5},{5,6},{6,7},{7,4},{8,9},{9,10},{10,1... | collective-permute-start | bytes 786440 | tf_op jit(solution)/shard_map/ppermute | solution.py:33
  153.2 2.8 %copy-start.7 = (bf16[2,1024,256]{2,1,0:T(8,128)(2,1)S(1)}, bf16[2,1024,256]{2,1,0:T(8,128)(2,1)}, u32[]{:S(2)}) copy-start(bf16[2,1024,256]{2,1,0:T(8,128)(2,1)} %param.25) | copy-start | bytes 3145732
  154.6 1.4 copy-start.4
  161.9 0.9 copy-start.13
  163.8 1.2 collective-permute-start.12
  165.0 3.6 %collective-permute-start.13 = (f32[1024]{0:T(1024)S(1)}, f32[1024]{0:T(1024)S(1)}, u32[]{:S(2)}, u32[]{:S(2)}) collective-permute-start(f32[1024]{0:T(1024)S(1)} %add.61), channel_id=1, source_target_pairs={{0,2},{1,3},{2,0},{3,1},{4,6},{5,7},{6,4},{7,5},{8,10},{9,11},{10,... | collective-permute-start | bytes 12296 | tf_op jit(solution)/shard_map/ppermute | solution.py:61
  165.9 4.6 %slice-start = ((s8[6291456]{0:T(1024)(128)(4,1)}), s8[4194304]{0:T(1024)(128)(4,1)S(1)}, s32[]{:S(2)}) async-start(s8[6291456]{0:T(1024)(128)(4,1)} %bitcast.121), calls=%async_computation.5 | async-start | bytes 8388608
  169.2 1.6 slice-start.1
Sparse Core Ops, SparseCore 0:
  10.2 66.2 all-gather.5
  88.3 26.8 all-gather.9
  119.2 37.0 all-gather.7
  174.1 34.1 reduce-scatter.1

commit v12 on v11

--- a/solution.py
+++ b/solution.py
@@ -22,7 +22,7 @@
     return table.reshape(6 * BANDS, coords.shape[1]).T.astype(jnp.bfloat16)
 
 
-def ring_gather(x, axis, n):
+def ring_gather(x, axis, n, take=False):
     if n == 1:
         return x
     if n > RING_MAX:
@@ -32,7 +32,10 @@
     for s in range(1, n):
         blocks.append(lax.ppermute(x, axis, [(i, (i - s) % n) for i in range(n)]))
     flipped = jnp.stack(blocks)
-    ordered = jnp.roll(flipped, idx, axis=0)
+    if take:
+        ordered = jnp.take(flipped, (jnp.arange(n) - idx) % n, axis=0)
+    else:
+        ordered = jnp.roll(flipped, idx, axis=0)
     return ordered.reshape((n * x.shape[0],) + x.shape[1:])
 
 
@@ -88,16 +91,20 @@
     nheads = local // HEAD
     column = lax.axis_index("heads") * local
     enc = encode(coords)
-    cross_full = ring_gather(cross_out, "heads", n_heads)
-    piece = lax.all_gather(
-        kv_weight.reshape(kv_weight.shape[0], 2 * local), "picks", axis=0, tiled=True
-    )
-    cross_full, piece = lax.optimization_barrier((cross_full, piece))
-    keys_vals = jnp.dot(
-        enc, piece.reshape(piece.shape[0], 2 * local), preferred_element_type=jnp.float32
-    ).astype(jnp.bfloat16)
-    keys = keys_vals[:, :local].reshape(count, nheads, HEAD)
-    values = keys_vals[:, local:].reshape(count, nheads, HEAD)
+    cross_full = ring_gather(cross_out, "heads", n_heads, take=True)
+    key_rows = lax.all_gather(kv_weight[:, 0, :], "picks", axis=0, tiled=True)
+    value_rows = lax.all_gather(kv_weight[:, 1, :], "picks", axis=0, tiled=True)
+    cross_full, value_rows = lax.optimization_barrier((cross_full, value_rows))
+    keys = (
+        jnp.dot(enc, key_rows, preferred_element_type=jnp.float32)
+        .astype(jnp.bfloat16)
+        .reshape(count, nheads, HEAD)
+    )
+    values = (
+        jnp.dot(enc, value_rows, preferred_element_type=jnp.float32)
+        .astype(jnp.bfloat16)
+        .reshape(count, nheads, HEAD)
+    )
     queries = lax.dynamic_slice_in_dim(latents, column, local, 1).reshape(lat_rows, nheads, HEAD)
     scores = jnp.einsum("lhc,thc->hlt", queries, keys, preferred_element_type=jnp.float32) * scale
     top = jnp.max(scores, axis=2)
@@ -120,7 +127,7 @@
         .reshape(lat_rows, local)
         .astype(jnp.bfloat16)
     )
-    out_full = ring_gather(self_out.T, "heads", n_heads).T
+    out_full = ring_gather(self_out.T, "heads", n_heads, take=True).T
     out_full, attended = lax.optimization_barrier((out_full, attended))
     dq_local, attended = lax.optimization_barrier((dec_query, attended))
     dq_full = lax.all_gather(dq_local, "picks", axis=0, tiled=True)

time: 217 us -> 228 us (1.051)
  local copies, waits for them, and re-layouts: 9.7 us -> 19 us
  waiting for transfers between devices: 96 us -> 86.7 us
  other arithmetic: 45.9 us -> 52.2 us
  matrix products: 26.8 us -> 31 us
    ppermute x12, waiting for transfers between devices: 38.6 us -> 27.5 us  [ring_gather(): blocks.append(lax.ppermute(x, axis, [(i, (i - s) % n) for i in range(n)]))]
    concatenate x4 -> x2, other arithmetic: 13.5 us -> 2.47 us  [ring_gather(): ordered = jnp.roll(flipped, idx, axis=0)]
    another operation x1 -> x3, other arithmetic: 22.8 us -> 30.4 us
    gather x0 -> x2, local copies, waits for them, and re-layouts: none -> 7.22 us  [ring_gather(): ordered = jnp.take(flipped, (jnp.arange(n) - idx) % n, axis=0)]
    select_n x0 -> x2, other arithmetic: none -> 4.79 us  [ring_gather(): ordered = jnp.take(flipped, (jnp.arange(n) - idx) % n, axis=0)]
    all_gather x1, waiting for transfers between devices: 7.49 us -> 10.6 us  [on_device(): lax.all_gather(numer.astype(jnp.bfloat16), 'picks', axis=0, tiled=False)]
    dot_general x1 -> x2, matrix products: 7.15 us -> 10.1 us  [the longest x1 5.09 us: on_device(): jnp.dot(enc, value_rows, preferred_element_type=jnp.float32)]
    concatenate x1, other arithmetic: 3.2 us -> 6.05 us  [encode(): table = jnp.concatenate([jnp.sin(angle), jnp.cos(angle)], axis=0)]
  transfers between devices with their start and end apart: 18 -> 19, of which waited for: 13 -> 11; matrix products, arithmetic and copies ran while one was open for 28% -> 31% of each run, Pallas kernels for 0% -> 0%
where the time goes in v12:
time: 228 us; the launch traced here: 227 us
  waiting for transfers between devices  86.7 us (38%)
  other arithmetic  52.2 us (23%)
  matrix products  31 us (14%)
  local copies, waits for them, and re-layouts  19 us (8%)
  between operations  14.2 us (6%)
  blocking collectives  13.3 us (6%)
  starting transfers between devices  11 us (5%)
    reduce_scatter x1, waiting for transfers between devices, on_device(): lax.psum_scatter(jnp.dot(enc.T, dquery, preferred_element_type=jnp.float3...  32.4 us
    ppermute x12, waiting for transfers between devices, ring_gather(): blocks.append(lax.ppermute(x, axis, [(i, (i - s) % n) for i in range(n)]))  27.5 us
    another operation x1, other arithmetic  24.5 us
    all_gather x1, blocking collectives, on_device(): lax.all_gather(jnp.stack([top, total]), 'picks', axis=0, tiled=False)  13.3 us
    all_gather x1, waiting for transfers between devices, on_device(): key_rows = lax.all_gather(kv_weight[:, 0, :], 'picks', axis=0, tiled=True)  13.2 us
    all_gather x1, waiting for transfers between devices, on_device(): lax.all_gather(numer.astype(jnp.bfloat16), 'picks', axis=0, tiled=False)  10.6 us
    ppermute x12, starting transfers between devices, ring_gather(): blocks.append(lax.ppermute(x, axis, [(i, (i - s) % n) for i in range(n)]))  9.8 us
    gather x2, local copies, waits for them, and re-layouts, ring_gather(): ordered = jnp.take(flipped, (jnp.arange(n) - idx) % n, axis=0)  7.22 us
  transfers between devices with their start and end apart: 19, of which 11 were waited for; matrix products, arithmetic and copies ran while one was open for 31% of the time, Pallas kernels for 0%

profile of v12, /device:TPU:0, one launch (start us, length us, event | category | flops | bytes accessed | tf_op | source)
XLA Modules:
  0.0 227.4 jit_solution(17091020113089275082)
XLA Ops:
  7.2 2.9 %fusion.66 = (bf16[768,1,256]{2,1,0:T(2,128)(2,1)S(1)}, bf16[768,1,256]{2,1,0:T(2,128)(2,1)S(1)}) fusion(bf16[768,2,256]{2,1,0:T(2,128)(2,1)} %param.20), kind=kLoop, calls=%fused_computation.121 | loop fusion | bytes 1572864 | tf_op jit(solution)/shard_map/slice | solution.py:95
  10.2 0.8 copy.117
  11.6 2.6 %collective-permute-start.4 = (bf16[256,1024]{1,0:T(8,128)(2,1)}, bf16[256,1024]{1,0:T(8,128)(2,1)}, u32[]{:S(2)}, u32[]{:S(2)}) collective-permute-start(bf16[256,1024]{1,0:T(8,128)(2,1)} %param.21), channel_id=1, source_target_pairs={{0,2},{1,3},{2,0},{3,1},{4,6},{5,7},{6,4},{7,5},{8,10},{9,11},{10,... | collective-permute-start | bytes 1572872 | tf_op jit(solution)/shard_map/ppermute | solution.py:33
  14.1 1.4 collective-permute-start.3
  17.1 1.0 constant_dynamic-slice_fusion.1
  18.1 24.5 %fusion = (bf16[3,512,1024]{2,1,0:T(8,128)(2,1)}, bf16[3,512,1024]{2,1,0:T(8,128)(2,1)}) fusion(f32[3,1024]{1,0:T(4,128)S(1)} %copy-done.8, f32[512]{0:T(512)S(1)} %maximum_multiply_fusion), kind=kLoop, calls=%fused_computation.4 | loop fusion | flops 4718592 | bytes 6305792 | tf_op jit(solution)/shard_map/convert
  42.8 1.4 collective-permute-start
  44.3 6.1 %pad_maximum_fusion = bf16[6,512,1024]{2,1,0:T(8,128)(2,1)} fusion(bf16[3,512,1024]{2,1,0:T(8,128)(2,1)} %get-tuple-element.29, bf16[3,512,1024]{2,1,0:T(8,128)(2,1)} %get-tuple-element.28), kind=kLoop, calls=%fused_computation.6 | loop fusion | flops 3145728 | bytes 12582912 | tf_op jit(solution)/shard_map/concatenate | solution.py:21
  50.3 3.1 %pad_maximum_fusion.2 = bf16[4,256,1024]{2,1,0:T(8,128)(2,1)} fusion(bf16[1,256,1024]{2,1,0:T(8,128)(2,1)} %bitcast.16, bf16[1,256,1024]{2,1,0:T(8,128)(2,1)} %bitcast.15, bf16[1,256,1024]{2,1,0:T(8,128)(2,1)} %bitcast.14, bf16[1,256,1024]{2,1,0:T(8,128)(2,1)} %bitcast.13), kind=kLoop, calls=%fused_computation.20 | loop fusion | flops 3145728 | bytes 4194304 | tf_op jit(solution)/shard_map/stack | solution.py:34
  53.5 3.6 %gather_fusion.1 = bf16[4,256,1024]{2,1,0:T(8,128)(2,1)} fusion(bf16[4,256,1024]{2,1,0:T(8,128)(2,1)} %pad_maximum_fusion.2, s32[1024]{0:T(1024)S(1)} %pad_clamp_fusion), kind=kCustom, calls=%fused_computation.1.clone | custom fusion | bytes 4194320 | tf_op jit(solution)/shard_map/jit(_take)/gather | solution.py:36
  57.1 2.6 %collective-permute-done = bf16[256,1024]{1,0:T(8,128)(2,1)S(1)} collective-permute-done((bf16[256,1024]{1,0:T(8,128)(2,1)S(1)}, bf16[256,1024]{1,0:T(8,128)(2,1)S(1)}, u32[]{:S(2)}, u32[]{:S(2)}) %collective-permute-start) | collective-permute-done | bytes 524320 | tf_op jit(solution)/shard_map/ppermute | solution.py:33
  59.7 2.7 %pad_maximum_fusion.1 = bf16[4,256,1024]{2,1,0:T(8,128)(2,1)} fusion(bf16[1,256,1024]{2,1,0:T(8,128)(2,1)S(1)} %bitcast.150, bf16[1,256,1024]{2,1,0:T(8,128)(2,1)} %bitcast.5, bf16[1,256,1024]{2,1,0:T(8,128)(2,1)S(1)} %bitcast.151, bf16[1,256,1024]{2,1,0:T(8,128)(2,1)S(1)} %bitcast.135), kind=kLoop, calls=%fused_computation.19 | loop fusion | flops 3145728 | bytes 4194304 | tf_op jit(solution)/shard_map/stack | solution.py:34
  62.4 3.6 %gather_fusion = bf16[4,256,1024]{2,1,0:T(8,128)(2,1)} fusion(bf16[4,256,1024]{2,1,0:T(8,128)(2,1)} %pad_maximum_fusion.1, s32[1024]{0:T(1024)S(1)} %pad_clamp_fusion), kind=kCustom, calls=%fused_computation.clone | custom fusion | bytes 4194320 | tf_op jit(solution)/shard_map/jit(_take)/gather | solution.py:36
  66.0 4.8 %broadcast_select_fusion = (bf16[4,256,1024]{2,1,0:T(8,128)(2,1)}, bf16[4,256,1024]{2,1,0:T(8,128)(2,1)}) fusion(bf16[4,256,1024]{2,1,0:T(8,128)(2,1)} %gather_fusion.1, pred[4]{0:T(512)(128)(4,1)S(1)} %compare_and_fusion, bf16[4,256,1024]{2,1,0:T(8,128)(2,1)} %gather_fusion), kind=kLoop, calls=%fused_computation.51 | loop fusion | flops 2097152 | bytes 8388612 | tf_op jit(solution)/shard_map/jit(_take)/select_n | solution.py:36
  70.8 5.1 %convolution_convert_fusion.3 = bf16[1024,256]{0,1:T(8,128)(2,1)S(1)} fusion(bf16[3072,1024]{1,0:T(8,128)(2,1)} %bitcast.124, bf16[3072,256]{1,0:T(8,128)(2,1)} %bitcast.175), kind=kOutput, calls=%fused_computation.61 | convolution fusion | flops 1610874880 | bytes 8388608 | tf_op jit(solution)/shard_map/dot_general | solution.py:104
  75.9 13.2 %all-gather.11.cloned.1.call-done = bf16[3072,1,256]{2,0,1:T(8,128)(2,1)} async-done(((bf16[768,1,256]{2,0,1:T(8,128)(2,1)}), bf16[3072,1,256]{2,0,1:T(8,128)(2,1)}) %all-gather.11.cloned.1.call-update) | async-done | bytes 1572880 | tf_op jit(solution)/shard_map/all_gather | solution.py:95
  89.1 5.1 %fusion.21 = bf16[1024,256]{0,1:T(8,128)(2,1)S(1)} fusion(bf16[3072,1024]{1,0:T(8,128)(2,1)} %bitcast.125, bf16[3072,1,256]{2,0,1:T(8,128)(2,1)} %all-gather.11.cloned.1.call-done), kind=kOutput, calls=%fused_computation.59 | convolution fusion | flops 1610874880 | bytes 8388608 | tf_op jit(solution)/shard_map/dot_general | solution.py:99
  94.2 0.8 multiply_reduce_fusion.1
  95.0 2.0 copy-done.2
  97.0 1.6 fusion.29
  98.9 3.1 %fusion.4 = f32[2,512]{1,0:T(2,128)S(1)} fusion(f32[2,512,1024]{2,1,0:T(8,128)} %copy-done.2, f32[2,512]{1,0:T(2,128)S(1)} %get-tuple-element.34), kind=kLoop, calls=%fused_computation.15 | loop fusion | flops 3144704 | bytes 4202496 | tf_op jit(solution)/shard_map/reduce_sum | solution.py:112
  102.0 13.3 %all-gather.3 = f32[8,2,512]{2,1,0:T(2,128)S(1)} all-gather(f32[2,2,512]{2,1,0:T(2,128)S(1)} %pad_maximum_fusion.3), channel_id=5, replica_groups=mesh['groups'=2,'picks'=4,'heads'=4] {'picks'}, dimensions={0}, use_global_device_ids=true | all-gather | bytes 40960 | tf_op jit(solution)/shard_map/all_gather | solution.py:117
  115.3 10.6 %all-gather.15.cloned.1.call-done = bf16[8,512,128]{2,1,0:T(8,128)(2,1)} async-done(((bf16[2,512,128]{2,1,0:T(8,128)(2,1)}), bf16[8,512,128]{2,1,0:T(8,128)(2,1)}) %all-gather.15.cloned.1.call-update) | async-done | bytes 1048592 | tf_op jit(solution)/shard_map/all_gather | solution.py:116
  125.9 1.8 multiply_reduce_fusion.2
  127.9 0.9 collective-permute-start.6
  129.9 5.4 %collective-permute-done.6 = bf16[256,512]{1,0:T(8,128)(2,1)S(1)} collective-permute-done((bf16[256,512]{1,0:T(8,128)(2,1)S(1)}, bf16[256,512]{1,0:T(8,128)(2,1)S(1)}, u32[]{:S(2)}, u32[]{:S(2)}) %collective-permute-start.6) | collective-permute-done | bytes 262176 | tf_op jit(solution)/shard_map/ppermute | solution.py:33
  135.3 7.0 %collective-permute-done.7 = bf16[256,512]{1,0:T(8,128)(2,1)S(1)} collective-permute-done((bf16[256,512]{1,0:T(8,128)(2,1)S(1)}, bf16[256,512]{1,0:T(8,128)(2,1)S(1)}, u32[]{:S(2)}, u32[]{:S(2)}) %collective-permute-start.7) | collective-permute-done | bytes 262176 | tf_op jit(solution)/shard_map/ppermute | solution.py:33
  142.3 1.2 fusion.46
  143.6 2.6 %multiply_reduce_fusion.4 = (f32[512]{0:T(512)S(1)}, f32[512,1024]{1,0:T(8,128)S(1)}) fusion(bf16[1024,512]{1,0:T(8,128)(2,1)S(1)} %bitcast.130, bf16[1024,1024]{1,0:T(8,128)(2,1)S(1)} %bitcast.123, bf16[512,1024]{1,0:T(8,128)(2,1)} %param.19), kind=kOutput, calls=%fused_computation.47 | convolution fusion | flops 1075838464 | bytes 6293504 | tf_op jit(solution)/shard_map/dot_general | solution.py:135
  146.2 1.1 fusion.24
  148.5 1.4 collective-permute-start.10
  150.2 4.2 %collective-permute-done.9 = bf16[256,512]{1,0:T(8,128)(2,1)S(1)} collective-permute-done((bf16[256,512]{1,0:T(8,128)(2,1)S(1)}, bf16[256,512]{1,0:T(8,128)(2,1)S(1)}, u32[]{:S(2)}, u32[]{:S(2)}) %collective-permute-start.9) | collective-permute-done | bytes 262176 | tf_op jit(solution)/shard_map/ppermute | solution.py:33
  154.4 8.0 %collective-permute-done.10 = bf16[256,512]{1,0:T(8,128)(2,1)S(1)} collective-permute-done((bf16[256,512]{1,0:T(8,128)(2,1)S(1)}, bf16[256,512]{1,0:T(8,128)(2,1)S(1)}, u32[]{:S(2)}, u32[]{:S(2)}) %collective-permute-start.10) | collective-permute-done | bytes 262176 | tf_op jit(solution)/shard_map/ppermute | solution.py:33
  162.6 1.2 fusion.39
  163.9 1.4 multiply_reduce_fusion.3
  165.3 1.3 copy-done.4
  166.6 0.8 fusion.28
  167.6 5.1 %convolution_convert_fusion.2 = bf16[1024,256]{0,1:T(8,128)(2,1)S(1)} fusion(bf16[3072,1024]{1,0:T(8,128)(2,1)} %bitcast.126, bf16[3072,256]{1,0:T(8,128)(2,1)} %all-gather.9.cloned.1.call-done), kind=kOutput, calls=%fused_computation.60 | convolution fusion | flops 1610874880 | bytes 8388608 | tf_op jit(solution)/shard_map/dot_general | solution.py:167
  172.6 0.8 fusion.3
  173.5 1.0 fusion.25
  174.8 0.9 collective-permute-done.12
  176.4 0.9 multiply_reduce_fusion
  177.3 2.0 collective-permute-done.13
  179.9 1.2 multiply_convert_fusion.4
  181.5 3.1 %convolution_convert_fusion = bf16[3072,256]{1,0:T(8,128)(2,1)} fusion(bf16[3072,1024]{1,0:T(8,128)(2,1)S(1)} %bitcast.129, bf16[1024,256]{0,1:T(8,128)(2,1)S(1)} %bitcast.177), kind=kOutput, calls=%fused_computation.12 | convolution fusion | flops 1611399168 | bytes 8388608 | tf_op jit(solution)/shard_map/dot_general | solution.py:193
  184.7 1.9 constant_dynamic-slice_fusion
  186.5 32.4 %reduce-scatter.2.cloned.1.call-done = bf16[768,256]{1,0:T(8,128)(2,1)} async-done(((bf16[3072,256]{1,0:T(8,128)(2,1)}), bf16[768,256]{1,0:T(8,128)(2,1)}) %reduce-scatter.2.cloned.1.call-update) | async-done | bytes 393232 | tf_op jit(solution)/shard_map/reduce_scatter | solution.py:192
  218.9 1.9 convert_element_type.104
  (82 shorter events, 7.7 us)
Async XLA Ops:
  7.2 139.0 %copy-start = (bf16[3,1024,256]{2,1,0:T(8,128)(2,1)S(1)}, bf16[3,1024,256]{2,1,0:T(8,128)(2,1)}, u32[]{:S(2)}) copy-start(bf16[3,1024,256]{2,1,0:T(8,128)(2,1)} %param.23) | copy-start | bytes 4718596
  7.2 8.3 %copy-start.7 = (bf16[1024,256]{1,0:T(8,128)(2,1)S(1)}, bf16[1024,256]{1,0:T(8,128)(2,1)}, u32[]{:S(2)}) copy-start(bf16[1024,256]{1,0:T(8,128)(2,1)} %param.24) | copy-start | bytes 1572868
  7.2 63.6 %all-gather.13.cloned.1.call-start = ((), (), s32[]{:S(2)}) async-start(), calls=%async_computation.4 | async-start | bytes 1966080 | tf_op jit(solution)/shard_map/all_gather | solution.py:96
  10.1 8.0 %copy-start.8 = (f32[3,1024]{1,0:T(4,128)S(1)}, f32[3,1024]{1,0:T(4,128)}, u32[]{:S(2)}) copy-start(f32[3,1024]{1,0:T(4,128)} %param.16) | copy-start | bytes 36868
  11.0 78.1 %all-gather.11.cloned.1.call-start = ((), (), s32[]{:S(2)}) async-start(), calls=%async_computation.3 | async-start | bytes 1966080 | tf_op jit(solution)/shard_map/all_gather | solution.py:95
  11.0 31.8 %collective-permute-start.5 = (bf16[256,1024]{1,0:T(8,128)(2,1)}, bf16[256,1024]{1,0:T(8,128)(2,1)}, u32[]{:S(2)}, u32[]{:S(2)}) collective-permute-start(bf16[256,1024]{1,0:T(8,128)(2,1)} %param.21), channel_id=1, source_target_pairs={{0,1},{1,2},{2,3},{3,0},{4,5},{5,6},{6,7},{7,4},{8,9},{9,10},{10,1... | collective-permute-start | bytes 1572872 | tf_op jit(solution)/shard_map/ppermute | solution.py:33
  11.6 38.8 %collective-permute-start.4 = (bf16[256,1024]{1,0:T(8,128)(2,1)}, bf16[256,1024]{1,0:T(8,128)(2,1)}, u32[]{:S(2)}, u32[]{:S(2)}) collective-permute-start(bf16[256,1024]{1,0:T(8,128)(2,1)} %param.21), channel_id=1, source_target_pairs={{0,2},{1,3},{2,0},{3,1},{4,6},{5,7},{6,4},{7,5},{8,10},{9,11},{10,... | collective-permute-start | bytes 1572872 | tf_op jit(solution)/shard_map/ppermute | solution.py:33
  14.1 36.2 %collective-permute-start.3 = (bf16[256,1024]{1,0:T(8,128)(2,1)}, bf16[256,1024]{1,0:T(8,128)(2,1)}, u32[]{:S(2)}, u32[]{:S(2)}) collective-permute-start(bf16[256,1024]{1,0:T(8,128)(2,1)} %param.21), channel_id=1, source_target_pairs={{0,3},{1,0},{2,1},{3,2},{4,7},{5,4},{6,5},{7,6},{8,11},{9,8},{10,9... | collective-permute-start | bytes 1572872 | tf_op jit(solution)/shard_map/ppermute | solution.py:33
  15.7 41.4 %collective-permute-start.2 = (bf16[256,1024]{1,0:T(8,128)(2,1)S(1)}, bf16[256,1024]{1,0:T(8,128)(2,1)S(1)}, u32[]{:S(2)}, u32[]{:S(2)}) collective-permute-start(bf16[256,1024]{1,0:T(8,128)(2,1)S(1)} %bitcast.132), channel_id=1, source_target_pairs={{0,1},{1,2},{2,3},{3,0},{4,5},{5,6},{6,7},{7,4},{8,9},{9,10},{10,1... | collective-permute-start | bytes 1572872 | tf_op jit(solution)/shard_map/ppermute | solution.py:33
  15.8 41.3 %collective-permute-start.1 = (bf16[256,1024]{1,0:T(8,128)(2,1)S(1)}, bf16[256,1024]{1,0:T(8,128)(2,1)}, u32[]{:S(2)}, u32[]{:S(2)}) collective-permute-start(bf16[256,1024]{1,0:T(8,128)(2,1)S(1)} %bitcast.133), channel_id=1, source_target_pairs={{0,2},{1,3},{2,0},{3,1},{4,6},{5,7},{6,4},{7,5},{8,10},{9,11},{10,... | collective-permute-start | bytes 1572872 | tf_op jit(solution)/shard_map/ppermute | solution.py:33
  17.0 108.9 %all-gather.15.cloned.1.call-start = ((), (), s32[]{:S(2)}) async-start(), calls=%async_computation.5 | async-start | bytes 1310720 | tf_op jit(solution)/shard_map/all_gather | solution.py:116
  42.8 16.9 %collective-permute-start = (bf16[256,1024]{1,0:T(8,128)(2,1)S(1)}, bf16[256,1024]{1,0:T(8,128)(2,1)S(1)}, u32[]{:S(2)}, u32[]{:S(2)}) collective-permute-start(bf16[256,1024]{1,0:T(8,128)(2,1)S(1)} %bitcast.134), channel_id=1, source_target_pairs={{0,3},{1,0},{2,1},{3,2},{4,7},{5,4},{6,5},{7,6},{8,11},{9,8},{10,9... | collective-permute-start | bytes 1572872 | tf_op jit(solution)/shard_map/ppermute | solution.py:33
  95.0 2.0 copy-start.2
  98.7 68.9 %all-gather.9.cloned.1.call-start = ((), (), s32[]{:S(2)}) async-start(), calls=%async_computation.1 | async-start | bytes 1966080 | tf_op jit(solution)/shard_map/all_gather | solution.py:133
  102.0 27.8 %copy-start.9 = (f32[2,1024]{1,0:T(2,128)S(1)}, f32[2,1024]{1,0:T(2,128)}, u32[]{:S(2)}) copy-start(f32[2,1024]{1,0:T(2,128)} %param.22) | copy-start | bytes 24580
  127.9 7.4 %collective-permute-start.6 = (bf16[256,512]{1,0:T(8,128)(2,1)S(1)}, bf16[256,512]{1,0:T(8,128)(2,1)S(1)}, u32[]{:S(2)}, u32[]{:S(2)}) collective-permute-start(bf16[256,512]{1,0:T(8,128)(2,1)S(1)} %bitcast.136), channel_id=1, source_target_pairs={{0,3},{1,0},{2,1},{3,2},{4,7},{5,4},{6,5},{7,6},{8,11},{9,8},{10,9... | collective-permute-start | bytes 786440 | tf_op jit(solution)/shard_map/ppermute | solution.py:33
  128.8 13.5 %collective-permute-start.7 = (bf16[256,512]{1,0:T(8,128)(2,1)S(1)}, bf16[256,512]{1,0:T(8,128)(2,1)S(1)}, u32[]{:S(2)}, u32[]{:S(2)}) collective-permute-start(bf16[256,512]{1,0:T(8,128)(2,1)S(1)} %bitcast.137), channel_id=1, source_target_pairs={{0,2},{1,3},{2,0},{3,1},{4,6},{5,7},{6,4},{7,5},{8,10},{9,11},{10,... | collective-permute-start | bytes 786440 | tf_op jit(solution)/shard_map/ppermute | solution.py:33
  129.6 12.7 %collective-permute-start.8 = (bf16[256,512]{1,0:T(8,128)(2,1)S(1)}, bf16[256,512]{1,0:T(8,128)(2,1)S(1)}, u32[]{:S(2)}, u32[]{:S(2)}) collective-permute-start(bf16[256,512]{1,0:T(8,128)(2,1)S(1)} %bitcast.138), channel_id=1, source_target_pairs={{0,1},{1,2},{2,3},{3,0},{4,5},{5,6},{6,7},{7,4},{8,9},{9,10},{10,1... | collective-permute-start | bytes 786440 | tf_op jit(solution)/shard_map/ppermute | solution.py:33
  129.8 89.1 %reduce-scatter.2.cloned.1.call-start = ((), (), s32[]{:S(2)}) async-start(), calls=%async_computation.2 | async-start | bytes 1966080 | tf_op jit(solution)/shard_map/reduce_scatter | solution.py:192
  129.9 13.7 %copy-start.3 = (bf16[4,256,1024]{2,1,0:T(8,128)(2,1)S(1)}, bf16[4,256,1024]{2,1,0:T(8,128)(2,1)}, u32[]{:S(2)}) copy-start(bf16[4,256,1024]{2,1,0:T(8,128)(2,1)} %get-tuple-element.32) | copy-start | bytes 6291460
  147.9 2.2 copy-start.10
  147.9 2.2 copy-start.12
  148.5 15.4 %copy-start.5 = (bf16[4,256,1024]{2,1,0:T(8,128)(2,1)S(1)}, bf16[4,256,1024]{2,1,0:T(8,128)(2,1)}, u32[]{:S(2)}) copy-start(bf16[4,256,1024]{2,1,0:T(8,128)(2,1)} %get-tuple-element.33) | copy-start | bytes 6291460
  148.5 5.9 %collective-permute-start.9 = (bf16[256,512]{1,0:T(8,128)(2,1)S(1)}, bf16[256,512]{1,0:T(8,128)(2,1)S(1)}, u32[]{:S(2)}, u32[]{:S(2)}) collective-permute-start(bf16[256,512]{1,0:T(8,128)(2,1)S(1)} %bitcast.156), channel_id=1, source_target_pairs={{0,3},{1,0},{2,1},{3,2},{4,7},{5,4},{6,5},{7,6},{8,11},{9,8},{10,9... | collective-permute-start | bytes 786440 | tf_op jit(solution)/shard_map/ppermute | solution.py:33
  148.5 13.8 %collective-permute-start.10 = (bf16[256,512]{1,0:T(8,128)(2,1)S(1)}, bf16[256,512]{1,0:T(8,128)(2,1)S(1)}, u32[]{:S(2)}, u32[]{:S(2)}) collective-permute-start(bf16[256,512]{1,0:T(8,128)(2,1)S(1)} %bitcast.157), channel_id=1, source_target_pairs={{0,2},{1,3},{2,0},{3,1},{4,6},{5,7},{6,4},{7,5},{8,10},{9,11},{10,... | collective-permute-start | bytes 786440 | tf_op jit(solution)/shard_map/ppermute | solution.py:33
  149.9 12.7 %collective-permute-start.11 = (bf16[256,512]{1,0:T(8,128)(2,1)S(1)}, bf16[256,512]{1,0:T(8,128)(2,1)S(1)}, u32[]{:S(2)}, u32[]{:S(2)}) collective-permute-start(bf16[256,512]{1,0:T(8,128)(2,1)S(1)} %bitcast.158), channel_id=1, source_target_pairs={{0,1},{1,2},{2,3},{3,0},{4,5},{5,6},{6,7},{7,4},{8,9},{9,10},{10,1... | collective-permute-start | bytes 786440 | tf_op jit(solution)/shard_map/ppermute | solution.py:33
  163.9 2.8 %copy-start.6 = (bf16[2,1024,256]{2,1,0:T(8,128)(2,1)S(1)}, bf16[2,1024,256]{2,1,0:T(8,128)(2,1)}, u32[]{:S(2)}) copy-start(bf16[2,1024,256]{2,1,0:T(8,128)(2,1)} %param.25) | copy-start | bytes 3145732
  165.3 1.4 copy-start.4
  172.6 0.9 copy-start.11
  174.5 1.2 collective-permute-start.12
  175.7 3.6 %collective-permute-start.13 = (f32[1024]{0:T(1024)S(1)}, f32[1024]{0:T(1024)S(1)}, u32[]{:S(2)}, u32[]{:S(2)}) collective-permute-start(f32[1024]{0:T(1024)S(1)} %add.66), channel_id=1, source_target_pairs={{0,2},{1,3},{2,0},{3,1},{4,6},{5,7},{6,4},{7,5},{8,10},{9,11},{10,... | collective-permute-start | bytes 12296 | tf_op jit(solution)/shard_map/ppermute | solution.py:64
  176.4 4.7 %slice-start = ((s8[6291456]{0:T(1024)(128)(4,1)}), s8[4194304]{0:T(1024)(128)(4,1)S(1)}, s32[]{:S(2)}) async-start(s8[6291456]{0:T(1024)(128)(4,1)} %bitcast.127), calls=%async_computation.6 | async-start | bytes 8388608
  179.9 1.6 slice-start.1
  181.5 39.3 %copy-start.1 = (bf16[3,1024,256]{2,1,0:T(8,128)(2,1)S(1)}, bf16[3,1024,256]{2,1,0:T(8,128)(2,1)}, u32[]{:S(2)}) copy-start(bf16[3,1024,256]{2,1,0:T(8,128)(2,1)} %param.23) | copy-start | bytes 4718596
Sparse Core Ops, SparseCore 0:
  11.1 39.7 all-gather.12
  53.1 35.9 all-gather.10
  98.8 27.0 all-gather.14
  129.9 36.7 all-gather.8
  184.8 34.0 reduce-scatter.1

commit v13 on v11

--- a/solution.py
+++ b/solution.py
@@ -89,15 +89,13 @@
     column = lax.axis_index("heads") * local
     enc = encode(coords)
     cross_full = ring_gather(cross_out, "heads", n_heads)
-    piece = lax.all_gather(
-        kv_weight.reshape(kv_weight.shape[0], 2 * local), "picks", axis=0, tiled=True
-    )
+    piece = lax.all_gather(kv_weight, "picks", axis=0, tiled=True)
     cross_full, piece = lax.optimization_barrier((cross_full, piece))
-    keys_vals = jnp.dot(
-        enc, piece.reshape(piece.shape[0], 2 * local), preferred_element_type=jnp.float32
+    keys_vals = jnp.einsum(
+        "tf,fjc->tjc", enc, piece, preferred_element_type=jnp.float32
     ).astype(jnp.bfloat16)
-    keys = keys_vals[:, :local].reshape(count, nheads, HEAD)
-    values = keys_vals[:, local:].reshape(count, nheads, HEAD)
+    keys = keys_vals[:, 0].reshape(count, nheads, HEAD)
+    values = keys_vals[:, 1].reshape(count, nheads, HEAD)
     queries = lax.dynamic_slice_in_dim(latents, column, local, 1).reshape(lat_rows, nheads, HEAD)
     scores = jnp.einsum("lhc,thc->hlt", queries, keys, preferred_element_type=jnp.float32) * scale
     top = jnp.max(scores, axis=2)

time: 217 us -> 216 us (level)
    unnamed x37 -> x34, local copies, waits for them, and re-layouts: 6.48 us -> 5.17 us
where the time goes in v13:
time: 216 us
  waiting for transfers between devices  97 us (45%)
  other arithmetic  45.7 us (21%)
  matrix products  26.8 us (12%)
  between operations  14.2 us (7%)
  blocking collectives  13.3 us (6%)
  starting transfers between devices  10.7 us (5%)
  local copies, waits for them, and re-layouts  8.39 us (4%)
    ppermute x12, waiting for transfers between devices, ring_gather(): blocks.append(lax.ppermute(x, axis, [(i, (i - s) % n) for i in range(n)]))  38.8 us
    reduce_scatter x1, waiting for transfers between devices, on_device(): lax.psum_scatter(jnp.dot(enc.T, dquery, preferred_element_type=jnp.float3...  32.4 us
    another operation x1, other arithmetic  22.8 us
    all_gather x1, waiting for transfers between devices, on_device(): piece = lax.all_gather(kv_weight, 'picks', axis=0, tiled=True)  14.5 us
    concatenate x4, other arithmetic, ring_gather(): ordered = jnp.roll(flipped, idx, axis=0)  13.3 us
    all_gather x1, blocking collectives, on_device(): lax.all_gather(jnp.stack([top, total]), 'picks', axis=0, tiled=False)  13.3 us
    ppermute x12, starting transfers between devices, ring_gather(): blocks.append(lax.ppermute(x, axis, [(i, (i - s) % n) for i in range(n)]))  9.4 us
    all_gather x1, waiting for transfers between devices, on_device(): lax.all_gather(numer.astype(jnp.bfloat16), 'picks', axis=0, tiled=False)  7.77 us
  transfers between devices with their start and end apart: 18, of which 13 were waited for; matrix products, arithmetic and copies ran while one was open for 28% of the time, Pallas kernels for 0%

profile of v13, /device:TPU:0, one launch (start us, length us, event | category | flops | bytes accessed | tf_op | source)
XLA Modules:
  0.0 216.1 jit_solution(17237952158772773728)
XLA Ops:
  7.2 0.7 all-gather.6.cloned.1.call-update
  8.0 1.2 copy.60
  9.2 2.4 %collective-permute-start = (bf16[256,1024]{1,0:T(8,128)(2,1)S(1)}, bf16[256,1024]{1,0:T(8,128)(2,1)S(1)}, u32[]{:S(2)}, u32[]{:S(2)}) collective-permute-start(bf16[256,1024]{1,0:T(8,128)(2,1)S(1)} %bitcast.124), channel_id=1, source_target_pairs={{0,3},{1,0},{2,1},{3,2},{4,7},{5,4},{6,5},{7,6},{8,11},{9,8},{10,9... | collective-permute-start | bytes 1572872 | tf_op jit(solution)/shard_map/ppermute | solution.py:33
  11.7 0.6 collective-permute-start.1
  12.4 1.7 collective-permute-start.4
  14.1 1.0 constant_dynamic-slice_fusion.1
  15.3 22.8 %fusion = (bf16[3,512,1024]{2,1,0:T(8,128)(2,1)S(1)}, bf16[3,512,1024]{2,1,0:T(8,128)(2,1)S(1)}) fusion(f32[3,1024]{1,0:T(4,128)S(1)} %copy-done.9, f32[512]{0:T(512)S(1)} %maximum_multiply_fusion), kind=kLoop, calls=%fused_computation.2 | loop fusion | flops 4718592 | bytes 6305792 | tf_op jit(solution)/shard_map/convert
  38.2 3.2 %pad_maximum_fusion = bf16[6,512,1024]{2,1,0:T(8,128)(2,1)} fusion(bf16[3,512,1024]{2,1,0:T(8,128)(2,1)S(1)} %get-tuple-element.29, bf16[3,512,1024]{2,1,0:T(8,128)(2,1)S(1)} %get-tuple-element.28), kind=kLoop, calls=%fused_computation.4 | loop fusion | flops 3145728 | bytes 12582912 | tf_op jit(solution)/shard_map/concatenate | solution.py:21
  41.4 5.1 %collective-permute-done.3 = bf16[256,1024]{1,0:T(8,128)(2,1)} collective-permute-done((bf16[256,1024]{1,0:T(8,128)(2,1)}, bf16[256,1024]{1,0:T(8,128)(2,1)}, u32[]{:S(2)}, u32[]{:S(2)}) %collective-permute-start.3) | collective-permute-done | bytes 524320 | tf_op jit(solution)/shard_map/ppermute | solution.py:33
  46.4 1.1 collective-permute-start.2
  47.5 8.8 %collective-permute-done.4 = bf16[256,1024]{1,0:T(8,128)(2,1)} collective-permute-done((bf16[256,1024]{1,0:T(8,128)(2,1)}, bf16[256,1024]{1,0:T(8,128)(2,1)}, u32[]{:S(2)}, u32[]{:S(2)}) %collective-permute-start.4) | collective-permute-done | bytes 524320 | tf_op jit(solution)/shard_map/ppermute | solution.py:33
  56.3 5.1 %fusion.14 = bf16[4,256,1024]{2,1,0:T(8,128)(2,1)} fusion(s32[]{:T(128)S(6)} %select_n.27, bf16[1,256,1024]{2,1,0:T(8,128)(2,1)S(1)} %bitcast.143, bf16[1,256,1024]{2,1,0:T(8,128)(2,1)} %bitcast.13, bf16[1,256,1024]{2,1,0:T(8,128)(2,1)} %bitcast.14, bf16[1,256,1024]{2,1,0:T(8,128)(2,1)} %bitcast.15), kind=kLoop, calls=%fused_computation.38 | loop fusion | flops 7340032 | bytes 4194308 | tf_op jit(solution)/shard_map/jit(_roll_dynamic)/concatenate | solution.py:35
  61.4 14.5 %all-gather.6.cloned.1.call-done = bf16[3072,2,256]{2,1,0:T(2,128)(2,1)} async-done(((bf16[768,2,256]{2,1,0:T(2,128)(2,1)}), bf16[3072,2,256]{2,1,0:T(2,128)(2,1)}) %all-gather.6.cloned.1.call-update) | async-done | bytes 3145744 | tf_op jit(solution)/shard_map/all_gather | solution.py:92
  75.8 7.1 %fusion.32 = bf16[1024,2,256]{0,2,1:T(8,128)(2,1)S(1)} fusion(bf16[3072,1024,1]{1,0,2:T(8,128)(2,1)} %bitcast.118, bf16[3072,2,256]{2,1,0:T(2,128)(2,1)} %all-gather.6.cloned.1.call-done), kind=kOutput, calls=%fused_computation.81 | convolution fusion | flops 3221749760 | bytes 10485760 | tf_op jit(solution)/shard_map/tf,fjc->tjc/dot_general | solution.py:94
  83.1 0.8 multiply_reduce_fusion.1
  83.9 2.0 copy-done.1
  86.0 1.6 fusion.43
  87.9 4.8 %fusion.21 = bf16[4,256,1024]{2,1,0:T(8,128)(2,1)} fusion(s32[]{:T(128)S(6)} %select_n.27, bf16[1,256,1024]{2,1,0:T(8,128)(2,1)S(1)} %bitcast.127, bf16[1,256,1024]{2,1,0:T(8,128)(2,1)S(1)} %bitcast.144, bf16[1,256,1024]{2,1,0:T(8,128)(2,1)} %bitcast.5, bf16[1,256,1024]{2,1,0:T(8,128)(2,1)} %bitcast.6), kind=kLoop, calls=%fused_computation.45 | loop fusion | flops 7340032 | bytes 4194308 | tf_op jit(solution)/shard_map/jit(_roll_dynamic)/concatenate | solution.py:35
  92.6 0.9 fusion.4
  93.6 13.3 %all-gather.1 = f32[8,2,512]{2,1,0:T(2,128)S(1)} all-gather(f32[2,2,512]{2,1,0:T(2,128)S(1)} %pad_maximum_fusion.1), channel_id=3, replica_groups=mesh['groups'=2,'picks'=4,'heads'=4] {'picks'}, dimensions={0}, use_global_device_ids=true | all-gather | bytes 40960 | tf_op jit(solution)/shard_map/all_gather | solution.py:108
  106.9 7.8 %all-gather.10.cloned.1.call-done = bf16[8,512,128]{2,1,0:T(8,128)(2,1)} async-done(((bf16[2,512,128]{2,1,0:T(8,128)(2,1)}), bf16[8,512,128]{2,1,0:T(8,128)(2,1)}) %all-gather.10.cloned.1.call-update) | async-done | bytes 1048592 | tf_op jit(solution)/shard_map/all_gather | solution.py:107
  114.7 1.8 multiply_reduce_fusion.2
  116.7 0.9 collective-permute-start.6
  117.6 0.7 collective-permute-start.7
  118.6 5.6 %collective-permute-done.6 = bf16[256,512]{1,0:T(8,128)(2,1)S(1)} collective-permute-done((bf16[256,512]{1,0:T(8,128)(2,1)S(1)}, bf16[256,512]{1,0:T(8,128)(2,1)S(1)}, u32[]{:S(2)}, u32[]{:S(2)}) %collective-permute-start.6) | collective-permute-done | bytes 262176 | tf_op jit(solution)/shard_map/ppermute | solution.py:33
  124.2 6.7 %collective-permute-done.7 = bf16[256,512]{1,0:T(8,128)(2,1)S(1)} collective-permute-done((bf16[256,512]{1,0:T(8,128)(2,1)S(1)}, bf16[256,512]{1,0:T(8,128)(2,1)S(1)}, u32[]{:S(2)}, u32[]{:S(2)}) %collective-permute-start.7) | collective-permute-done | bytes 262176 | tf_op jit(solution)/shard_map/ppermute | solution.py:33
  131.1 2.2 %fusion.60 = bf16[4,256,512]{2,1,0:T(8,128)(2,1)S(1)} fusion(s32[]{:T(128)S(6)} %select_n.27, bf16[1,256,512]{2,1,0:T(8,128)(2,1)S(1)} %bitcast.133, bf16[1,256,512]{2,1,0:T(8,128)(2,1)S(1)} %bitcast.147, bf16[1,256,512]{2,1,0:T(8,128)(2,1)S(1)} %bitcast.148, bf16[1,256,512]{2,1,0:T(8,128)(2,1)} %bitcast.32), kind=kLoop, calls=%fused_computation.103 | loop fusion | flops 3670016 | bytes 2097156 | tf_op jit(solution)/shard_map/jit(_roll_dynamic)/concatenate | solution.py:35
  133.4 1.4 multiply_reduce_fusion.4
  134.8 1.1 fusion.38
  137.1 1.5 collective-permute-start.10
  138.9 4.0 %collective-permute-done.9 = bf16[256,512]{1,0:T(8,128)(2,1)S(1)} collective-permute-done((bf16[256,512]{1,0:T(8,128)(2,1)S(1)}, bf16[256,512]{1,0:T(8,128)(2,1)S(1)}, u32[]{:S(2)}, u32[]{:S(2)}) %collective-permute-start.9) | collective-permute-done | bytes 262176 | tf_op jit(solution)/shard_map/ppermute | solution.py:33
  142.9 8.3 %collective-permute-done.10 = bf16[256,512]{1,0:T(8,128)(2,1)S(1)} collective-permute-done((bf16[256,512]{1,0:T(8,128)(2,1)S(1)}, bf16[256,512]{1,0:T(8,128)(2,1)S(1)}, u32[]{:S(2)}, u32[]{:S(2)}) %collective-permute-start.10) | collective-permute-done | bytes 262176 | tf_op jit(solution)/shard_map/ppermute | solution.py:33
  151.3 1.2 fusion.53
  152.6 1.4 multiply_reduce_fusion.3
  154.0 1.3 copy-done.4
  155.3 0.8 fusion.42
  156.3 5.1 %convolution_convert_fusion.2 = bf16[1024,256]{0,1:T(8,128)(2,1)S(1)} fusion(bf16[3072,1024]{1,0:T(8,128)(2,1)} %bitcast.119, bf16[3072,256]{1,0:T(8,128)(2,1)} %all-gather.8.cloned.1.call-done), kind=kOutput, calls=%fused_computation.84 | convolution fusion | flops 1610874880 | bytes 8388608 | tf_op jit(solution)/shard_map/dot_general | solution.py:158
  161.3 0.8 fusion.3
  162.2 1.0 fusion.39
  163.4 0.9 collective-permute-done.12
  164.4 0.9 collective-permute-start.13
  165.3 0.9 multiply_reduce_fusion
  166.1 1.9 collective-permute-done.13
  168.6 1.2 multiply_convert_fusion.4
  170.2 3.1 %convolution_convert_fusion = bf16[3072,256]{1,0:T(8,128)(2,1)} fusion(bf16[3072,1024]{1,0:T(8,128)(2,1)S(1)} %bitcast.122, bf16[1024,256]{0,1:T(8,128)(2,1)S(1)} %bitcast.168), kind=kOutput, calls=%fused_computation.26 | convolution fusion | flops 1611399168 | bytes 8388608 | tf_op jit(solution)/shard_map/dot_general | solution.py:184
  173.4 1.9 constant_dynamic-slice_fusion
  175.2 32.4 %reduce-scatter.2.cloned.1.call-done = bf16[768,256]{1,0:T(8,128)(2,1)} async-done(((bf16[3072,256]{1,0:T(8,128)(2,1)}), bf16[768,256]{1,0:T(8,128)(2,1)}) %reduce-scatter.2.cloned.1.call-update) | async-done | bytes 393232 | tf_op jit(solution)/shard_map/reduce_scatter | solution.py:183
  207.6 1.9 convert_element_type.100
  (72 shorter events, 4.4 us)
Async XLA Ops:
  7.2 127.6 %copy-start = (bf16[3,1024,256]{2,1,0:T(8,128)(2,1)S(1)}, bf16[3,1024,256]{2,1,0:T(8,128)(2,1)}, u32[]{:S(2)}) copy-start(bf16[3,1024,256]{2,1,0:T(8,128)(2,1)} %param.23) | copy-start | bytes 4718596
  7.2 8.1 %copy-start.9 = (f32[3,1024]{1,0:T(4,128)S(1)}, f32[3,1024]{1,0:T(4,128)}, u32[]{:S(2)}) copy-start(f32[3,1024]{1,0:T(4,128)} %param.16) | copy-start | bytes 36868
  7.2 68.7 %all-gather.6.cloned.1.call-start = ((), (), s32[]{:S(2)}) async-start(), calls=%async_computation.1 | async-start | bytes 3932160 | tf_op jit(solution)/shard_map/all_gather | solution.py:92
  7.9 106.8 %all-gather.10.cloned.1.call-start = ((), (), s32[]{:S(2)}) async-start(), calls=%async_computation.4 | async-start | bytes 1310720 | tf_op jit(solution)/shard_map/all_gather | solution.py:107
  9.2 78.6 %collective-permute-start = (bf16[256,1024]{1,0:T(8,128)(2,1)S(1)}, bf16[256,1024]{1,0:T(8,128)(2,1)S(1)}, u32[]{:S(2)}, u32[]{:S(2)}) collective-permute-start(bf16[256,1024]{1,0:T(8,128)(2,1)S(1)} %bitcast.124), channel_id=1, source_target_pairs={{0,3},{1,0},{2,1},{3,2},{4,7},{5,4},{6,5},{7,6},{8,11},{9,8},{10,9... | collective-permute-start | bytes 1572872 | tf_op jit(solution)/shard_map/ppermute | solution.py:33
  11.7 76.2 %collective-permute-start.1 = (bf16[256,1024]{1,0:T(8,128)(2,1)S(1)}, bf16[256,1024]{1,0:T(8,128)(2,1)}, u32[]{:S(2)}, u32[]{:S(2)}) collective-permute-start(bf16[256,1024]{1,0:T(8,128)(2,1)S(1)} %bitcast.125), channel_id=1, source_target_pairs={{0,2},{1,3},{2,0},{3,1},{4,6},{5,7},{6,4},{7,5},{8,10},{9,11},{10,... | collective-permute-start | bytes 1572872 | tf_op jit(solution)/shard_map/ppermute | solution.py:33
  12.3 34.1 %collective-permute-start.3 = (bf16[256,1024]{1,0:T(8,128)(2,1)}, bf16[256,1024]{1,0:T(8,128)(2,1)}, u32[]{:S(2)}, u32[]{:S(2)}) collective-permute-start(bf16[256,1024]{1,0:T(8,128)(2,1)} %param.21), channel_id=1, source_target_pairs={{0,3},{1,0},{2,1},{3,2},{4,7},{5,4},{6,5},{7,6},{8,11},{9,8},{10,9... | collective-permute-start | bytes 1572872 | tf_op jit(solution)/shard_map/ppermute | solution.py:33
  12.4 43.9 %collective-permute-start.4 = (bf16[256,1024]{1,0:T(8,128)(2,1)}, bf16[256,1024]{1,0:T(8,128)(2,1)}, u32[]{:S(2)}, u32[]{:S(2)}) collective-permute-start(bf16[256,1024]{1,0:T(8,128)(2,1)} %param.21), channel_id=1, source_target_pairs={{0,2},{1,3},{2,0},{3,1},{4,6},{5,7},{6,4},{7,5},{8,10},{9,11},{10,... | collective-permute-start | bytes 1572872 | tf_op jit(solution)/shard_map/ppermute | solution.py:33
  14.1 42.2 %collective-permute-start.5 = (bf16[256,1024]{1,0:T(8,128)(2,1)}, bf16[256,1024]{1,0:T(8,128)(2,1)}, u32[]{:S(2)}, u32[]{:S(2)}) collective-permute-start(bf16[256,1024]{1,0:T(8,128)(2,1)} %param.21), channel_id=1, source_target_pairs={{0,1},{1,2},{2,3},{3,0},{4,5},{5,6},{6,7},{7,4},{8,9},{9,10},{10,1... | collective-permute-start | bytes 1572872 | tf_op jit(solution)/shard_map/ppermute | solution.py:33
  38.2 18.1 %copy-start.8 = (bf16[256,1024]{1,0:T(8,128)(2,1)S(1)}, bf16[256,1024]{1,0:T(8,128)(2,1)}, u32[]{:S(2)}) copy-start(bf16[256,1024]{1,0:T(8,128)(2,1)} %param.21) | copy-start | bytes 1572868
  46.4 41.4 %collective-permute-start.2 = (bf16[256,1024]{1,0:T(8,128)(2,1)S(1)}, bf16[256,1024]{1,0:T(8,128)(2,1)}, u32[]{:S(2)}, u32[]{:S(2)}) collective-permute-start(bf16[256,1024]{1,0:T(8,128)(2,1)S(1)} %bitcast.126), channel_id=1, source_target_pairs={{0,1},{1,2},{2,3},{3,0},{4,5},{5,6},{6,7},{7,4},{8,9},{9,10},{10,1... | collective-permute-start | bytes 1572872 | tf_op jit(solution)/shard_map/ppermute | solution.py:33
  83.9 2.0 copy-start.1
  87.6 68.7 %all-gather.8.cloned.1.call-start = ((), (), s32[]{:S(2)}) async-start(), calls=%async_computation.2 | async-start | bytes 1966080 | tf_op jit(solution)/shard_map/all_gather | solution.py:124
  87.8 4.8 %copy-start.2 = (f32[2,512,1024]{2,1,0:T(8,128)S(1)}, f32[2,512,1024]{2,1,0:T(8,128)}, u32[]{:S(2)}) copy-start(f32[2,512,1024]{2,1,0:T(8,128)} %copy-done.1) | copy-start | bytes 12582916
  93.5 24.9 %copy-start.10 = (f32[2,1024]{1,0:T(2,128)S(1)}, f32[2,1024]{1,0:T(2,128)}, u32[]{:S(2)}) copy-start(f32[2,1024]{1,0:T(2,128)} %param.22) | copy-start | bytes 24580
  116.7 16.7 %copy-start.6 = (bf16[512,1024]{1,0:T(8,128)(2,1)S(1)}, bf16[512,1024]{1,0:T(8,128)(2,1)}, u32[]{:S(2)}) copy-start(bf16[512,1024]{1,0:T(8,128)(2,1)} %param.19) | copy-start | bytes 3145732
  116.7 7.5 %collective-permute-start.6 = (bf16[256,512]{1,0:T(8,128)(2,1)S(1)}, bf16[256,512]{1,0:T(8,128)(2,1)S(1)}, u32[]{:S(2)}, u32[]{:S(2)}) collective-permute-start(bf16[256,512]{1,0:T(8,128)(2,1)S(1)} %bitcast.130), channel_id=1, source_target_pairs={{0,3},{1,0},{2,1},{3,2},{4,7},{5,4},{6,5},{7,6},{8,11},{9,8},{10,9... | collective-permute-start | bytes 786440 | tf_op jit(solution)/shard_map/ppermute | solution.py:33
  117.6 13.3 %collective-permute-start.7 = (bf16[256,512]{1,0:T(8,128)(2,1)S(1)}, bf16[256,512]{1,0:T(8,128)(2,1)S(1)}, u32[]{:S(2)}, u32[]{:S(2)}) collective-permute-start(bf16[256,512]{1,0:T(8,128)(2,1)S(1)} %bitcast.131), channel_id=1, source_target_pairs={{0,2},{1,3},{2,0},{3,1},{4,6},{5,7},{6,4},{7,5},{8,10},{9,11},{10,... | collective-permute-start | bytes 786440 | tf_op jit(solution)/shard_map/ppermute | solution.py:33
  118.3 12.8 %collective-permute-start.8 = (bf16[256,512]{1,0:T(8,128)(2,1)S(1)}, bf16[256,512]{1,0:T(8,128)(2,1)}, u32[]{:S(2)}, u32[]{:S(2)}) collective-permute-start(bf16[256,512]{1,0:T(8,128)(2,1)S(1)} %bitcast.132), channel_id=1, source_target_pairs={{0,1},{1,2},{2,3},{3,0},{4,5},{5,6},{6,7},{7,4},{8,9},{9,10},{10,1... | collective-permute-start | bytes 786440 | tf_op jit(solution)/shard_map/ppermute | solution.py:33
  118.5 89.1 %reduce-scatter.2.cloned.1.call-start = ((), (), s32[]{:S(2)}) async-start(), calls=%async_computation.3 | async-start | bytes 1966080 | tf_op jit(solution)/shard_map/reduce_scatter | solution.py:183
  118.6 14.8 %copy-start.3 = (bf16[4,256,1024]{2,1,0:T(8,128)(2,1)S(1)}, bf16[4,256,1024]{2,1,0:T(8,128)(2,1)}, u32[]{:S(2)}) copy-start(bf16[4,256,1024]{2,1,0:T(8,128)(2,1)} %fusion.14) | copy-start | bytes 6291460
  136.5 2.3 %copy-start.11 = (s32[1024]{0:T(1024)S(1)}, s32[1024]{0:T(1024)}, u32[]{:S(2)}) copy-start(s32[1024]{0:T(1024)} %param.17) | copy-start | bytes 12292
  136.5 2.3 %copy-start.13 = (f32[64]{0:T(128)S(1)}, f32[64]{0:T(128)}, u32[]{:S(2)}) copy-start(f32[64]{0:T(128)} %param.18) | copy-start | bytes 772
  137.1 15.5 %copy-start.5 = (bf16[4,256,1024]{2,1,0:T(8,128)(2,1)S(1)}, bf16[4,256,1024]{2,1,0:T(8,128)(2,1)}, u32[]{:S(2)}) copy-start(bf16[4,256,1024]{2,1,0:T(8,128)(2,1)} %fusion.21) | copy-start | bytes 6291460
  137.1 5.8 %collective-permute-start.9 = (bf16[256,512]{1,0:T(8,128)(2,1)S(1)}, bf16[256,512]{1,0:T(8,128)(2,1)S(1)}, u32[]{:S(2)}, u32[]{:S(2)}) collective-permute-start(bf16[256,512]{1,0:T(8,128)(2,1)S(1)} %bitcast.149), channel_id=1, source_target_pairs={{0,3},{1,0},{2,1},{3,2},{4,7},{5,4},{6,5},{7,6},{8,11},{9,8},{10,9... | collective-permute-start | bytes 786440 | tf_op jit(solution)/shard_map/ppermute | solution.py:33
  137.1 14.0 %collective-permute-start.10 = (bf16[256,512]{1,0:T(8,128)(2,1)S(1)}, bf16[256,512]{1,0:T(8,128)(2,1)S(1)}, u32[]{:S(2)}, u32[]{:S(2)}) collective-permute-start(bf16[256,512]{1,0:T(8,128)(2,1)S(1)} %bitcast.150), channel_id=1, source_target_pairs={{0,2},{1,3},{2,0},{3,1},{4,6},{5,7},{6,4},{7,5},{8,10},{9,11},{10,... | collective-permute-start | bytes 786440 | tf_op jit(solution)/shard_map/ppermute | solution.py:33
  138.6 12.7 %collective-permute-start.11 = (bf16[256,512]{1,0:T(8,128)(2,1)S(1)}, bf16[256,512]{1,0:T(8,128)(2,1)S(1)}, u32[]{:S(2)}, u32[]{:S(2)}) collective-permute-start(bf16[256,512]{1,0:T(8,128)(2,1)S(1)} %bitcast.151), channel_id=1, source_target_pairs={{0,1},{1,2},{2,3},{3,0},{4,5},{5,6},{6,7},{7,4},{8,9},{9,10},{10,1... | collective-permute-start | bytes 786440 | tf_op jit(solution)/shard_map/ppermute | solution.py:33
  152.6 2.8 %copy-start.7 = (bf16[2,1024,256]{2,1,0:T(8,128)(2,1)S(1)}, bf16[2,1024,256]{2,1,0:T(8,128)(2,1)}, u32[]{:S(2)}) copy-start(bf16[2,1024,256]{2,1,0:T(8,128)(2,1)} %param.25) | copy-start | bytes 3145732
  154.0 1.4 copy-start.4
  161.3 0.9 copy-start.12
  163.2 1.2 collective-permute-start.12
  164.4 3.6 %collective-permute-start.13 = (f32[1024]{0:T(1024)S(1)}, f32[1024]{0:T(1024)S(1)}, u32[]{:S(2)}, u32[]{:S(2)}) collective-permute-start(f32[1024]{0:T(1024)S(1)} %add.61), channel_id=1, source_target_pairs={{0,2},{1,3},{2,0},{3,1},{4,6},{5,7},{6,4},{7,5},{8,10},{9,11},{10,... | collective-permute-start | bytes 12296 | tf_op jit(solution)/shard_map/ppermute | solution.py:61
  165.3 4.6 %slice-start = ((s8[6291456]{0:T(1024)(128)(4,1)}), s8[4194304]{0:T(1024)(128)(4,1)S(1)}, s32[]{:S(2)}) async-start(s8[6291456]{0:T(1024)(128)(4,1)} %bitcast.120), calls=%async_computation.5 | async-start | bytes 8388608
  168.6 1.6 slice-start.1
Sparse Core Ops, SparseCore 0:
  9.6 66.2 all-gather.5
  87.7 26.9 all-gather.9
  118.7 36.9 all-gather.7
  173.5 34.0 reduce-scatter.1

commit v14 on v13

--- a/solution.py
+++ b/solution.py
@@ -57,8 +57,10 @@
 def pair_sum(x, axis, n):
     if n != 4:
         return lax.psum(x, axis)
-    x = x + lax.ppermute(x, axis, [(k, k ^ 1) for k in range(n)])
-    return x + lax.ppermute(x, axis, [(k, k ^ 2) for k in range(n)])
+    idx = lax.axis_index(axis)
+    got = [x] + [lax.ppermute(x, axis, [(k, k ^ m) for k in range(n)]) for m in range(1, n)]
+    terms = jnp.take(jnp.stack(got), jnp.arange(n) ^ idx, axis=0)
+    return (terms[0] + terms[1]) + (terms[2] + terms[3])
 
 
 def on_device(

time: 216 us -> 220 us (1.019)
  matrix products: 26.8 us -> 31.6 us
    dot_general x1, matrix products: 3.14 us -> 5.78 us  [on_device(): jnp.dot(enc.T, dquery, preferred_element_type=jnp.float32)]
    another operation x1 -> x2, other arithmetic: 22.8 us -> 22.9 us
  transfers between devices with their start and end apart: 18 -> 19, of which waited for: 13 -> 14; matrix products, arithmetic and copies ran while one was open for 28% -> 28% of each run, Pallas kernels for 0% -> 0%
where the time goes in v14:
time: 220 us; the launch traced here: 219 us
  waiting for transfers between devices  95.4 us (43%)
  other arithmetic  45.2 us (21%)
  matrix products  31.6 us (14%)
  between operations  14.2 us (6%)
  blocking collectives  13.3 us (6%)
  starting transfers between devices  11.7 us (5%)
  local copies, waits for them, and re-layouts  7.67 us (3%)
    ppermute x12, waiting for transfers between devices, ring_gather(): blocks.append(lax.ppermute(x, axis, [(i, (i - s) % n) for i in range(n)]))  38.7 us
    reduce_scatter x1, waiting for transfers between devices, on_device(): lax.psum_scatter(jnp.dot(enc.T, dquery, preferred_element_type=jnp.float3...  31.8 us
    another operation x1, other arithmetic  22.8 us
    all_gather x1, waiting for transfers between devices, on_device(): piece = lax.all_gather(kv_weight, 'picks', axis=0, tiled=True)  14.5 us
    all_gather x1, blocking collectives, on_device(): lax.all_gather(jnp.stack([top, total]), 'picks', axis=0, tiled=False)  13.3 us
    concatenate x4, other arithmetic, ring_gather(): ordered = jnp.roll(flipped, idx, axis=0)  13.3 us
    ppermute x12, starting transfers between devices, ring_gather(): blocks.append(lax.ppermute(x, axis, [(i, (i - s) % n) for i in range(n)]))  9.45 us
    all_gather x1, waiting for transfers between devices, on_device(): lax.all_gather(numer.astype(jnp.bfloat16), 'picks', axis=0, tiled=False)  7.69 us
  transfers between devices with their start and end apart: 19, of which 14 were waited for; matrix products, arithmetic and copies ran while one was open for 28% of the time, Pallas kernels for 0%

profile of v14, /device:TPU:0, one launch (start us, length us, event | category | flops | bytes accessed | tf_op | source)
XLA Modules:
  0.0 219.1 jit_solution(12278226778303111203)
XLA Ops:
  7.2 0.7 all-gather.6.cloned.1.call-update
  8.0 1.2 copy.60
  9.2 2.4 %collective-permute-start = (bf16[256,1024]{1,0:T(8,128)(2,1)S(1)}, bf16[256,1024]{1,0:T(8,128)(2,1)S(1)}, u32[]{:S(2)}, u32[]{:S(2)}) collective-permute-start(bf16[256,1024]{1,0:T(8,128)(2,1)S(1)} %bitcast.129), channel_id=1, source_target_pairs={{0,3},{1,0},{2,1},{3,2},{4,7},{5,4},{6,5},{7,6},{8,11},{9,8},{10,9... | collective-permute-start | bytes 1572872 | tf_op jit(solution)/shard_map/ppermute | solution.py:33
  11.7 0.6 collective-permute-start.1
  12.4 1.7 collective-permute-start.4
  14.1 1.0 constant_dynamic-slice_fusion.1
  15.3 22.8 %fusion = (bf16[3,512,1024]{2,1,0:T(8,128)(2,1)S(1)}, bf16[3,512,1024]{2,1,0:T(8,128)(2,1)S(1)}) fusion(f32[3,1024]{1,0:T(4,128)S(1)} %copy-done.10, f32[512]{0:T(512)S(1)} %maximum_multiply_fusion), kind=kLoop, calls=%fused_computation.3 | loop fusion | flops 4718592 | bytes 6305792 | tf_op jit(solution)/shard_map/convert
  38.2 3.2 %pad_maximum_fusion = bf16[6,512,1024]{2,1,0:T(8,128)(2,1)} fusion(bf16[3,512,1024]{2,1,0:T(8,128)(2,1)S(1)} %get-tuple-element.27, bf16[3,512,1024]{2,1,0:T(8,128)(2,1)S(1)} %get-tuple-element.26), kind=kLoop, calls=%fused_computation.5 | loop fusion | flops 3145728 | bytes 12582912 | tf_op jit(solution)/shard_map/concatenate | solution.py:21
  41.4 5.1 %collective-permute-done.3 = bf16[256,1024]{1,0:T(8,128)(2,1)} collective-permute-done((bf16[256,1024]{1,0:T(8,128)(2,1)}, bf16[256,1024]{1,0:T(8,128)(2,1)}, u32[]{:S(2)}, u32[]{:S(2)}) %collective-permute-start.3) | collective-permute-done | bytes 524320 | tf_op jit(solution)/shard_map/ppermute | solution.py:33
  46.4 1.1 collective-permute-start.2
  47.5 8.8 %collective-permute-done.4 = bf16[256,1024]{1,0:T(8,128)(2,1)} collective-permute-done((bf16[256,1024]{1,0:T(8,128)(2,1)}, bf16[256,1024]{1,0:T(8,128)(2,1)}, u32[]{:S(2)}, u32[]{:S(2)}) %collective-permute-start.4) | collective-permute-done | bytes 524320 | tf_op jit(solution)/shard_map/ppermute | solution.py:33
  56.3 5.1 %fusion.14 = bf16[4,256,1024]{2,1,0:T(8,128)(2,1)} fusion(s32[]{:T(128)S(6)} %select_n.50, bf16[1,256,1024]{2,1,0:T(8,128)(2,1)S(1)} %bitcast.148, bf16[1,256,1024]{2,1,0:T(8,128)(2,1)} %bitcast.13, bf16[1,256,1024]{2,1,0:T(8,128)(2,1)} %bitcast.14, bf16[1,256,1024]{2,1,0:T(8,128)(2,1)} %bitcast.15), kind=kLoop, calls=%fused_computation.39 | loop fusion | flops 7340032 | bytes 4194308 | tf_op jit(solution)/shard_map/jit(_roll_dynamic)/concatenate | solution.py:35
  61.3 14.5 %all-gather.6.cloned.1.call-done = bf16[3072,2,256]{2,1,0:T(2,128)(2,1)} async-done(((bf16[768,2,256]{2,1,0:T(2,128)(2,1)}), bf16[3072,2,256]{2,1,0:T(2,128)(2,1)}) %all-gather.6.cloned.1.call-update) | async-done | bytes 3145744 | tf_op jit(solution)/shard_map/all_gather | solution.py:94
  75.8 7.1 %fusion.32 = bf16[1024,2,256]{0,2,1:T(8,128)(2,1)S(1)} fusion(bf16[3072,1024,1]{1,0,2:T(8,128)(2,1)} %bitcast.125, bf16[3072,2,256]{2,1,0:T(2,128)(2,1)} %all-gather.6.cloned.1.call-done), kind=kOutput, calls=%fused_computation.82 | convolution fusion | flops 3221749760 | bytes 10485760 | tf_op jit(solution)/shard_map/tf,fjc->tjc/dot_general | solution.py:96
  83.1 0.8 multiply_reduce_fusion.1
  83.9 2.0 copy-done.2
  86.0 1.6 fusion.45
  87.8 4.8 %fusion.21 = bf16[4,256,1024]{2,1,0:T(8,128)(2,1)} fusion(s32[]{:T(128)S(6)} %select_n.50, bf16[1,256,1024]{2,1,0:T(8,128)(2,1)S(1)} %bitcast.132, bf16[1,256,1024]{2,1,0:T(8,128)(2,1)S(1)} %bitcast.149, bf16[1,256,1024]{2,1,0:T(8,128)(2,1)} %bitcast.5, bf16[1,256,1024]{2,1,0:T(8,128)(2,1)} %bitcast.6), kind=kLoop, calls=%fused_computation.46 | loop fusion | flops 7340032 | bytes 4194308 | tf_op jit(solution)/shard_map/jit(_roll_dynamic)/concatenate | solution.py:35
  92.6 0.9 fusion.4
  93.6 13.3 %all-gather.1 = f32[8,2,512]{2,1,0:T(2,128)S(1)} all-gather(f32[2,2,512]{2,1,0:T(2,128)S(1)} %pad_maximum_fusion.2), channel_id=3, replica_groups=mesh['groups'=2,'picks'=4,'heads'=4] {'picks'}, dimensions={0}, use_global_device_ids=true | all-gather | bytes 40960 | tf_op jit(solution)/shard_map/all_gather | solution.py:110
  106.9 7.7 %all-gather.10.cloned.1.call-done = bf16[8,512,128]{2,1,0:T(8,128)(2,1)} async-done(((bf16[2,512,128]{2,1,0:T(8,128)(2,1)}), bf16[8,512,128]{2,1,0:T(8,128)(2,1)}) %all-gather.10.cloned.1.call-update) | async-done | bytes 1048592 | tf_op jit(solution)/shard_map/all_gather | solution.py:109
  114.6 1.8 multiply_reduce_fusion.2
  116.7 1.0 collective-permute-start.6
  117.6 0.6 collective-permute-start.7
  118.5 5.7 %collective-permute-done.6 = bf16[256,512]{1,0:T(8,128)(2,1)S(1)} collective-permute-done((bf16[256,512]{1,0:T(8,128)(2,1)S(1)}, bf16[256,512]{1,0:T(8,128)(2,1)S(1)}, u32[]{:S(2)}, u32[]{:S(2)}) %collective-permute-start.6) | collective-permute-done | bytes 262176 | tf_op jit(solution)/shard_map/ppermute | solution.py:33
  124.2 6.7 %collective-permute-done.7 = bf16[256,512]{1,0:T(8,128)(2,1)S(1)} collective-permute-done((bf16[256,512]{1,0:T(8,128)(2,1)S(1)}, bf16[256,512]{1,0:T(8,128)(2,1)S(1)}, u32[]{:S(2)}, u32[]{:S(2)}) %collective-permute-start.7) | collective-permute-done | bytes 262176 | tf_op jit(solution)/shard_map/ppermute | solution.py:33
  131.1 2.2 %fusion.62 = bf16[4,256,512]{2,1,0:T(8,128)(2,1)S(1)} fusion(s32[]{:T(128)S(6)} %select_n.50, bf16[1,256,512]{2,1,0:T(8,128)(2,1)S(1)} %bitcast.138, bf16[1,256,512]{2,1,0:T(8,128)(2,1)S(1)} %bitcast.152, bf16[1,256,512]{2,1,0:T(8,128)(2,1)S(1)} %bitcast.157, bf16[1,256,512]{2,1,0:T(8,128)(2,1)} %bitcast.32), kind=kLoop, calls=%fused_computation.106 | loop fusion | flops 3670016 | bytes 2097156 | tf_op jit(solution)/shard_map/jit(_roll_dynamic)/concatenate | solution.py:35
  133.3 1.4 multiply_reduce_fusion.4
  134.7 1.1 fusion.40
  137.1 1.5 collective-permute-start.10
  138.9 3.8 %collective-permute-done.9 = bf16[256,512]{1,0:T(8,128)(2,1)S(1)} collective-permute-done((bf16[256,512]{1,0:T(8,128)(2,1)S(1)}, bf16[256,512]{1,0:T(8,128)(2,1)S(1)}, u32[]{:S(2)}, u32[]{:S(2)}) %collective-permute-start.9) | collective-permute-done | bytes 262176 | tf_op jit(solution)/shard_map/ppermute | solution.py:33
  142.7 8.4 %collective-permute-done.10 = bf16[256,512]{1,0:T(8,128)(2,1)S(1)} collective-permute-done((bf16[256,512]{1,0:T(8,128)(2,1)S(1)}, bf16[256,512]{1,0:T(8,128)(2,1)S(1)}, u32[]{:S(2)}, u32[]{:S(2)}) %collective-permute-start.10) | collective-permute-done | bytes 262176 | tf_op jit(solution)/shard_map/ppermute | solution.py:33
  151.3 1.2 fusion.55
  152.6 1.4 multiply_reduce_fusion.3
  154.0 0.9 fusion.44
  155.7 5.1 %convolution_convert_fusion.2 = bf16[1024,256]{0,1:T(8,128)(2,1)S(1)} fusion(bf16[3072,1024]{1,0:T(8,128)(2,1)} %bitcast.126, bf16[3072,256]{1,0:T(8,128)(2,1)} %all-gather.8.cloned.1.call-done), kind=kOutput, calls=%fused_computation.86 | convolution fusion | flops 1610874880 | bytes 8388608 | tf_op jit(solution)/shard_map/dot_general | solution.py:160
  160.8 0.8 fusion.3
  161.6 1.0 fusion.41
  162.6 0.8 collective-permute-start.14
  163.4 0.7 collective-permute-start.13
  164.5 0.9 multiply_reduce_fusion
  165.7 1.3 collective-permute-done.13
  167.1 0.6 gather_fusion
  167.7 3.4 %fusion.39 = bf16[2,128,1024]{2,1,0:T(8,128)(2,1)S(1)} fusion(bf16[512,2,128]{0,2,1:T(8,128)(2,1)S(1)} %bitcast.143, f32[2,1024]{1,0:T(2,128)S(1)} %multiply_reduce_fusion, f32[2,512]{1,0:T(2,128)S(1)} %bitcast.167, f32[1024]{0:T(1024)S(1)} %subtract_multiply_fusion, f32[2,1024,512]{1,2,0:T(8,128)} %copy-done.1, f32[2,1024]{1,0:T(2,128)S(1)} %get-tuple-element.38), kind=kOutput, calls=%fused_computation.87 | convolution fusion | flops 274202624 | bytes 5005312 | tf_op jit(solution)/shard_map/htl,lhc->thc/dot_general | solution.py:181
  171.2 5.8 %convolution_convert_fusion = bf16[3072,256]{1,0:T(8,128)(2,1)} fusion(bf16[3072,1024]{1,0:T(8,128)(2,1)} %bitcast.127, bf16[1024,256]{0,1:T(8,128)(2,1)S(1)} %bitcast.179), kind=kOutput, calls=%fused_computation.27 | convolution fusion | flops 1611399168 | bytes 8388608 | tf_op jit(solution)/shard_map/dot_general | solution.py:186
  177.0 1.9 constant_dynamic-slice_fusion
  178.8 31.8 %reduce-scatter.2.cloned.1.call-done = bf16[768,256]{1,0:T(8,128)(2,1)} async-done(((bf16[3072,256]{1,0:T(8,128)(2,1)}), bf16[768,256]{1,0:T(8,128)(2,1)}) %reduce-scatter.2.cloned.1.call-update) | async-done | bytes 393232 | tf_op jit(solution)/shard_map/reduce_scatter | solution.py:185
  210.6 1.9 convert_element_type.100
  (79 shorter events, 4.8 us)
Async XLA Ops:
  7.2 127.5 %copy-start = (bf16[3,1024,256]{2,1,0:T(8,128)(2,1)S(1)}, bf16[3,1024,256]{2,1,0:T(8,128)(2,1)}, u32[]{:S(2)}) copy-start(bf16[3,1024,256]{2,1,0:T(8,128)(2,1)} %param.23) | copy-start | bytes 4718596
  7.2 8.1 %copy-start.10 = (f32[3,1024]{1,0:T(4,128)S(1)}, f32[3,1024]{1,0:T(4,128)}, u32[]{:S(2)}) copy-start(f32[3,1024]{1,0:T(4,128)} %param.16) | copy-start | bytes 36868
  7.2 68.7 %all-gather.6.cloned.1.call-start = ((), (), s32[]{:S(2)}) async-start(), calls=%async_computation.1 | async-start | bytes 3932160 | tf_op jit(solution)/shard_map/all_gather | solution.py:94
  7.9 106.7 %all-gather.10.cloned.1.call-start = ((), (), s32[]{:S(2)}) async-start(), calls=%async_computation.4 | async-start | bytes 1310720 | tf_op jit(solution)/shard_map/all_gather | solution.py:109
  9.2 78.6 %collective-permute-start = (bf16[256,1024]{1,0:T(8,128)(2,1)S(1)}, bf16[256,1024]{1,0:T(8,128)(2,1)S(1)}, u32[]{:S(2)}, u32[]{:S(2)}) collective-permute-start(bf16[256,1024]{1,0:T(8,128)(2,1)S(1)} %bitcast.129), channel_id=1, source_target_pairs={{0,3},{1,0},{2,1},{3,2},{4,7},{5,4},{6,5},{7,6},{8,11},{9,8},{10,9... | collective-permute-start | bytes 1572872 | tf_op jit(solution)/shard_map/ppermute | solution.py:33
  11.7 76.2 %collective-permute-start.1 = (bf16[256,1024]{1,0:T(8,128)(2,1)S(1)}, bf16[256,1024]{1,0:T(8,128)(2,1)}, u32[]{:S(2)}, u32[]{:S(2)}) collective-permute-start(bf16[256,1024]{1,0:T(8,128)(2,1)S(1)} %bitcast.130), channel_id=1, source_target_pairs={{0,2},{1,3},{2,0},{3,1},{4,6},{5,7},{6,4},{7,5},{8,10},{9,11},{10,... | collective-permute-start | bytes 1572872 | tf_op jit(solution)/shard_map/ppermute | solution.py:33
  12.3 34.1 %collective-permute-start.3 = (bf16[256,1024]{1,0:T(8,128)(2,1)}, bf16[256,1024]{1,0:T(8,128)(2,1)}, u32[]{:S(2)}, u32[]{:S(2)}) collective-permute-start(bf16[256,1024]{1,0:T(8,128)(2,1)} %param.21), channel_id=1, source_target_pairs={{0,3},{1,0},{2,1},{3,2},{4,7},{5,4},{6,5},{7,6},{8,11},{9,8},{10,9... | collective-permute-start | bytes 1572872 | tf_op jit(solution)/shard_map/ppermute | solution.py:33
  12.4 43.9 %collective-permute-start.4 = (bf16[256,1024]{1,0:T(8,128)(2,1)}, bf16[256,1024]{1,0:T(8,128)(2,1)}, u32[]{:S(2)}, u32[]{:S(2)}) collective-permute-start(bf16[256,1024]{1,0:T(8,128)(2,1)} %param.21), channel_id=1, source_target_pairs={{0,2},{1,3},{2,0},{3,1},{4,6},{5,7},{6,4},{7,5},{8,10},{9,11},{10,... | collective-permute-start | bytes 1572872 | tf_op jit(solution)/shard_map/ppermute | solution.py:33
  14.1 42.2 %collective-permute-start.5 = (bf16[256,1024]{1,0:T(8,128)(2,1)}, bf16[256,1024]{1,0:T(8,128)(2,1)}, u32[]{:S(2)}, u32[]{:S(2)}) collective-permute-start(bf16[256,1024]{1,0:T(8,128)(2,1)} %param.21), channel_id=1, source_target_pairs={{0,1},{1,2},{2,3},{3,0},{4,5},{5,6},{6,7},{7,4},{8,9},{9,10},{10,1... | collective-permute-start | bytes 1572872 | tf_op jit(solution)/shard_map/ppermute | solution.py:33
  38.2 18.1 %copy-start.9 = (bf16[256,1024]{1,0:T(8,128)(2,1)S(1)}, bf16[256,1024]{1,0:T(8,128)(2,1)}, u32[]{:S(2)}) copy-start(bf16[256,1024]{1,0:T(8,128)(2,1)} %param.21) | copy-start | bytes 1572868
  46.4 41.4 %collective-permute-start.2 = (bf16[256,1024]{1,0:T(8,128)(2,1)S(1)}, bf16[256,1024]{1,0:T(8,128)(2,1)}, u32[]{:S(2)}, u32[]{:S(2)}) collective-permute-start(bf16[256,1024]{1,0:T(8,128)(2,1)S(1)} %bitcast.131), channel_id=1, source_target_pairs={{0,1},{1,2},{2,3},{3,0},{4,5},{5,6},{6,7},{7,4},{8,9},{9,10},{10,1... | collective-permute-start | bytes 1572872 | tf_op jit(solution)/shard_map/ppermute | solution.py:33
  83.9 2.0 copy-start.2
  87.6 68.1 %all-gather.8.cloned.1.call-start = ((), (), s32[]{:S(2)}) async-start(), calls=%async_computation.2 | async-start | bytes 1966080 | tf_op jit(solution)/shard_map/all_gather | solution.py:126
  87.8 4.8 %copy-start.3 = (f32[2,512,1024]{2,1,0:T(8,128)S(1)}, f32[2,512,1024]{2,1,0:T(8,128)}, u32[]{:S(2)}) copy-start(f32[2,512,1024]{2,1,0:T(8,128)} %copy-done.2) | copy-start | bytes 12582916
  93.6 24.9 %copy-start.12 = (f32[2,1024]{1,0:T(2,128)S(1)}, f32[2,1024]{1,0:T(2,128)}, u32[]{:S(2)}) copy-start(f32[2,1024]{1,0:T(2,128)} %param.22) | copy-start | bytes 24580
  116.6 16.7 %copy-start.7 = (bf16[512,1024]{1,0:T(8,128)(2,1)S(1)}, bf16[512,1024]{1,0:T(8,128)(2,1)}, u32[]{:S(2)}) copy-start(bf16[512,1024]{1,0:T(8,128)(2,1)} %param.19) | copy-start | bytes 3145732
  116.7 7.5 %collective-permute-start.6 = (bf16[256,512]{1,0:T(8,128)(2,1)S(1)}, bf16[256,512]{1,0:T(8,128)(2,1)S(1)}, u32[]{:S(2)}, u32[]{:S(2)}) collective-permute-start(bf16[256,512]{1,0:T(8,128)(2,1)S(1)} %bitcast.135), channel_id=1, source_target_pairs={{0,3},{1,0},{2,1},{3,2},{4,7},{5,4},{6,5},{7,6},{8,11},{9,8},{10,9... | collective-permute-start | bytes 786440 | tf_op jit(solution)/shard_map/ppermute | solution.py:33
  117.6 13.2 %collective-permute-start.7 = (bf16[256,512]{1,0:T(8,128)(2,1)S(1)}, bf16[256,512]{1,0:T(8,128)(2,1)S(1)}, u32[]{:S(2)}, u32[]{:S(2)}) collective-permute-start(bf16[256,512]{1,0:T(8,128)(2,1)S(1)} %bitcast.136), channel_id=1, source_target_pairs={{0,2},{1,3},{2,0},{3,1},{4,6},{5,7},{6,4},{7,5},{8,10},{9,11},{10,... | collective-permute-start | bytes 786440 | tf_op jit(solution)/shard_map/ppermute | solution.py:33
  118.3 12.8 %collective-permute-start.8 = (bf16[256,512]{1,0:T(8,128)(2,1)S(1)}, bf16[256,512]{1,0:T(8,128)(2,1)}, u32[]{:S(2)}, u32[]{:S(2)}) collective-permute-start(bf16[256,512]{1,0:T(8,128)(2,1)S(1)} %bitcast.137), channel_id=1, source_target_pairs={{0,1},{1,2},{2,3},{3,0},{4,5},{5,6},{6,7},{7,4},{8,9},{9,10},{10,1... | collective-permute-start | bytes 786440 | tf_op jit(solution)/shard_map/ppermute | solution.py:33
  118.5 92.2 %reduce-scatter.2.cloned.1.call-start = ((), (), s32[]{:S(2)}) async-start(), calls=%async_computation.3 | async-start | bytes 1966080 | tf_op jit(solution)/shard_map/reduce_scatter | solution.py:185
  118.5 14.8 %copy-start.4 = (bf16[4,256,1024]{2,1,0:T(8,128)(2,1)S(1)}, bf16[4,256,1024]{2,1,0:T(8,128)(2,1)}, u32[]{:S(2)}) copy-start(bf16[4,256,1024]{2,1,0:T(8,128)(2,1)} %fusion.14) | copy-start | bytes 6291460
  136.4 2.3 %copy-start.13 = (s32[1024]{0:T(1024)S(1)}, s32[1024]{0:T(1024)}, u32[]{:S(2)}) copy-start(s32[1024]{0:T(1024)} %param.17) | copy-start | bytes 12292
  136.4 2.3 %copy-start.15 = (f32[64]{0:T(128)S(1)}, f32[64]{0:T(128)}, u32[]{:S(2)}) copy-start(f32[64]{0:T(128)} %param.18) | copy-start | bytes 772
  137.0 15.5 %copy-start.6 = (bf16[4,256,1024]{2,1,0:T(8,128)(2,1)S(1)}, bf16[4,256,1024]{2,1,0:T(8,128)(2,1)}, u32[]{:S(2)}) copy-start(bf16[4,256,1024]{2,1,0:T(8,128)(2,1)} %fusion.21) | copy-start | bytes 6291460
  137.0 5.7 %collective-permute-start.9 = (bf16[256,512]{1,0:T(8,128)(2,1)S(1)}, bf16[256,512]{1,0:T(8,128)(2,1)S(1)}, u32[]{:S(2)}, u32[]{:S(2)}) collective-permute-start(bf16[256,512]{1,0:T(8,128)(2,1)S(1)} %bitcast.153), channel_id=1, source_target_pairs={{0,3},{1,0},{2,1},{3,2},{4,7},{5,4},{6,5},{7,6},{8,11},{9,8},{10,9... | collective-permute-start | bytes 786440 | tf_op jit(solution)/shard_map/ppermute | solution.py:33
  137.1 14.1 %collective-permute-start.10 = (bf16[256,512]{1,0:T(8,128)(2,1)S(1)}, bf16[256,512]{1,0:T(8,128)(2,1)S(1)}, u32[]{:S(2)}, u32[]{:S(2)}) collective-permute-start(bf16[256,512]{1,0:T(8,128)(2,1)S(1)} %bitcast.154), channel_id=1, source_target_pairs={{0,2},{1,3},{2,0},{3,1},{4,6},{5,7},{6,4},{7,5},{8,10},{9,11},{10,... | collective-permute-start | bytes 786440 | tf_op jit(solution)/shard_map/ppermute | solution.py:33
  138.6 12.7 %collective-permute-start.11 = (bf16[256,512]{1,0:T(8,128)(2,1)S(1)}, bf16[256,512]{1,0:T(8,128)(2,1)S(1)}, u32[]{:S(2)}, u32[]{:S(2)}) collective-permute-start(bf16[256,512]{1,0:T(8,128)(2,1)S(1)} %bitcast.155), channel_id=1, source_target_pairs={{0,1},{1,2},{2,3},{3,0},{4,5},{5,6},{6,7},{7,4},{8,9},{9,10},{10,1... | collective-permute-start | bytes 786440 | tf_op jit(solution)/shard_map/ppermute | solution.py:33
  152.5 1.4 copy-start.8
  153.9 1.3 copy-start.5
  154.0 1.3 copy-start.14
  161.6 2.9 %copy-start.1 = (f32[2,1024,512]{1,2,0:T(8,128)}, f32[2,1024,512]{1,2,0:T(8,128)S(1)}, u32[]{:S(2)}) copy-start(f32[2,1024,512]{1,2,0:T(8,128)S(1)} %get-tuple-element.39) | copy-start | bytes 12582916
  162.6 3.1 %collective-permute-start.14 = (f32[1024]{0:T(1024)S(1)}, f32[1024]{0:T(1024)S(1)}, u32[]{:S(2)}, u32[]{:S(2)}) collective-permute-start(f32[1024]{0:T(1024)S(1)} %fusion.41), channel_id=1, source_target_pairs={{0,3},{1,2},{2,1},{3,0},{4,7},{5,6},{6,5},{7,4},{8,11},{9,10},{10,... | collective-permute-start | bytes 12296 | tf_op jit(solution)/shard_map/ppermute | solution.py:61
  163.4 3.6 %collective-permute-start.13 = (f32[1024]{0:T(1024)S(1)}, f32[1024]{0:T(1024)S(1)}, u32[]{:S(2)}, u32[]{:S(2)}) collective-permute-start(f32[1024]{0:T(1024)S(1)} %fusion.41), channel_id=1, source_target_pairs={{0,2},{1,3},{2,0},{3,1},{4,6},{5,7},{6,4},{7,5},{8,10},{9,11},{10,... | collective-permute-start | bytes 12296 | tf_op jit(solution)/shard_map/ppermute | solution.py:61
  164.2 2.9 %collective-permute-start.12 = (f32[1024]{0:T(1024)S(1)}, f32[1024]{0:T(1024)S(1)}, u32[]{:S(2)}, u32[]{:S(2)}) collective-permute-start(f32[1024]{0:T(1024)S(1)} %fusion.41), channel_id=1, source_target_pairs={{0,1},{1,0},{2,3},{3,2},{4,5},{5,4},{6,7},{7,6},{8,9},{9,8},{10,11... | collective-permute-start | bytes 12296 | tf_op jit(solution)/shard_map/ppermute | solution.py:61
  167.7 3.4 %copy-start.11 = (f32[1,1024]{1,0:T(1,128)}, f32[1,1024]{1,0:T(1,128)S(1)}, u32[]{:S(2)}) copy-start(f32[1,1024]{1,0:T(1,128)S(1)} %fusion.73) | copy-start | bytes 12292
Sparse Core Ops, SparseCore 0:
  9.6 66.2 all-gather.5
  87.7 26.8 all-gather.9
  118.6 37.0 all-gather.7
  177.1 33.5 reduce-scatter.1

commit v15 on v13

--- a/solution.py
+++ b/solution.py
@@ -180,12 +180,16 @@
     field = pair_sum(jnp.sum(out * read[None, :, :], axis=(1, 2)), "heads", n_heads)
     miss = field - target
     dquery = (miss[:, None, None] * pull).reshape(count, local).astype(jnp.bfloat16)
-    grad_query = lax.psum_scatter(
-        jnp.dot(enc.T, dquery, preferred_element_type=jnp.float32).astype(jnp.bfloat16),
-        "picks",
-        scatter_dimension=0,
-        tiled=True,
-    ).astype(jnp.float32)
+    grad_query = (
+        lax.psum_scatter(
+            jnp.dot(dquery.T, enc, preferred_element_type=jnp.float32).astype(jnp.bfloat16),
+            "picks",
+            scatter_dimension=1,
+            tiled=True,
+        )
+        .astype(jnp.float32)
+        .T
+    )
     return (field, latents_out, grad_query)
 
 

time: 216 us -> 217 us (level)
    unnamed x34 -> x35, local copies, waits for them, and re-layouts: 5.17 us -> 6.33 us
where the time goes in v15:
time: 217 us; the launch traced here: 216 us
  waiting for transfers between devices  97 us (45%)
  other arithmetic  44.9 us (21%)
  matrix products  26.7 us (12%)
  between operations  14.2 us (7%)
  blocking collectives  13.3 us (6%)
  starting transfers between devices  10.7 us (5%)
  local copies, waits for them, and re-layouts  9.54 us (4%)
    ppermute x12, waiting for transfers between devices, ring_gather(): blocks.append(lax.ppermute(x, axis, [(i, (i - s) % n) for i in range(n)]))  38.8 us
    reduce_scatter x1, waiting for transfers between devices, on_device(): lax.psum_scatter(jnp.dot(dquery.T, enc, preferred_element_type=jnp.float3...  32.4 us
    another operation x1, other arithmetic  22.8 us
    all_gather x1, waiting for transfers between devices, on_device(): piece = lax.all_gather(kv_weight, 'picks', axis=0, tiled=True)  14.5 us
    concatenate x4, other arithmetic, ring_gather(): ordered = jnp.roll(flipped, idx, axis=0)  13.3 us
    all_gather x1, blocking collectives, on_device(): lax.all_gather(jnp.stack([top, total]), 'picks', axis=0, tiled=False)  13.3 us
    ppermute x12, starting transfers between devices, ring_gather(): blocks.append(lax.ppermute(x, axis, [(i, (i - s) % n) for i in range(n)]))  9.4 us
    all_gather x1, waiting for transfers between devices, on_device(): lax.all_gather(numer.astype(jnp.bfloat16), 'picks', axis=0, tiled=False)  7.77 us
  transfers between devices with their start and end apart: 18, of which 13 were waited for; matrix products, arithmetic and copies ran while one was open for 28% of the time, Pallas kernels for 0%

profile of v15, /device:TPU:0, one launch (start us, length us, event | category | flops | bytes accessed | tf_op | source)
XLA Modules:
  0.0 216.2 jit_solution(13057628321937038008)
XLA Ops:
  7.2 0.7 all-gather.6.cloned.1.call-update
  8.0 1.2 copy.63
  9.2 2.4 %collective-permute-start = (bf16[256,1024]{1,0:T(8,128)(2,1)S(1)}, bf16[256,1024]{1,0:T(8,128)(2,1)S(1)}, u32[]{:S(2)}, u32[]{:S(2)}) collective-permute-start(bf16[256,1024]{1,0:T(8,128)(2,1)S(1)} %bitcast.126), channel_id=1, source_target_pairs={{0,3},{1,0},{2,1},{3,2},{4,7},{5,4},{6,5},{7,6},{8,11},{9,8},{10,9... | collective-permute-start | bytes 1572872 | tf_op jit(solution)/shard_map/ppermute | solution.py:33
  12.4 1.7 collective-permute-start.4
  14.1 1.0 constant_dynamic-slice_fusion.1
  15.3 22.8 %fusion = (bf16[3,512,1024]{2,1,0:T(8,128)(2,1)S(1)}, bf16[3,512,1024]{2,1,0:T(8,128)(2,1)S(1)}) fusion(f32[3,1024]{1,0:T(4,128)S(1)} %copy-done.9, f32[512]{0:T(512)S(1)} %maximum_multiply_fusion), kind=kLoop, calls=%fused_computation.2 | loop fusion | flops 4718592 | bytes 6305792 | tf_op jit(solution)/shard_map/convert.1
  38.2 3.2 %pad_maximum_fusion = bf16[6,512,1024]{2,1,0:T(8,128)(2,1)} fusion(bf16[3,512,1024]{2,1,0:T(8,128)(2,1)S(1)} %get-tuple-element.41, bf16[3,512,1024]{2,1,0:T(8,128)(2,1)S(1)} %get-tuple-element.40), kind=kLoop, calls=%fused_computation.4 | loop fusion | flops 3145728 | bytes 12582912 | tf_op jit(solution)/shard_map/concatenate | solution.py:21
  41.4 5.1 %collective-permute-done.3 = bf16[256,1024]{1,0:T(8,128)(2,1)} collective-permute-done((bf16[256,1024]{1,0:T(8,128)(2,1)}, bf16[256,1024]{1,0:T(8,128)(2,1)}, u32[]{:S(2)}, u32[]{:S(2)}) %collective-permute-start.3) | collective-permute-done | bytes 524320 | tf_op jit(solution)/shard_map/ppermute | solution.py:33
  46.4 1.1 collective-permute-start.2
  47.5 8.8 %collective-permute-done.4 = bf16[256,1024]{1,0:T(8,128)(2,1)} collective-permute-done((bf16[256,1024]{1,0:T(8,128)(2,1)}, bf16[256,1024]{1,0:T(8,128)(2,1)}, u32[]{:S(2)}, u32[]{:S(2)}) %collective-permute-start.4) | collective-permute-done | bytes 524320 | tf_op jit(solution)/shard_map/ppermute | solution.py:33
  56.3 5.1 %fusion.14 = bf16[4,256,1024]{2,1,0:T(8,128)(2,1)} fusion(s32[]{:T(128)S(6)} %select_n.27, bf16[1,256,1024]{2,1,0:T(8,128)(2,1)S(1)} %bitcast.145, bf16[1,256,1024]{2,1,0:T(8,128)(2,1)} %bitcast.13, bf16[1,256,1024]{2,1,0:T(8,128)(2,1)} %bitcast.14, bf16[1,256,1024]{2,1,0:T(8,128)(2,1)} %bitcast.15), kind=kLoop, calls=%fused_computation.38 | loop fusion | flops 7340032 | bytes 4194308 | tf_op jit(solution)/shard_map/jit(_roll_dynamic)/concatenate | solution.py:35
  61.4 14.5 %all-gather.6.cloned.1.call-done = bf16[3072,2,256]{2,1,0:T(2,128)(2,1)} async-done(((bf16[768,2,256]{2,1,0:T(2,128)(2,1)}), bf16[3072,2,256]{2,1,0:T(2,128)(2,1)}) %all-gather.6.cloned.1.call-update) | async-done | bytes 3145744 | tf_op jit(solution)/shard_map/all_gather | solution.py:92
  75.8 7.1 %fusion.32 = bf16[1024,2,256]{0,2,1:T(8,128)(2,1)S(1)} fusion(bf16[3072,1024,1]{1,0,2:T(8,128)(2,1)} %bitcast.120, bf16[3072,2,256]{2,1,0:T(2,128)(2,1)} %all-gather.6.cloned.1.call-done), kind=kOutput, calls=%fused_computation.81 | convolution fusion | flops 3221749760 | bytes 10485760 | tf_op jit(solution)/shard_map/tf,fjc->tjc/dot_general | solution.py:94
  83.1 0.8 multiply_reduce_fusion.1
  83.9 2.0 copy-done.1
  86.0 1.6 fusion.43
  87.9 4.8 %fusion.21 = bf16[4,256,1024]{2,1,0:T(8,128)(2,1)} fusion(s32[]{:T(128)S(6)} %select_n.27, bf16[1,256,1024]{2,1,0:T(8,128)(2,1)S(1)} %bitcast.129, bf16[1,256,1024]{2,1,0:T(8,128)(2,1)S(1)} %bitcast.146, bf16[1,256,1024]{2,1,0:T(8,128)(2,1)} %bitcast.5, bf16[1,256,1024]{2,1,0:T(8,128)(2,1)} %bitcast.6), kind=kLoop, calls=%fused_computation.45 | loop fusion | flops 7340032 | bytes 4194308 | tf_op jit(solution)/shard_map/jit(_roll_dynamic)/concatenate | solution.py:35
  92.6 0.9 fusion.4
  93.6 13.3 %all-gather.1 = f32[8,2,512]{2,1,0:T(2,128)S(1)} all-gather(f32[2,2,512]{2,1,0:T(2,128)S(1)} %pad_maximum_fusion.1), channel_id=3, replica_groups=mesh['groups'=2,'picks'=4,'heads'=4] {'picks'}, dimensions={0}, use_global_device_ids=true | all-gather | bytes 40960 | tf_op jit(solution)/shard_map/all_gather | solution.py:108
  106.9 7.8 %all-gather.10.cloned.1.call-done = bf16[8,512,128]{2,1,0:T(8,128)(2,1)} async-done(((bf16[2,512,128]{2,1,0:T(8,128)(2,1)}), bf16[8,512,128]{2,1,0:T(8,128)(2,1)}) %all-gather.10.cloned.1.call-update) | async-done | bytes 1048592 | tf_op jit(solution)/shard_map/all_gather | solution.py:107
  114.7 1.8 multiply_reduce_fusion.2
  116.7 0.9 collective-permute-start.6
  117.6 0.7 collective-permute-start.7
  118.6 5.6 %collective-permute-done.6 = bf16[256,512]{1,0:T(8,128)(2,1)S(1)} collective-permute-done((bf16[256,512]{1,0:T(8,128)(2,1)S(1)}, bf16[256,512]{1,0:T(8,128)(2,1)S(1)}, u32[]{:S(2)}, u32[]{:S(2)}) %collective-permute-start.6) | collective-permute-done | bytes 262176 | tf_op jit(solution)/shard_map/ppermute | solution.py:33
  124.2 6.7 %collective-permute-done.7 = bf16[256,512]{1,0:T(8,128)(2,1)S(1)} collective-permute-done((bf16[256,512]{1,0:T(8,128)(2,1)S(1)}, bf16[256,512]{1,0:T(8,128)(2,1)S(1)}, u32[]{:S(2)}, u32[]{:S(2)}) %collective-permute-start.7) | collective-permute-done | bytes 262176 | tf_op jit(solution)/shard_map/ppermute | solution.py:33
  131.1 2.2 %fusion.60 = bf16[4,256,512]{2,1,0:T(8,128)(2,1)S(1)} fusion(s32[]{:T(128)S(6)} %select_n.27, bf16[1,256,512]{2,1,0:T(8,128)(2,1)S(1)} %bitcast.135, bf16[1,256,512]{2,1,0:T(8,128)(2,1)S(1)} %bitcast.149, bf16[1,256,512]{2,1,0:T(8,128)(2,1)S(1)} %bitcast.150, bf16[1,256,512]{2,1,0:T(8,128)(2,1)} %bitcast.32), kind=kLoop, calls=%fused_computation.103 | loop fusion | flops 3670016 | bytes 2097156 | tf_op jit(solution)/shard_map/jit(_roll_dynamic)/concatenate | solution.py:35
  133.4 1.4 multiply_reduce_fusion.4
  134.8 1.1 fusion.38
  137.1 1.5 collective-permute-start.10
  138.9 4.0 %collective-permute-done.9 = bf16[256,512]{1,0:T(8,128)(2,1)S(1)} collective-permute-done((bf16[256,512]{1,0:T(8,128)(2,1)S(1)}, bf16[256,512]{1,0:T(8,128)(2,1)S(1)}, u32[]{:S(2)}, u32[]{:S(2)}) %collective-permute-start.9) | collective-permute-done | bytes 262176 | tf_op jit(solution)/shard_map/ppermute | solution.py:33
  142.9 8.3 %collective-permute-done.10 = bf16[256,512]{1,0:T(8,128)(2,1)S(1)} collective-permute-done((bf16[256,512]{1,0:T(8,128)(2,1)S(1)}, bf16[256,512]{1,0:T(8,128)(2,1)S(1)}, u32[]{:S(2)}, u32[]{:S(2)}) %collective-permute-start.10) | collective-permute-done | bytes 262176 | tf_op jit(solution)/shard_map/ppermute | solution.py:33
  151.3 1.2 fusion.53
  152.6 1.4 multiply_reduce_fusion.3
  154.0 1.3 copy-done.4
  155.3 0.8 fusion.42
  156.3 5.1 %convolution_convert_fusion.2 = bf16[1024,256]{0,1:T(8,128)(2,1)S(1)} fusion(bf16[3072,1024]{1,0:T(8,128)(2,1)} %bitcast.121, bf16[3072,256]{1,0:T(8,128)(2,1)} %all-gather.8.cloned.1.call-done), kind=kOutput, calls=%fused_computation.84 | convolution fusion | flops 1610874880 | bytes 8388608 | tf_op jit(solution)/shard_map/dot_general | solution.py:158
  161.3 0.8 fusion.3
  162.2 1.0 fusion.39
  163.4 0.9 collective-permute-done.12
  164.4 0.9 collective-permute-start.13
  165.3 0.9 multiply_reduce_fusion
  166.1 1.9 collective-permute-done.13
  168.6 1.2 multiply_convert_fusion.4
  170.2 3.0 %convolution_convert_fusion = bf16[256,3072]{1,0:T(8,128)(2,1)} fusion(bf16[1024,256]{0,1:T(8,128)(2,1)S(1)} %bitcast.170, bf16[3072,1024]{1,0:T(8,128)(2,1)S(1)} %bitcast.124), kind=kOutput, calls=%fused_computation.26 | convolution fusion | flops 1611399168 | bytes 8388608 | tf_op jit(solution)/shard_map/dot_general | solution.py:185
  173.2 1.9 constant_dynamic-slice_fusion
  175.1 32.4 %reduce-scatter.2.cloned.1.call-done = bf16[256,768]{1,0:T(8,128)(2,1)} async-done(((bf16[256,3072]{1,0:T(8,128)(2,1)}), bf16[256,768]{1,0:T(8,128)(2,1)}) %reduce-scatter.2.cloned.1.call-update) | async-done | bytes 393232 | tf_op jit(solution)/shard_map/reduce_scatter | solution.py:184
  207.5 1.0 convert_bitcast_fusion
  208.5 1.1 copy.79
  (73 shorter events, 5.1 us)
Async XLA Ops:
  7.2 127.6 %copy-start = (bf16[3,1024,256]{2,1,0:T(8,128)(2,1)S(1)}, bf16[3,1024,256]{2,1,0:T(8,128)(2,1)}, u32[]{:S(2)}) copy-start(bf16[3,1024,256]{2,1,0:T(8,128)(2,1)} %param.23) | copy-start | bytes 4718596
  7.2 8.1 %copy-start.9 = (f32[3,1024]{1,0:T(4,128)S(1)}, f32[3,1024]{1,0:T(4,128)}, u32[]{:S(2)}) copy-start(f32[3,1024]{1,0:T(4,128)} %param.16) | copy-start | bytes 36868
  7.2 68.7 %all-gather.6.cloned.1.call-start = ((), (), s32[]{:S(2)}) async-start(), calls=%async_computation.1 | async-start | bytes 3932160 | tf_op jit(solution)/shard_map/all_gather | solution.py:92
  7.9 106.8 %all-gather.10.cloned.1.call-start = ((), (), s32[]{:S(2)}) async-start(), calls=%async_computation.4 | async-start | bytes 1310720 | tf_op jit(solution)/shard_map/all_gather | solution.py:107
  9.2 78.6 %collective-permute-start = (bf16[256,1024]{1,0:T(8,128)(2,1)S(1)}, bf16[256,1024]{1,0:T(8,128)(2,1)S(1)}, u32[]{:S(2)}, u32[]{:S(2)}) collective-permute-start(bf16[256,1024]{1,0:T(8,128)(2,1)S(1)} %bitcast.126), channel_id=1, source_target_pairs={{0,3},{1,0},{2,1},{3,2},{4,7},{5,4},{6,5},{7,6},{8,11},{9,8},{10,9... | collective-permute-start | bytes 1572872 | tf_op jit(solution)/shard_map/ppermute | solution.py:33
  11.7 76.2 %collective-permute-start.1 = (bf16[256,1024]{1,0:T(8,128)(2,1)S(1)}, bf16[256,1024]{1,0:T(8,128)(2,1)}, u32[]{:S(2)}, u32[]{:S(2)}) collective-permute-start(bf16[256,1024]{1,0:T(8,128)(2,1)S(1)} %bitcast.127), channel_id=1, source_target_pairs={{0,2},{1,3},{2,0},{3,1},{4,6},{5,7},{6,4},{7,5},{8,10},{9,11},{10,... | collective-permute-start | bytes 1572872 | tf_op jit(solution)/shard_map/ppermute | solution.py:33
  12.3 34.1 %collective-permute-start.3 = (bf16[256,1024]{1,0:T(8,128)(2,1)}, bf16[256,1024]{1,0:T(8,128)(2,1)}, u32[]{:S(2)}, u32[]{:S(2)}) collective-permute-start(bf16[256,1024]{1,0:T(8,128)(2,1)} %param.21), channel_id=1, source_target_pairs={{0,3},{1,0},{2,1},{3,2},{4,7},{5,4},{6,5},{7,6},{8,11},{9,8},{10,9... | collective-permute-start | bytes 1572872 | tf_op jit(solution)/shard_map/ppermute | solution.py:33
  12.4 43.9 %collective-permute-start.4 = (bf16[256,1024]{1,0:T(8,128)(2,1)}, bf16[256,1024]{1,0:T(8,128)(2,1)}, u32[]{:S(2)}, u32[]{:S(2)}) collective-permute-start(bf16[256,1024]{1,0:T(8,128)(2,1)} %param.21), channel_id=1, source_target_pairs={{0,2},{1,3},{2,0},{3,1},{4,6},{5,7},{6,4},{7,5},{8,10},{9,11},{10,... | collective-permute-start | bytes 1572872 | tf_op jit(solution)/shard_map/ppermute | solution.py:33
  14.1 42.2 %collective-permute-start.5 = (bf16[256,1024]{1,0:T(8,128)(2,1)}, bf16[256,1024]{1,0:T(8,128)(2,1)}, u32[]{:S(2)}, u32[]{:S(2)}) collective-permute-start(bf16[256,1024]{1,0:T(8,128)(2,1)} %param.21), channel_id=1, source_target_pairs={{0,1},{1,2},{2,3},{3,0},{4,5},{5,6},{6,7},{7,4},{8,9},{9,10},{10,1... | collective-permute-start | bytes 1572872 | tf_op jit(solution)/shard_map/ppermute | solution.py:33
  38.2 18.1 %copy-start.8 = (bf16[256,1024]{1,0:T(8,128)(2,1)S(1)}, bf16[256,1024]{1,0:T(8,128)(2,1)}, u32[]{:S(2)}) copy-start(bf16[256,1024]{1,0:T(8,128)(2,1)} %param.21) | copy-start | bytes 1572868
  46.4 41.4 %collective-permute-start.2 = (bf16[256,1024]{1,0:T(8,128)(2,1)S(1)}, bf16[256,1024]{1,0:T(8,128)(2,1)}, u32[]{:S(2)}, u32[]{:S(2)}) collective-permute-start(bf16[256,1024]{1,0:T(8,128)(2,1)S(1)} %bitcast.128), channel_id=1, source_target_pairs={{0,1},{1,2},{2,3},{3,0},{4,5},{5,6},{6,7},{7,4},{8,9},{9,10},{10,1... | collective-permute-start | bytes 1572872 | tf_op jit(solution)/shard_map/ppermute | solution.py:33
  83.9 2.0 copy-start.1
  87.6 68.7 %all-gather.8.cloned.1.call-start = ((), (), s32[]{:S(2)}) async-start(), calls=%async_computation.2 | async-start | bytes 1966080 | tf_op jit(solution)/shard_map/all_gather | solution.py:124
  87.8 4.8 %copy-start.2 = (f32[2,512,1024]{2,1,0:T(8,128)S(1)}, f32[2,512,1024]{2,1,0:T(8,128)}, u32[]{:S(2)}) copy-start(f32[2,512,1024]{2,1,0:T(8,128)} %copy-done.1) | copy-start | bytes 12582916
  93.5 24.9 %copy-start.10 = (f32[2,1024]{1,0:T(2,128)S(1)}, f32[2,1024]{1,0:T(2,128)}, u32[]{:S(2)}) copy-start(f32[2,1024]{1,0:T(2,128)} %param.22) | copy-start | bytes 24580
  116.7 16.7 %copy-start.6 = (bf16[512,1024]{1,0:T(8,128)(2,1)S(1)}, bf16[512,1024]{1,0:T(8,128)(2,1)}, u32[]{:S(2)}) copy-start(bf16[512,1024]{1,0:T(8,128)(2,1)} %param.19) | copy-start | bytes 3145732
  116.7 7.5 %collective-permute-start.6 = (bf16[256,512]{1,0:T(8,128)(2,1)S(1)}, bf16[256,512]{1,0:T(8,128)(2,1)S(1)}, u32[]{:S(2)}, u32[]{:S(2)}) collective-permute-start(bf16[256,512]{1,0:T(8,128)(2,1)S(1)} %bitcast.132), channel_id=1, source_target_pairs={{0,3},{1,0},{2,1},{3,2},{4,7},{5,4},{6,5},{7,6},{8,11},{9,8},{10,9... | collective-permute-start | bytes 786440 | tf_op jit(solution)/shard_map/ppermute | solution.py:33
  117.6 13.3 %collective-permute-start.7 = (bf16[256,512]{1,0:T(8,128)(2,1)S(1)}, bf16[256,512]{1,0:T(8,128)(2,1)S(1)}, u32[]{:S(2)}, u32[]{:S(2)}) collective-permute-start(bf16[256,512]{1,0:T(8,128)(2,1)S(1)} %bitcast.133), channel_id=1, source_target_pairs={{0,2},{1,3},{2,0},{3,1},{4,6},{5,7},{6,4},{7,5},{8,10},{9,11},{10,... | collective-permute-start | bytes 786440 | tf_op jit(solution)/shard_map/ppermute | solution.py:33
  118.3 12.8 %collective-permute-start.8 = (bf16[256,512]{1,0:T(8,128)(2,1)S(1)}, bf16[256,512]{1,0:T(8,128)(2,1)}, u32[]{:S(2)}, u32[]{:S(2)}) collective-permute-start(bf16[256,512]{1,0:T(8,128)(2,1)S(1)} %bitcast.134), channel_id=1, source_target_pairs={{0,1},{1,2},{2,3},{3,0},{4,5},{5,6},{6,7},{7,4},{8,9},{9,10},{10,1... | collective-permute-start | bytes 786440 | tf_op jit(solution)/shard_map/ppermute | solution.py:33
  118.5 89.0 %reduce-scatter.2.cloned.1.call-start = ((), (), s32[]{:S(2)}) async-start(), calls=%async_computation.3 | async-start | bytes 1966080 | tf_op jit(solution)/shard_map/reduce_scatter | solution.py:184
  118.6 14.8 %copy-start.3 = (bf16[4,256,1024]{2,1,0:T(8,128)(2,1)S(1)}, bf16[4,256,1024]{2,1,0:T(8,128)(2,1)}, u32[]{:S(2)}) copy-start(bf16[4,256,1024]{2,1,0:T(8,128)(2,1)} %fusion.14) | copy-start | bytes 6291460
  136.5 2.3 %copy-start.11 = (s32[1024]{0:T(1024)S(1)}, s32[1024]{0:T(1024)}, u32[]{:S(2)}) copy-start(s32[1024]{0:T(1024)} %param.17) | copy-start | bytes 12292
  136.5 2.3 %copy-start.13 = (f32[64]{0:T(128)S(1)}, f32[64]{0:T(128)}, u32[]{:S(2)}) copy-start(f32[64]{0:T(128)} %param.18) | copy-start | bytes 772
  137.1 15.5 %copy-start.5 = (bf16[4,256,1024]{2,1,0:T(8,128)(2,1)S(1)}, bf16[4,256,1024]{2,1,0:T(8,128)(2,1)}, u32[]{:S(2)}) copy-start(bf16[4,256,1024]{2,1,0:T(8,128)(2,1)} %fusion.21) | copy-start | bytes 6291460
  137.1 5.8 %collective-permute-start.9 = (bf16[256,512]{1,0:T(8,128)(2,1)S(1)}, bf16[256,512]{1,0:T(8,128)(2,1)S(1)}, u32[]{:S(2)}, u32[]{:S(2)}) collective-permute-start(bf16[256,512]{1,0:T(8,128)(2,1)S(1)} %bitcast.151), channel_id=1, source_target_pairs={{0,3},{1,0},{2,1},{3,2},{4,7},{5,4},{6,5},{7,6},{8,11},{9,8},{10,9... | collective-permute-start | bytes 786440 | tf_op jit(solution)/shard_map/ppermute | solution.py:33
  137.1 14.0 %collective-permute-start.10 = (bf16[256,512]{1,0:T(8,128)(2,1)S(1)}, bf16[256,512]{1,0:T(8,128)(2,1)S(1)}, u32[]{:S(2)}, u32[]{:S(2)}) collective-permute-start(bf16[256,512]{1,0:T(8,128)(2,1)S(1)} %bitcast.152), channel_id=1, source_target_pairs={{0,2},{1,3},{2,0},{3,1},{4,6},{5,7},{6,4},{7,5},{8,10},{9,11},{10,... | collective-permute-start | bytes 786440 | tf_op jit(solution)/shard_map/ppermute | solution.py:33
  138.6 12.7 %collective-permute-start.11 = (bf16[256,512]{1,0:T(8,128)(2,1)S(1)}, bf16[256,512]{1,0:T(8,128)(2,1)S(1)}, u32[]{:S(2)}, u32[]{:S(2)}) collective-permute-start(bf16[256,512]{1,0:T(8,128)(2,1)S(1)} %bitcast.153), channel_id=1, source_target_pairs={{0,1},{1,2},{2,3},{3,0},{4,5},{5,6},{6,7},{7,4},{8,9},{9,10},{10,1... | collective-permute-start | bytes 786440 | tf_op jit(solution)/shard_map/ppermute | solution.py:33
  152.6 2.8 %copy-start.7 = (bf16[2,1024,256]{2,1,0:T(8,128)(2,1)S(1)}, bf16[2,1024,256]{2,1,0:T(8,128)(2,1)}, u32[]{:S(2)}) copy-start(bf16[2,1024,256]{2,1,0:T(8,128)(2,1)} %param.25) | copy-start | bytes 3145732
  154.0 1.4 copy-start.4
  161.3 0.9 copy-start.12
  163.2 1.2 collective-permute-start.12
  164.4 3.6 %collective-permute-start.13 = (f32[1024]{0:T(1024)S(1)}, f32[1024]{0:T(1024)S(1)}, u32[]{:S(2)}, u32[]{:S(2)}) collective-permute-start(f32[1024]{0:T(1024)S(1)} %add.61), channel_id=1, source_target_pairs={{0,2},{1,3},{2,0},{3,1},{4,6},{5,7},{6,4},{7,5},{8,10},{9,11},{10,... | collective-permute-start | bytes 12296 | tf_op jit(solution)/shard_map/ppermute | solution.py:61
  165.3 4.6 %slice-start = ((s8[6291456]{0:T(1024)(128)(4,1)}), s8[4194304]{0:T(1024)(128)(4,1)S(1)}, s32[]{:S(2)}) async-start(s8[6291456]{0:T(1024)(128)(4,1)} %bitcast.122), calls=%async_computation.5 | async-start | bytes 8388608
  168.6 1.6 slice-start.1
Sparse Core Ops, SparseCore 0:
  9.6 66.2 all-gather.5
  87.7 26.9 all-gather.9
  118.7 36.9 all-gather.7
  173.3 34.0 reduce-scatter.1

commit v16 on v13

--- a/solution.py
+++ b/solution.py
@@ -59,6 +59,18 @@
         return lax.psum(x, axis)
     x = x + lax.ppermute(x, axis, [(k, k ^ 1) for k in range(n)])
     return x + lax.ppermute(x, axis, [(k, k ^ 2) for k in range(n)])
+
+
+def pair_gather(x, axis, n):
+    near = lax.ppermute(x, axis, [(k, k ^ 1) for k in range(n)])
+    far = lax.ppermute(x, axis, [(k, k ^ 2) for k in range(n)])
+    far_near = lax.ppermute(far, axis, [(k, k ^ 1) for k in range(n)])
+    return jnp.concatenate([x, near, far, far_near], axis=0)
+
+
+def xor_blocks(x, idx, n):
+    blocks = x.reshape((n, x.shape[0] // n) + x.shape[1:])
+    return jnp.take(blocks, jnp.arange(n) ^ idx, axis=0).reshape(x.shape)
 
 
 def on_device(
@@ -90,7 +102,11 @@
     enc = encode(coords)
     cross_full = ring_gather(cross_out, "heads", n_heads)
     piece = lax.all_gather(kv_weight, "picks", axis=0, tiled=True)
-    cross_full, piece = lax.optimization_barrier((cross_full, piece))
+    paired = n_heads == 4
+    out_full = ring_gather(self_out.T, "heads", n_heads).T
+    if paired:
+        out_full = xor_blocks(out_full, lax.axis_index("heads"), n_heads)
+    out_full, cross_full, piece = lax.optimization_barrier((out_full, cross_full, piece))
     keys_vals = jnp.einsum(
         "tf,fjc->tjc", enc, piece, preferred_element_type=jnp.float32
     ).astype(jnp.bfloat16)
@@ -118,8 +134,6 @@
         .reshape(lat_rows, local)
         .astype(jnp.bfloat16)
     )
-    out_full = ring_gather(self_out.T, "heads", n_heads).T
-    out_full, attended = lax.optimization_barrier((out_full, attended))
     dq_local, attended = lax.optimization_barrier((dec_query, attended))
     dq_full = lax.all_gather(dq_local, "picks", axis=0, tiled=True)
     attended_full = ring_gather(attended.T, "heads", n_heads).T
@@ -143,7 +157,8 @@
         .astype(jnp.bfloat16)
         .reshape(lat_rows, local)
     )
-    every_head = ring_gather(head_out.T, "heads", n_heads).T
+    head_gather = pair_gather if paired else ring_gather
+    every_head = head_gather(head_out.T, "heads", n_heads).T
     out_whole = whole + jnp.dot(every_head, out_full, preferred_element_type=jnp.float32)
     latents_out = lax.dynamic_slice_in_dim(out_whole, column, local, 1)
     power_two = jnp.mean(out_whole * out_whole, axis=1, keepdims=True)

time: 216 us -> 217 us (level)
  waiting for transfers between devices: 97 us -> 79.9 us
  local copies, waits for them, and re-layouts: 8.39 us -> 23.1 us
    ppermute x12 -> x9, waiting for transfers between devices: 38.8 us -> 10.6 us  [ring_gather(): blocks.append(lax.ppermute(x, axis, [(i, (i - s) % n) for i in range(n)]))]
    ppermute x0 -> x3, waiting for transfers between devices: none -> 6.81 us  [the longest x1 5.42 us: pair_gather(): far = lax.ppermute(x, axis, [(k, k ^ 2) for k in range(n)])]
    unnamed x34 -> x41, local copies, waits for them, and re-layouts: 5.17 us -> 10.2 us
    all_gather x1, waiting for transfers between devices: 0.02 us -> 4.26 us  [on_device(): dq_full = lax.all_gather(dq_local, 'picks', axis=0, tiled=True)]
    transpose x0 -> x1, local copies, waits for them, and re-layouts: none -> 3.94 us  [on_device(): out_full = ring_gather(self_out.T, 'heads', n_heads).T]
    gather x0 -> x1, local copies, waits for them, and re-layouts: none -> 3.6 us  [xor_blocks(): return jnp.take(blocks, jnp.arange(n) ^ idx, axis=0).reshape(x.shape)]
    concatenate x4 -> x2, other arithmetic: 13.3 us -> 9.82 us  [ring_gather(): ordered = jnp.roll(flipped, idx, axis=0)]
    select_n x0 -> x2, other arithmetic: none -> 3.22 us  [xor_blocks(): return jnp.take(blocks, jnp.arange(n) ^ idx, axis=0).reshape(x.shape)]
  transfers between devices with their start and end apart: 18 -> 18, of which waited for: 13 -> 10; matrix products, arithmetic and copies ran while one was open for 28% -> 32% of each run, Pallas kernels for 0% -> 0%
where the time goes in v16:
time: 217 us; the launch traced here: 216 us
  waiting for transfers between devices  79.9 us (37%)
  other arithmetic  47.6 us (22%)
  matrix products  26.8 us (12%)
  local copies, waits for them, and re-layouts  23.1 us (11%)
  between operations  14.1 us (6%)
  blocking collectives  13.2 us (6%)
  starting transfers between devices  11.2 us (5%)
    reduce_scatter x1, waiting for transfers between devices, on_device(): lax.psum_scatter(jnp.dot(enc.T, dquery, preferred_element_type=jnp.float3...  32.4 us
    another operation x1, other arithmetic  22.9 us
    all_gather x1, blocking collectives, on_device(): lax.all_gather(jnp.stack([top, total]), 'picks', axis=0, tiled=False)  13.2 us
    all_gather x1, waiting for transfers between devices, on_device(): piece = lax.all_gather(kv_weight, 'picks', axis=0, tiled=True)  12.3 us
    all_gather x1, waiting for transfers between devices, on_device(): lax.all_gather(numer.astype(jnp.bfloat16), 'picks', axis=0, tiled=False)  10.6 us
    ppermute x9, waiting for transfers between devices, ring_gather(): blocks.append(lax.ppermute(x, axis, [(i, (i - s) % n) for i in range(n)]))  10.6 us
    unnamed x41, local copies, waits for them, and re-layouts  10.2 us
    concatenate x2, other arithmetic, ring_gather(): ordered = jnp.roll(flipped, idx, axis=0)  9.82 us
  transfers between devices with their start and end apart: 18, of which 10 were waited for; matrix products, arithmetic and copies ran while one was open for 32% of the time, Pallas kernels for 0%

profile of v16, /device:TPU:0, one launch (start us, length us, event | category | flops | bytes accessed | tf_op | source)
XLA Modules:
  0.0 216.1 jit_solution(3298902447690401683)
XLA Ops:
  8.0 1.2 copy.63
  9.2 2.4 %collective-permute-start = (bf16[256,1024]{1,0:T(8,128)(2,1)S(1)}, bf16[256,1024]{1,0:T(8,128)(2,1)}, u32[]{:S(2)}, u32[]{:S(2)}) collective-permute-start(bf16[256,1024]{1,0:T(8,128)(2,1)S(1)} %bitcast.137), channel_id=1, source_target_pairs={{0,3},{1,0},{2,1},{3,2},{4,7},{5,4},{6,5},{7,6},{8,11},{9,8},{10,9... | collective-permute-start | bytes 1572872 | tf_op jit(solution)/shard_map/ppermute | solution.py:33
  12.5 1.6 collective-permute-start.3
  14.0 1.4 collective-permute-start.4
  15.6 1.0 constant_dynamic-slice_fusion.2
  16.8 22.9 %fusion = (bf16[3,512,1024]{2,1,0:T(8,128)(2,1)S(1)}, bf16[3,512,1024]{2,1,0:T(8,128)(2,1)S(1)}) fusion(f32[3,1024]{1,0:T(4,128)S(1)} %copy-done.9, f32[512]{0:T(512)S(1)} %maximum_multiply_fusion), kind=kLoop, calls=%fused_computation.3 | loop fusion | flops 4718592 | bytes 6305792 | tf_op jit(solution)/shard_map/convert
  39.7 3.2 %pad_maximum_fusion = bf16[6,512,1024]{2,1,0:T(8,128)(2,1)} fusion(bf16[3,512,1024]{2,1,0:T(8,128)(2,1)S(1)} %get-tuple-element.26, bf16[3,512,1024]{2,1,0:T(8,128)(2,1)S(1)} %get-tuple-element.25), kind=kLoop, calls=%fused_computation.5 | loop fusion | flops 3145728 | bytes 12582912 | tf_op jit(solution)/shard_map/concatenate | solution.py:21
  42.9 5.1 %fusion.21 = bf16[4,256,1024]{2,1,0:T(8,128)(2,1)} fusion(s32[]{:T(128)S(6)} %select_n.54, bf16[1,256,1024]{2,1,0:T(8,128)(2,1)S(1)} %bitcast.140, bf16[1,256,1024]{2,1,0:T(8,128)(2,1)} %bitcast.7, bf16[1,256,1024]{2,1,0:T(8,128)(2,1)} %bitcast.8, bf16[1,256,1024]{2,1,0:T(8,128)(2,1)} %bitcast.9), kind=kLoop, calls=%fused_computation.46 | loop fusion | flops 7340032 | bytes 4194308 | tf_op jit(solution)/shard_map/jit(_roll_dynamic)/concatenate | solution.py:35
  48.0 3.9 %copy.64 = bf16[1024,1024]{1,0:T(8,128)(2,1)} copy(bf16[1024,1024]{0,1:T(8,128)(2,1)} %bitcast.124) | data formatting | bytes 4194304 | tf_op jit(solution)/shard_map/transpose | solution.py:106
  51.9 3.6 %gather_fusion = bf16[4,256,1024]{2,1,0:T(8,128)(2,1)} fusion(bf16[4,256,1024]{2,1,0:T(8,128)(2,1)} %bitcast.125, s32[1024]{0:T(1024)S(1)} %pad_clamp_fusion), kind=kCustom, calls=%fused_computation | custom fusion | bytes 4194320 | tf_op jit(solution)/shard_map/jit(_take)/gather | solution.py:73
  55.5 3.2 %bitcast_select_fusion = bf16[1024,1024]{1,0:T(8,128)(2,1)} fusion(bf16[4,256,1024]{2,1,0:T(8,128)(2,1)} %gather_fusion, pred[1024]{0:T(1024)(128)(4,1)S(1)} %broadcast_in_dim.17), kind=kLoop, calls=%fused_computation.50 | loop fusion | flops 1048576 | bytes 4195328 | tf_op jit(solution)/shard_map/jit(_take)/select_n | solution.py:73
  58.8 4.7 %fusion.14 = bf16[4,256,1024]{2,1,0:T(8,128)(2,1)} fusion(s32[]{:T(128)S(6)} %select_n.54, bf16[1,256,1024]{2,1,0:T(8,128)(2,1)S(1)} %bitcast.150, bf16[1,256,1024]{2,1,0:T(8,128)(2,1)S(1)} %bitcast.151, bf16[1,256,1024]{2,1,0:T(8,128)(2,1)} %bitcast.17, bf16[1,256,1024]{2,1,0:T(8,128)(2,1)} %bitcast.18), kind=kLoop, calls=%fused_computation.39 | loop fusion | flops 7340032 | bytes 4194308 | tf_op jit(solution)/shard_map/jit(_roll_dynamic)/concatenate | solution.py:35
  63.5 12.3 %all-gather.6.cloned.1.call-done = bf16[3072,2,256]{2,1,0:T(2,128)(2,1)} async-done(((bf16[768,2,256]{2,1,0:T(2,128)(2,1)}), bf16[3072,2,256]{2,1,0:T(2,128)(2,1)}) %all-gather.6.cloned.1.call-update) | async-done | bytes 3145744 | tf_op jit(solution)/shard_map/all_gather | solution.py:104
  75.8 7.1 %fusion.32 = bf16[1024,2,256]{0,2,1:T(8,128)(2,1)S(1)} fusion(bf16[3072,1024,1]{1,0,2:T(8,128)(2,1)} %bitcast.126, bf16[3072,2,256]{2,1,0:T(2,128)(2,1)} %all-gather.6.cloned.1.call-done), kind=kOutput, calls=%fused_computation.67 | convolution fusion | flops 3221749760 | bytes 10485760 | tf_op jit(solution)/shard_map/tf,fjc->tjc/dot_general | solution.py:110
  83.1 0.8 multiply_reduce_fusion.1
  83.9 2.0 copy-done.2
  86.0 1.6 fusion.43
  87.6 3.1 %fusion.4 = f32[2,512]{1,0:T(2,128)S(1)} fusion(f32[2,512,1024]{2,1,0:T(8,128)} %copy-done.2, f32[2,512]{1,0:T(2,128)S(1)} %get-tuple-element.29), kind=kLoop, calls=%fused_computation.30 | loop fusion | flops 3144704 | bytes 4202496 | tf_op jit(solution)/shard_map/reduce_sum | solution.py:119
  90.7 13.2 %all-gather.1 = f32[8,2,512]{2,1,0:T(2,128)S(1)} all-gather(f32[2,2,512]{2,1,0:T(2,128)S(1)} %pad_maximum_fusion.1), channel_id=3, replica_groups=mesh['groups'=2,'picks'=4,'heads'=4] {'picks'}, dimensions={0}, use_global_device_ids=true | all-gather | bytes 40960 | tf_op jit(solution)/shard_map/all_gather | solution.py:124
  104.0 10.6 %all-gather.10.cloned.1.call-done = bf16[8,512,128]{2,1,0:T(8,128)(2,1)} async-done(((bf16[2,512,128]{2,1,0:T(8,128)(2,1)}), bf16[8,512,128]{2,1,0:T(8,128)(2,1)}) %all-gather.10.cloned.1.call-update) | async-done | bytes 1048592 | tf_op jit(solution)/shard_map/all_gather | solution.py:123
  114.6 1.8 multiply_reduce_fusion.2
  116.6 0.8 collective-permute-start.6
  117.5 0.8 collective-permute-start.7
  119.5 4.4 %collective-permute-done.6 = bf16[256,512]{1,0:T(8,128)(2,1)S(1)} collective-permute-done((bf16[256,512]{1,0:T(8,128)(2,1)S(1)}, bf16[256,512]{1,0:T(8,128)(2,1)S(1)}, u32[]{:S(2)}, u32[]{:S(2)}) %collective-permute-start.6) | collective-permute-done | bytes 262176 | tf_op jit(solution)/shard_map/ppermute | solution.py:33
  124.6 6.2 %collective-permute-done.7 = bf16[256,512]{1,0:T(8,128)(2,1)S(1)} collective-permute-done((bf16[256,512]{1,0:T(8,128)(2,1)S(1)}, bf16[256,512]{1,0:T(8,128)(2,1)S(1)}, u32[]{:S(2)}, u32[]{:S(2)}) %collective-permute-start.7) | collective-permute-done | bytes 262176 | tf_op jit(solution)/shard_map/ppermute | solution.py:33
  134.4 0.7 bitcast_dynamic-update-slice_fusion.3
  135.1 1.3 constant_dynamic-slice_fusion.1
  136.4 1.4 multiply_reduce_fusion.4
  137.8 1.1 fusion.38
  140.1 1.2 collective-permute-start.10
  141.4 5.4 %collective-permute-done.10 = bf16[256,512]{1,0:T(8,128)(2,1)S(1)} collective-permute-done((bf16[256,512]{1,0:T(8,128)(2,1)S(1)}, bf16[256,512]{1,0:T(8,128)(2,1)S(1)}, u32[]{:S(2)}, u32[]{:S(2)}) %collective-permute-start.10) | collective-permute-done | bytes 262176 | tf_op jit(solution)/shard_map/ppermute | solution.py:66
  146.9 1.4 collective-permute-done.11
  148.3 1.4 multiply_reduce_fusion.3
  149.7 1.3 copy-done.4
  151.1 0.9 fusion.42
  152.0 4.3 %all-gather.8.cloned.1.call-done = bf16[3072,256]{1,0:T(8,128)(2,1)} async-done(((bf16[768,256]{1,0:T(8,128)(2,1)}), bf16[3072,256]{1,0:T(8,128)(2,1)}) %all-gather.8.cloned.1.call-update) | async-done | bytes 1572880 | tf_op jit(solution)/shard_map/all_gather | solution.py:138
  156.2 5.1 %convolution_convert_fusion.2 = bf16[1024,256]{0,1:T(8,128)(2,1)S(1)} fusion(bf16[3072,1024]{1,0:T(8,128)(2,1)} %bitcast.127, bf16[3072,256]{1,0:T(8,128)(2,1)} %all-gather.8.cloned.1.call-done), kind=kOutput, calls=%fused_computation.70 | convolution fusion | flops 1610874880 | bytes 8388608 | tf_op jit(solution)/shard_map/dot_general | solution.py:173
  161.3 0.8 fusion.3
  162.1 1.0 fusion.39
  163.4 0.9 collective-permute-done.12
  164.4 1.5 collective-permute-start.13
  165.8 0.9 multiply_reduce_fusion
  166.7 1.3 collective-permute-done.13
  168.6 1.2 multiply_convert_fusion.4
  170.2 3.1 %convolution_convert_fusion = bf16[3072,256]{1,0:T(8,128)(2,1)} fusion(bf16[3072,1024]{1,0:T(8,128)(2,1)S(1)} %bitcast.130, bf16[1024,256]{0,1:T(8,128)(2,1)S(1)} %bitcast.169), kind=kOutput, calls=%fused_computation.27 | convolution fusion | flops 1611399168 | bytes 8388608 | tf_op jit(solution)/shard_map/dot_general | solution.py:199
  173.3 1.9 constant_dynamic-slice_fusion
  175.2 32.4 %reduce-scatter.2.cloned.1.call-done = bf16[768,256]{1,0:T(8,128)(2,1)} async-done(((bf16[3072,256]{1,0:T(8,128)(2,1)}), bf16[768,256]{1,0:T(8,128)(2,1)}) %reduce-scatter.2.cloned.1.call-update) | async-done | bytes 393232 | tf_op jit(solution)/shard_map/reduce_scatter | solution.py:198
  207.6 1.9 convert_element_type.100
  (87 shorter events, 10.5 us)
Async XLA Ops:
  7.2 130.6 %copy-start = (bf16[3,1024,256]{2,1,0:T(8,128)(2,1)S(1)}, bf16[3,1024,256]{2,1,0:T(8,128)(2,1)}, u32[]{:S(2)}) copy-start(bf16[3,1024,256]{2,1,0:T(8,128)(2,1)} %param.21) | copy-start | bytes 4718596
  7.2 9.6 %copy-start.9 = (f32[3,1024]{1,0:T(4,128)S(1)}, f32[3,1024]{1,0:T(4,128)}, u32[]{:S(2)}) copy-start(f32[3,1024]{1,0:T(4,128)} %param.14) | copy-start | bytes 36868
  7.2 68.6 %all-gather.6.cloned.1.call-start = ((), (), s32[]{:S(2)}) async-start(), calls=%async_computation.1 | async-start | bytes 3932160 | tf_op jit(solution)/shard_map/all_gather | solution.py:104
  7.9 106.6 %all-gather.10.cloned.1.call-start = ((), (), s32[]{:S(2)}) async-start(), calls=%async_computation.4 | async-start | bytes 1310720 | tf_op jit(solution)/shard_map/all_gather | solution.py:123
  9.2 33.7 %collective-permute-start = (bf16[256,1024]{1,0:T(8,128)(2,1)S(1)}, bf16[256,1024]{1,0:T(8,128)(2,1)}, u32[]{:S(2)}, u32[]{:S(2)}) collective-permute-start(bf16[256,1024]{1,0:T(8,128)(2,1)S(1)} %bitcast.137), channel_id=1, source_target_pairs={{0,3},{1,0},{2,1},{3,2},{4,7},{5,4},{6,5},{7,6},{8,11},{9,8},{10,9... | collective-permute-start | bytes 1572872 | tf_op jit(solution)/shard_map/ppermute | solution.py:33
  11.7 31.2 %collective-permute-start.1 = (bf16[256,1024]{1,0:T(8,128)(2,1)S(1)}, bf16[256,1024]{1,0:T(8,128)(2,1)}, u32[]{:S(2)}, u32[]{:S(2)}) collective-permute-start(bf16[256,1024]{1,0:T(8,128)(2,1)S(1)} %bitcast.138), channel_id=1, source_target_pairs={{0,2},{1,3},{2,0},{3,1},{4,6},{5,7},{6,4},{7,5},{8,10},{9,11},{10,... | collective-permute-start | bytes 1572872 | tf_op jit(solution)/shard_map/ppermute | solution.py:33
  12.3 30.6 %collective-permute-start.2 = (bf16[256,1024]{1,0:T(8,128)(2,1)S(1)}, bf16[256,1024]{1,0:T(8,128)(2,1)}, u32[]{:S(2)}, u32[]{:S(2)}) collective-permute-start(bf16[256,1024]{1,0:T(8,128)(2,1)S(1)} %bitcast.139), channel_id=1, source_target_pairs={{0,1},{1,2},{2,3},{3,0},{4,5},{5,6},{6,7},{7,4},{8,9},{9,10},{10,1... | collective-permute-start | bytes 1572872 | tf_op jit(solution)/shard_map/ppermute | solution.py:33
  12.5 46.3 %collective-permute-start.3 = (bf16[256,1024]{1,0:T(8,128)(2,1)}, bf16[256,1024]{1,0:T(8,128)(2,1)S(1)}, u32[]{:S(2)}, u32[]{:S(2)}) collective-permute-start(bf16[256,1024]{1,0:T(8,128)(2,1)} %param.19), channel_id=1, source_target_pairs={{0,3},{1,0},{2,1},{3,2},{4,7},{5,4},{6,5},{7,6},{8,11},{9,8},{10,9... | collective-permute-start | bytes 1572872 | tf_op jit(solution)/shard_map/ppermute | solution.py:33
  14.0 44.7 %collective-permute-start.4 = (bf16[256,1024]{1,0:T(8,128)(2,1)}, bf16[256,1024]{1,0:T(8,128)(2,1)}, u32[]{:S(2)}, u32[]{:S(2)}) collective-permute-start(bf16[256,1024]{1,0:T(8,128)(2,1)} %param.19), channel_id=1, source_target_pairs={{0,2},{1,3},{2,0},{3,1},{4,6},{5,7},{6,4},{7,5},{8,10},{9,11},{10,... | collective-permute-start | bytes 1572872 | tf_op jit(solution)/shard_map/ppermute | solution.py:33
  39.7 3.2 %copy-start.8 = (bf16[256,1024]{1,0:T(8,128)(2,1)S(1)}, bf16[256,1024]{1,0:T(8,128)(2,1)}, u32[]{:S(2)}) copy-start(bf16[256,1024]{1,0:T(8,128)(2,1)} %param.19) | copy-start | bytes 1572868
  42.9 15.9 %collective-permute-start.5 = (bf16[256,1024]{1,0:T(8,128)(2,1)S(1)}, bf16[256,1024]{1,0:T(8,128)(2,1)}, u32[]{:S(2)}, u32[]{:S(2)}) collective-permute-start(bf16[256,1024]{1,0:T(8,128)(2,1)S(1)} %copy-done.8), channel_id=1, source_target_pairs={{0,1},{1,2},{2,3},{3,0},{4,5},{5,6},{6,7},{7,4},{8,9},{9,10},{10,1... | collective-permute-start | bytes 1572872 | tf_op jit(solution)/shard_map/ppermute | solution.py:33
  83.9 2.0 copy-start.2
  87.6 68.7 %all-gather.8.cloned.1.call-start = ((), (), s32[]{:S(2)}) async-start(), calls=%async_computation.2 | async-start | bytes 1966080 | tf_op jit(solution)/shard_map/all_gather | solution.py:138
  90.7 26.8 %copy-start.10 = (f32[2,1024]{1,0:T(2,128)S(1)}, f32[2,1024]{1,0:T(2,128)}, u32[]{:S(2)}) copy-start(f32[2,1024]{1,0:T(2,128)} %param.20) | copy-start | bytes 24580
  116.6 7.2 %collective-permute-start.6 = (bf16[256,512]{1,0:T(8,128)(2,1)S(1)}, bf16[256,512]{1,0:T(8,128)(2,1)S(1)}, u32[]{:S(2)}, u32[]{:S(2)}) collective-permute-start(bf16[256,512]{1,0:T(8,128)(2,1)S(1)} %bitcast.132), channel_id=1, source_target_pairs={{0,3},{1,0},{2,1},{3,2},{4,7},{5,4},{6,5},{7,6},{8,11},{9,8},{10,9... | collective-permute-start | bytes 786440 | tf_op jit(solution)/shard_map/ppermute | solution.py:33
  117.5 13.3 %collective-permute-start.7 = (bf16[256,512]{1,0:T(8,128)(2,1)S(1)}, bf16[256,512]{1,0:T(8,128)(2,1)S(1)}, u32[]{:S(2)}, u32[]{:S(2)}) collective-permute-start(bf16[256,512]{1,0:T(8,128)(2,1)S(1)} %bitcast.133), channel_id=1, source_target_pairs={{0,2},{1,3},{2,0},{3,1},{4,6},{5,7},{6,4},{7,5},{8,10},{9,11},{10,... | collective-permute-start | bytes 786440 | tf_op jit(solution)/shard_map/ppermute | solution.py:33
  119.0 12.5 %collective-permute-start.8 = (bf16[256,512]{1,0:T(8,128)(2,1)S(1)}, bf16[256,512]{1,0:T(8,128)(2,1)S(1)}, u32[]{:S(2)}, u32[]{:S(2)}) collective-permute-start(bf16[256,512]{1,0:T(8,128)(2,1)S(1)} %bitcast.135), channel_id=1, source_target_pairs={{0,1},{1,2},{2,3},{3,0},{4,5},{5,6},{6,7},{7,4},{8,9},{9,10},{10,1... | collective-permute-start | bytes 786440 | tf_op jit(solution)/shard_map/ppermute | solution.py:33
  119.2 88.4 %reduce-scatter.2.cloned.1.call-start = ((), (), s32[]{:S(2)}) async-start(), calls=%async_computation.3 | async-start | bytes 1966080 | tf_op jit(solution)/shard_map/reduce_scatter | solution.py:198
  132.2 4.2 %copy-start.3 = (bf16[4,256,1024]{2,1,0:T(8,128)(2,1)S(1)}, bf16[4,256,1024]{2,1,0:T(8,128)(2,1)}, u32[]{:S(2)}) copy-start(bf16[4,256,1024]{2,1,0:T(8,128)(2,1)} %fusion.14) | copy-start | bytes 6291460
  132.2 4.2 %copy-start.6 = (bf16[512,1024]{1,0:T(8,128)(2,1)S(1)}, bf16[512,1024]{1,0:T(8,128)(2,1)}, u32[]{:S(2)}) copy-start(bf16[512,1024]{1,0:T(8,128)(2,1)} %param.17) | copy-start | bytes 3145732
  139.5 7.2 %copy-start.11 = (s32[1024]{0:T(1024)S(1)}, s32[1024]{0:T(1024)}, u32[]{:S(2)}) copy-start(s32[1024]{0:T(1024)} %param.15) | copy-start | bytes 12292
  139.6 7.2 %copy-start.13 = (f32[64]{0:T(128)S(1)}, f32[64]{0:T(128)}, u32[]{:S(2)}) copy-start(f32[64]{0:T(128)} %param.16) | copy-start | bytes 772
  139.6 8.8 %copy-start.5 = (bf16[1024,1024]{1,0:T(8,128)(2,1)S(1)}, bf16[1024,1024]{1,0:T(8,128)(2,1)}, u32[]{:S(2)}) copy-start(bf16[1024,1024]{1,0:T(8,128)(2,1)} %bitcast_select_fusion) | copy-start | bytes 6291460
  140.1 6.7 %collective-permute-start.10 = (bf16[256,512]{1,0:T(8,128)(2,1)S(1)}, bf16[256,512]{1,0:T(8,128)(2,1)S(1)}, u32[]{:S(2)}, u32[]{:S(2)}) collective-permute-start(bf16[256,512]{1,0:T(8,128)(2,1)S(1)} %bitcast.166), channel_id=1, source_target_pairs={{0,2},{1,3},{2,0},{3,1},{4,6},{5,7},{6,4},{7,5},{8,10},{9,11},{10,... | collective-permute-start | bytes 786440 | tf_op jit(solution)/shard_map/ppermute | solution.py:66
  141.4 5.6 %collective-permute-start.9 = (bf16[256,512]{1,0:T(8,128)(2,1)S(1)}, bf16[256,512]{1,0:T(8,128)(2,1)S(1)}, u32[]{:S(2)}, u32[]{:S(2)}) collective-permute-start(bf16[256,512]{1,0:T(8,128)(2,1)S(1)} %bitcast.167), channel_id=1, source_target_pairs={{0,1},{1,0},{2,3},{3,2},{4,5},{5,4},{6,7},{7,6},{8,9},{9,8},{10,11... | collective-permute-start | bytes 786440 | tf_op jit(solution)/shard_map/ppermute | solution.py:65
  146.8 1.5 collective-permute-start.11
  146.9 4.1 %copy-start.7 = (bf16[2,1024,256]{2,1,0:T(8,128)(2,1)S(1)}, bf16[2,1024,256]{2,1,0:T(8,128)(2,1)}, u32[]{:S(2)}) copy-start(bf16[2,1024,256]{2,1,0:T(8,128)(2,1)} %param.23) | copy-start | bytes 3145732
  149.7 1.4 copy-start.4
  161.3 0.9 copy-start.12
  163.1 1.2 collective-permute-start.12
  164.4 3.6 %collective-permute-start.13 = (f32[1024]{0:T(1024)S(1)}, f32[1024]{0:T(1024)S(1)}, u32[]{:S(2)}, u32[]{:S(2)}) collective-permute-start(f32[1024]{0:T(1024)S(1)} %add.82), channel_id=1, source_target_pairs={{0,2},{1,3},{2,0},{3,1},{4,6},{5,7},{6,4},{7,5},{8,10},{9,11},{10,... | collective-permute-start | bytes 12296 | tf_op jit(solution)/shard_map/ppermute | solution.py:61
  165.8 4.0 %slice-start = ((s8[6291456]{0:T(1024)(128)(4,1)}), s8[4194304]{0:T(1024)(128)(4,1)S(1)}, s32[]{:S(2)}) async-start(s8[6291456]{0:T(1024)(128)(4,1)} %bitcast.128), calls=%async_computation.5 | async-start | bytes 8388608
  168.6 1.6 slice-start.1
  170.2 39.4 %copy-start.1 = (bf16[3,1024,256]{2,1,0:T(8,128)(2,1)S(1)}, bf16[3,1024,256]{2,1,0:T(8,128)(2,1)}, u32[]{:S(2)}) copy-start(bf16[3,1024,256]{2,1,0:T(8,128)(2,1)} %param.21) | copy-start | bytes 4718596
Sparse Core Ops, SparseCore 0:
  9.6 66.1 all-gather.5
  87.7 26.8 all-gather.9
  119.3 36.8 all-gather.7
  173.4 34.1 reduce-scatter.1

commit v17 on v13

--- a/solution.py
+++ b/solution.py
@@ -104,7 +104,8 @@
     numer = jnp.einsum(
         "hlt,thc->hlc", expo.astype(jnp.bfloat16), values, preferred_element_type=jnp.float32
     )
-    all_numer = lax.all_gather(numer.astype(jnp.bfloat16), "picks", axis=0, tiled=False)
+    part = numer.astype(jnp.bfloat16)
+    all_numer = ring_gather(part[None], "picks", n_picks)
     all_stats = lax.all_gather(jnp.stack([top, total]), "picks", axis=0, tiled=False)
     best = jnp.max(all_stats[:, 0], axis=0)
     factor = jnp.exp(all_stats[:, 0] - best[None])

time: 216 us -> 217 us (level)
  blocking collectives: 13.3 us -> 28.7 us
  waiting for transfers between devices: 97 us -> 83.1 us
  starting transfers between devices: 10.7 us -> 14.1 us
    all_gather x1, blocking collectives: 13.3 us -> 28.7 us  [on_device(): lax.all_gather(jnp.stack([top, total]), 'picks', axis=0, tiled=False)]
    all_gather x1 -> x0, waiting for transfers between devices: 7.77 us -> none  [on_device(): lax.all_gather(numer.astype(jnp.bfloat16), 'picks', axis=0, tiled=False)]
    ppermute x12 -> x15, waiting for transfers between devices: 38.8 us -> 35.3 us  [ring_gather(): blocks.append(lax.ppermute(x, axis, [(i, (i - s) % n) for i in range(n)]))]
    ppermute x12 -> x15, starting transfers between devices: 9.4 us -> 12.2 us  [ring_gather(): blocks.append(lax.ppermute(x, axis, [(i, (i - s) % n) for i in range(n)]))]
    unnamed x34 -> x36, local copies, waits for them, and re-layouts: 5.17 us -> 3.36 us
  transfers between devices with their start and end apart: 18 -> 20, of which waited for: 13 -> 10; matrix products, arithmetic and copies ran while one was open for 28% -> 23% of each run, Pallas kernels for 0% -> 0%
where the time goes in v17:
time: 217 us
  waiting for transfers between devices  83.1 us (38%)
  other arithmetic  44.3 us (20%)
  blocking collectives  28.7 us (13%)
  matrix products  26.1 us (12%)
  between operations  14.2 us (7%)
  starting transfers between devices  14.1 us (6%)
  local copies, waits for them, and re-layouts  6.61 us (3%)
    ppermute x15, waiting for transfers between devices, ring_gather(): blocks.append(lax.ppermute(x, axis, [(i, (i - s) % n) for i in range(n)]))  35.3 us
    reduce_scatter x1, waiting for transfers between devices, on_device(): lax.psum_scatter(jnp.dot(enc.T, dquery, preferred_element_type=jnp.float3...  32 us
    all_gather x1, blocking collectives, on_device(): lax.all_gather(jnp.stack([top, total]), 'picks', axis=0, tiled=False)  28.7 us
    another operation x1, other arithmetic  22.8 us
    concatenate x4, other arithmetic, ring_gather(): ordered = jnp.roll(flipped, idx, axis=0)  12.9 us
    all_gather x1, waiting for transfers between devices, on_device(): piece = lax.all_gather(kv_weight, 'picks', axis=0, tiled=True)  12.8 us
    ppermute x15, starting transfers between devices, ring_gather(): blocks.append(lax.ppermute(x, axis, [(i, (i - s) % n) for i in range(n)]))  12.2 us
    dot_general x1, matrix products, on_device(): jnp.einsum('tf,fjc->tjc', enc, piece, preferred_element_type=jnp.float32)  7.15 us
  transfers between devices with their start and end apart: 20, of which 10 were waited for; matrix products, arithmetic and copies ran while one was open for 23% of the time, Pallas kernels for 0%

profile of v17, /device:TPU:0, one launch (start us, length us, event | category | flops | bytes accessed | tf_op | source)
XLA Modules:
  0.0 217.1 jit_solution(16055427302016570836)
XLA Ops:
  7.2 0.7 all-gather.4.cloned.1.call-update
  8.0 1.2 copy.60
  9.2 2.4 %collective-permute-start = (bf16[256,1024]{1,0:T(8,128)(2,1)S(1)}, bf16[256,1024]{1,0:T(8,128)(2,1)}, u32[]{:S(2)}, u32[]{:S(2)}) collective-permute-start(bf16[256,1024]{1,0:T(8,128)(2,1)S(1)} %bitcast.138), channel_id=1, source_target_pairs={{0,3},{1,0},{2,1},{3,2},{4,7},{5,4},{6,5},{7,6},{8,11},{9,8},{10,9... | collective-permute-start | bytes 1572872 | tf_op jit(solution)/shard_map/ppermute | solution.py:33
  11.7 0.6 collective-permute-start.1
  12.5 1.6 collective-permute-start.3
  14.0 1.4 collective-permute-start.4
  15.5 1.0 constant_dynamic-slice_fusion.1
  16.7 22.8 %fusion = (bf16[3,512,1024]{2,1,0:T(8,128)(2,1)S(1)}, bf16[3,512,1024]{2,1,0:T(8,128)(2,1)S(1)}) fusion(f32[3,1024]{1,0:T(4,128)S(1)} %copy-done.7, f32[512]{0:T(512)S(1)} %maximum_multiply_fusion), kind=kLoop, calls=%fused_computation.2 | loop fusion | flops 4718592 | bytes 6305792 | tf_op jit(solution)/shard_map/convert
  39.5 3.2 %pad_maximum_fusion = bf16[6,512,1024]{2,1,0:T(8,128)(2,1)} fusion(bf16[3,512,1024]{2,1,0:T(8,128)(2,1)S(1)} %get-tuple-element.29, bf16[3,512,1024]{2,1,0:T(8,128)(2,1)S(1)} %get-tuple-element.28), kind=kLoop, calls=%fused_computation.4 | loop fusion | flops 3145728 | bytes 12582912 | tf_op jit(solution)/shard_map/concatenate | solution.py:21
  42.8 5.0 %fusion.21 = bf16[4,256,1024]{2,1,0:T(8,128)(2,1)} fusion(s32[]{:T(128)S(6)} %select_n.39, bf16[1,256,1024]{2,1,0:T(8,128)(2,1)S(1)} %bitcast.141, bf16[1,256,1024]{2,1,0:T(8,128)(2,1)} %bitcast.4, bf16[1,256,1024]{2,1,0:T(8,128)(2,1)} %bitcast.5, bf16[1,256,1024]{2,1,0:T(8,128)(2,1)} %bitcast.6), kind=kLoop, calls=%fused_computation.45 | loop fusion | flops 7340032 | bytes 4194308 | tf_op jit(solution)/shard_map/jit(_roll_dynamic)/concatenate | solution.py:35
  47.8 10.8 %collective-permute-done.4 = bf16[256,1024]{1,0:T(8,128)(2,1)} collective-permute-done((bf16[256,1024]{1,0:T(8,128)(2,1)}, bf16[256,1024]{1,0:T(8,128)(2,1)}, u32[]{:S(2)}, u32[]{:S(2)}) %collective-permute-start.4) | collective-permute-done | bytes 524320 | tf_op jit(solution)/shard_map/ppermute | solution.py:33
  58.6 4.4 %fusion.14 = bf16[4,256,1024]{2,1,0:T(8,128)(2,1)} fusion(s32[]{:T(128)S(6)} %select_n.39, bf16[1,256,1024]{2,1,0:T(8,128)(2,1)S(1)} %bitcast.156, bf16[1,256,1024]{2,1,0:T(8,128)(2,1)S(1)} %bitcast.157, bf16[1,256,1024]{2,1,0:T(8,128)(2,1)} %bitcast.14, bf16[1,256,1024]{2,1,0:T(8,128)(2,1)S(1)} %bitcast.158), kind=kLoop, calls=%fused_computation.38 | loop fusion | flops 7340032 | bytes 4194308 | tf_op jit(solution)/shard_map/jit(_roll_dynamic)/concatenate | solution.py:35
  63.0 12.8 %all-gather.4.cloned.1.call-done = bf16[3072,2,256]{2,1,0:T(2,128)(2,1)} async-done(((bf16[768,2,256]{2,1,0:T(2,128)(2,1)}), bf16[3072,2,256]{2,1,0:T(2,128)(2,1)}) %all-gather.4.cloned.1.call-update) | async-done | bytes 3145744 | tf_op jit(solution)/shard_map/all_gather | solution.py:92
  75.9 7.1 %fusion.32 = bf16[1024,2,256]{0,2,1:T(8,128)(2,1)S(1)} fusion(bf16[3072,1024,1]{1,0,2:T(8,128)(2,1)} %bitcast.132, bf16[3072,2,256]{2,1,0:T(2,128)(2,1)} %all-gather.4.cloned.1.call-done), kind=kOutput, calls=%fused_computation.81 | convolution fusion | flops 3221749760 | bytes 10485760 | tf_op jit(solution)/shard_map/tf,fjc->tjc/dot_general | solution.py:94
  83.1 0.8 multiply_reduce_fusion.1
  83.9 0.9 fusion.4
  84.9 0.9 bitcast_dynamic-update-slice_fusion.6
  85.8 0.8 collective-permute-start.6
  87.0 1.9 collective-permute-start.8
  88.9 28.7 %all-gather = f32[8,2,512]{2,1,0:T(2,128)S(1)} all-gather(f32[2,2,512]{2,1,0:T(2,128)S(1)} %pad_maximum_fusion.1), channel_id=2, replica_groups=mesh['groups'=2,'picks'=4,'heads'=4] {'picks'}, dimensions={0}, use_global_device_ids=true | all-gather | bytes 40960 | tf_op jit(solution)/shard_map/all_gather | solution.py:109
  118.0 0.7 multiply_reduce_fusion.2
  119.1 1.8 collective-permute-start.10
  121.4 3.1 %collective-permute-done.9 = bf16[256,512]{1,0:T(8,128)(2,1)S(1)} collective-permute-done((bf16[256,512]{1,0:T(8,128)(2,1)S(1)}, bf16[256,512]{1,0:T(8,128)(2,1)S(1)}, u32[]{:S(2)}, u32[]{:S(2)}) %collective-permute-start.9) | collective-permute-done | bytes 262176 | tf_op jit(solution)/shard_map/ppermute | solution.py:33
  124.5 8.9 %collective-permute-done.10 = bf16[256,512]{1,0:T(8,128)(2,1)S(1)} collective-permute-done((bf16[256,512]{1,0:T(8,128)(2,1)S(1)}, bf16[256,512]{1,0:T(8,128)(2,1)S(1)}, u32[]{:S(2)}, u32[]{:S(2)}) %collective-permute-start.10) | collective-permute-done | bytes 262176 | tf_op jit(solution)/shard_map/ppermute | solution.py:33
  133.5 2.2 %fusion.60 = bf16[4,256,512]{2,1,0:T(8,128)(2,1)S(1)} fusion(s32[]{:T(128)S(6)} %select_n.39, bf16[1,256,512]{2,1,0:T(8,128)(2,1)S(1)} %bitcast.147, bf16[1,256,512]{2,1,0:T(8,128)(2,1)S(1)} %bitcast.161, bf16[1,256,512]{2,1,0:T(8,128)(2,1)S(1)} %bitcast.162, bf16[1,256,512]{2,1,0:T(8,128)(2,1)} %bitcast.37), kind=kLoop, calls=%fused_computation.103 | loop fusion | flops 3670016 | bytes 2097156 | tf_op jit(solution)/shard_map/jit(_roll_dynamic)/concatenate | solution.py:35
  135.7 1.4 multiply_reduce_fusion.4
  137.1 1.1 fusion.38
  139.4 0.6 collective-permute-start.13
  140.4 5.7 %collective-permute-done.12 = bf16[256,512]{1,0:T(8,128)(2,1)S(1)} collective-permute-done((bf16[256,512]{1,0:T(8,128)(2,1)S(1)}, bf16[256,512]{1,0:T(8,128)(2,1)S(1)}, u32[]{:S(2)}, u32[]{:S(2)}) %collective-permute-start.12) | collective-permute-done | bytes 262176 | tf_op jit(solution)/shard_map/ppermute | solution.py:33
  146.0 5.7 %collective-permute-done.13 = bf16[256,512]{1,0:T(8,128)(2,1)S(1)} collective-permute-done((bf16[256,512]{1,0:T(8,128)(2,1)S(1)}, bf16[256,512]{1,0:T(8,128)(2,1)S(1)}, u32[]{:S(2)}, u32[]{:S(2)}) %collective-permute-start.13) | collective-permute-done | bytes 262176 | tf_op jit(solution)/shard_map/ppermute | solution.py:33
  151.8 1.0 collective-permute-done.14
  152.8 1.2 fusion.53
  154.0 1.4 multiply_reduce_fusion.3
  155.4 1.3 copy-done.2
  156.8 0.8 fusion.42
  157.7 5.1 %convolution_convert_fusion.2 = bf16[1024,256]{0,1:T(8,128)(2,1)S(1)} fusion(bf16[3072,1024]{1,0:T(8,128)(2,1)} %bitcast.133, bf16[3072,256]{1,0:T(8,128)(2,1)} %all-gather.6.cloned.1.call-done), kind=kOutput, calls=%fused_computation.84 | convolution fusion | flops 1610874880 | bytes 8388608 | tf_op jit(solution)/shard_map/dot_general | solution.py:159
  162.8 0.8 fusion.3
  163.6 1.0 fusion.39
  164.9 0.9 collective-permute-done.15
  165.9 1.5 collective-permute-start.16
  167.3 0.9 multiply_reduce_fusion
  168.2 1.3 collective-permute-done.16
  169.5 0.6 subtract_multiply_fusion
  170.1 1.2 multiply_convert_fusion.4
  171.7 3.1 %convolution_convert_fusion = bf16[3072,256]{1,0:T(8,128)(2,1)} fusion(bf16[3072,1024]{1,0:T(8,128)(2,1)S(1)} %bitcast.136, bf16[1024,256]{0,1:T(8,128)(2,1)S(1)} %bitcast.185), kind=kOutput, calls=%fused_computation.26 | convolution fusion | flops 1611399168 | bytes 8388608 | tf_op jit(solution)/shard_map/dot_general | solution.py:185
  174.8 1.9 constant_dynamic-slice_fusion
  176.7 32.0 %reduce-scatter.2.cloned.1.call-done = bf16[768,256]{1,0:T(8,128)(2,1)} async-done(((bf16[3072,256]{1,0:T(8,128)(2,1)}), bf16[768,256]{1,0:T(8,128)(2,1)}) %reduce-scatter.2.cloned.1.call-update) | async-done | bytes 393232 | tf_op jit(solution)/shard_map/reduce_scatter | solution.py:184
  208.7 1.9 convert_element_type.100
  (78 shorter events, 4.3 us)
Async XLA Ops:
  7.2 129.9 %copy-start = (bf16[3,1024,256]{2,1,0:T(8,128)(2,1)S(1)}, bf16[3,1024,256]{2,1,0:T(8,128)(2,1)}, u32[]{:S(2)}) copy-start(bf16[3,1024,256]{2,1,0:T(8,128)(2,1)} %param.23) | copy-start | bytes 4718596
  7.2 9.5 %copy-start.7 = (f32[3,1024]{1,0:T(4,128)S(1)}, f32[3,1024]{1,0:T(4,128)}, u32[]{:S(2)}) copy-start(f32[3,1024]{1,0:T(4,128)} %param.16) | copy-start | bytes 36868
  7.2 68.7 %all-gather.4.cloned.1.call-start = ((), (), s32[]{:S(2)}) async-start(), calls=%async_computation.1 | async-start | bytes 3932160 | tf_op jit(solution)/shard_map/all_gather | solution.py:92
  7.9 149.8 %all-gather.6.cloned.1.call-start = ((), (), s32[]{:S(2)}) async-start(), calls=%async_computation.2 | async-start | bytes 1966080 | tf_op jit(solution)/shard_map/all_gather | solution.py:125
  9.2 33.5 %collective-permute-start = (bf16[256,1024]{1,0:T(8,128)(2,1)S(1)}, bf16[256,1024]{1,0:T(8,128)(2,1)}, u32[]{:S(2)}, u32[]{:S(2)}) collective-permute-start(bf16[256,1024]{1,0:T(8,128)(2,1)S(1)} %bitcast.138), channel_id=1, source_target_pairs={{0,3},{1,0},{2,1},{3,2},{4,7},{5,4},{6,5},{7,6},{8,11},{9,8},{10,9... | collective-permute-start | bytes 1572872 | tf_op jit(solution)/shard_map/ppermute | solution.py:33
  11.7 31.1 %collective-permute-start.1 = (bf16[256,1024]{1,0:T(8,128)(2,1)S(1)}, bf16[256,1024]{1,0:T(8,128)(2,1)}, u32[]{:S(2)}, u32[]{:S(2)}) collective-permute-start(bf16[256,1024]{1,0:T(8,128)(2,1)S(1)} %bitcast.139), channel_id=1, source_target_pairs={{0,2},{1,3},{2,0},{3,1},{4,6},{5,7},{6,4},{7,5},{8,10},{9,11},{10,... | collective-permute-start | bytes 1572872 | tf_op jit(solution)/shard_map/ppermute | solution.py:33
  12.3 30.5 %collective-permute-start.2 = (bf16[256,1024]{1,0:T(8,128)(2,1)S(1)}, bf16[256,1024]{1,0:T(8,128)(2,1)}, u32[]{:S(2)}, u32[]{:S(2)}) collective-permute-start(bf16[256,1024]{1,0:T(8,128)(2,1)S(1)} %bitcast.140), channel_id=1, source_target_pairs={{0,1},{1,2},{2,3},{3,0},{4,5},{5,6},{6,7},{7,4},{8,9},{9,10},{10,1... | collective-permute-start | bytes 1572872 | tf_op jit(solution)/shard_map/ppermute | solution.py:33
  12.5 35.3 %collective-permute-start.3 = (bf16[256,1024]{1,0:T(8,128)(2,1)}, bf16[256,1024]{1,0:T(8,128)(2,1)S(1)}, u32[]{:S(2)}, u32[]{:S(2)}) collective-permute-start(bf16[256,1024]{1,0:T(8,128)(2,1)} %param.21), channel_id=1, source_target_pairs={{0,3},{1,0},{2,1},{3,2},{4,7},{5,4},{6,5},{7,6},{8,11},{9,8},{10,9... | collective-permute-start | bytes 1572872 | tf_op jit(solution)/shard_map/ppermute | solution.py:33
  14.0 44.6 %collective-permute-start.4 = (bf16[256,1024]{1,0:T(8,128)(2,1)}, bf16[256,1024]{1,0:T(8,128)(2,1)}, u32[]{:S(2)}, u32[]{:S(2)}) collective-permute-start(bf16[256,1024]{1,0:T(8,128)(2,1)} %param.21), channel_id=1, source_target_pairs={{0,2},{1,3},{2,0},{3,1},{4,6},{5,7},{6,4},{7,5},{8,10},{9,11},{10,... | collective-permute-start | bytes 1572872 | tf_op jit(solution)/shard_map/ppermute | solution.py:33
  39.5 3.2 %copy-start.6 = (bf16[256,1024]{1,0:T(8,128)(2,1)S(1)}, bf16[256,1024]{1,0:T(8,128)(2,1)}, u32[]{:S(2)}) copy-start(bf16[256,1024]{1,0:T(8,128)(2,1)} %param.21) | copy-start | bytes 1572868
  42.8 15.9 %collective-permute-start.5 = (bf16[256,1024]{1,0:T(8,128)(2,1)S(1)}, bf16[256,1024]{1,0:T(8,128)(2,1)S(1)}, u32[]{:S(2)}, u32[]{:S(2)}) collective-permute-start(bf16[256,1024]{1,0:T(8,128)(2,1)S(1)} %copy-done.6), channel_id=1, source_target_pairs={{0,1},{1,2},{2,3},{3,0},{4,5},{5,6},{6,7},{7,4},{8,9},{9,10},{10,1... | collective-permute-start | bytes 1572872 | tf_op jit(solution)/shard_map/ppermute | solution.py:33
  85.8 31.9 %collective-permute-start.6 = (bf16[1,2,512,128]{3,2,1,0:T(8,128)(2,1)S(1)}, bf16[1,2,512,128]{3,2,1,0:T(8,128)(2,1)S(1)}, u32[]{:S(2)}, u32[]{:S(2)}) collective-permute-start(bf16[1,2,512,128]{3,2,1,0:T(8,128)(2,1)S(1)} %bitcast.170), channel_id=1, source_target_pairs={{0,12},{4,0},{8,4},{12,8},{1,13},{5,1},{9,5},{13,9},{2,14},{6,2},{... | collective-permute-start | bytes 786440 | tf_op jit(solution)/shard_map/ppermute | solution.py:33
  86.6 31.2 %collective-permute-start.7 = (bf16[1,2,512,128]{3,2,1,0:T(8,128)(2,1)S(1)}, bf16[1,2,512,128]{3,2,1,0:T(8,128)(2,1)S(1)}, u32[]{:S(2)}, u32[]{:S(2)}) collective-permute-start(bf16[1,2,512,128]{3,2,1,0:T(8,128)(2,1)S(1)} %bitcast.171), channel_id=1, source_target_pairs={{0,8},{4,12},{8,0},{12,4},{1,9},{5,13},{9,1},{13,5},{2,10},{6,14},... | collective-permute-start | bytes 786440 | tf_op jit(solution)/shard_map/ppermute | solution.py:33
  87.0 30.8 %collective-permute-start.8 = (bf16[1,2,512,128]{3,2,1,0:T(8,128)(2,1)S(1)}, bf16[1,2,512,128]{3,2,1,0:T(8,128)(2,1)S(1)}, u32[]{:S(2)}, u32[]{:S(2)}) collective-permute-start(bf16[1,2,512,128]{3,2,1,0:T(8,128)(2,1)S(1)} %bitcast.172), channel_id=1, source_target_pairs={{0,4},{4,8},{8,12},{12,0},{1,5},{5,9},{9,13},{13,1},{2,6},{6,10},{... | collective-permute-start | bytes 786440 | tf_op jit(solution)/shard_map/ppermute | solution.py:33
  118.0 3.1 %copy-start.8 = (f32[2,1024]{1,0:T(2,128)S(1)}, f32[2,1024]{1,0:T(2,128)}, u32[]{:S(2)}) copy-start(f32[2,1024]{1,0:T(2,128)} %param.22) | copy-start | bytes 24580
  119.0 16.7 %copy-start.4 = (bf16[512,1024]{1,0:T(8,128)(2,1)S(1)}, bf16[512,1024]{1,0:T(8,128)(2,1)}, u32[]{:S(2)}) copy-start(bf16[512,1024]{1,0:T(8,128)(2,1)} %param.19) | copy-start | bytes 3145732
  119.0 5.5 %collective-permute-start.9 = (bf16[256,512]{1,0:T(8,128)(2,1)S(1)}, bf16[256,512]{1,0:T(8,128)(2,1)S(1)}, u32[]{:S(2)}, u32[]{:S(2)}) collective-permute-start(bf16[256,512]{1,0:T(8,128)(2,1)S(1)} %bitcast.144), channel_id=1, source_target_pairs={{0,3},{1,0},{2,1},{3,2},{4,7},{5,4},{6,5},{7,6},{8,11},{9,8},{10,9... | collective-permute-start | bytes 786440 | tf_op jit(solution)/shard_map/ppermute | solution.py:33
  119.1 14.3 %collective-permute-start.10 = (bf16[256,512]{1,0:T(8,128)(2,1)S(1)}, bf16[256,512]{1,0:T(8,128)(2,1)S(1)}, u32[]{:S(2)}, u32[]{:S(2)}) collective-permute-start(bf16[256,512]{1,0:T(8,128)(2,1)S(1)} %bitcast.145), channel_id=1, source_target_pairs={{0,2},{1,3},{2,0},{3,1},{4,6},{5,7},{6,4},{7,5},{8,10},{9,11},{10,... | collective-permute-start | bytes 786440 | tf_op jit(solution)/shard_map/ppermute | solution.py:33
  120.9 12.6 %collective-permute-start.11 = (bf16[256,512]{1,0:T(8,128)(2,1)S(1)}, bf16[256,512]{1,0:T(8,128)(2,1)}, u32[]{:S(2)}, u32[]{:S(2)}) collective-permute-start(bf16[256,512]{1,0:T(8,128)(2,1)S(1)} %bitcast.146), channel_id=1, source_target_pairs={{0,1},{1,2},{2,3},{3,0},{4,5},{5,6},{6,7},{7,4},{8,9},{9,10},{10,1... | collective-permute-start | bytes 786440 | tf_op jit(solution)/shard_map/ppermute | solution.py:33
  121.1 87.6 %reduce-scatter.2.cloned.1.call-start = ((), (), s32[]{:S(2)}) async-start(), calls=%async_computation.3 | async-start | bytes 1966080 | tf_op jit(solution)/shard_map/reduce_scatter | solution.py:184
  121.4 14.3 %copy-start.1 = (bf16[4,256,1024]{2,1,0:T(8,128)(2,1)S(1)}, bf16[4,256,1024]{2,1,0:T(8,128)(2,1)}, u32[]{:S(2)}) copy-start(bf16[4,256,1024]{2,1,0:T(8,128)(2,1)} %fusion.14) | copy-start | bytes 6291460
  138.8 1.4 copy-start.9
  138.8 1.4 copy-start.11
  139.4 14.6 %copy-start.3 = (bf16[4,256,1024]{2,1,0:T(8,128)(2,1)S(1)}, bf16[4,256,1024]{2,1,0:T(8,128)(2,1)}, u32[]{:S(2)}) copy-start(bf16[4,256,1024]{2,1,0:T(8,128)(2,1)} %fusion.21) | copy-start | bytes 6291460
  139.4 6.6 %collective-permute-start.12 = (bf16[256,512]{1,0:T(8,128)(2,1)S(1)}, bf16[256,512]{1,0:T(8,128)(2,1)S(1)}, u32[]{:S(2)}, u32[]{:S(2)}) collective-permute-start(bf16[256,512]{1,0:T(8,128)(2,1)S(1)} %bitcast.163), channel_id=1, source_target_pairs={{0,3},{1,0},{2,1},{3,2},{4,7},{5,4},{6,5},{7,6},{8,11},{9,8},{10,9... | collective-permute-start | bytes 786440 | tf_op jit(solution)/shard_map/ppermute | solution.py:33
  139.4 12.3 %collective-permute-start.13 = (bf16[256,512]{1,0:T(8,128)(2,1)S(1)}, bf16[256,512]{1,0:T(8,128)(2,1)S(1)}, u32[]{:S(2)}, u32[]{:S(2)}) collective-permute-start(bf16[256,512]{1,0:T(8,128)(2,1)S(1)} %bitcast.164), channel_id=1, source_target_pairs={{0,2},{1,3},{2,0},{3,1},{4,6},{5,7},{6,4},{7,5},{8,10},{9,11},{10,... | collective-permute-start | bytes 786440 | tf_op jit(solution)/shard_map/ppermute | solution.py:33
  140.1 12.7 %collective-permute-start.14 = (bf16[256,512]{1,0:T(8,128)(2,1)S(1)}, bf16[256,512]{1,0:T(8,128)(2,1)S(1)}, u32[]{:S(2)}, u32[]{:S(2)}) collective-permute-start(bf16[256,512]{1,0:T(8,128)(2,1)S(1)} %bitcast.165), channel_id=1, source_target_pairs={{0,1},{1,2},{2,3},{3,0},{4,5},{5,6},{6,7},{7,4},{8,9},{9,10},{10,1... | collective-permute-start | bytes 786440 | tf_op jit(solution)/shard_map/ppermute | solution.py:33
  154.0 2.8 %copy-start.5 = (bf16[2,1024,256]{2,1,0:T(8,128)(2,1)S(1)}, bf16[2,1024,256]{2,1,0:T(8,128)(2,1)}, u32[]{:S(2)}) copy-start(bf16[2,1024,256]{2,1,0:T(8,128)(2,1)} %param.25) | copy-start | bytes 3145732
  155.4 1.4 copy-start.2
  162.8 0.9 copy-start.10
  164.6 1.2 collective-permute-start.15
  165.9 3.6 %collective-permute-start.16 = (f32[1024]{0:T(1024)S(1)}, f32[1024]{0:T(1024)S(1)}, u32[]{:S(2)}, u32[]{:S(2)}) collective-permute-start(f32[1024]{0:T(1024)S(1)} %add.72), channel_id=1, source_target_pairs={{0,2},{1,3},{2,0},{3,1},{4,6},{5,7},{6,4},{7,5},{8,10},{9,11},{10,... | collective-permute-start | bytes 12296 | tf_op jit(solution)/shard_map/ppermute | solution.py:61
  167.3 4.0 %slice-start = ((s8[6291456]{0:T(1024)(128)(4,1)}), s8[4194304]{0:T(1024)(128)(4,1)S(1)}, s32[]{:S(2)}) async-start(s8[6291456]{0:T(1024)(128)(4,1)} %bitcast.134), calls=%async_computation.4 | async-start | bytes 8388608
  170.1 1.6 slice-start.1
Sparse Core Ops, SparseCore 0:
  9.6 66.2 all-gather.3
  121.2 35.3 all-gather.5
  174.9 33.6 reduce-scatter.1
